TPU v7x, 128 devices: a whole 4x4x4 slice. The times are simulated.
128 devices in a mesh: gx: 8 (over y, x_lo), gy: 16 (over x_hi, z, core).
Axes of the slice: x: 4 (x_hi: 2, x_lo: 2; x = x_hi * 2 + x_lo), y: 4, z: 4, core: 2. Of those that a mesh axis runs over, the one named last changes fastest.
Arguments:
- sources: float32 [2, 2, 1024, 2048], P(None, None, 'gx', 'gy'), may hold values from -9 to 9
- wavenumber: float32 [1024, 2048], P('gx', 'gy'), may hold values from 0.2 to 0.8
- row_inverse: float32 [32, 2, 64, 64], P('gy'), may hold values from -0.3 to 0.3
- col_inverse: float32 [16, 2, 64, 64], P('gx'), may hold values from -0.3 to 0.3
- reach_steps: int32 [8, 16, 4], P('gx', 'gy'), may hold values from 1 to 4, as said below
Outputs:
- fields: float32 [2, 2, 1024, 2048], P(None, None, 'gx', 'gy')
Inputs may be any that keep to these rules, and one draw needn't show every extreme that they name: `reach_steps`: every value occurs somewhere in every draw.
All inputs are finite; a program needn't handle non-finite values.
Results may differ from a plain program's by a relative error of at most 0.0003.
Values sent between devices are 32-bit elements; how exact they have to be, the bound alone decides.
No kernel may reach another device: no remote copies, remote signals or barrier semaphores. Data moves between devices by JAX's collectives and lax.ppermute only.
A program may use at most 64 MiB of HBM per device.

v0:
```python
import jax
import jax.numpy as jnp
from jax import lax
from jax.sharding import PartitionSpec as P
from jax.experimental import pallas as pl
from jax.experimental.pallas import tpu as pltpu

ITERS = 2
SWEEPS = 4


DAMPING = 0.5
ROBIN_COEF = 0.5


def with_halo(shard, sides, width):
    for axis, dim in sides:
        peers, length = (lax.axis_size(axis), shard.shape[dim])
        up = [(i, (i + 1) % peers) for i in range(peers - 1)]
        down = [(j, i) for i, j in up]
        last = lax.slice_in_dim(shard, length - width, length, axis=dim)
        first = lax.slice_in_dim(shard, 0, width, axis=dim)
        before = lax.ppermute(last, axis, up)
        after = lax.ppermute(first, axis, down)
        shard = jnp.concatenate([before, shard, after], axis=dim)
    return shard


def to_index(value):
    return jnp.asarray(value).astype(jnp.int32)


def slice_line(values, start, axis):
    starts = [to_index(0) for _ in range(values.ndim)]
    starts[axis] = to_index(start)
    sizes = list(values.shape)
    sizes[axis] = 1
    return lax.dynamic_slice(values, starts, sizes)


def fill_ghost(values, upper, lower, left, right, signs):
    upper, lower, left, right = (to_index(upper), to_index(lower), to_index(left), to_index(right))
    height, breadth = (values.shape[2], values.shape[3])
    row_ids = lax.broadcasted_iota(jnp.int32, (height, 1), 0)
    col_ids = lax.broadcasted_iota(jnp.int32, (1, breadth), 1)
    upper_row = slice_line(values, upper, 2)
    lower_row = slice_line(values, lower - 1, 2)
    values = jnp.where(row_ids < upper, upper_row, jnp.where(row_ids >= lower, lower_row, values))
    left_col = slice_line(values, left, 3)
    right_col = slice_line(values, right - 1, 3)
    values = jnp.where(col_ids < left, left_col, jnp.where(col_ids >= right, right_col, values))
    inside = (row_ids >= upper) & (row_ids < lower) & (col_ids >= left) & (col_ids < right)
    real_part = values[:, 0]
    imag_part = values[:, 1]
    ghost_cycle = jnp.stack(
        [real_part + signs * ROBIN_COEF * imag_part, imag_part - signs * ROBIN_COEF * real_part],
        axis=1,
    )
    return jnp.where(inside, values, ghost_cycle)


def apply_operator(padded, wave_cells, signs):
    centre = padded[:, :, 1:-1, 1:-1]
    edge_sum = (
        padded[:, :, :-2, 1:-1]
        + padded[:, :, 2:, 1:-1]
        + padded[:, :, 1:-1, :-2]
        + padded[:, :, 1:-1, 2:]
    )
    corner_sum = (
        padded[:, :, :-2, :-2]
        + padded[:, :, :-2, 2:]
        + padded[:, :, 2:, :-2]
        + padded[:, :, 2:, 2:]
    )
    laplace = (4.0 * edge_sum + corner_sum - 20.0 * centre) / 6.0
    real_part = centre[:, 0]
    imag_part = centre[:, 1]
    mass_term = jnp.stack(
        [real_part - signs * DAMPING * imag_part, imag_part + signs * DAMPING * real_part], axis=1
    )
    return -laplace - wave_cells * mass_term


def combine_parts(products, signs, shape):
    real_out = products[0][:, 0] - signs[..., None] * products[1][:, 1]
    imag_out = products[0][:, 1] + signs[..., None] * products[1][:, 0]
    return jnp.stack([real_out, imag_out], axis=1).reshape(shape)


def along_rows(values, inverse, signs):
    block = inverse.shape[-1]
    blocked = values.reshape(values.shape[0], 2, values.shape[2], values.shape[3] // block, block)
    products = jnp.einsum("qmok,fchqk->mfchqo", inverse, blocked, precision=lax.Precision.HIGHEST)
    return combine_parts(products, signs, values.shape)


def along_cols(values, inverse, signs):
    block = inverse.shape[-1]
    blocked = values.reshape(values.shape[0], 2, values.shape[2] // block, block, values.shape[3])
    products = jnp.einsum("qmok,fcqkw->mfcqow", inverse, blocked, precision=lax.Precision.HIGHEST)
    return combine_parts(products, signs, values.shape)


def solve_local(resid_ext, wave_ext, row_blocks, col_blocks, live_rect, signs):
    upper, lower, left, right = [to_index(v) for v in live_rect]
    height, breadth = (resid_ext.shape[2], resid_ext.shape[3])
    row_ids = lax.broadcasted_iota(jnp.int32, (height, 1), 0)
    col_ids = lax.broadcasted_iota(jnp.int32, (1, breadth), 1)
    live_mask = (
        (row_ids >= upper) & (row_ids < lower) & (col_ids >= left) & (col_ids < right)
    ).astype(resid_ext.dtype)
    local_res = resid_ext * live_mask
    correction = jnp.zeros_like(resid_ext)
    for sweep_index in range(SWEEPS):
        if sweep_index > 0:
            padded = jnp.pad(correction, ((0, 0), (0, 0), (1, 1), (1, 1)))
            padded = fill_ghost(padded, upper + 1, lower + 1, left + 1, right + 1, signs)
            local_res = live_mask * (resid_ext - apply_operator(padded, wave_ext, signs))
        if sweep_index % 2 == 0:
            update = along_rows(local_res, row_blocks, signs)
        else:
            update = along_cols(local_res, col_blocks, signs)
        correction = correction + live_mask * update
    return correction


def exchange(x, row_width, col_width, extra=None):
    row_count = lax.axis_size("gx")
    col_count = lax.axis_size("gy")
    height, breadth = (x.shape[-2], x.shape[-1])
    pieces = {}
    for dr in (-1, 0, 1):
        for dc in (-1, 0, 1):
            if dr == 0 and dc == 0:
                continue
            slab = x
            if dr == -1:
                slab = lax.slice_in_dim(slab, height - row_width, height, axis=x.ndim - 2)
            elif dr == 1:
                slab = lax.slice_in_dim(slab, 0, row_width, axis=x.ndim - 2)
            if dc == -1:
                slab = lax.slice_in_dim(slab, breadth - col_width, breadth, axis=x.ndim - 1)
            elif dc == 1:
                slab = lax.slice_in_dim(slab, 0, col_width, axis=x.ndim - 1)
            if extra is not None and (dr, dc) in extra:
                slab = jnp.concatenate([slab, extra[(dr, dc)]], axis=0)
            perm = []
            for r in range(row_count):
                for c in range(col_count):
                    rr, cc = (r - dr, c - dc)
                    if 0 <= rr < row_count and 0 <= cc < col_count:
                        perm.append((r * col_count + c, rr * col_count + cc))
            pieces[(dr, dc)] = lax.ppermute(slab, ("gx", "gy"), perm)
    return pieces


def exchange_axis(x, axis, dim, width, extra_lo=None, extra_hi=None):
    peers, length = (lax.axis_size(axis), x.shape[dim])
    up = [(i, i + 1) for i in range(peers - 1)]
    down = [(j, i) for i, j in up]
    last = lax.slice_in_dim(x, length - width, length, axis=dim)
    first = lax.slice_in_dim(x, 0, width, axis=dim)
    if extra_lo is not None:
        last = jnp.concatenate([last, extra_lo], axis=0)
        first = jnp.concatenate([first, extra_hi], axis=0)
    return lax.ppermute(last, axis, up), lax.ppermute(first, axis, down)


def assemble(pieces, centre, lead):
    rows = []
    for dr in (-1, 0, 1):
        row = []
        for dc in (-1, 0, 1):
            part = centre if (dr == 0 and dc == 0) else pieces[(dr, dc)][:lead]
            row.append(part)
        rows.append(jnp.concatenate(row, axis=-1))
    return jnp.concatenate(rows, axis=-2)


def shift_rows(x, step):
    return pltpu.roll(x, step % x.shape[0], 0)


def shift_cols(x, step):
    return pltpu.roll(x, step % x.shape[1], 1)


def solve_kernel(rect_ref, resid_ref, data_ref, wrow_ref, wcol_ref, out_ref):
    height, breadth = (resid_ref.shape[1], resid_ref.shape[2])
    half = height // 2
    upper, lower, left, right = (rect_ref[0], rect_ref[1], rect_ref[2], rect_ref[3])
    row_ids = lax.broadcasted_iota(jnp.int32, (height, breadth), 0)
    col_ids = lax.broadcasted_iota(jnp.int32, (height, breadth), 1)
    live = (row_ids >= upper) & (row_ids < lower) & (col_ids >= left) & (col_ids < right)
    top, bottom = (row_ids == upper, row_ids == lower - 1)
    first, last = (col_ids == left, col_ids == right - 1)
    wave = data_ref[4]
    zero = jnp.zeros((height, breadth), jnp.float32)

    def mask(x):
        return jnp.where(live, x, zero)

    def neighbours(x):
        up = jnp.where(top, x, shift_rows(x, 1))
        down = jnp.where(bottom, x, shift_rows(x, -1))
        edge, edge_ghost, corner, corner_ghost = (zero, zero, zero, zero)
        for line, line_flag in ((up, top), (x, None), (down, bottom)):
            lft = jnp.where(first, line, shift_cols(line, 1))
            rgt = jnp.where(last, line, shift_cols(line, -1))
            lft_flag = first if line_flag is None else (first | line_flag)
            rgt_flag = last if line_flag is None else (last | line_flag)
            if line_flag is None:
                edge = edge + lft + rgt
                edge_ghost = edge_ghost + jnp.where(lft_flag, lft, zero) + jnp.where(rgt_flag, rgt, zero)
            else:
                edge = edge + line
                edge_ghost = edge_ghost + jnp.where(line_flag, line, zero)
                corner = corner + lft + rgt
                corner_ghost = corner_ghost + jnp.where(lft_flag, lft, zero) + jnp.where(rgt_flag, rgt, zero)
        return edge, edge_ghost, corner, corner_ghost

    def operator(real_part, imag_part, sign):
        er, egr, cr, cgr = neighbours(real_part)
        ei, egi, ci, cgi = neighbours(imag_part)
        edge_r = er + sign * ROBIN_COEF * egi
        edge_i = ei - sign * ROBIN_COEF * egr
        corner_r = cr + sign * ROBIN_COEF * cgi
        corner_i = ci - sign * ROBIN_COEF * cgr
        lap_r = (4.0 * edge_r + corner_r - 20.0 * real_part) / 6.0
        lap_i = (4.0 * edge_i + corner_i - 20.0 * imag_part) / 6.0
        mass_r = real_part - sign * DAMPING * imag_part
        mass_i = imag_part + sign * DAMPING * real_part
        return (-lap_r - wave * mass_r, -lap_i - wave * mass_i)

    def dot(a, b):
        return jnp.dot(a, b, precision=lax.Precision.HIGHEST, preferred_element_type=jnp.float32)

    def rows_apply(real_part, imag_part, sign):
        outs_r, outs_i = ([], [])
        for h in range(breadth // half):
            cols = slice(h * half, (h + 1) * half)
            stacked = jnp.concatenate([real_part[:, cols], imag_part[:, cols]], axis=0)
            prod = dot(stacked, wrow_ref[h])
            outs_r.append(prod[:height, :half] - sign * prod[height:, half:])
            outs_i.append(prod[height:, :half] + sign * prod[:height, half:])
        return (jnp.concatenate(outs_r, axis=1), jnp.concatenate(outs_i, axis=1))

    def cols_apply(real_part, imag_part, sign):
        outs_r, outs_i = ([], [])
        for h in range(height // half):
            rows = slice(h * half, (h + 1) * half)
            stacked = jnp.concatenate([real_part[rows, :], imag_part[rows, :]], axis=1)
            prod = dot(wcol_ref[h], stacked)
            outs_r.append(prod[:half, :breadth] - sign * prod[half:, breadth:])
            outs_i.append(prod[:half, breadth:] + sign * prod[half:, :breadth])
        return (jnp.concatenate(outs_r, axis=0), jnp.concatenate(outs_i, axis=0))

    def problem_body(problem, carry):
        sign = 1.0 - 2.0 * problem.astype(jnp.float32)
        res_r = resid_ref[2 * problem]
        res_i = resid_ref[2 * problem + 1]
        up_r, up_i = rows_apply(mask(res_r), mask(res_i), sign)
        out_ref[problem, 0] = mask(up_r)
        out_ref[problem, 1] = mask(up_i)

        def sweep_body(step, inner):
            cor_r = out_ref[problem, 0]
            cor_i = out_ref[problem, 1]
            op_r, op_i = operator(cor_r, cor_i, sign)
            loc_r, loc_i = (mask(resid_ref[2 * problem] - op_r), mask(resid_ref[2 * problem + 1] - op_i))
            up_r, up_i = lax.cond(
                step % 2 == 0,
                lambda: cols_apply(loc_r, loc_i, sign),
                lambda: rows_apply(loc_r, loc_i, sign),
            )
            out_ref[problem, 0] = cor_r + mask(up_r)
            out_ref[problem, 1] = cor_i + mask(up_i)
            return inner

        lax.fori_loop(0, SWEEPS - 1, sweep_body, 0)
        return carry

    lax.fori_loop(0, out_ref.shape[0], problem_body, 0)


def line_matrices(row_blocks, col_blocks):
    block = row_blocks.shape[-1]
    eye = jnp.eye(2, dtype=row_blocks.dtype)
    halves = row_blocks.shape[0] // 2
    rows_t = jnp.transpose(row_blocks, (0, 3, 1, 2)).reshape(halves, 2, block, 2, block)
    row_mats = jnp.einsum("hakmo,ab->hakmbo", rows_t, eye).reshape(halves, 2 * block, 4 * block)
    cols = col_blocks.reshape(halves, 2, 2, block, block)
    col_mats = jnp.einsum("hamok,ab->hmaobk", cols, eye).reshape(halves, 4 * block, 2 * block)
    return row_mats, col_mats


def solve_local_kernel(resid_planes, data_ext, row_mats, col_mats, live_rect, interpret=False):
    rect = jnp.stack([to_index(v) for v in live_rect])
    out_shape = (2, 2) + resid_planes.shape[1:]
    vmem = pltpu.MemorySpace.VMEM if hasattr(pltpu, "MemorySpace") else pltpu.VMEM
    return pl.pallas_call(
        solve_kernel,
        out_shape=jax.ShapeDtypeStruct(out_shape, resid_planes.dtype),
        in_specs=[pl.BlockSpec(memory_space=pltpu.SMEM)] + [pl.BlockSpec(memory_space=vmem)] * 4,
        out_specs=pl.BlockSpec(memory_space=vmem),
        interpret=interpret,
    )(rect, resid_planes, data_ext, row_mats, col_mats)


def shards(sources, wavenumber, row_inverse, col_inverse, reach_steps):
    own_rows, own_cols = (sources.shape[2], sources.shape[3])
    block = row_inverse.shape[-1]
    step_cells = block // 4
    signs = jnp.array([1.0, -1.0], dtype=sources.dtype).reshape(2, 1, 1)
    row_rank = to_index(lax.axis_index("gx"))
    col_rank = to_index(lax.axis_index("gy"))
    row_count = lax.axis_size("gx")
    col_count = lax.axis_size("gy")
    zero = to_index(0)
    widths = reach_steps.reshape(4) * step_cells
    upper_w = jnp.where(row_rank > 0, widths[0], zero)
    lower_w = jnp.where(row_rank < row_count - 1, widths[1], zero)
    left_w = jnp.where(col_rank > 0, widths[2], zero)
    right_w = jnp.where(col_rank < col_count - 1, widths[3], zero)
    live_rect = (
        block - upper_w,
        block + own_rows + lower_w,
        block - left_w,
        block + own_cols + right_w,
    )
    stacked = jnp.concatenate([sources.reshape(4, own_rows, own_cols), wavenumber[None]], axis=0)
    lead = stacked.shape[0]
    col_pair = col_inverse.shape[0]
    row_pair = row_inverse.shape[0]
    inv_rows = col_inverse.shape[1] * block * block // own_cols
    before, after = exchange_axis(
        stacked, "gx", 1, block,
        col_inverse[col_pair - 1].reshape(1, inv_rows, own_cols), col_inverse[0].reshape(1, inv_rows, own_cols),
    )
    tall = jnp.concatenate([before[:lead, :block], stacked, after[:lead, :block]], axis=1)
    def inv_slab(mats):
        flat = mats.reshape(1, -1, block)
        return jnp.pad(flat, ((0, 0), (0, tall.shape[1] - flat.shape[1]), (0, 0)))
    left, right = exchange_axis(tall, "gy", 2, block, inv_slab(row_inverse[row_pair - 1]), inv_slab(row_inverse[0]))
    stacked_ext = jnp.concatenate([left[:lead], tall, right[:lead]], axis=2)
    sources_ext = stacked_ext[:4].reshape(2, 2, own_rows + 2 * block, own_cols + 2 * block)
    wave_ext = stacked_ext[4]
    inv_shape = (1,) + row_inverse.shape[1:]
    inv_size = row_inverse.shape[1] * block * block // block
    col_blocks = jnp.concatenate(
        [before[lead:].reshape(inv_shape), col_inverse, after[lead:].reshape(inv_shape)], axis=0
    )
    row_blocks = jnp.concatenate(
        [left[lead:, :inv_size].reshape(inv_shape), row_inverse, right[lead:, :inv_size].reshape(inv_shape)], axis=0
    )
    row_mats, col_mats = line_matrices(row_blocks, col_blocks)
    width = block + 1
    grid_upper = to_index(jnp.where(row_rank == 0, width, 0))
    grid_lower = to_index(jnp.where(row_rank == row_count - 1, width + own_rows, own_rows + 2 * width))
    grid_left = to_index(jnp.where(col_rank == 0, width, 0))
    grid_right = to_index(jnp.where(col_rank == col_count - 1, width + own_cols, own_cols + 2 * width))
    solution = None
    for iteration in range(ITERS):
        if iteration == 0:
            resid_planes = stacked_ext
        else:
            before, after = exchange_axis(solution, "gx", 2, width)
            tall = jnp.concatenate([before, solution, after], axis=2)
            left, right = exchange_axis(tall, "gy", 3, width)
            padded = jnp.concatenate([left, tall, right], axis=3)
            padded = fill_ghost(padded, grid_upper, grid_lower, grid_left, grid_right, signs)
            resid_ext = sources_ext - apply_operator(padded, wave_ext, signs)
            resid_planes = resid_ext.reshape((4,) + resid_ext.shape[2:])
        correction = solve_local_kernel(resid_planes, stacked_ext, row_mats, col_mats, live_rect)
        own = correction[:, :, block : block + own_rows, block : block + own_cols]
        solution = own if solution is None else solution + own
    return solution


def solution(mesh):
    return jax.shard_map(
        shards,
        mesh=mesh,
        in_specs=(
            P(None, None, "gx", "gy"),
            P("gx", "gy"),
            P("gy", None, None, None),
            P("gx", None, None, None),
            P("gx", "gy", None),
        ),
        out_specs=P(None, None, "gx", "gy"),
        check_vma=False,
    )
```

profile of v0, /device:TPU:6, one launch (start us, length us, event | category | flops | bytes accessed | tf_op | source)
XLA Modules:
  0.0 118.8 jit_solution(960837055002861900)
XLA Ops:
  0.0 0.9 fusion.14
  1.0 0.1 reshape_squeeze.12
  1.0 0.9 fusion.8
  2.0 3.8 %collective-permute-start = (f32[6,64,128]{2,1,0:T(8,128)S(1)}, f32[6,64,128]{2,1,0:T(8,128)S(1)}, u32[]{:S(2)}, u32[]{:S(2)}) collective-permute-start(f32[6,64,128]{2,1,0:T(8,128)S(1)} %pad_maximum_fusion.7), channel_id=1, source_target_pairs={{0,16},{16,32},{32,48},{48,64},{64,80},{80,96},{96,112},{1,17},{17... | collective-permute-start | bytes 589832 | tf_op jit(solution)/shard_map/ppermute | solution.py:167
  5.7 0.1 reshape_squeeze.13
  5.8 0.9 fusion.7
  6.8 2.1 %collective-permute-start.1 = (f32[6,64,128]{2,1,0:T(8,128)S(1)}, f32[6,64,128]{2,1,0:T(8,128)S(1)}, u32[]{:S(2)}, u32[]{:S(2)}) collective-permute-start(f32[6,64,128]{2,1,0:T(8,128)S(1)} %fusion.7), channel_id=1, source_target_pairs={{16,0},{32,16},{48,32},{64,48},{80,64},{96,80},{112,96},{17,1},{33... | collective-permute-start | bytes 589832 | tf_op jit(solution)/shard_map/ppermute | solution.py:167
  8.9 0.7 fusion.15
  12.3 3.6 %collective-permute-done.1 = f32[6,64,128]{2,1,0:T(8,128)S(1)} collective-permute-done((f32[6,64,128]{2,1,0:T(8,128)S(1)}, f32[6,64,128]{2,1,0:T(8,128)S(1)}, u32[]{:S(2)}, u32[]{:S(2)}) %collective-permute-start.1) | collective-permute-done | bytes 196640 | tf_op jit(solution)/shard_map/ppermute | solution.py:167
  16.0 0.2 fusion.11
  16.2 0.3 copy-done.5
  16.6 0.1 select_maximum_fusion.1
  16.6 0.2 copy.11
  16.9 0.0 slice-start.1
  16.9 2.1 %collective-permute-start.2 = (f32[6,256,64]{1,2,0:T(8,128)S(1)}, f32[6,256,64]{1,2,0:T(8,128)S(1)}, u32[]{:S(2)}, u32[]{:S(2)}) collective-permute-start(f32[6,256,64]{1,2,0:T(8,128)S(1)} %copy.11), channel_id=1, source_target_pairs={{0,1},{1,2},{2,3},{3,4},{4,5},{5,6},{6,7},{7,8},{8,9},{9,10},{10,1... | collective-permute-start | bytes 1179656 | tf_op jit(solution)/shard_map/ppermute | solution.py:167
  19.0 0.1 select_maximum_fusion
  19.0 0.2 copy.13
  19.3 7.3 %collective-permute-start.3 = (f32[6,256,64]{1,2,0:T(8,128)S(1)}, f32[6,256,64]{1,2,0:T(8,128)}, u32[]{:S(2)}, u32[]{:S(2)}) collective-permute-start(f32[6,256,64]{1,2,0:T(8,128)S(1)} %copy.13), channel_id=1, source_target_pairs={{1,0},{2,1},{3,2},{4,3},{5,4},{6,5},{7,6},{8,7},{9,8},{10,9},{11,1... | collective-permute-start | bytes 1179656 | tf_op jit(solution)/shard_map/ppermute | solution.py:167
  26.6 0.7 pad_add_fusion.rect_ref
  27.2 0.1 reshape.95
  27.3 0.1 reshape.96
  27.4 0.3 multiply_bitcast_fusion
  27.7 1.0 reshape.99.wcol_ref
  28.7 1.1 collective-permute-done.2
  29.8 0.2 copy.27
  30.0 1.8 %collective-permute-done.3 = f32[6,256,64]{1,2,0:T(8,128)} collective-permute-done((f32[6,256,64]{1,2,0:T(8,128)S(1)}, f32[6,256,64]{1,2,0:T(8,128)}, u32[]{:S(2)}, u32[]{:S(2)}) %collective-permute-start.3) | collective-permute-done | bytes 393248 | tf_op jit(solution)/shard_map/ppermute | solution.py:167
  31.8 1.0 slice.179
  32.8 0.2 copy.28
  33.1 0.1 copy.23
  33.2 0.8 slice.181
  33.9 0.1 copy.24
  34.1 0.2 copy.17
  34.2 0.2 multiply_bitcast_fusion.1
  34.5 1.2 reshape.94.wrow_ref
  35.6 1.7 %pad_maximum_fusion.1.resid_ref.data_ref = f32[5,256,256]{2,1,0:T(8,128)} fusion(f32[5,256,64]{2,1,0:T(8,128)S(1)} %copy.28, f32[5,64,128]{2,1,0:T(8,128)S(1)} %slice.175, f32[1,128,128]{2,1,0:T(8,128)S(1)} %bitcast.47, f32[4,128,128]{2,1,0:T(8,128)S(1)} %bitcast.42, f32[5,64,128]{2,1,0:T(8,128)S(1)} %slice.174, f32[5,256,64]{2,1,0:T(8,128)S(1)} %copy.27), kind=kLoop, calls=%fused_computation.4 | loop fusion | flops 1638400 | bytes 2621440 | tf_op jit(solution)/shard_map/concatenate | solution.py:346
  37.3 21.0 %shard_map.64 = f32[2,2,256,256]{3,2,1,0:T(8,128)} custom-call(s32[4]{0:T(128)} %pad_add_fusion.rect_ref, f32[5,256,256]{2,1,0:T(8,128)} %pad_maximum_fusion.1.resid_ref.data_ref, f32[5,256,256]{2,1,0:T(8,128)} %pad_maximum_fusion.1.resid_ref.data_ref, f32[2,128,256]{2,1,0:T(8,128)} %reshape.94.wrow_ref, f32[2,256,128]{2,1,0:T(8,128)} %reshape.99.wcol_ref), custom_call_target="tpu_custom_call" | custom-call | tf_op jit(solution)/shard_map/pallas_call | solution.py:302
  58.3 1.2 %fusion.10 = (f32[2,2,65,128]{3,2,1,0:T(8,128)S(1)}, f32[2,2,65,128]{3,2,1,0:T(8,128)S(1)}) fusion(f32[2,2,256,256]{3,2,1,0:T(8,128)} %shard_map.64), kind=kLoop, calls=%fused_computation.60 | loop fusion | bytes 532480 | tf_op jit(solution)/shard_map/slice | solution.py:162
  59.5 3.6 %collective-permute-start.4 = (f32[2,2,65,128]{3,2,1,0:T(8,128)S(1)}, f32[2,2,65,128]{3,2,1,0:T(8,128)S(1)}, u32[]{:S(2)}, u32[]{:S(2)}) collective-permute-start(f32[2,2,65,128]{3,2,1,0:T(8,128)S(1)} %get-tuple-element.13), channel_id=1, source_target_pairs={{0,16},{16,32},{32,48},{48,64},{64,80},{80,96},{96,112},{1,17},{17... | collective-permute-start | bytes 399368 | tf_op jit(solution)/shard_map/ppermute | solution.py:167
  63.1 2.3 %collective-permute-start.5 = (f32[2,2,65,128]{3,2,1,0:T(8,128)S(1)}, f32[2,2,65,128]{3,2,1,0:T(8,128)S(1)}, u32[]{:S(2)}, u32[]{:S(2)}) collective-permute-start(f32[2,2,65,128]{3,2,1,0:T(8,128)S(1)} %get-tuple-element.14), channel_id=1, source_target_pairs={{16,0},{32,16},{48,32},{64,48},{80,64},{96,80},{112,96},{17,1},{33... | collective-permute-start | bytes 399368 | tf_op jit(solution)/shard_map/ppermute | solution.py:167
  65.4 0.1 and_and_fusion
  65.5 1.2 slice.184
  66.7 0.3 collective-permute-done.4
  67.0 4.0 %collective-permute-done.5 = f32[2,2,65,128]{3,2,1,0:T(8,128)S(1)} collective-permute-done((f32[2,2,65,128]{3,2,1,0:T(8,128)S(1)}, f32[2,2,65,128]{3,2,1,0:T(8,128)S(1)}, u32[]{:S(2)}, u32[]{:S(2)}) %collective-permute-start.5) | collective-permute-done | bytes 133152 | tf_op jit(solution)/shard_map/ppermute | solution.py:167
  71.1 0.2 fusion.12
  71.3 0.3 copy.19
  71.6 2.1 %collective-permute-start.6 = (f32[2,2,258,65]{2,1,3,0:T(2,128)S(1)}, f32[2,2,258,65]{2,1,3,0:T(2,128)S(1)}, u32[]{:S(2)}, u32[]{:S(2)}) collective-permute-start(f32[2,2,258,65]{2,1,3,0:T(2,128)S(1)} %copy.19), channel_id=1, source_target_pairs={{0,1},{1,2},{2,3},{3,4},{4,5},{5,6},{6,7},{7,8},{8,9},{9,10},{10,1... | collective-permute-start | bytes 804968 | tf_op jit(solution)/shard_map/ppermute | solution.py:167
  73.6 1.0 copy.20
  74.7 7.4 %collective-permute-start.7 = (f32[2,2,258,65]{2,1,3,0:T(2,128)}, f32[2,2,258,65]{2,1,3,0:T(2,128)}, u32[]{:S(2)}, u32[]{:S(2)}) collective-permute-start(f32[2,2,258,65]{2,1,3,0:T(2,128)} %copy.20), channel_id=1, source_target_pairs={{1,0},{2,1},{3,2},{4,3},{5,4},{6,5},{7,6},{8,7},{9,8},{10,9},{11,1... | collective-permute-start | bytes 804968 | tf_op jit(solution)/shard_map/ppermute | solution.py:167
  82.2 2.3 %collective-permute-done.6 = f32[2,2,258,65]{2,1,3,0:T(2,128)S(1)} collective-permute-done((f32[2,2,258,65]{2,1,3,0:T(2,128)S(1)}, f32[2,2,258,65]{2,1,3,0:T(2,128)S(1)}, u32[]{:S(2)}, u32[]{:S(2)}) %collective-permute-start.6) | collective-permute-done | bytes 268352 | tf_op jit(solution)/shard_map/ppermute | solution.py:167
  84.5 0.3 copy.21
  84.8 2.8 %collective-permute-done.7 = f32[2,2,258,65]{2,1,3,0:T(2,128)} collective-permute-done((f32[2,2,258,65]{2,1,3,0:T(2,128)}, f32[2,2,258,65]{2,1,3,0:T(2,128)}, u32[]{:S(2)}, u32[]{:S(2)}) %collective-permute-start.7) | collective-permute-done | bytes 268352 | tf_op jit(solution)/shard_map/ppermute | solution.py:167
  87.6 1.2 %copy.22 = f32[2,2,258,65]{3,2,1,0:T(8,128)S(1)} copy(f32[2,2,258,65]{2,1,3,0:T(2,128)} %collective-permute-done.7) | data formatting | bytes 536640 | tf_op jit(solution)/shard_map/ppermute | solution.py:167
  88.8 0.6 pad_maximum_fusion
  89.5 0.2 select_select_fusion.1
  89.8 0.8 dynamic-slice_reduce_fusion.1
  90.6 0.4 select_select_fusion
  91.0 0.2 copy-done.6
  91.3 0.2 multiply_add_fusion
  91.5 0.5 maximum_select_fusion
  92.0 0.3 multiply_subtract_fusion.1
  92.3 0.9 slice-done
  93.2 2.7 %fusion.4 = f32[2,2,256,256]{3,2,1,0:T(8,128)} fusion(f32[2,2,256,256]{3,2,1,0:T(8,128)S(1)} %bitcast.38, f32[2,2,258,258]{3,2,1,0:T(8,128)S(1)} %maximum_select_fusion, f32[2,1,256,256]{3,2,1,0:T(8,128)S(1)} %get-tuple-element.8, f32[2,1,256,256]{3,2,1,0:T(8,128)S(1)} %get-tuple-element.7, f32[256,256]{1,0:T(8,128)S(1)} %slice_bitcast_fusion), kind=kLoop, calls=%fused_computation.10 | loop fusion | flops 4194304 | bytes 12845056 | tf_op jit(solution)/shard_map/sub | solution.py:373
  95.9 20.8 %shard_map.65 = f32[2,2,256,256]{3,2,1,0:T(8,128)} custom-call(s32[4]{0:T(128)} %pad_add_fusion.rect_ref, f32[4,256,256]{2,1,0:T(8,128)} %bitcast.43, f32[5,256,256]{2,1,0:T(8,128)} %pad_maximum_fusion.1.resid_ref.data_ref, f32[2,128,256]{2,1,0:T(8,128)} %reshape.94.wrow_ref, f32[2,256,128]{2,1,0:T(8,128)} %reshape.99.wcol_ref), custom_call_target="tpu_custom_call" | custom-call | tf_op jit(solution)/shard_map/pallas_call | solution.py:302
  116.7 2.1 %slice_add_fusion.6 = f32[2,2,128,128]{3,2,1,0:T(8,128)} fusion(f32[2,2,256,256]{3,2,1,0:T(8,128)} %shard_map.65, f32[2,2,256,256]{3,2,1,0:T(8,128)} %shard_map.64), kind=kLoop, calls=%fused_computation.36 | loop fusion | flops 65536 | bytes 786432 | tf_op jit(solution)/shard_map/add | solution.py:377
  (37 shorter events, 0.3 us)
Async XLA Ops:
  0.0 15.9 %copy-start.1 = (f32[2,2,128,128]{3,2,1,0:T(8,128)S(1)}, f32[2,2,128,128]{3,2,1,0:T(8,128)}, u32[]{:S(2)}) copy-start(f32[2,2,128,128]{3,2,1,0:T(8,128)} %param.6) | copy-start | bytes 786436
  0.0 15.9 %copy-start.2 = (f32[128,128]{1,0:T(8,128)S(1)}, f32[128,128]{1,0:T(8,128)}, u32[]{:S(2)}) copy-start(f32[128,128]{1,0:T(8,128)} %param.7) | copy-start | bytes 196612
  0.0 8.9 %copy-start.7 = (s32[1,1,4]{2,1,0:T(1,128)S(1)}, s32[1,1,4]{2,1,0:T(1,128)}, u32[]{:S(2)}) copy-start(s32[1,1,4]{2,1,0:T(1,128)} %param.10) | copy-start | bytes 52
  0.0 12.2 %copy-start.4 = (f32[2,2,64,64]{3,2,1,0:T(8,128)S(1)}, f32[2,2,64,64]{3,2,1,0:T(8,128)}, u32[]{:S(2)}) copy-start(f32[2,2,64,64]{3,2,1,0:T(8,128)} %param.8) | copy-start | bytes 196612
  2.0 10.3 %collective-permute-start = (f32[6,64,128]{2,1,0:T(8,128)S(1)}, f32[6,64,128]{2,1,0:T(8,128)S(1)}, u32[]{:S(2)}, u32[]{:S(2)}) collective-permute-start(f32[6,64,128]{2,1,0:T(8,128)S(1)} %pad_maximum_fusion.7), channel_id=1, source_target_pairs={{0,16},{16,32},{32,48},{48,64},{64,80},{80,96},{96,112},{1,17},{17... | collective-permute-start | bytes 589832 | tf_op jit(solution)/shard_map/ppermute | solution.py:167
  6.8 9.2 %collective-permute-start.1 = (f32[6,64,128]{2,1,0:T(8,128)S(1)}, f32[6,64,128]{2,1,0:T(8,128)S(1)}, u32[]{:S(2)}, u32[]{:S(2)}) collective-permute-start(f32[6,64,128]{2,1,0:T(8,128)S(1)} %fusion.7), channel_id=1, source_target_pairs={{16,0},{32,16},{48,32},{64,48},{80,64},{96,80},{112,96},{17,1},{33... | collective-permute-start | bytes 589832 | tf_op jit(solution)/shard_map/ppermute | solution.py:167
  15.9 0.7 copy-start.5
  16.9 10.4 %slice-start.1 = ((f32[6,64,128]{2,1,0:T(8,128)}), f32[1,64,128]{2,1,0:T(8,128)S(1)}, s32[]{:S(2)}) async-start(f32[6,64,128]{2,1,0:T(8,128)} %copy-done.5), calls=%async_computation.1 | async-start | bytes 65536 | tf_op jit(solution)/shard_map/slice | solution.py:352
  16.9 10.5 %copy-start.3 = (f32[2,2,64,64]{3,2,1,0:T(8,128)S(1)}, f32[2,2,64,64]{3,2,1,0:T(8,128)}, u32[]{:S(2)}) copy-start(f32[2,2,64,64]{3,2,1,0:T(8,128)} %param.9) | copy-start | bytes 196612
  16.9 12.8 %collective-permute-start.2 = (f32[6,256,64]{1,2,0:T(8,128)S(1)}, f32[6,256,64]{1,2,0:T(8,128)S(1)}, u32[]{:S(2)}, u32[]{:S(2)}) collective-permute-start(f32[6,256,64]{1,2,0:T(8,128)S(1)} %copy.11), channel_id=1, source_target_pairs={{0,1},{1,2},{2,3},{3,4},{4,5},{5,6},{6,7},{7,8},{8,9},{9,10},{10,1... | collective-permute-start | bytes 1179656 | tf_op jit(solution)/shard_map/ppermute | solution.py:167
  19.3 12.5 %collective-permute-start.3 = (f32[6,256,64]{1,2,0:T(8,128)S(1)}, f32[6,256,64]{1,2,0:T(8,128)}, u32[]{:S(2)}, u32[]{:S(2)}) collective-permute-start(f32[6,256,64]{1,2,0:T(8,128)S(1)} %copy.13), channel_id=1, source_target_pairs={{1,0},{2,1},{3,2},{4,3},{5,4},{6,5},{7,6},{8,7},{9,8},{10,9},{11,1... | collective-permute-start | bytes 1179656 | tf_op jit(solution)/shard_map/ppermute | solution.py:167
  59.5 7.5 %collective-permute-start.4 = (f32[2,2,65,128]{3,2,1,0:T(8,128)S(1)}, f32[2,2,65,128]{3,2,1,0:T(8,128)S(1)}, u32[]{:S(2)}, u32[]{:S(2)}) collective-permute-start(f32[2,2,65,128]{3,2,1,0:T(8,128)S(1)} %get-tuple-element.13), channel_id=1, source_target_pairs={{0,16},{16,32},{32,48},{48,64},{64,80},{80,96},{96,112},{1,17},{17... | collective-permute-start | bytes 399368 | tf_op jit(solution)/shard_map/ppermute | solution.py:167
  63.1 7.9 %collective-permute-start.5 = (f32[2,2,65,128]{3,2,1,0:T(8,128)S(1)}, f32[2,2,65,128]{3,2,1,0:T(8,128)S(1)}, u32[]{:S(2)}, u32[]{:S(2)}) collective-permute-start(f32[2,2,65,128]{3,2,1,0:T(8,128)S(1)} %get-tuple-element.14), channel_id=1, source_target_pairs={{16,0},{32,16},{48,32},{64,48},{80,64},{96,80},{112,96},{17,1},{33... | collective-permute-start | bytes 399368 | tf_op jit(solution)/shard_map/ppermute | solution.py:167
  71.6 10.6 %copy-start = (f32[5,256,256]{2,1,0:T(8,128)S(1)}, f32[5,256,256]{2,1,0:T(8,128)}, u32[]{:S(2)}) copy-start(f32[5,256,256]{2,1,0:T(8,128)} %pad_maximum_fusion.1.resid_ref.data_ref) | copy-start | bytes 3932164
  71.6 12.9 %collective-permute-start.6 = (f32[2,2,258,65]{2,1,3,0:T(2,128)S(1)}, f32[2,2,258,65]{2,1,3,0:T(2,128)S(1)}, u32[]{:S(2)}, u32[]{:S(2)}) collective-permute-start(f32[2,2,258,65]{2,1,3,0:T(2,128)S(1)} %copy.19), channel_id=1, source_target_pairs={{0,1},{1,2},{2,3},{3,4},{4,5},{5,6},{6,7},{7,8},{8,9},{9,10},{10,1... | collective-permute-start | bytes 804968 | tf_op jit(solution)/shard_map/ppermute | solution.py:167
  74.7 12.9 %collective-permute-start.7 = (f32[2,2,258,65]{2,1,3,0:T(2,128)}, f32[2,2,258,65]{2,1,3,0:T(2,128)}, u32[]{:S(2)}, u32[]{:S(2)}) collective-permute-start(f32[2,2,258,65]{2,1,3,0:T(2,128)} %copy.20), channel_id=1, source_target_pairs={{1,0},{2,1},{3,2},{4,3},{5,4},{6,5},{7,6},{8,7},{9,8},{10,9},{11,1... | collective-permute-start | bytes 804968 | tf_op jit(solution)/shard_map/ppermute | solution.py:167
  90.6 0.7 copy-start.6
  91.9 1.2 %slice-start = ((f32[5,256,256]{2,1,0:T(8,128)}), f32[4,256,256]{2,1,0:T(8,128)S(1)}, s32[]{:S(2)}) async-start(f32[5,256,256]{2,1,0:T(8,128)} %pad_maximum_fusion.1.resid_ref.data_ref), calls=%async_computation | async-start | bytes 2097152 | tf_op jit(solution)/shard_map/slice | solution.py:347
where the time goes:
time: 121 us; the launch traced here: 119 us
  Pallas kernels  41.8 us (35%)
  starting transfers between devices  30.5 us (25%)
  waiting for transfers between devices  16 us (13%)
  local copies, waits for them, and re-layouts  15.2 us (13%)
  other arithmetic  12.2 us (10%)
  between operations  3.09 us (3%)
    pallas_call x2, Pallas kernels, solve_local_kernel(): pl.pallas_call(solve_kernel, out_shape=jax.ShapeDtypeStruct(out_shape, re...  41.8 us
    ppermute x8, starting transfers between devices, exchange_axis(): return (lax.ppermute(last, axis, up), lax.ppermute(first, axis, down))  30.5 us
    ppermute x8, waiting for transfers between devices, exchange_axis(): return (lax.ppermute(last, axis, up), lax.ppermute(first, axis, down))  16 us
    sub x1, other arithmetic, shards(): resid_ext = sources_ext - apply_operator(padded, wave_ext, signs)  2.7 us
  transfers between devices with their start and end apart: 8, of which 7 were waited for; matrix products, arithmetic and copies ran while one was open for 6% of the time, Pallas kernels for 0%

commit v1 on v0

--- a/solution.py
+++ b/solution.py
@@ -234,7 +234,7 @@
         return (-lap_r - wave * mass_r, -lap_i - wave * mass_i)
 
     def dot(a, b):
-        return jnp.dot(a, b, precision=lax.Precision.HIGHEST, preferred_element_type=jnp.float32)
+        return jnp.dot(a, b, precision=lax.Precision.HIGH, preferred_element_type=jnp.float32)
 
     def rows_apply(real_part, imag_part, sign):
         outs_r, outs_i = ([], [])

time: 121 us -> 114 us (0.942)
  Pallas kernels: 41.8 us -> 35.3 us
    pallas_call x2, Pallas kernels: 41.8 us -> 35.3 us  [solve_local_kernel(): pl.pallas_call(solve_kernel, out_shape=jax.ShapeDtypeStruct(out_shape, re...]
where the time goes in v1:
time: 114 us; the launch traced here: 112 us
  Pallas kernels  35.3 us (31%)
  starting transfers between devices  30.5 us (27%)
  waiting for transfers between devices  16 us (14%)
  local copies, waits for them, and re-layouts  15.2 us (13%)
  other arithmetic  12.2 us (11%)
  between operations  3.09 us (3%)
    pallas_call x2, Pallas kernels, solve_local_kernel(): pl.pallas_call(solve_kernel, out_shape=jax.ShapeDtypeStruct(out_shape, re...  35.3 us
    ppermute x8, starting transfers between devices, exchange_axis(): return (lax.ppermute(last, axis, up), lax.ppermute(first, axis, down))  30.5 us
    ppermute x8, waiting for transfers between devices, exchange_axis(): return (lax.ppermute(last, axis, up), lax.ppermute(first, axis, down))  16 us
    sub x1, other arithmetic, shards(): resid_ext = sources_ext - apply_operator(padded, wave_ext, signs)  2.7 us
  transfers between devices with their start and end apart: 8, of which 7 were waited for; matrix products, arithmetic and copies ran while one was open for 6% of the time, Pallas kernels for 0%

profile of v1, /device:TPU:6, one launch (start us, length us, event | category | flops | bytes accessed | tf_op | source)
XLA Modules:
  0.0 112.3 jit_solution(12492340423883879652)
XLA Ops:
  0.0 0.9 fusion.14
  1.0 0.1 reshape_squeeze.12
  1.0 0.9 fusion.8
  2.0 3.8 %collective-permute-start = (f32[6,64,128]{2,1,0:T(8,128)S(1)}, f32[6,64,128]{2,1,0:T(8,128)S(1)}, u32[]{:S(2)}, u32[]{:S(2)}) collective-permute-start(f32[6,64,128]{2,1,0:T(8,128)S(1)} %pad_maximum_fusion.7), channel_id=1, source_target_pairs={{0,16},{16,32},{32,48},{48,64},{64,80},{80,96},{96,112},{1,17},{17... | collective-permute-start | bytes 589832 | tf_op jit(solution)/shard_map/ppermute | solution.py:167
  5.7 0.1 reshape_squeeze.13
  5.8 0.9 fusion.7
  6.8 2.1 %collective-permute-start.1 = (f32[6,64,128]{2,1,0:T(8,128)S(1)}, f32[6,64,128]{2,1,0:T(8,128)S(1)}, u32[]{:S(2)}, u32[]{:S(2)}) collective-permute-start(f32[6,64,128]{2,1,0:T(8,128)S(1)} %fusion.7), channel_id=1, source_target_pairs={{16,0},{32,16},{48,32},{64,48},{80,64},{96,80},{112,96},{17,1},{33... | collective-permute-start | bytes 589832 | tf_op jit(solution)/shard_map/ppermute | solution.py:167
  8.9 0.7 fusion.15
  12.3 3.6 %collective-permute-done.1 = f32[6,64,128]{2,1,0:T(8,128)S(1)} collective-permute-done((f32[6,64,128]{2,1,0:T(8,128)S(1)}, f32[6,64,128]{2,1,0:T(8,128)S(1)}, u32[]{:S(2)}, u32[]{:S(2)}) %collective-permute-start.1) | collective-permute-done | bytes 196640 | tf_op jit(solution)/shard_map/ppermute | solution.py:167
  16.0 0.2 fusion.11
  16.2 0.3 copy-done.5
  16.6 0.1 select_maximum_fusion.1
  16.6 0.2 copy.11
  16.9 0.0 slice-start.1
  16.9 2.1 %collective-permute-start.2 = (f32[6,256,64]{1,2,0:T(8,128)S(1)}, f32[6,256,64]{1,2,0:T(8,128)S(1)}, u32[]{:S(2)}, u32[]{:S(2)}) collective-permute-start(f32[6,256,64]{1,2,0:T(8,128)S(1)} %copy.11), channel_id=1, source_target_pairs={{0,1},{1,2},{2,3},{3,4},{4,5},{5,6},{6,7},{7,8},{8,9},{9,10},{10,1... | collective-permute-start | bytes 1179656 | tf_op jit(solution)/shard_map/ppermute | solution.py:167
  19.0 0.1 select_maximum_fusion
  19.0 0.2 copy.13
  19.3 7.3 %collective-permute-start.3 = (f32[6,256,64]{1,2,0:T(8,128)S(1)}, f32[6,256,64]{1,2,0:T(8,128)}, u32[]{:S(2)}, u32[]{:S(2)}) collective-permute-start(f32[6,256,64]{1,2,0:T(8,128)S(1)} %copy.13), channel_id=1, source_target_pairs={{1,0},{2,1},{3,2},{4,3},{5,4},{6,5},{7,6},{8,7},{9,8},{10,9},{11,1... | collective-permute-start | bytes 1179656 | tf_op jit(solution)/shard_map/ppermute | solution.py:167
  26.6 0.7 pad_add_fusion.rect_ref
  27.2 0.1 reshape.95
  27.3 0.1 reshape.96
  27.4 0.3 multiply_bitcast_fusion
  27.7 1.0 reshape.99.wcol_ref
  28.7 1.1 collective-permute-done.2
  29.8 0.2 copy.27
  30.0 1.8 %collective-permute-done.3 = f32[6,256,64]{1,2,0:T(8,128)} collective-permute-done((f32[6,256,64]{1,2,0:T(8,128)S(1)}, f32[6,256,64]{1,2,0:T(8,128)}, u32[]{:S(2)}, u32[]{:S(2)}) %collective-permute-start.3) | collective-permute-done | bytes 393248 | tf_op jit(solution)/shard_map/ppermute | solution.py:167
  31.8 1.0 slice.179
  32.8 0.2 copy.28
  33.1 0.1 copy.23
  33.2 0.8 slice.181
  33.9 0.1 copy.24
  34.1 0.2 copy.17
  34.2 0.2 multiply_bitcast_fusion.1
  34.5 1.2 %reshape.94.wrow_ref = f32[2,128,256]{2,1,0:T(8,128)} reshape(f32[2,2,64,2,2,64]{5,4,3,2,1,0:T(2,128)S(1)} %multiply_bitcast_fusion.1) | data formatting | bytes 524288 | tf_op jit(solution)/shard_map/reshape | solution.py:292
  35.6 1.7 %pad_maximum_fusion.1.resid_ref.data_ref = f32[5,256,256]{2,1,0:T(8,128)} fusion(f32[5,256,64]{2,1,0:T(8,128)S(1)} %copy.28, f32[5,64,128]{2,1,0:T(8,128)S(1)} %slice.175, f32[1,128,128]{2,1,0:T(8,128)S(1)} %bitcast.47, f32[4,128,128]{2,1,0:T(8,128)S(1)} %bitcast.42, f32[5,64,128]{2,1,0:T(8,128)S(1)} %slice.174, f32[5,256,64]{2,1,0:T(8,128)S(1)} %copy.27), kind=kLoop, calls=%fused_computation.4 | loop fusion | flops 1638400 | bytes 2621440 | tf_op jit(solution)/shard_map/concatenate | solution.py:346
  37.3 17.7 %shard_map.64 = f32[2,2,256,256]{3,2,1,0:T(8,128)} custom-call(s32[4]{0:T(128)} %pad_add_fusion.rect_ref, f32[5,256,256]{2,1,0:T(8,128)} %pad_maximum_fusion.1.resid_ref.data_ref, f32[5,256,256]{2,1,0:T(8,128)} %pad_maximum_fusion.1.resid_ref.data_ref, f32[2,128,256]{2,1,0:T(8,128)} %reshape.94.wrow_ref, f32[2,256,128]{2,1,0:T(8,128)} %reshape.99.wcol_ref), custom_call_target="tpu_custom_call" | custom-call | tf_op jit(solution)/shard_map/pallas_call | solution.py:302
  55.0 1.2 %fusion.10 = (f32[2,2,65,128]{3,2,1,0:T(8,128)S(1)}, f32[2,2,65,128]{3,2,1,0:T(8,128)S(1)}) fusion(f32[2,2,256,256]{3,2,1,0:T(8,128)} %shard_map.64), kind=kLoop, calls=%fused_computation.60 | loop fusion | bytes 532480 | tf_op jit(solution)/shard_map/slice | solution.py:162
  56.2 3.6 %collective-permute-start.4 = (f32[2,2,65,128]{3,2,1,0:T(8,128)S(1)}, f32[2,2,65,128]{3,2,1,0:T(8,128)S(1)}, u32[]{:S(2)}, u32[]{:S(2)}) collective-permute-start(f32[2,2,65,128]{3,2,1,0:T(8,128)S(1)} %get-tuple-element.13), channel_id=1, source_target_pairs={{0,16},{16,32},{32,48},{48,64},{64,80},{80,96},{96,112},{1,17},{17... | collective-permute-start | bytes 399368 | tf_op jit(solution)/shard_map/ppermute | solution.py:167
  59.8 2.3 %collective-permute-start.5 = (f32[2,2,65,128]{3,2,1,0:T(8,128)S(1)}, f32[2,2,65,128]{3,2,1,0:T(8,128)S(1)}, u32[]{:S(2)}, u32[]{:S(2)}) collective-permute-start(f32[2,2,65,128]{3,2,1,0:T(8,128)S(1)} %get-tuple-element.14), channel_id=1, source_target_pairs={{16,0},{32,16},{48,32},{64,48},{80,64},{96,80},{112,96},{17,1},{33... | collective-permute-start | bytes 399368 | tf_op jit(solution)/shard_map/ppermute | solution.py:167
  62.1 0.1 and_and_fusion
  62.2 1.2 %slice.184 = f32[2,2,128,128]{3,2,1,0:T(8,128)S(1)} slice(f32[2,2,256,256]{3,2,1,0:T(8,128)} %shard_map.64), slice={[0:2], [0:2], [64:192], [64:192]} | slice | bytes 524288 | tf_op jit(solution)/shard_map/slice | solution.py:376
  63.4 0.3 collective-permute-done.4
  63.7 4.0 %collective-permute-done.5 = f32[2,2,65,128]{3,2,1,0:T(8,128)S(1)} collective-permute-done((f32[2,2,65,128]{3,2,1,0:T(8,128)S(1)}, f32[2,2,65,128]{3,2,1,0:T(8,128)S(1)}, u32[]{:S(2)}, u32[]{:S(2)}) %collective-permute-start.5) | collective-permute-done | bytes 133152 | tf_op jit(solution)/shard_map/ppermute | solution.py:167
  67.8 0.2 fusion.12
  68.0 0.3 copy.19
  68.3 2.1 %collective-permute-start.6 = (f32[2,2,258,65]{2,1,3,0:T(2,128)S(1)}, f32[2,2,258,65]{2,1,3,0:T(2,128)S(1)}, u32[]{:S(2)}, u32[]{:S(2)}) collective-permute-start(f32[2,2,258,65]{2,1,3,0:T(2,128)S(1)} %copy.19), channel_id=1, source_target_pairs={{0,1},{1,2},{2,3},{3,4},{4,5},{5,6},{6,7},{7,8},{8,9},{9,10},{10,1... | collective-permute-start | bytes 804968 | tf_op jit(solution)/shard_map/ppermute | solution.py:167
  70.4 1.0 copy.20
  71.4 7.4 %collective-permute-start.7 = (f32[2,2,258,65]{2,1,3,0:T(2,128)}, f32[2,2,258,65]{2,1,3,0:T(2,128)}, u32[]{:S(2)}, u32[]{:S(2)}) collective-permute-start(f32[2,2,258,65]{2,1,3,0:T(2,128)} %copy.20), channel_id=1, source_target_pairs={{1,0},{2,1},{3,2},{4,3},{5,4},{6,5},{7,6},{8,7},{9,8},{10,9},{11,1... | collective-permute-start | bytes 804968 | tf_op jit(solution)/shard_map/ppermute | solution.py:167
  78.9 2.3 %collective-permute-done.6 = f32[2,2,258,65]{2,1,3,0:T(2,128)S(1)} collective-permute-done((f32[2,2,258,65]{2,1,3,0:T(2,128)S(1)}, f32[2,2,258,65]{2,1,3,0:T(2,128)S(1)}, u32[]{:S(2)}, u32[]{:S(2)}) %collective-permute-start.6) | collective-permute-done | bytes 268352 | tf_op jit(solution)/shard_map/ppermute | solution.py:167
  81.2 0.3 copy.21
  81.5 2.8 %collective-permute-done.7 = f32[2,2,258,65]{2,1,3,0:T(2,128)} collective-permute-done((f32[2,2,258,65]{2,1,3,0:T(2,128)}, f32[2,2,258,65]{2,1,3,0:T(2,128)}, u32[]{:S(2)}, u32[]{:S(2)}) %collective-permute-start.7) | collective-permute-done | bytes 268352 | tf_op jit(solution)/shard_map/ppermute | solution.py:167
  84.3 1.2 %copy.22 = f32[2,2,258,65]{3,2,1,0:T(8,128)S(1)} copy(f32[2,2,258,65]{2,1,3,0:T(2,128)} %collective-permute-done.7) | data formatting | bytes 536640 | tf_op jit(solution)/shard_map/ppermute | solution.py:167
  85.6 0.6 pad_maximum_fusion
  86.3 0.2 select_select_fusion.1
  86.5 0.8 dynamic-slice_reduce_fusion.1
  87.3 0.4 select_select_fusion
  87.8 0.2 copy-done.6
  88.0 0.2 multiply_add_fusion
  88.2 0.5 maximum_select_fusion
  88.7 0.3 multiply_subtract_fusion.1
  89.0 0.9 slice-done
  89.9 2.7 %fusion.4 = f32[2,2,256,256]{3,2,1,0:T(8,128)} fusion(f32[2,2,256,256]{3,2,1,0:T(8,128)S(1)} %bitcast.38, f32[2,2,258,258]{3,2,1,0:T(8,128)S(1)} %maximum_select_fusion, f32[2,1,256,256]{3,2,1,0:T(8,128)S(1)} %get-tuple-element.8, f32[2,1,256,256]{3,2,1,0:T(8,128)S(1)} %get-tuple-element.7, f32[256,256]{1,0:T(8,128)S(1)} %slice_bitcast_fusion), kind=kLoop, calls=%fused_computation.10 | loop fusion | flops 4194304 | bytes 12845056 | tf_op jit(solution)/shard_map/sub | solution.py:373
  92.6 17.6 %shard_map.65 = f32[2,2,256,256]{3,2,1,0:T(8,128)} custom-call(s32[4]{0:T(128)} %pad_add_fusion.rect_ref, f32[4,256,256]{2,1,0:T(8,128)} %bitcast.43, f32[5,256,256]{2,1,0:T(8,128)} %pad_maximum_fusion.1.resid_ref.data_ref, f32[2,128,256]{2,1,0:T(8,128)} %reshape.94.wrow_ref, f32[2,256,128]{2,1,0:T(8,128)} %reshape.99.wcol_ref), custom_call_target="tpu_custom_call" | custom-call | tf_op jit(solution)/shard_map/pallas_call | solution.py:302
  110.2 2.1 %slice_add_fusion.6 = f32[2,2,128,128]{3,2,1,0:T(8,128)} fusion(f32[2,2,256,256]{3,2,1,0:T(8,128)} %shard_map.65, f32[2,2,256,256]{3,2,1,0:T(8,128)} %shard_map.64), kind=kLoop, calls=%fused_computation.36 | loop fusion | flops 65536 | bytes 786432 | tf_op jit(solution)/shard_map/add | solution.py:377
  (37 shorter events, 0.3 us)
Async XLA Ops:
  0.0 15.9 %copy-start.1 = (f32[2,2,128,128]{3,2,1,0:T(8,128)S(1)}, f32[2,2,128,128]{3,2,1,0:T(8,128)}, u32[]{:S(2)}) copy-start(f32[2,2,128,128]{3,2,1,0:T(8,128)} %param.6) | copy-start | bytes 786436
  0.0 15.9 %copy-start.2 = (f32[128,128]{1,0:T(8,128)S(1)}, f32[128,128]{1,0:T(8,128)}, u32[]{:S(2)}) copy-start(f32[128,128]{1,0:T(8,128)} %param.7) | copy-start | bytes 196612
  0.0 8.9 %copy-start.7 = (s32[1,1,4]{2,1,0:T(1,128)S(1)}, s32[1,1,4]{2,1,0:T(1,128)}, u32[]{:S(2)}) copy-start(s32[1,1,4]{2,1,0:T(1,128)} %param.10) | copy-start | bytes 52
  0.0 12.2 %copy-start.4 = (f32[2,2,64,64]{3,2,1,0:T(8,128)S(1)}, f32[2,2,64,64]{3,2,1,0:T(8,128)}, u32[]{:S(2)}) copy-start(f32[2,2,64,64]{3,2,1,0:T(8,128)} %param.8) | copy-start | bytes 196612
  2.0 10.3 %collective-permute-start = (f32[6,64,128]{2,1,0:T(8,128)S(1)}, f32[6,64,128]{2,1,0:T(8,128)S(1)}, u32[]{:S(2)}, u32[]{:S(2)}) collective-permute-start(f32[6,64,128]{2,1,0:T(8,128)S(1)} %pad_maximum_fusion.7), channel_id=1, source_target_pairs={{0,16},{16,32},{32,48},{48,64},{64,80},{80,96},{96,112},{1,17},{17... | collective-permute-start | bytes 589832 | tf_op jit(solution)/shard_map/ppermute | solution.py:167
  6.8 9.2 %collective-permute-start.1 = (f32[6,64,128]{2,1,0:T(8,128)S(1)}, f32[6,64,128]{2,1,0:T(8,128)S(1)}, u32[]{:S(2)}, u32[]{:S(2)}) collective-permute-start(f32[6,64,128]{2,1,0:T(8,128)S(1)} %fusion.7), channel_id=1, source_target_pairs={{16,0},{32,16},{48,32},{64,48},{80,64},{96,80},{112,96},{17,1},{33... | collective-permute-start | bytes 589832 | tf_op jit(solution)/shard_map/ppermute | solution.py:167
  15.9 0.7 copy-start.5
  16.9 10.4 %slice-start.1 = ((f32[6,64,128]{2,1,0:T(8,128)}), f32[1,64,128]{2,1,0:T(8,128)S(1)}, s32[]{:S(2)}) async-start(f32[6,64,128]{2,1,0:T(8,128)} %copy-done.5), calls=%async_computation.1 | async-start | bytes 65536 | tf_op jit(solution)/shard_map/slice | solution.py:352
  16.9 10.5 %copy-start.3 = (f32[2,2,64,64]{3,2,1,0:T(8,128)S(1)}, f32[2,2,64,64]{3,2,1,0:T(8,128)}, u32[]{:S(2)}) copy-start(f32[2,2,64,64]{3,2,1,0:T(8,128)} %param.9) | copy-start | bytes 196612
  16.9 12.8 %collective-permute-start.2 = (f32[6,256,64]{1,2,0:T(8,128)S(1)}, f32[6,256,64]{1,2,0:T(8,128)S(1)}, u32[]{:S(2)}, u32[]{:S(2)}) collective-permute-start(f32[6,256,64]{1,2,0:T(8,128)S(1)} %copy.11), channel_id=1, source_target_pairs={{0,1},{1,2},{2,3},{3,4},{4,5},{5,6},{6,7},{7,8},{8,9},{9,10},{10,1... | collective-permute-start | bytes 1179656 | tf_op jit(solution)/shard_map/ppermute | solution.py:167
  19.3 12.5 %collective-permute-start.3 = (f32[6,256,64]{1,2,0:T(8,128)S(1)}, f32[6,256,64]{1,2,0:T(8,128)}, u32[]{:S(2)}, u32[]{:S(2)}) collective-permute-start(f32[6,256,64]{1,2,0:T(8,128)S(1)} %copy.13), channel_id=1, source_target_pairs={{1,0},{2,1},{3,2},{4,3},{5,4},{6,5},{7,6},{8,7},{9,8},{10,9},{11,1... | collective-permute-start | bytes 1179656 | tf_op jit(solution)/shard_map/ppermute | solution.py:167
  56.2 7.5 %collective-permute-start.4 = (f32[2,2,65,128]{3,2,1,0:T(8,128)S(1)}, f32[2,2,65,128]{3,2,1,0:T(8,128)S(1)}, u32[]{:S(2)}, u32[]{:S(2)}) collective-permute-start(f32[2,2,65,128]{3,2,1,0:T(8,128)S(1)} %get-tuple-element.13), channel_id=1, source_target_pairs={{0,16},{16,32},{32,48},{48,64},{64,80},{80,96},{96,112},{1,17},{17... | collective-permute-start | bytes 399368 | tf_op jit(solution)/shard_map/ppermute | solution.py:167
  59.8 7.9 %collective-permute-start.5 = (f32[2,2,65,128]{3,2,1,0:T(8,128)S(1)}, f32[2,2,65,128]{3,2,1,0:T(8,128)S(1)}, u32[]{:S(2)}, u32[]{:S(2)}) collective-permute-start(f32[2,2,65,128]{3,2,1,0:T(8,128)S(1)} %get-tuple-element.14), channel_id=1, source_target_pairs={{16,0},{32,16},{48,32},{64,48},{80,64},{96,80},{112,96},{17,1},{33... | collective-permute-start | bytes 399368 | tf_op jit(solution)/shard_map/ppermute | solution.py:167
  68.3 10.6 %copy-start = (f32[5,256,256]{2,1,0:T(8,128)S(1)}, f32[5,256,256]{2,1,0:T(8,128)}, u32[]{:S(2)}) copy-start(f32[5,256,256]{2,1,0:T(8,128)} %pad_maximum_fusion.1.resid_ref.data_ref) | copy-start | bytes 3932164
  68.3 12.9 %collective-permute-start.6 = (f32[2,2,258,65]{2,1,3,0:T(2,128)S(1)}, f32[2,2,258,65]{2,1,3,0:T(2,128)S(1)}, u32[]{:S(2)}, u32[]{:S(2)}) collective-permute-start(f32[2,2,258,65]{2,1,3,0:T(2,128)S(1)} %copy.19), channel_id=1, source_target_pairs={{0,1},{1,2},{2,3},{3,4},{4,5},{5,6},{6,7},{7,8},{8,9},{9,10},{10,1... | collective-permute-start | bytes 804968 | tf_op jit(solution)/shard_map/ppermute | solution.py:167
  71.4 12.9 %collective-permute-start.7 = (f32[2,2,258,65]{2,1,3,0:T(2,128)}, f32[2,2,258,65]{2,1,3,0:T(2,128)}, u32[]{:S(2)}, u32[]{:S(2)}) collective-permute-start(f32[2,2,258,65]{2,1,3,0:T(2,128)} %copy.20), channel_id=1, source_target_pairs={{1,0},{2,1},{3,2},{4,3},{5,4},{6,5},{7,6},{8,7},{9,8},{10,9},{11,1... | collective-permute-start | bytes 804968 | tf_op jit(solution)/shard_map/ppermute | solution.py:167
  87.3 0.7 copy-start.6
  88.7 1.2 %slice-start = ((f32[5,256,256]{2,1,0:T(8,128)}), f32[4,256,256]{2,1,0:T(8,128)S(1)}, s32[]{:S(2)}) async-start(f32[5,256,256]{2,1,0:T(8,128)} %pad_maximum_fusion.1.resid_ref.data_ref), calls=%async_computation | async-start | bytes 2097152 | tf_op jit(solution)/shard_map/slice | solution.py:347

commit v2 on v1

--- a/solution.py
+++ b/solution.py
@@ -178,14 +178,6 @@
     return jnp.concatenate(rows, axis=-2)
 
 
-def shift_rows(x, step):
-    return pltpu.roll(x, step % x.shape[0], 0)
-
-
-def shift_cols(x, step):
-    return pltpu.roll(x, step % x.shape[1], 1)
-
-
 def solve_kernel(rect_ref, resid_ref, data_ref, wrow_ref, wcol_ref, out_ref):
     height, breadth = (resid_ref.shape[1], resid_ref.shape[2])
     half = height // 2
@@ -195,40 +187,37 @@
     live = (row_ids >= upper) & (row_ids < lower) & (col_ids >= left) & (col_ids < right)
     top, bottom = (row_ids == upper, row_ids == lower - 1)
     first, last = (col_ids == left, col_ids == right - 1)
-    wave = data_ref[4]
+    row_flag = top.astype(jnp.float32) + bottom.astype(jnp.float32)
+    col_flag = first.astype(jnp.float32) + last.astype(jnp.float32)
+    edge_flag = 4.0 * (row_flag + col_flag)
     zero = jnp.zeros((height, breadth), jnp.float32)
 
     def mask(x):
         return jnp.where(live, x, zero)
 
-    def neighbours(x):
-        up = jnp.where(top, x, shift_rows(x, 1))
-        down = jnp.where(bottom, x, shift_rows(x, -1))
-        edge, edge_ghost, corner, corner_ghost = (zero, zero, zero, zero)
-        for line, line_flag in ((up, top), (x, None), (down, bottom)):
-            lft = jnp.where(first, line, shift_cols(line, 1))
-            rgt = jnp.where(last, line, shift_cols(line, -1))
-            lft_flag = first if line_flag is None else (first | line_flag)
-            rgt_flag = last if line_flag is None else (last | line_flag)
-            if line_flag is None:
-                edge = edge + lft + rgt
-                edge_ghost = edge_ghost + jnp.where(lft_flag, lft, zero) + jnp.where(rgt_flag, rgt, zero)
-            else:
-                edge = edge + line
-                edge_ghost = edge_ghost + jnp.where(line_flag, line, zero)
-                corner = corner + lft + rgt
-                corner_ghost = corner_ghost + jnp.where(lft_flag, lft, zero) + jnp.where(rgt_flag, rgt, zero)
-        return edge, edge_ghost, corner, corner_ghost
+    def rows_sum(x):
+        up = jnp.where(top, x, pltpu.roll(x, 1, 0))
+        down = jnp.where(bottom, x, pltpu.roll(x, height - 1, 0))
+        return up + down
+
+    def cols_sum(x):
+        lft = jnp.where(first, x, pltpu.roll(x, 1, 1))
+        rgt = jnp.where(last, x, pltpu.roll(x, breadth - 1, 1))
+        return lft + rgt
+
+    def stencil(x):
+        vertical = rows_sum(x)
+        ghost_rows = row_flag * x
+        total = 4.0 * (vertical + cols_sum(x)) + cols_sum(vertical)
+        ghost = edge_flag * x + cols_sum(ghost_rows) + col_flag * (vertical - ghost_rows)
+        return total, ghost
 
     def operator(real_part, imag_part, sign):
-        er, egr, cr, cgr = neighbours(real_part)
-        ei, egi, ci, cgi = neighbours(imag_part)
-        edge_r = er + sign * ROBIN_COEF * egi
-        edge_i = ei - sign * ROBIN_COEF * egr
-        corner_r = cr + sign * ROBIN_COEF * cgi
-        corner_i = ci - sign * ROBIN_COEF * cgr
-        lap_r = (4.0 * edge_r + corner_r - 20.0 * real_part) / 6.0
-        lap_i = (4.0 * edge_i + corner_i - 20.0 * imag_part) / 6.0
+        wave = data_ref[4]
+        total_r, ghost_r = stencil(real_part)
+        total_i, ghost_i = stencil(imag_part)
+        lap_r = (total_r + sign * ROBIN_COEF * ghost_i - 20.0 * real_part) / 6.0
+        lap_i = (total_i - sign * ROBIN_COEF * ghost_r - 20.0 * imag_part) / 6.0
         mass_r = real_part - sign * DAMPING * imag_part
         mass_i = imag_part + sign * DAMPING * real_part
         return (-lap_r - wave * mass_r, -lap_i - wave * mass_i)
@@ -240,27 +229,25 @@
         outs_r, outs_i = ([], [])
         for h in range(breadth // half):
             cols = slice(h * half, (h + 1) * half)
-            stacked = jnp.concatenate([real_part[:, cols], imag_part[:, cols]], axis=0)
-            prod = dot(stacked, wrow_ref[h])
-            outs_r.append(prod[:height, :half] - sign * prod[height:, half:])
-            outs_i.append(prod[height:, :half] + sign * prod[:height, half:])
+            prod_r = dot(real_part[:, cols], wrow_ref[h])
+            prod_i = dot(imag_part[:, cols], wrow_ref[h])
+            outs_r.append(prod_r[:, :half] - sign * prod_i[:, half:])
+            outs_i.append(prod_i[:, :half] + sign * prod_r[:, half:])
         return (jnp.concatenate(outs_r, axis=1), jnp.concatenate(outs_i, axis=1))
 
     def cols_apply(real_part, imag_part, sign):
         outs_r, outs_i = ([], [])
         for h in range(height // half):
             rows = slice(h * half, (h + 1) * half)
-            stacked = jnp.concatenate([real_part[rows, :], imag_part[rows, :]], axis=1)
-            prod = dot(wcol_ref[h], stacked)
-            outs_r.append(prod[:half, :breadth] - sign * prod[half:, breadth:])
-            outs_i.append(prod[:half, breadth:] + sign * prod[half:, :breadth])
+            prod_r = dot(wcol_ref[h], real_part[rows, :])
+            prod_i = dot(wcol_ref[h], imag_part[rows, :])
+            outs_r.append(prod_r[:half] - sign * prod_i[half:])
+            outs_i.append(prod_i[:half] + sign * prod_r[half:])
         return (jnp.concatenate(outs_r, axis=0), jnp.concatenate(outs_i, axis=0))
 
     def problem_body(problem, carry):
         sign = 1.0 - 2.0 * problem.astype(jnp.float32)
-        res_r = resid_ref[2 * problem]
-        res_i = resid_ref[2 * problem + 1]
-        up_r, up_i = rows_apply(mask(res_r), mask(res_i), sign)
+        up_r, up_i = rows_apply(mask(resid_ref[2 * problem]), mask(resid_ref[2 * problem + 1]), sign)
         out_ref[problem, 0] = mask(up_r)
         out_ref[problem, 1] = mask(up_i)
 

time: 114 us -> 113 us (level)
  no operation moved by 1% of the time
where the time goes in v2:
time: 113 us; the launch traced here: 111 us
  Pallas kernels  34.2 us (30%)
  starting transfers between devices  30.5 us (27%)
  waiting for transfers between devices  16 us (14%)
  local copies, waits for them, and re-layouts  15.2 us (13%)
  other arithmetic  12.2 us (11%)
  between operations  3.09 us (3%)
    pallas_call x2, Pallas kernels, solve_local_kernel(): pl.pallas_call(solve_kernel, out_shape=jax.ShapeDtypeStruct(out_shape, re...  34.2 us
    ppermute x8, starting transfers between devices, exchange_axis(): return (lax.ppermute(last, axis, up), lax.ppermute(first, axis, down))  30.5 us
    ppermute x8, waiting for transfers between devices, exchange_axis(): return (lax.ppermute(last, axis, up), lax.ppermute(first, axis, down))  16 us
    sub x1, other arithmetic, shards(): resid_ext = sources_ext - apply_operator(padded, wave_ext, signs)  2.7 us
  transfers between devices with their start and end apart: 8, of which 7 were waited for; matrix products, arithmetic and copies ran while one was open for 6% of the time, Pallas kernels for 0%

profile of v2, /device:TPU:6, one launch (start us, length us, event | category | flops | bytes accessed | tf_op | source)
XLA Modules:
  0.0 111.2 jit_solution(14560140886421888495)
XLA Ops:
  0.0 0.9 fusion.14
  1.0 0.1 reshape_squeeze.12
  1.0 0.9 fusion.8
  2.0 3.8 %collective-permute-start = (f32[6,64,128]{2,1,0:T(8,128)S(1)}, f32[6,64,128]{2,1,0:T(8,128)S(1)}, u32[]{:S(2)}, u32[]{:S(2)}) collective-permute-start(f32[6,64,128]{2,1,0:T(8,128)S(1)} %pad_maximum_fusion.7), channel_id=1, source_target_pairs={{0,16},{16,32},{32,48},{48,64},{64,80},{80,96},{96,112},{1,17},{17... | collective-permute-start | bytes 589832 | tf_op jit(solution)/shard_map/ppermute | solution.py:167
  5.7 0.1 reshape_squeeze.13
  5.8 0.9 fusion.7
  6.8 2.1 %collective-permute-start.1 = (f32[6,64,128]{2,1,0:T(8,128)S(1)}, f32[6,64,128]{2,1,0:T(8,128)S(1)}, u32[]{:S(2)}, u32[]{:S(2)}) collective-permute-start(f32[6,64,128]{2,1,0:T(8,128)S(1)} %fusion.7), channel_id=1, source_target_pairs={{16,0},{32,16},{48,32},{64,48},{80,64},{96,80},{112,96},{17,1},{33... | collective-permute-start | bytes 589832 | tf_op jit(solution)/shard_map/ppermute | solution.py:167
  8.9 0.7 fusion.15
  12.3 3.6 %collective-permute-done.1 = f32[6,64,128]{2,1,0:T(8,128)S(1)} collective-permute-done((f32[6,64,128]{2,1,0:T(8,128)S(1)}, f32[6,64,128]{2,1,0:T(8,128)S(1)}, u32[]{:S(2)}, u32[]{:S(2)}) %collective-permute-start.1) | collective-permute-done | bytes 196640 | tf_op jit(solution)/shard_map/ppermute | solution.py:167
  16.0 0.2 fusion.11
  16.2 0.3 copy-done.5
  16.6 0.1 select_maximum_fusion.1
  16.6 0.2 copy.11
  16.9 0.0 slice-start.1
  16.9 2.1 %collective-permute-start.2 = (f32[6,256,64]{1,2,0:T(8,128)S(1)}, f32[6,256,64]{1,2,0:T(8,128)S(1)}, u32[]{:S(2)}, u32[]{:S(2)}) collective-permute-start(f32[6,256,64]{1,2,0:T(8,128)S(1)} %copy.11), channel_id=1, source_target_pairs={{0,1},{1,2},{2,3},{3,4},{4,5},{5,6},{6,7},{7,8},{8,9},{9,10},{10,1... | collective-permute-start | bytes 1179656 | tf_op jit(solution)/shard_map/ppermute | solution.py:167
  19.0 0.1 select_maximum_fusion
  19.0 0.2 copy.13
  19.3 7.3 %collective-permute-start.3 = (f32[6,256,64]{1,2,0:T(8,128)S(1)}, f32[6,256,64]{1,2,0:T(8,128)}, u32[]{:S(2)}, u32[]{:S(2)}) collective-permute-start(f32[6,256,64]{1,2,0:T(8,128)S(1)} %copy.13), channel_id=1, source_target_pairs={{1,0},{2,1},{3,2},{4,3},{5,4},{6,5},{7,6},{8,7},{9,8},{10,9},{11,1... | collective-permute-start | bytes 1179656 | tf_op jit(solution)/shard_map/ppermute | solution.py:167
  26.6 0.7 pad_add_fusion.rect_ref
  27.2 0.1 reshape.95
  27.3 0.1 reshape.96
  27.4 0.3 multiply_bitcast_fusion
  27.7 1.0 reshape.99.wcol_ref
  28.7 1.1 collective-permute-done.2
  29.8 0.2 copy.27
  30.0 1.8 %collective-permute-done.3 = f32[6,256,64]{1,2,0:T(8,128)} collective-permute-done((f32[6,256,64]{1,2,0:T(8,128)S(1)}, f32[6,256,64]{1,2,0:T(8,128)}, u32[]{:S(2)}, u32[]{:S(2)}) %collective-permute-start.3) | collective-permute-done | bytes 393248 | tf_op jit(solution)/shard_map/ppermute | solution.py:167
  31.8 1.0 slice.179
  32.8 0.2 copy.28
  33.1 0.1 copy.23
  33.2 0.8 slice.181
  33.9 0.1 copy.24
  34.1 0.2 copy.17
  34.2 0.2 multiply_bitcast_fusion.1
  34.5 1.2 %reshape.94.wrow_ref = f32[2,128,256]{2,1,0:T(8,128)} reshape(f32[2,2,64,2,2,64]{5,4,3,2,1,0:T(2,128)S(1)} %multiply_bitcast_fusion.1) | data formatting | bytes 524288 | tf_op jit(solution)/shard_map/reshape | solution.py:279
  35.6 1.7 %pad_maximum_fusion.1.resid_ref.data_ref = f32[5,256,256]{2,1,0:T(8,128)} fusion(f32[5,256,64]{2,1,0:T(8,128)S(1)} %copy.28, f32[5,64,128]{2,1,0:T(8,128)S(1)} %slice.175, f32[1,128,128]{2,1,0:T(8,128)S(1)} %bitcast.47, f32[4,128,128]{2,1,0:T(8,128)S(1)} %bitcast.42, f32[5,64,128]{2,1,0:T(8,128)S(1)} %slice.174, f32[5,256,64]{2,1,0:T(8,128)S(1)} %copy.27), kind=kLoop, calls=%fused_computation.4 | loop fusion | flops 1638400 | bytes 2621440 | tf_op jit(solution)/shard_map/concatenate | solution.py:333
  37.3 17.1 %shard_map.64 = f32[2,2,256,256]{3,2,1,0:T(8,128)} custom-call(s32[4]{0:T(128)} %pad_add_fusion.rect_ref, f32[5,256,256]{2,1,0:T(8,128)} %pad_maximum_fusion.1.resid_ref.data_ref, f32[5,256,256]{2,1,0:T(8,128)} %pad_maximum_fusion.1.resid_ref.data_ref, f32[2,128,256]{2,1,0:T(8,128)} %reshape.94.wrow_ref, f32[2,256,128]{2,1,0:T(8,128)} %reshape.99.wcol_ref), custom_call_target="tpu_custom_call" | custom-call | tf_op jit(solution)/shard_map/pallas_call | solution.py:289
  54.4 1.2 %fusion.10 = (f32[2,2,65,128]{3,2,1,0:T(8,128)S(1)}, f32[2,2,65,128]{3,2,1,0:T(8,128)S(1)}) fusion(f32[2,2,256,256]{3,2,1,0:T(8,128)} %shard_map.64), kind=kLoop, calls=%fused_computation.60 | loop fusion | bytes 532480 | tf_op jit(solution)/shard_map/slice | solution.py:162
  55.6 3.6 %collective-permute-start.4 = (f32[2,2,65,128]{3,2,1,0:T(8,128)S(1)}, f32[2,2,65,128]{3,2,1,0:T(8,128)S(1)}, u32[]{:S(2)}, u32[]{:S(2)}) collective-permute-start(f32[2,2,65,128]{3,2,1,0:T(8,128)S(1)} %get-tuple-element.13), channel_id=1, source_target_pairs={{0,16},{16,32},{32,48},{48,64},{64,80},{80,96},{96,112},{1,17},{17... | collective-permute-start | bytes 399368 | tf_op jit(solution)/shard_map/ppermute | solution.py:167
  59.3 2.2 %collective-permute-start.5 = (f32[2,2,65,128]{3,2,1,0:T(8,128)S(1)}, f32[2,2,65,128]{3,2,1,0:T(8,128)S(1)}, u32[]{:S(2)}, u32[]{:S(2)}) collective-permute-start(f32[2,2,65,128]{3,2,1,0:T(8,128)S(1)} %get-tuple-element.14), channel_id=1, source_target_pairs={{16,0},{32,16},{48,32},{64,48},{80,64},{96,80},{112,96},{17,1},{33... | collective-permute-start | bytes 399368 | tf_op jit(solution)/shard_map/ppermute | solution.py:167
  61.5 0.1 and_and_fusion
  61.6 1.2 %slice.184 = f32[2,2,128,128]{3,2,1,0:T(8,128)S(1)} slice(f32[2,2,256,256]{3,2,1,0:T(8,128)} %shard_map.64), slice={[0:2], [0:2], [64:192], [64:192]} | slice | bytes 524288 | tf_op jit(solution)/shard_map/slice | solution.py:363
  62.8 0.4 collective-permute-done.4
  63.2 4.0 %collective-permute-done.5 = f32[2,2,65,128]{3,2,1,0:T(8,128)S(1)} collective-permute-done((f32[2,2,65,128]{3,2,1,0:T(8,128)S(1)}, f32[2,2,65,128]{3,2,1,0:T(8,128)S(1)}, u32[]{:S(2)}, u32[]{:S(2)}) %collective-permute-start.5) | collective-permute-done | bytes 133152 | tf_op jit(solution)/shard_map/ppermute | solution.py:167
  67.2 0.2 fusion.12
  67.4 0.3 copy.19
  67.8 2.1 %collective-permute-start.6 = (f32[2,2,258,65]{2,1,3,0:T(2,128)S(1)}, f32[2,2,258,65]{2,1,3,0:T(2,128)S(1)}, u32[]{:S(2)}, u32[]{:S(2)}) collective-permute-start(f32[2,2,258,65]{2,1,3,0:T(2,128)S(1)} %copy.19), channel_id=1, source_target_pairs={{0,1},{1,2},{2,3},{3,4},{4,5},{5,6},{6,7},{7,8},{8,9},{9,10},{10,1... | collective-permute-start | bytes 804968 | tf_op jit(solution)/shard_map/ppermute | solution.py:167
  69.8 1.0 copy.20
  70.9 7.4 %collective-permute-start.7 = (f32[2,2,258,65]{2,1,3,0:T(2,128)}, f32[2,2,258,65]{2,1,3,0:T(2,128)}, u32[]{:S(2)}, u32[]{:S(2)}) collective-permute-start(f32[2,2,258,65]{2,1,3,0:T(2,128)} %copy.20), channel_id=1, source_target_pairs={{1,0},{2,1},{3,2},{4,3},{5,4},{6,5},{7,6},{8,7},{9,8},{10,9},{11,1... | collective-permute-start | bytes 804968 | tf_op jit(solution)/shard_map/ppermute | solution.py:167
  78.3 2.3 %collective-permute-done.6 = f32[2,2,258,65]{2,1,3,0:T(2,128)S(1)} collective-permute-done((f32[2,2,258,65]{2,1,3,0:T(2,128)S(1)}, f32[2,2,258,65]{2,1,3,0:T(2,128)S(1)}, u32[]{:S(2)}, u32[]{:S(2)}) %collective-permute-start.6) | collective-permute-done | bytes 268352 | tf_op jit(solution)/shard_map/ppermute | solution.py:167
  80.7 0.3 copy.21
  80.9 2.8 %collective-permute-done.7 = f32[2,2,258,65]{2,1,3,0:T(2,128)} collective-permute-done((f32[2,2,258,65]{2,1,3,0:T(2,128)}, f32[2,2,258,65]{2,1,3,0:T(2,128)}, u32[]{:S(2)}, u32[]{:S(2)}) %collective-permute-start.7) | collective-permute-done | bytes 268352 | tf_op jit(solution)/shard_map/ppermute | solution.py:167
  83.8 1.2 %copy.22 = f32[2,2,258,65]{3,2,1,0:T(8,128)S(1)} copy(f32[2,2,258,65]{2,1,3,0:T(2,128)} %collective-permute-done.7) | data formatting | bytes 536640 | tf_op jit(solution)/shard_map/ppermute | solution.py:167
  85.0 0.6 pad_maximum_fusion
  85.7 0.2 select_select_fusion.1
  86.0 0.8 dynamic-slice_reduce_fusion.1
  86.8 0.4 select_select_fusion
  87.2 0.2 copy-done.6
  87.4 0.2 multiply_add_fusion
  87.6 0.5 maximum_select_fusion
  88.1 0.3 multiply_subtract_fusion.1
  88.5 0.9 slice-done
  89.3 2.7 %fusion.4 = f32[2,2,256,256]{3,2,1,0:T(8,128)} fusion(f32[2,2,256,256]{3,2,1,0:T(8,128)S(1)} %bitcast.38, f32[2,2,258,258]{3,2,1,0:T(8,128)S(1)} %maximum_select_fusion, f32[2,1,256,256]{3,2,1,0:T(8,128)S(1)} %get-tuple-element.8, f32[2,1,256,256]{3,2,1,0:T(8,128)S(1)} %get-tuple-element.7, f32[256,256]{1,0:T(8,128)S(1)} %slice_bitcast_fusion), kind=kLoop, calls=%fused_computation.10 | loop fusion | flops 4194304 | bytes 12845056 | tf_op jit(solution)/shard_map/sub | solution.py:360
  92.0 17.0 %shard_map.65 = f32[2,2,256,256]{3,2,1,0:T(8,128)} custom-call(s32[4]{0:T(128)} %pad_add_fusion.rect_ref, f32[4,256,256]{2,1,0:T(8,128)} %bitcast.43, f32[5,256,256]{2,1,0:T(8,128)} %pad_maximum_fusion.1.resid_ref.data_ref, f32[2,128,256]{2,1,0:T(8,128)} %reshape.94.wrow_ref, f32[2,256,128]{2,1,0:T(8,128)} %reshape.99.wcol_ref), custom_call_target="tpu_custom_call" | custom-call | tf_op jit(solution)/shard_map/pallas_call | solution.py:289
  109.1 2.1 %slice_add_fusion.6 = f32[2,2,128,128]{3,2,1,0:T(8,128)} fusion(f32[2,2,256,256]{3,2,1,0:T(8,128)} %shard_map.65, f32[2,2,256,256]{3,2,1,0:T(8,128)} %shard_map.64), kind=kLoop, calls=%fused_computation.36 | loop fusion | flops 65536 | bytes 786432 | tf_op jit(solution)/shard_map/add | solution.py:364
  (37 shorter events, 0.3 us)
Async XLA Ops:
  0.0 15.9 %copy-start.1 = (f32[2,2,128,128]{3,2,1,0:T(8,128)S(1)}, f32[2,2,128,128]{3,2,1,0:T(8,128)}, u32[]{:S(2)}) copy-start(f32[2,2,128,128]{3,2,1,0:T(8,128)} %param.6) | copy-start | bytes 786436
  0.0 15.9 %copy-start.2 = (f32[128,128]{1,0:T(8,128)S(1)}, f32[128,128]{1,0:T(8,128)}, u32[]{:S(2)}) copy-start(f32[128,128]{1,0:T(8,128)} %param.7) | copy-start | bytes 196612
  0.0 8.9 %copy-start.7 = (s32[1,1,4]{2,1,0:T(1,128)S(1)}, s32[1,1,4]{2,1,0:T(1,128)}, u32[]{:S(2)}) copy-start(s32[1,1,4]{2,1,0:T(1,128)} %param.10) | copy-start | bytes 52
  0.0 12.2 %copy-start.4 = (f32[2,2,64,64]{3,2,1,0:T(8,128)S(1)}, f32[2,2,64,64]{3,2,1,0:T(8,128)}, u32[]{:S(2)}) copy-start(f32[2,2,64,64]{3,2,1,0:T(8,128)} %param.8) | copy-start | bytes 196612
  2.0 10.3 %collective-permute-start = (f32[6,64,128]{2,1,0:T(8,128)S(1)}, f32[6,64,128]{2,1,0:T(8,128)S(1)}, u32[]{:S(2)}, u32[]{:S(2)}) collective-permute-start(f32[6,64,128]{2,1,0:T(8,128)S(1)} %pad_maximum_fusion.7), channel_id=1, source_target_pairs={{0,16},{16,32},{32,48},{48,64},{64,80},{80,96},{96,112},{1,17},{17... | collective-permute-start | bytes 589832 | tf_op jit(solution)/shard_map/ppermute | solution.py:167
  6.8 9.2 %collective-permute-start.1 = (f32[6,64,128]{2,1,0:T(8,128)S(1)}, f32[6,64,128]{2,1,0:T(8,128)S(1)}, u32[]{:S(2)}, u32[]{:S(2)}) collective-permute-start(f32[6,64,128]{2,1,0:T(8,128)S(1)} %fusion.7), channel_id=1, source_target_pairs={{16,0},{32,16},{48,32},{64,48},{80,64},{96,80},{112,96},{17,1},{33... | collective-permute-start | bytes 589832 | tf_op jit(solution)/shard_map/ppermute | solution.py:167
  15.9 0.7 copy-start.5
  16.9 10.4 %slice-start.1 = ((f32[6,64,128]{2,1,0:T(8,128)}), f32[1,64,128]{2,1,0:T(8,128)S(1)}, s32[]{:S(2)}) async-start(f32[6,64,128]{2,1,0:T(8,128)} %copy-done.5), calls=%async_computation.1 | async-start | bytes 65536 | tf_op jit(solution)/shard_map/slice | solution.py:339
  16.9 10.5 %copy-start.3 = (f32[2,2,64,64]{3,2,1,0:T(8,128)S(1)}, f32[2,2,64,64]{3,2,1,0:T(8,128)}, u32[]{:S(2)}) copy-start(f32[2,2,64,64]{3,2,1,0:T(8,128)} %param.9) | copy-start | bytes 196612
  16.9 12.8 %collective-permute-start.2 = (f32[6,256,64]{1,2,0:T(8,128)S(1)}, f32[6,256,64]{1,2,0:T(8,128)S(1)}, u32[]{:S(2)}, u32[]{:S(2)}) collective-permute-start(f32[6,256,64]{1,2,0:T(8,128)S(1)} %copy.11), channel_id=1, source_target_pairs={{0,1},{1,2},{2,3},{3,4},{4,5},{5,6},{6,7},{7,8},{8,9},{9,10},{10,1... | collective-permute-start | bytes 1179656 | tf_op jit(solution)/shard_map/ppermute | solution.py:167
  19.3 12.5 %collective-permute-start.3 = (f32[6,256,64]{1,2,0:T(8,128)S(1)}, f32[6,256,64]{1,2,0:T(8,128)}, u32[]{:S(2)}, u32[]{:S(2)}) collective-permute-start(f32[6,256,64]{1,2,0:T(8,128)S(1)} %copy.13), channel_id=1, source_target_pairs={{1,0},{2,1},{3,2},{4,3},{5,4},{6,5},{7,6},{8,7},{9,8},{10,9},{11,1... | collective-permute-start | bytes 1179656 | tf_op jit(solution)/shard_map/ppermute | solution.py:167
  55.6 7.5 %collective-permute-start.4 = (f32[2,2,65,128]{3,2,1,0:T(8,128)S(1)}, f32[2,2,65,128]{3,2,1,0:T(8,128)S(1)}, u32[]{:S(2)}, u32[]{:S(2)}) collective-permute-start(f32[2,2,65,128]{3,2,1,0:T(8,128)S(1)} %get-tuple-element.13), channel_id=1, source_target_pairs={{0,16},{16,32},{32,48},{48,64},{64,80},{80,96},{96,112},{1,17},{17... | collective-permute-start | bytes 399368 | tf_op jit(solution)/shard_map/ppermute | solution.py:167
  59.3 7.9 %collective-permute-start.5 = (f32[2,2,65,128]{3,2,1,0:T(8,128)S(1)}, f32[2,2,65,128]{3,2,1,0:T(8,128)S(1)}, u32[]{:S(2)}, u32[]{:S(2)}) collective-permute-start(f32[2,2,65,128]{3,2,1,0:T(8,128)S(1)} %get-tuple-element.14), channel_id=1, source_target_pairs={{16,0},{32,16},{48,32},{64,48},{80,64},{96,80},{112,96},{17,1},{33... | collective-permute-start | bytes 399368 | tf_op jit(solution)/shard_map/ppermute | solution.py:167
  67.8 10.6 %copy-start = (f32[5,256,256]{2,1,0:T(8,128)S(1)}, f32[5,256,256]{2,1,0:T(8,128)}, u32[]{:S(2)}) copy-start(f32[5,256,256]{2,1,0:T(8,128)} %pad_maximum_fusion.1.resid_ref.data_ref) | copy-start | bytes 3932164
  67.8 12.9 %collective-permute-start.6 = (f32[2,2,258,65]{2,1,3,0:T(2,128)S(1)}, f32[2,2,258,65]{2,1,3,0:T(2,128)S(1)}, u32[]{:S(2)}, u32[]{:S(2)}) collective-permute-start(f32[2,2,258,65]{2,1,3,0:T(2,128)S(1)} %copy.19), channel_id=1, source_target_pairs={{0,1},{1,2},{2,3},{3,4},{4,5},{5,6},{6,7},{7,8},{8,9},{9,10},{10,1... | collective-permute-start | bytes 804968 | tf_op jit(solution)/shard_map/ppermute | solution.py:167
  70.9 12.9 %collective-permute-start.7 = (f32[2,2,258,65]{2,1,3,0:T(2,128)}, f32[2,2,258,65]{2,1,3,0:T(2,128)}, u32[]{:S(2)}, u32[]{:S(2)}) collective-permute-start(f32[2,2,258,65]{2,1,3,0:T(2,128)} %copy.20), channel_id=1, source_target_pairs={{1,0},{2,1},{3,2},{4,3},{5,4},{6,5},{7,6},{8,7},{9,8},{10,9},{11,1... | collective-permute-start | bytes 804968 | tf_op jit(solution)/shard_map/ppermute | solution.py:167
  86.8 0.7 copy-start.6
  88.1 1.2 %slice-start = ((f32[5,256,256]{2,1,0:T(8,128)}), f32[4,256,256]{2,1,0:T(8,128)S(1)}, s32[]{:S(2)}) async-start(f32[5,256,256]{2,1,0:T(8,128)} %pad_maximum_fusion.1.resid_ref.data_ref), calls=%async_computation | async-start | bytes 2097152 | tf_op jit(solution)/shard_map/slice | solution.py:334

commit v3 on v2

--- a/solution.py
+++ b/solution.py
@@ -251,21 +251,15 @@
         out_ref[problem, 0] = mask(up_r)
         out_ref[problem, 1] = mask(up_i)
 
-        def sweep_body(step, inner):
-            cor_r = out_ref[problem, 0]
-            cor_i = out_ref[problem, 1]
+        cor_r, cor_i = (mask(up_r), mask(up_i))
+        for step in range(SWEEPS - 1):
             op_r, op_i = operator(cor_r, cor_i, sign)
             loc_r, loc_i = (mask(resid_ref[2 * problem] - op_r), mask(resid_ref[2 * problem + 1] - op_i))
-            up_r, up_i = lax.cond(
-                step % 2 == 0,
-                lambda: cols_apply(loc_r, loc_i, sign),
-                lambda: rows_apply(loc_r, loc_i, sign),
-            )
-            out_ref[problem, 0] = cor_r + mask(up_r)
-            out_ref[problem, 1] = cor_i + mask(up_i)
-            return inner
-
-        lax.fori_loop(0, SWEEPS - 1, sweep_body, 0)
+            apply = cols_apply if step % 2 == 0 else rows_apply
+            up_r, up_i = apply(loc_r, loc_i, sign)
+            cor_r, cor_i = (cor_r + mask(up_r), cor_i + mask(up_i))
+        out_ref[problem, 0] = cor_r
+        out_ref[problem, 1] = cor_i
         return carry
 
     lax.fori_loop(0, out_ref.shape[0], problem_body, 0)

time: 113 us -> 103 us (0.912)
  Pallas kernels: 34.2 us -> 24.2 us
    pallas_call x2, Pallas kernels: 34.2 us -> 24.2 us  [solve_local_kernel(): pl.pallas_call(solve_kernel, out_shape=jax.ShapeDtypeStruct(out_shape, re...]
  transfers between devices with their start and end apart: 8 -> 8, of which waited for: 7 -> 7; matrix products, arithmetic and copies ran while one was open for 6% -> 7% of each run, Pallas kernels for 0% -> 0%
where the time goes in v3:
time: 103 us; the launch traced here: 101 us
  starting transfers between devices  30.5 us (30%)
  Pallas kernels  24.2 us (23%)
  waiting for transfers between devices  16 us (16%)
  local copies, waits for them, and re-layouts  15.2 us (15%)
  other arithmetic  12.2 us (12%)
  between operations  3.09 us (3%)
    ppermute x8, starting transfers between devices, exchange_axis(): return (lax.ppermute(last, axis, up), lax.ppermute(first, axis, down))  30.5 us
    pallas_call x2, Pallas kernels, solve_local_kernel(): pl.pallas_call(solve_kernel, out_shape=jax.ShapeDtypeStruct(out_shape, re...  24.2 us
    ppermute x8, waiting for transfers between devices, exchange_axis(): return (lax.ppermute(last, axis, up), lax.ppermute(first, axis, down))  16 us
    sub x1, other arithmetic, shards(): resid_ext = sources_ext - apply_operator(padded, wave_ext, signs)  2.7 us
    add x1, other arithmetic, shards(): solution = own if solution is None else solution + own  2.11 us
  transfers between devices with their start and end apart: 8, of which 7 were waited for; matrix products, arithmetic and copies ran while one was open for 7% of the time, Pallas kernels for 0%

profile of v3, /device:TPU:6, one launch (start us, length us, event | category | flops | bytes accessed | tf_op | source)
XLA Modules:
  0.0 101.2 jit_solution(11979887925156185431)
XLA Ops:
  0.0 0.9 fusion.14
  1.0 0.1 reshape_squeeze.12
  1.0 0.9 fusion.8
  2.0 3.8 %collective-permute-start = (f32[6,64,128]{2,1,0:T(8,128)S(1)}, f32[6,64,128]{2,1,0:T(8,128)S(1)}, u32[]{:S(2)}, u32[]{:S(2)}) collective-permute-start(f32[6,64,128]{2,1,0:T(8,128)S(1)} %pad_maximum_fusion.7), channel_id=1, source_target_pairs={{0,16},{16,32},{32,48},{48,64},{64,80},{80,96},{96,112},{1,17},{17... | collective-permute-start | bytes 589832 | tf_op jit(solution)/shard_map/ppermute | solution.py:167
  5.7 0.1 reshape_squeeze.13
  5.8 0.9 fusion.7
  6.8 2.1 %collective-permute-start.1 = (f32[6,64,128]{2,1,0:T(8,128)S(1)}, f32[6,64,128]{2,1,0:T(8,128)S(1)}, u32[]{:S(2)}, u32[]{:S(2)}) collective-permute-start(f32[6,64,128]{2,1,0:T(8,128)S(1)} %fusion.7), channel_id=1, source_target_pairs={{16,0},{32,16},{48,32},{64,48},{80,64},{96,80},{112,96},{17,1},{33... | collective-permute-start | bytes 589832 | tf_op jit(solution)/shard_map/ppermute | solution.py:167
  8.9 0.7 fusion.15
  12.3 3.6 %collective-permute-done.1 = f32[6,64,128]{2,1,0:T(8,128)S(1)} collective-permute-done((f32[6,64,128]{2,1,0:T(8,128)S(1)}, f32[6,64,128]{2,1,0:T(8,128)S(1)}, u32[]{:S(2)}, u32[]{:S(2)}) %collective-permute-start.1) | collective-permute-done | bytes 196640 | tf_op jit(solution)/shard_map/ppermute | solution.py:167
  16.0 0.2 fusion.11
  16.2 0.3 copy-done.5
  16.6 0.1 select_maximum_fusion.1
  16.6 0.2 copy.11
  16.9 0.0 slice-start.1
  16.9 2.1 %collective-permute-start.2 = (f32[6,256,64]{1,2,0:T(8,128)S(1)}, f32[6,256,64]{1,2,0:T(8,128)S(1)}, u32[]{:S(2)}, u32[]{:S(2)}) collective-permute-start(f32[6,256,64]{1,2,0:T(8,128)S(1)} %copy.11), channel_id=1, source_target_pairs={{0,1},{1,2},{2,3},{3,4},{4,5},{5,6},{6,7},{7,8},{8,9},{9,10},{10,1... | collective-permute-start | bytes 1179656 | tf_op jit(solution)/shard_map/ppermute | solution.py:167
  19.0 0.1 select_maximum_fusion
  19.0 0.2 copy.13
  19.3 7.3 %collective-permute-start.3 = (f32[6,256,64]{1,2,0:T(8,128)S(1)}, f32[6,256,64]{1,2,0:T(8,128)}, u32[]{:S(2)}, u32[]{:S(2)}) collective-permute-start(f32[6,256,64]{1,2,0:T(8,128)S(1)} %copy.13), channel_id=1, source_target_pairs={{1,0},{2,1},{3,2},{4,3},{5,4},{6,5},{7,6},{8,7},{9,8},{10,9},{11,1... | collective-permute-start | bytes 1179656 | tf_op jit(solution)/shard_map/ppermute | solution.py:167
  26.6 0.7 pad_add_fusion.rect_ref
  27.2 0.1 reshape.95
  27.3 0.1 reshape.96
  27.4 0.3 multiply_bitcast_fusion
  27.7 1.0 %reshape.99.wcol_ref = f32[2,256,128]{2,1,0:T(8,128)} reshape(f32[2,2,2,64,2,64]{5,4,3,2,1,0:T(2,128)S(1)} %multiply_bitcast_fusion) | data formatting | bytes 524288 | tf_op jit(solution)/shard_map/reshape | solution.py:275
  28.7 1.1 %collective-permute-done.2 = f32[6,256,64]{1,2,0:T(8,128)S(1)} collective-permute-done((f32[6,256,64]{1,2,0:T(8,128)S(1)}, f32[6,256,64]{1,2,0:T(8,128)S(1)}, u32[]{:S(2)}, u32[]{:S(2)}) %collective-permute-start.2) | collective-permute-done | bytes 393248 | tf_op jit(solution)/shard_map/ppermute | solution.py:167
  29.8 0.2 copy.27
  30.0 1.8 %collective-permute-done.3 = f32[6,256,64]{1,2,0:T(8,128)} collective-permute-done((f32[6,256,64]{1,2,0:T(8,128)S(1)}, f32[6,256,64]{1,2,0:T(8,128)}, u32[]{:S(2)}, u32[]{:S(2)}) %collective-permute-start.3) | collective-permute-done | bytes 393248 | tf_op jit(solution)/shard_map/ppermute | solution.py:167
  31.8 1.0 slice.179
  32.8 0.2 copy.28
  33.1 0.1 copy.23
  33.2 0.8 slice.181
  33.9 0.1 copy.24
  34.1 0.2 copy.17
  34.2 0.2 multiply_bitcast_fusion.1
  34.5 1.2 %reshape.94.wrow_ref = f32[2,128,256]{2,1,0:T(8,128)} reshape(f32[2,2,64,2,2,64]{5,4,3,2,1,0:T(2,128)S(1)} %multiply_bitcast_fusion.1) | data formatting | bytes 524288 | tf_op jit(solution)/shard_map/reshape | solution.py:273
  35.6 1.7 %pad_maximum_fusion.1.resid_ref.data_ref = f32[5,256,256]{2,1,0:T(8,128)} fusion(f32[5,256,64]{2,1,0:T(8,128)S(1)} %copy.28, f32[5,64,128]{2,1,0:T(8,128)S(1)} %slice.175, f32[1,128,128]{2,1,0:T(8,128)S(1)} %bitcast.47, f32[4,128,128]{2,1,0:T(8,128)S(1)} %bitcast.42, f32[5,64,128]{2,1,0:T(8,128)S(1)} %slice.174, f32[5,256,64]{2,1,0:T(8,128)S(1)} %copy.27), kind=kLoop, calls=%fused_computation.4 | loop fusion | flops 1638400 | bytes 2621440 | tf_op jit(solution)/shard_map/concatenate | solution.py:327
  37.3 12.2 %shard_map.64 = f32[2,2,256,256]{3,2,1,0:T(8,128)} custom-call(s32[4]{0:T(128)} %pad_add_fusion.rect_ref, f32[5,256,256]{2,1,0:T(8,128)} %pad_maximum_fusion.1.resid_ref.data_ref, f32[5,256,256]{2,1,0:T(8,128)} %pad_maximum_fusion.1.resid_ref.data_ref, f32[2,128,256]{2,1,0:T(8,128)} %reshape.94.wrow_ref, f32[2,256,128]{2,1,0:T(8,128)} %reshape.99.wcol_ref), custom_call_target="tpu_custom_call" | custom-call | tf_op jit(solution)/shard_map/pallas_call | solution.py:283
  49.5 1.2 %fusion.10 = (f32[2,2,65,128]{3,2,1,0:T(8,128)S(1)}, f32[2,2,65,128]{3,2,1,0:T(8,128)S(1)}) fusion(f32[2,2,256,256]{3,2,1,0:T(8,128)} %shard_map.64), kind=kLoop, calls=%fused_computation.60 | loop fusion | bytes 532480 | tf_op jit(solution)/shard_map/slice | solution.py:162
  50.7 3.6 %collective-permute-start.4 = (f32[2,2,65,128]{3,2,1,0:T(8,128)S(1)}, f32[2,2,65,128]{3,2,1,0:T(8,128)S(1)}, u32[]{:S(2)}, u32[]{:S(2)}) collective-permute-start(f32[2,2,65,128]{3,2,1,0:T(8,128)S(1)} %get-tuple-element.13), channel_id=1, source_target_pairs={{0,16},{16,32},{32,48},{48,64},{64,80},{80,96},{96,112},{1,17},{17... | collective-permute-start | bytes 399368 | tf_op jit(solution)/shard_map/ppermute | solution.py:167
  54.3 2.3 %collective-permute-start.5 = (f32[2,2,65,128]{3,2,1,0:T(8,128)S(1)}, f32[2,2,65,128]{3,2,1,0:T(8,128)S(1)}, u32[]{:S(2)}, u32[]{:S(2)}) collective-permute-start(f32[2,2,65,128]{3,2,1,0:T(8,128)S(1)} %get-tuple-element.14), channel_id=1, source_target_pairs={{16,0},{32,16},{48,32},{64,48},{80,64},{96,80},{112,96},{17,1},{33... | collective-permute-start | bytes 399368 | tf_op jit(solution)/shard_map/ppermute | solution.py:167
  56.5 0.1 and_and_fusion
  56.7 1.2 %slice.184 = f32[2,2,128,128]{3,2,1,0:T(8,128)S(1)} slice(f32[2,2,256,256]{3,2,1,0:T(8,128)} %shard_map.64), slice={[0:2], [0:2], [64:192], [64:192]} | slice | bytes 524288 | tf_op jit(solution)/shard_map/slice | solution.py:357
  57.9 0.3 collective-permute-done.4
  58.2 4.0 %collective-permute-done.5 = f32[2,2,65,128]{3,2,1,0:T(8,128)S(1)} collective-permute-done((f32[2,2,65,128]{3,2,1,0:T(8,128)S(1)}, f32[2,2,65,128]{3,2,1,0:T(8,128)S(1)}, u32[]{:S(2)}, u32[]{:S(2)}) %collective-permute-start.5) | collective-permute-done | bytes 133152 | tf_op jit(solution)/shard_map/ppermute | solution.py:167
  62.2 0.2 fusion.12
  62.5 0.3 copy.19
  62.8 2.1 %collective-permute-start.6 = (f32[2,2,258,65]{2,1,3,0:T(2,128)S(1)}, f32[2,2,258,65]{2,1,3,0:T(2,128)S(1)}, u32[]{:S(2)}, u32[]{:S(2)}) collective-permute-start(f32[2,2,258,65]{2,1,3,0:T(2,128)S(1)} %copy.19), channel_id=1, source_target_pairs={{0,1},{1,2},{2,3},{3,4},{4,5},{5,6},{6,7},{7,8},{8,9},{9,10},{10,1... | collective-permute-start | bytes 804968 | tf_op jit(solution)/shard_map/ppermute | solution.py:167
  64.8 1.0 %copy.20 = f32[2,2,258,65]{2,1,3,0:T(2,128)} copy(f32[2,2,258,65]{3,2,1,0:T(8,128)S(1)} %get-tuple-element.18) | data formatting | bytes 536640 | tf_op jit(solution)/shard_map/slice | solution.py:163
  65.9 7.4 %collective-permute-start.7 = (f32[2,2,258,65]{2,1,3,0:T(2,128)}, f32[2,2,258,65]{2,1,3,0:T(2,128)}, u32[]{:S(2)}, u32[]{:S(2)}) collective-permute-start(f32[2,2,258,65]{2,1,3,0:T(2,128)} %copy.20), channel_id=1, source_target_pairs={{1,0},{2,1},{3,2},{4,3},{5,4},{6,5},{7,6},{8,7},{9,8},{10,9},{11,1... | collective-permute-start | bytes 804968 | tf_op jit(solution)/shard_map/ppermute | solution.py:167
  73.4 2.3 %collective-permute-done.6 = f32[2,2,258,65]{2,1,3,0:T(2,128)S(1)} collective-permute-done((f32[2,2,258,65]{2,1,3,0:T(2,128)S(1)}, f32[2,2,258,65]{2,1,3,0:T(2,128)S(1)}, u32[]{:S(2)}, u32[]{:S(2)}) %collective-permute-start.6) | collective-permute-done | bytes 268352 | tf_op jit(solution)/shard_map/ppermute | solution.py:167
  75.7 0.3 copy.21
  75.9 2.8 %collective-permute-done.7 = f32[2,2,258,65]{2,1,3,0:T(2,128)} collective-permute-done((f32[2,2,258,65]{2,1,3,0:T(2,128)}, f32[2,2,258,65]{2,1,3,0:T(2,128)}, u32[]{:S(2)}, u32[]{:S(2)}) %collective-permute-start.7) | collective-permute-done | bytes 268352 | tf_op jit(solution)/shard_map/ppermute | solution.py:167
  78.8 1.2 %copy.22 = f32[2,2,258,65]{3,2,1,0:T(8,128)S(1)} copy(f32[2,2,258,65]{2,1,3,0:T(2,128)} %collective-permute-done.7) | data formatting | bytes 536640 | tf_op jit(solution)/shard_map/ppermute | solution.py:167
  80.0 0.6 pad_maximum_fusion
  80.7 0.2 select_select_fusion.1
  81.0 0.8 dynamic-slice_reduce_fusion.1
  81.8 0.4 select_select_fusion
  82.2 0.2 copy-done.6
  82.5 0.2 multiply_add_fusion
  82.7 0.5 maximum_select_fusion
  83.1 0.3 multiply_subtract_fusion.1
  83.5 0.9 slice-done
  84.4 2.7 %fusion.4 = f32[2,2,256,256]{3,2,1,0:T(8,128)} fusion(f32[2,2,256,256]{3,2,1,0:T(8,128)S(1)} %bitcast.38, f32[2,2,258,258]{3,2,1,0:T(8,128)S(1)} %maximum_select_fusion, f32[2,1,256,256]{3,2,1,0:T(8,128)S(1)} %get-tuple-element.8, f32[2,1,256,256]{3,2,1,0:T(8,128)S(1)} %get-tuple-element.7, f32[256,256]{1,0:T(8,128)S(1)} %slice_bitcast_fusion), kind=kLoop, calls=%fused_computation.10 | loop fusion | flops 4194304 | bytes 12845056 | tf_op jit(solution)/shard_map/sub | solution.py:354
  87.1 12.0 %shard_map.65 = f32[2,2,256,256]{3,2,1,0:T(8,128)} custom-call(s32[4]{0:T(128)} %pad_add_fusion.rect_ref, f32[4,256,256]{2,1,0:T(8,128)} %bitcast.43, f32[5,256,256]{2,1,0:T(8,128)} %pad_maximum_fusion.1.resid_ref.data_ref, f32[2,128,256]{2,1,0:T(8,128)} %reshape.94.wrow_ref, f32[2,256,128]{2,1,0:T(8,128)} %reshape.99.wcol_ref), custom_call_target="tpu_custom_call" | custom-call | tf_op jit(solution)/shard_map/pallas_call | solution.py:283
  99.1 2.1 %slice_add_fusion.6 = f32[2,2,128,128]{3,2,1,0:T(8,128)} fusion(f32[2,2,256,256]{3,2,1,0:T(8,128)} %shard_map.65, f32[2,2,256,256]{3,2,1,0:T(8,128)} %shard_map.64), kind=kLoop, calls=%fused_computation.36 | loop fusion | flops 65536 | bytes 786432 | tf_op jit(solution)/shard_map/add | solution.py:358
  (37 shorter events, 0.3 us)
Async XLA Ops:
  0.0 15.9 %copy-start.1 = (f32[2,2,128,128]{3,2,1,0:T(8,128)S(1)}, f32[2,2,128,128]{3,2,1,0:T(8,128)}, u32[]{:S(2)}) copy-start(f32[2,2,128,128]{3,2,1,0:T(8,128)} %param.6) | copy-start | bytes 786436
  0.0 15.9 %copy-start.2 = (f32[128,128]{1,0:T(8,128)S(1)}, f32[128,128]{1,0:T(8,128)}, u32[]{:S(2)}) copy-start(f32[128,128]{1,0:T(8,128)} %param.7) | copy-start | bytes 196612
  0.0 8.9 %copy-start.7 = (s32[1,1,4]{2,1,0:T(1,128)S(1)}, s32[1,1,4]{2,1,0:T(1,128)}, u32[]{:S(2)}) copy-start(s32[1,1,4]{2,1,0:T(1,128)} %param.10) | copy-start | bytes 52
  0.0 12.2 %copy-start.4 = (f32[2,2,64,64]{3,2,1,0:T(8,128)S(1)}, f32[2,2,64,64]{3,2,1,0:T(8,128)}, u32[]{:S(2)}) copy-start(f32[2,2,64,64]{3,2,1,0:T(8,128)} %param.8) | copy-start | bytes 196612
  2.0 10.3 %collective-permute-start = (f32[6,64,128]{2,1,0:T(8,128)S(1)}, f32[6,64,128]{2,1,0:T(8,128)S(1)}, u32[]{:S(2)}, u32[]{:S(2)}) collective-permute-start(f32[6,64,128]{2,1,0:T(8,128)S(1)} %pad_maximum_fusion.7), channel_id=1, source_target_pairs={{0,16},{16,32},{32,48},{48,64},{64,80},{80,96},{96,112},{1,17},{17... | collective-permute-start | bytes 589832 | tf_op jit(solution)/shard_map/ppermute | solution.py:167
  6.8 9.2 %collective-permute-start.1 = (f32[6,64,128]{2,1,0:T(8,128)S(1)}, f32[6,64,128]{2,1,0:T(8,128)S(1)}, u32[]{:S(2)}, u32[]{:S(2)}) collective-permute-start(f32[6,64,128]{2,1,0:T(8,128)S(1)} %fusion.7), channel_id=1, source_target_pairs={{16,0},{32,16},{48,32},{64,48},{80,64},{96,80},{112,96},{17,1},{33... | collective-permute-start | bytes 589832 | tf_op jit(solution)/shard_map/ppermute | solution.py:167
  15.9 0.7 copy-start.5
  16.9 10.4 %slice-start.1 = ((f32[6,64,128]{2,1,0:T(8,128)}), f32[1,64,128]{2,1,0:T(8,128)S(1)}, s32[]{:S(2)}) async-start(f32[6,64,128]{2,1,0:T(8,128)} %copy-done.5), calls=%async_computation.1 | async-start | bytes 65536 | tf_op jit(solution)/shard_map/slice | solution.py:333
  16.9 10.5 %copy-start.3 = (f32[2,2,64,64]{3,2,1,0:T(8,128)S(1)}, f32[2,2,64,64]{3,2,1,0:T(8,128)}, u32[]{:S(2)}) copy-start(f32[2,2,64,64]{3,2,1,0:T(8,128)} %param.9) | copy-start | bytes 196612
  16.9 12.8 %collective-permute-start.2 = (f32[6,256,64]{1,2,0:T(8,128)S(1)}, f32[6,256,64]{1,2,0:T(8,128)S(1)}, u32[]{:S(2)}, u32[]{:S(2)}) collective-permute-start(f32[6,256,64]{1,2,0:T(8,128)S(1)} %copy.11), channel_id=1, source_target_pairs={{0,1},{1,2},{2,3},{3,4},{4,5},{5,6},{6,7},{7,8},{8,9},{9,10},{10,1... | collective-permute-start | bytes 1179656 | tf_op jit(solution)/shard_map/ppermute | solution.py:167
  19.3 12.5 %collective-permute-start.3 = (f32[6,256,64]{1,2,0:T(8,128)S(1)}, f32[6,256,64]{1,2,0:T(8,128)}, u32[]{:S(2)}, u32[]{:S(2)}) collective-permute-start(f32[6,256,64]{1,2,0:T(8,128)S(1)} %copy.13), channel_id=1, source_target_pairs={{1,0},{2,1},{3,2},{4,3},{5,4},{6,5},{7,6},{8,7},{9,8},{10,9},{11,1... | collective-permute-start | bytes 1179656 | tf_op jit(solution)/shard_map/ppermute | solution.py:167
  50.7 7.5 %collective-permute-start.4 = (f32[2,2,65,128]{3,2,1,0:T(8,128)S(1)}, f32[2,2,65,128]{3,2,1,0:T(8,128)S(1)}, u32[]{:S(2)}, u32[]{:S(2)}) collective-permute-start(f32[2,2,65,128]{3,2,1,0:T(8,128)S(1)} %get-tuple-element.13), channel_id=1, source_target_pairs={{0,16},{16,32},{32,48},{48,64},{64,80},{80,96},{96,112},{1,17},{17... | collective-permute-start | bytes 399368 | tf_op jit(solution)/shard_map/ppermute | solution.py:167
  54.3 7.9 %collective-permute-start.5 = (f32[2,2,65,128]{3,2,1,0:T(8,128)S(1)}, f32[2,2,65,128]{3,2,1,0:T(8,128)S(1)}, u32[]{:S(2)}, u32[]{:S(2)}) collective-permute-start(f32[2,2,65,128]{3,2,1,0:T(8,128)S(1)} %get-tuple-element.14), channel_id=1, source_target_pairs={{16,0},{32,16},{48,32},{64,48},{80,64},{96,80},{112,96},{17,1},{33... | collective-permute-start | bytes 399368 | tf_op jit(solution)/shard_map/ppermute | solution.py:167
  62.8 10.6 %copy-start = (f32[5,256,256]{2,1,0:T(8,128)S(1)}, f32[5,256,256]{2,1,0:T(8,128)}, u32[]{:S(2)}) copy-start(f32[5,256,256]{2,1,0:T(8,128)} %pad_maximum_fusion.1.resid_ref.data_ref) | copy-start | bytes 3932164
  62.8 12.9 %collective-permute-start.6 = (f32[2,2,258,65]{2,1,3,0:T(2,128)S(1)}, f32[2,2,258,65]{2,1,3,0:T(2,128)S(1)}, u32[]{:S(2)}, u32[]{:S(2)}) collective-permute-start(f32[2,2,258,65]{2,1,3,0:T(2,128)S(1)} %copy.19), channel_id=1, source_target_pairs={{0,1},{1,2},{2,3},{3,4},{4,5},{5,6},{6,7},{7,8},{8,9},{9,10},{10,1... | collective-permute-start | bytes 804968 | tf_op jit(solution)/shard_map/ppermute | solution.py:167
  65.9 12.9 %collective-permute-start.7 = (f32[2,2,258,65]{2,1,3,0:T(2,128)}, f32[2,2,258,65]{2,1,3,0:T(2,128)}, u32[]{:S(2)}, u32[]{:S(2)}) collective-permute-start(f32[2,2,258,65]{2,1,3,0:T(2,128)} %copy.20), channel_id=1, source_target_pairs={{1,0},{2,1},{3,2},{4,3},{5,4},{6,5},{7,6},{8,7},{9,8},{10,9},{11,1... | collective-permute-start | bytes 804968 | tf_op jit(solution)/shard_map/ppermute | solution.py:167
  81.8 0.7 copy-start.6
  83.1 1.2 %slice-start = ((f32[5,256,256]{2,1,0:T(8,128)}), f32[4,256,256]{2,1,0:T(8,128)S(1)}, s32[]{:S(2)}) async-start(f32[5,256,256]{2,1,0:T(8,128)} %pad_maximum_fusion.1.resid_ref.data_ref), calls=%async_computation | async-start | bytes 2097152 | tf_op jit(solution)/shard_map/slice | solution.py:328

commit v4 on v3

--- a/solution.py
+++ b/solution.py
@@ -57,6 +57,32 @@
         axis=1,
     )
     return jnp.where(inside, values, ghost_cycle)
+
+
+def grid_ghost(values, width, edges, signs):
+    at_top, at_bottom, at_left, at_right = edges
+    height, breadth = (values.shape[2], values.shape[3])
+    row_ids = lax.broadcasted_iota(jnp.int32, (height, 1), 0)
+    col_ids = lax.broadcasted_iota(jnp.int32, (1, breadth), 1)
+    above = at_top & (row_ids < width)
+    below = at_bottom & (row_ids >= height - width)
+    values = jnp.where(
+        above, values[:, :, width : width + 1], jnp.where(below, values[:, :, height - width - 1 : height - width], values)
+    )
+    before = at_left & (col_ids < width)
+    after = at_right & (col_ids >= breadth - width)
+    values = jnp.where(
+        before, values[:, :, :, width : width + 1],
+        jnp.where(after, values[:, :, :, breadth - width - 1 : breadth - width], values),
+    )
+    outside = above | below | before | after
+    real_part = values[:, 0]
+    imag_part = values[:, 1]
+    ghost_cycle = jnp.stack(
+        [real_part + signs * ROBIN_COEF * imag_part, imag_part - signs * ROBIN_COEF * real_part],
+        axis=1,
+    )
+    return jnp.where(outside, ghost_cycle, values)
 
 
 def apply_operator(padded, wave_cells, signs):
@@ -178,7 +204,9 @@
     return jnp.concatenate(rows, axis=-2)
 
 
-def solve_kernel(rect_ref, resid_ref, data_ref, wrow_ref, wcol_ref, out_ref):
+def solve_kernel(rect_ref, resid_ref, data_ref, wrow_ref, wcol_ref, *refs):
+    out_ref = refs[-1]
+    base_ref = refs[0] if len(refs) > 1 else None
     height, breadth = (resid_ref.shape[1], resid_ref.shape[2])
     half = height // 2
     upper, lower, left, right = (rect_ref[0], rect_ref[1], rect_ref[2], rect_ref[3])
@@ -248,9 +276,6 @@
     def problem_body(problem, carry):
         sign = 1.0 - 2.0 * problem.astype(jnp.float32)
         up_r, up_i = rows_apply(mask(resid_ref[2 * problem]), mask(resid_ref[2 * problem + 1]), sign)
-        out_ref[problem, 0] = mask(up_r)
-        out_ref[problem, 1] = mask(up_i)
-
         cor_r, cor_i = (mask(up_r), mask(up_i))
         for step in range(SWEEPS - 1):
             op_r, op_i = operator(cor_r, cor_i, sign)
@@ -258,6 +283,8 @@
             apply = cols_apply if step % 2 == 0 else rows_apply
             up_r, up_i = apply(loc_r, loc_i, sign)
             cor_r, cor_i = (cor_r + mask(up_r), cor_i + mask(up_i))
+        if base_ref is not None:
+            cor_r, cor_i = (cor_r + base_ref[problem, 0], cor_i + base_ref[problem, 1])
         out_ref[problem, 0] = cor_r
         out_ref[problem, 1] = cor_i
         return carry
@@ -276,17 +303,18 @@
     return row_mats, col_mats
 
 
-def solve_local_kernel(resid_planes, data_ext, row_mats, col_mats, live_rect, interpret=False):
+def solve_local_kernel(resid_planes, data_ext, row_mats, col_mats, live_rect, base=None, interpret=False):
+    extra = [] if base is None else [base]
     rect = jnp.stack([to_index(v) for v in live_rect])
     out_shape = (2, 2) + resid_planes.shape[1:]
     vmem = pltpu.MemorySpace.VMEM if hasattr(pltpu, "MemorySpace") else pltpu.VMEM
     return pl.pallas_call(
         solve_kernel,
         out_shape=jax.ShapeDtypeStruct(out_shape, resid_planes.dtype),
-        in_specs=[pl.BlockSpec(memory_space=pltpu.SMEM)] + [pl.BlockSpec(memory_space=vmem)] * 4,
+        in_specs=[pl.BlockSpec(memory_space=pltpu.SMEM)] + [pl.BlockSpec(memory_space=vmem)] * (4 + len(extra)),
         out_specs=pl.BlockSpec(memory_space=vmem),
         interpret=interpret,
-    )(rect, resid_planes, data_ext, row_mats, col_mats)
+    )(rect, resid_planes, data_ext, row_mats, col_mats, *extra)
 
 
 def shards(sources, wavenumber, row_inverse, col_inverse, reach_steps):
@@ -337,11 +365,9 @@
     )
     row_mats, col_mats = line_matrices(row_blocks, col_blocks)
     width = block + 1
-    grid_upper = to_index(jnp.where(row_rank == 0, width, 0))
-    grid_lower = to_index(jnp.where(row_rank == row_count - 1, width + own_rows, own_rows + 2 * width))
-    grid_left = to_index(jnp.where(col_rank == 0, width, 0))
-    grid_right = to_index(jnp.where(col_rank == col_count - 1, width + own_cols, own_cols + 2 * width))
+    edges = (row_rank == 0, row_rank == row_count - 1, col_rank == 0, col_rank == col_count - 1)
     solution = None
+    base = None
     for iteration in range(ITERS):
         if iteration == 0:
             resid_planes = stacked_ext
@@ -350,12 +376,12 @@
             tall = jnp.concatenate([before, solution, after], axis=2)
             left, right = exchange_axis(tall, "gy", 3, width)
             padded = jnp.concatenate([left, tall, right], axis=3)
-            padded = fill_ghost(padded, grid_upper, grid_lower, grid_left, grid_right, signs)
+            padded = grid_ghost(padded, width, edges, signs)
             resid_ext = sources_ext - apply_operator(padded, wave_ext, signs)
             resid_planes = resid_ext.reshape((4,) + resid_ext.shape[2:])
-        correction = solve_local_kernel(resid_planes, stacked_ext, row_mats, col_mats, live_rect)
-        own = correction[:, :, block : block + own_rows, block : block + own_cols]
-        solution = own if solution is None else solution + own
+        correction = solve_local_kernel(resid_planes, stacked_ext, row_mats, col_mats, live_rect, base=base)
+        base = correction
+        solution = correction[:, :, block : block + own_rows, block : block + own_cols]
     return solution
 
 

time: 103 us -> 103 us (level)
  other arithmetic: 12.2 us -> 10.1 us
  local copies, waits for them, and re-layouts: 15.2 us -> 17.1 us
    slice x1 -> x4, local copies, waits for them, and re-layouts: 1.17 us -> 3.87 us  [the longest x2 3.05 us: shards(): solution = correction[:, :, block:block + own_rows, block:block + own_cols]]
    add x2 -> x1, other arithmetic: 2.31 us -> 0.2 us  [grid_ghost(): real_part + signs * ROBIN_COEF * imag_part]
where the time goes in v4:
time: 103 us; the launch traced here: 101 us
  starting transfers between devices  30.5 us (30%)
  Pallas kernels  24.6 us (24%)
  local copies, waits for them, and re-layouts  17.1 us (17%)
  waiting for transfers between devices  16 us (16%)
  other arithmetic  10.1 us (10%)
  between operations  3.12 us (3%)
    ppermute x8, starting transfers between devices, exchange_axis(): return (lax.ppermute(last, axis, up), lax.ppermute(first, axis, down))  30.5 us
    pallas_call x2, Pallas kernels, solve_local_kernel(): pl.pallas_call(solve_kernel, out_shape=jax.ShapeDtypeStruct(out_shape, re...  24.6 us
    ppermute x8, waiting for transfers between devices, exchange_axis(): return (lax.ppermute(last, axis, up), lax.ppermute(first, axis, down))  16 us
    slice x2, local copies, waits for them, and re-layouts, shards(): solution = correction[:, :, block:block + own_rows, block:block + own_cols]  3.05 us
    sub x1, other arithmetic, shards(): resid_ext = sources_ext - apply_operator(padded, wave_ext, signs)  2.72 us
  transfers between devices with their start and end apart: 8, of which 7 were waited for; matrix products, arithmetic and copies ran while one was open for 7% of the time, Pallas kernels for 0%

profile of v4, /device:TPU:6, one launch (start us, length us, event | category | flops | bytes accessed | tf_op | source)
XLA Modules:
  0.0 101.3 jit_solution(947392138966998178)
XLA Ops:
  0.0 0.9 fusion.19
  1.0 0.1 reshape_squeeze.12
  1.0 0.9 fusion.8
  2.0 3.8 %collective-permute-start = (f32[6,64,128]{2,1,0:T(8,128)S(1)}, f32[6,64,128]{2,1,0:T(8,128)S(1)}, u32[]{:S(2)}, u32[]{:S(2)}) collective-permute-start(f32[6,64,128]{2,1,0:T(8,128)S(1)} %pad_maximum_fusion.7), channel_id=1, source_target_pairs={{0,16},{16,32},{32,48},{48,64},{64,80},{80,96},{96,112},{1,17},{17... | collective-permute-start | bytes 589832 | tf_op jit(solution)/shard_map/ppermute | solution.py:193
  5.7 0.1 reshape_squeeze.13
  5.8 0.9 fusion.7
  6.8 2.1 %collective-permute-start.1 = (f32[6,64,128]{2,1,0:T(8,128)S(1)}, f32[6,64,128]{2,1,0:T(8,128)S(1)}, u32[]{:S(2)}, u32[]{:S(2)}) collective-permute-start(f32[6,64,128]{2,1,0:T(8,128)S(1)} %fusion.7), channel_id=1, source_target_pairs={{16,0},{32,16},{48,32},{64,48},{80,64},{96,80},{112,96},{17,1},{33... | collective-permute-start | bytes 589832 | tf_op jit(solution)/shard_map/ppermute | solution.py:193
  8.9 0.7 fusion.20
  12.3 3.6 %collective-permute-done.1 = f32[6,64,128]{2,1,0:T(8,128)S(1)} collective-permute-done((f32[6,64,128]{2,1,0:T(8,128)S(1)}, f32[6,64,128]{2,1,0:T(8,128)S(1)}, u32[]{:S(2)}, u32[]{:S(2)}) %collective-permute-start.1) | collective-permute-done | bytes 196640 | tf_op jit(solution)/shard_map/ppermute | solution.py:193
  16.0 0.2 fusion.16
  16.2 0.3 copy-done.5
  16.6 0.1 select_maximum_fusion.1
  16.6 0.2 copy.11
  16.9 0.0 slice-start.1
  16.9 2.1 %collective-permute-start.2 = (f32[6,256,64]{1,2,0:T(8,128)S(1)}, f32[6,256,64]{1,2,0:T(8,128)S(1)}, u32[]{:S(2)}, u32[]{:S(2)}) collective-permute-start(f32[6,256,64]{1,2,0:T(8,128)S(1)} %copy.11), channel_id=1, source_target_pairs={{0,1},{1,2},{2,3},{3,4},{4,5},{5,6},{6,7},{7,8},{8,9},{9,10},{10,1... | collective-permute-start | bytes 1179656 | tf_op jit(solution)/shard_map/ppermute | solution.py:193
  19.0 0.1 select_maximum_fusion
  19.0 0.2 copy.13
  19.3 7.3 %collective-permute-start.3 = (f32[6,256,64]{1,2,0:T(8,128)S(1)}, f32[6,256,64]{1,2,0:T(8,128)}, u32[]{:S(2)}, u32[]{:S(2)}) collective-permute-start(f32[6,256,64]{1,2,0:T(8,128)S(1)} %copy.13), channel_id=1, source_target_pairs={{1,0},{2,1},{3,2},{4,3},{5,4},{6,5},{7,6},{8,7},{9,8},{10,9},{11,1... | collective-permute-start | bytes 1179656 | tf_op jit(solution)/shard_map/ppermute | solution.py:193
  26.6 0.6 pad_add_fusion.rect_ref
  27.2 0.1 reshape.96
  27.3 0.1 reshape.97
  27.4 0.3 multiply_bitcast_fusion
  27.6 1.0 %reshape.100.wcol_ref = f32[2,256,128]{2,1,0:T(8,128)} reshape(f32[2,2,2,64,2,64]{5,4,3,2,1,0:T(2,128)S(1)} %multiply_bitcast_fusion) | data formatting | bytes 524288 | tf_op jit(solution)/shard_map/reshape | solution.py:302
  28.7 1.1 %collective-permute-done.2 = f32[6,256,64]{1,2,0:T(8,128)S(1)} collective-permute-done((f32[6,256,64]{1,2,0:T(8,128)S(1)}, f32[6,256,64]{1,2,0:T(8,128)S(1)}, u32[]{:S(2)}, u32[]{:S(2)}) %collective-permute-start.2) | collective-permute-done | bytes 393248 | tf_op jit(solution)/shard_map/ppermute | solution.py:193
  29.8 0.2 copy.27
  30.0 1.8 %collective-permute-done.3 = f32[6,256,64]{1,2,0:T(8,128)} collective-permute-done((f32[6,256,64]{1,2,0:T(8,128)S(1)}, f32[6,256,64]{1,2,0:T(8,128)}, u32[]{:S(2)}, u32[]{:S(2)}) %collective-permute-start.3) | collective-permute-done | bytes 393248 | tf_op jit(solution)/shard_map/ppermute | solution.py:193
  31.8 1.0 slice.195
  32.8 0.2 copy.28
  33.1 0.1 copy.23
  33.2 0.8 slice.198
  33.9 0.1 copy.24
  34.1 0.2 copy.17
  34.2 0.2 multiply_bitcast_fusion.1
  34.5 1.2 %reshape.95.wrow_ref = f32[2,128,256]{2,1,0:T(8,128)} reshape(f32[2,2,64,2,2,64]{5,4,3,2,1,0:T(2,128)S(1)} %multiply_bitcast_fusion.1) | data formatting | bytes 524288 | tf_op jit(solution)/shard_map/reshape | solution.py:300
  35.6 1.6 %pad_maximum_fusion.1.resid_ref.data_ref = f32[5,256,256]{2,1,0:T(8,128)} fusion(f32[5,256,64]{2,1,0:T(8,128)S(1)} %copy.28, f32[5,64,128]{2,1,0:T(8,128)S(1)} %slice.191, f32[1,128,128]{2,1,0:T(8,128)S(1)} %bitcast.47, f32[4,128,128]{2,1,0:T(8,128)S(1)} %bitcast.43, f32[5,64,128]{2,1,0:T(8,128)S(1)} %slice.190, f32[5,256,64]{2,1,0:T(8,128)S(1)} %copy.27), kind=kLoop, calls=%fused_computation.4 | loop fusion | flops 1638400 | bytes 2621440 | tf_op jit(solution)/shard_map/concatenate | solution.py:355
  37.3 12.2 %shard_map.64.refs_0_ = f32[2,2,256,256]{3,2,1,0:T(8,128)} custom-call(s32[4]{0:T(128)} %pad_add_fusion.rect_ref, f32[5,256,256]{2,1,0:T(8,128)} %pad_maximum_fusion.1.resid_ref.data_ref, f32[5,256,256]{2,1,0:T(8,128)} %pad_maximum_fusion.1.resid_ref.data_ref, f32[2,128,256]{2,1,0:T(8,128)} %reshape.95.wrow_ref, f32[2,256,128]{2,1,0:T(8,128)} %reshape.100.wcol_ref), custom_call_target="tpu_custom_call" | custom-call | tf_op jit(solution)/shard_map/pallas_call | solution.py:311
  49.5 1.2 %fusion.15 = (f32[2,2,65,128]{3,2,1,0:T(8,128)S(1)}, f32[2,2,65,128]{3,2,1,0:T(8,128)S(1)}) fusion(f32[2,2,256,256]{3,2,1,0:T(8,128)} %shard_map.64.refs_0_), kind=kLoop, calls=%fused_computation.56 | loop fusion | bytes 532480 | tf_op jit(solution)/shard_map/slice | solution.py:188
  50.7 3.6 %collective-permute-start.4 = (f32[2,2,65,128]{3,2,1,0:T(8,128)S(1)}, f32[2,2,65,128]{3,2,1,0:T(8,128)S(1)}, u32[]{:S(2)}, u32[]{:S(2)}) collective-permute-start(f32[2,2,65,128]{3,2,1,0:T(8,128)S(1)} %get-tuple-element.13), channel_id=1, source_target_pairs={{0,16},{16,32},{32,48},{48,64},{64,80},{80,96},{96,112},{1,17},{17... | collective-permute-start | bytes 399368 | tf_op jit(solution)/shard_map/ppermute | solution.py:193
  54.3 2.3 %collective-permute-start.5 = (f32[2,2,65,128]{3,2,1,0:T(8,128)S(1)}, f32[2,2,65,128]{3,2,1,0:T(8,128)S(1)}, u32[]{:S(2)}, u32[]{:S(2)}) collective-permute-start(f32[2,2,65,128]{3,2,1,0:T(8,128)S(1)} %get-tuple-element.14), channel_id=1, source_target_pairs={{16,0},{32,16},{48,32},{64,48},{80,64},{96,80},{112,96},{17,1},{33... | collective-permute-start | bytes 399368 | tf_op jit(solution)/shard_map/ppermute | solution.py:193
  56.5 0.1 or_or_fusion
  56.7 1.2 %slice.202 = f32[2,2,128,128]{3,2,1,0:T(8,128)S(1)} slice(f32[2,2,256,256]{3,2,1,0:T(8,128)} %shard_map.64.refs_0_), slice={[0:2], [0:2], [64:192], [64:192]} | slice | bytes 524288 | tf_op jit(solution)/shard_map/slice | solution.py:384
  57.8 0.3 collective-permute-done.4
  58.2 4.0 %collective-permute-done.5 = f32[2,2,65,128]{3,2,1,0:T(8,128)S(1)} collective-permute-done((f32[2,2,65,128]{3,2,1,0:T(8,128)S(1)}, f32[2,2,65,128]{3,2,1,0:T(8,128)S(1)}, u32[]{:S(2)}, u32[]{:S(2)}) %collective-permute-start.5) | collective-permute-done | bytes 133152 | tf_op jit(solution)/shard_map/ppermute | solution.py:193
  62.2 0.2 fusion.17
  62.4 0.3 copy.19
  62.8 2.1 %collective-permute-start.6 = (f32[2,2,258,65]{2,1,3,0:T(2,128)S(1)}, f32[2,2,258,65]{2,1,3,0:T(2,128)S(1)}, u32[]{:S(2)}, u32[]{:S(2)}) collective-permute-start(f32[2,2,258,65]{2,1,3,0:T(2,128)S(1)} %copy.19), channel_id=1, source_target_pairs={{0,1},{1,2},{2,3},{3,4},{4,5},{5,6},{6,7},{7,8},{8,9},{9,10},{10,1... | collective-permute-start | bytes 804968 | tf_op jit(solution)/shard_map/ppermute | solution.py:193
  64.8 1.1 %copy.20 = f32[2,2,258,65]{2,1,3,0:T(2,128)} copy(f32[2,2,258,65]{3,2,1,0:T(8,128)S(1)} %get-tuple-element.18) | data formatting | bytes 536640 | tf_op jit(solution)/shard_map/slice | solution.py:189
  65.9 7.4 %collective-permute-start.7 = (f32[2,2,258,65]{2,1,3,0:T(2,128)}, f32[2,2,258,65]{2,1,3,0:T(2,128)}, u32[]{:S(2)}, u32[]{:S(2)}) collective-permute-start(f32[2,2,258,65]{2,1,3,0:T(2,128)} %copy.20), channel_id=1, source_target_pairs={{1,0},{2,1},{3,2},{4,3},{5,4},{6,5},{7,6},{8,7},{9,8},{10,9},{11,1... | collective-permute-start | bytes 804968 | tf_op jit(solution)/shard_map/ppermute | solution.py:193
  73.4 2.3 %collective-permute-done.6 = f32[2,2,258,65]{2,1,3,0:T(2,128)S(1)} collective-permute-done((f32[2,2,258,65]{2,1,3,0:T(2,128)S(1)}, f32[2,2,258,65]{2,1,3,0:T(2,128)S(1)}, u32[]{:S(2)}, u32[]{:S(2)}) %collective-permute-start.6) | collective-permute-done | bytes 268352 | tf_op jit(solution)/shard_map/ppermute | solution.py:193
  75.7 0.3 copy.21
  75.9 2.8 %collective-permute-done.7 = f32[2,2,258,65]{2,1,3,0:T(2,128)} collective-permute-done((f32[2,2,258,65]{2,1,3,0:T(2,128)}, f32[2,2,258,65]{2,1,3,0:T(2,128)}, u32[]{:S(2)}, u32[]{:S(2)}) %collective-permute-start.7) | collective-permute-done | bytes 268352 | tf_op jit(solution)/shard_map/ppermute | solution.py:193
  78.8 1.2 %copy.22 = f32[2,2,258,65]{3,2,1,0:T(8,128)S(1)} copy(f32[2,2,258,65]{2,1,3,0:T(2,128)} %collective-permute-done.7) | data formatting | bytes 536640 | tf_op jit(solution)/shard_map/ppermute | solution.py:193
  80.0 0.6 pad_maximum_fusion
  80.7 0.2 select_select_fusion.1
  81.0 0.8 slice_reduce_fusion.1
  81.8 0.4 select_select_fusion
  82.2 0.2 copy-done.6
  82.4 0.2 multiply_add_fusion
  82.6 0.5 maximum_select_fusion
  83.1 0.3 multiply_subtract_fusion.1
  83.5 0.9 slice-done
  84.3 2.7 %fusion.4 = f32[2,2,256,256]{3,2,1,0:T(8,128)} fusion(f32[2,2,256,256]{3,2,1,0:T(8,128)S(1)} %bitcast.38, f32[2,2,258,258]{3,2,1,0:T(8,128)S(1)} %maximum_select_fusion, f32[2,1,256,256]{3,2,1,0:T(8,128)S(1)} %get-tuple-element.8, f32[2,1,256,256]{3,2,1,0:T(8,128)S(1)} %get-tuple-element.7, f32[256,256]{1,0:T(8,128)S(1)} %slice_bitcast_fusion), kind=kLoop, calls=%fused_computation.10 | loop fusion | flops 4194304 | bytes 12845056 | tf_op jit(solution)/shard_map/sub | solution.py:380
  87.1 12.4 %shard_map.65 = f32[2,2,256,256]{3,2,1,0:T(8,128)} custom-call(s32[4]{0:T(128)} %pad_add_fusion.rect_ref, f32[4,256,256]{2,1,0:T(8,128)} %bitcast.39, f32[5,256,256]{2,1,0:T(8,128)} %pad_maximum_fusion.1.resid_ref.data_ref, f32[2,128,256]{2,1,0:T(8,128)} %reshape.95.wrow_ref, f32[2,256,128]{2,1,0:T(8,128)} %reshape.100.wcol_ref, ...), custom_call_target="tpu_custom_call" | custom-call | tf_op jit(solution)/shard_map/pallas_call | solution.py:311
  99.4 1.9 %slice.224 = f32[2,2,128,128]{3,2,1,0:T(8,128)} slice(f32[2,2,256,256]{3,2,1,0:T(8,128)} %shard_map.65), slice={[0:2], [0:2], [64:192], [64:192]} | slice | bytes 524288 | tf_op jit(solution)/shard_map/slice | solution.py:384
  (36 shorter events, 0.3 us)
Async XLA Ops:
  0.0 15.9 %copy-start.1 = (f32[2,2,128,128]{3,2,1,0:T(8,128)S(1)}, f32[2,2,128,128]{3,2,1,0:T(8,128)}, u32[]{:S(2)}) copy-start(f32[2,2,128,128]{3,2,1,0:T(8,128)} %param.6) | copy-start | bytes 786436
  0.0 15.9 %copy-start.2 = (f32[128,128]{1,0:T(8,128)S(1)}, f32[128,128]{1,0:T(8,128)}, u32[]{:S(2)}) copy-start(f32[128,128]{1,0:T(8,128)} %param.7) | copy-start | bytes 196612
  0.0 8.9 %copy-start.7 = (s32[1,1,4]{2,1,0:T(1,128)S(1)}, s32[1,1,4]{2,1,0:T(1,128)}, u32[]{:S(2)}) copy-start(s32[1,1,4]{2,1,0:T(1,128)} %param.10) | copy-start | bytes 52
  0.0 12.3 %copy-start.4 = (f32[2,2,64,64]{3,2,1,0:T(8,128)S(1)}, f32[2,2,64,64]{3,2,1,0:T(8,128)}, u32[]{:S(2)}) copy-start(f32[2,2,64,64]{3,2,1,0:T(8,128)} %param.8) | copy-start | bytes 196612
  2.0 10.3 %collective-permute-start = (f32[6,64,128]{2,1,0:T(8,128)S(1)}, f32[6,64,128]{2,1,0:T(8,128)S(1)}, u32[]{:S(2)}, u32[]{:S(2)}) collective-permute-start(f32[6,64,128]{2,1,0:T(8,128)S(1)} %pad_maximum_fusion.7), channel_id=1, source_target_pairs={{0,16},{16,32},{32,48},{48,64},{64,80},{80,96},{96,112},{1,17},{17... | collective-permute-start | bytes 589832 | tf_op jit(solution)/shard_map/ppermute | solution.py:193
  6.8 9.2 %collective-permute-start.1 = (f32[6,64,128]{2,1,0:T(8,128)S(1)}, f32[6,64,128]{2,1,0:T(8,128)S(1)}, u32[]{:S(2)}, u32[]{:S(2)}) collective-permute-start(f32[6,64,128]{2,1,0:T(8,128)S(1)} %fusion.7), channel_id=1, source_target_pairs={{16,0},{32,16},{48,32},{64,48},{80,64},{96,80},{112,96},{17,1},{33... | collective-permute-start | bytes 589832 | tf_op jit(solution)/shard_map/ppermute | solution.py:193
  15.9 0.7 copy-start.5
  16.9 10.4 %slice-start.1 = ((f32[6,64,128]{2,1,0:T(8,128)}), f32[1,64,128]{2,1,0:T(8,128)S(1)}, s32[]{:S(2)}) async-start(f32[6,64,128]{2,1,0:T(8,128)} %copy-done.5), calls=%async_computation.1 | async-start | bytes 65536 | tf_op jit(solution)/shard_map/slice | solution.py:361
  16.9 10.4 %copy-start.3 = (f32[2,2,64,64]{3,2,1,0:T(8,128)S(1)}, f32[2,2,64,64]{3,2,1,0:T(8,128)}, u32[]{:S(2)}) copy-start(f32[2,2,64,64]{3,2,1,0:T(8,128)} %param.9) | copy-start | bytes 196612
  16.9 12.8 %collective-permute-start.2 = (f32[6,256,64]{1,2,0:T(8,128)S(1)}, f32[6,256,64]{1,2,0:T(8,128)S(1)}, u32[]{:S(2)}, u32[]{:S(2)}) collective-permute-start(f32[6,256,64]{1,2,0:T(8,128)S(1)} %copy.11), channel_id=1, source_target_pairs={{0,1},{1,2},{2,3},{3,4},{4,5},{5,6},{6,7},{7,8},{8,9},{9,10},{10,1... | collective-permute-start | bytes 1179656 | tf_op jit(solution)/shard_map/ppermute | solution.py:193
  19.3 12.5 %collective-permute-start.3 = (f32[6,256,64]{1,2,0:T(8,128)S(1)}, f32[6,256,64]{1,2,0:T(8,128)}, u32[]{:S(2)}, u32[]{:S(2)}) collective-permute-start(f32[6,256,64]{1,2,0:T(8,128)S(1)} %copy.13), channel_id=1, source_target_pairs={{1,0},{2,1},{3,2},{4,3},{5,4},{6,5},{7,6},{8,7},{9,8},{10,9},{11,1... | collective-permute-start | bytes 1179656 | tf_op jit(solution)/shard_map/ppermute | solution.py:193
  50.7 7.5 %collective-permute-start.4 = (f32[2,2,65,128]{3,2,1,0:T(8,128)S(1)}, f32[2,2,65,128]{3,2,1,0:T(8,128)S(1)}, u32[]{:S(2)}, u32[]{:S(2)}) collective-permute-start(f32[2,2,65,128]{3,2,1,0:T(8,128)S(1)} %get-tuple-element.13), channel_id=1, source_target_pairs={{0,16},{16,32},{32,48},{48,64},{64,80},{80,96},{96,112},{1,17},{17... | collective-permute-start | bytes 399368 | tf_op jit(solution)/shard_map/ppermute | solution.py:193
  54.3 7.9 %collective-permute-start.5 = (f32[2,2,65,128]{3,2,1,0:T(8,128)S(1)}, f32[2,2,65,128]{3,2,1,0:T(8,128)S(1)}, u32[]{:S(2)}, u32[]{:S(2)}) collective-permute-start(f32[2,2,65,128]{3,2,1,0:T(8,128)S(1)} %get-tuple-element.14), channel_id=1, source_target_pairs={{16,0},{32,16},{48,32},{64,48},{80,64},{96,80},{112,96},{17,1},{33... | collective-permute-start | bytes 399368 | tf_op jit(solution)/shard_map/ppermute | solution.py:193
  62.8 10.6 %copy-start = (f32[5,256,256]{2,1,0:T(8,128)S(1)}, f32[5,256,256]{2,1,0:T(8,128)}, u32[]{:S(2)}) copy-start(f32[5,256,256]{2,1,0:T(8,128)} %pad_maximum_fusion.1.resid_ref.data_ref) | copy-start | bytes 3932164
  62.8 12.9 %collective-permute-start.6 = (f32[2,2,258,65]{2,1,3,0:T(2,128)S(1)}, f32[2,2,258,65]{2,1,3,0:T(2,128)S(1)}, u32[]{:S(2)}, u32[]{:S(2)}) collective-permute-start(f32[2,2,258,65]{2,1,3,0:T(2,128)S(1)} %copy.19), channel_id=1, source_target_pairs={{0,1},{1,2},{2,3},{3,4},{4,5},{5,6},{6,7},{7,8},{8,9},{9,10},{10,1... | collective-permute-start | bytes 804968 | tf_op jit(solution)/shard_map/ppermute | solution.py:193
  65.9 12.9 %collective-permute-start.7 = (f32[2,2,258,65]{2,1,3,0:T(2,128)}, f32[2,2,258,65]{2,1,3,0:T(2,128)}, u32[]{:S(2)}, u32[]{:S(2)}) collective-permute-start(f32[2,2,258,65]{2,1,3,0:T(2,128)} %copy.20), channel_id=1, source_target_pairs={{1,0},{2,1},{3,2},{4,3},{5,4},{6,5},{7,6},{8,7},{9,8},{10,9},{11,1... | collective-permute-start | bytes 804968 | tf_op jit(solution)/shard_map/ppermute | solution.py:193
  81.8 0.7 copy-start.6
  83.1 1.2 %slice-start = ((f32[5,256,256]{2,1,0:T(8,128)}), f32[4,256,256]{2,1,0:T(8,128)S(1)}, s32[]{:S(2)}) async-start(f32[5,256,256]{2,1,0:T(8,128)} %pad_maximum_fusion.1.resid_ref.data_ref), calls=%async_computation | async-start | bytes 2097152 | tf_op jit(solution)/shard_map/slice | solution.py:356

commit v5 on v4

--- a/solution.py
+++ b/solution.py
@@ -1,3 +1,5 @@
+import functools
+
 import jax
 import jax.numpy as jnp
 from jax import lax
@@ -204,9 +206,12 @@
     return jnp.concatenate(rows, axis=-2)
 
 
-def solve_kernel(rect_ref, resid_ref, data_ref, wrow_ref, wcol_ref, *refs):
-    out_ref = refs[-1]
-    base_ref = refs[0] if len(refs) > 1 else None
+def solve_kernel(rect_ref, resid_ref, data_ref, wrow_ref, wcol_ref, *refs, has_base, last, own_rows, own_cols, slab):
+    base_ref = refs[0] if has_base else None
+    outs = refs[1:] if has_base else refs
+    full_ref = None if last else outs[0]
+    own_ref = outs[-1] if last else outs[1]
+    top_ref, bottom_ref = (None, None) if last else outs[2:4]
     height, breadth = (resid_ref.shape[1], resid_ref.shape[2])
     half = height // 2
     upper, lower, left, right = (rect_ref[0], rect_ref[1], rect_ref[2], rect_ref[3])
@@ -285,11 +290,18 @@
             cor_r, cor_i = (cor_r + mask(up_r), cor_i + mask(up_i))
         if base_ref is not None:
             cor_r, cor_i = (cor_r + base_ref[problem, 0], cor_i + base_ref[problem, 1])
-        out_ref[problem, 0] = cor_r
-        out_ref[problem, 1] = cor_i
+        first_row = (height - own_rows) // 2
+        for part, value in ((0, cor_r), (1, cor_i)):
+            if full_ref is not None:
+                full_ref[problem, part] = value
+            own = pltpu.roll(value, breadth - (breadth - own_cols) // 2, 1)[first_row : first_row + own_rows, :own_cols]
+            own_ref[problem, part] = own
+            if top_ref is not None:
+                top_ref[problem, part] = own[:slab]
+                bottom_ref[problem, part] = own[own_rows - slab :]
         return carry
 
-    lax.fori_loop(0, out_ref.shape[0], problem_body, 0)
+    lax.fori_loop(0, resid_ref.shape[0] // 2, problem_body, 0)
 
 
 def line_matrices(row_blocks, col_blocks):
@@ -303,16 +315,24 @@
     return row_mats, col_mats
 
 
-def solve_local_kernel(resid_planes, data_ext, row_mats, col_mats, live_rect, base=None, interpret=False):
+def solve_local_kernel(resid_planes, data_ext, row_mats, col_mats, live_rect, own_shape, slab, base=None, last=False,
+                       interpret=False):
     extra = [] if base is None else [base]
     rect = jnp.stack([to_index(v) for v in live_rect])
-    out_shape = (2, 2) + resid_planes.shape[1:]
+    dtype = resid_planes.dtype
+    shapes = [] if last else [(2, 2) + resid_planes.shape[1:]]
+    shapes.append((2, 2) + own_shape)
+    if not last:
+        shapes += [(2, 2, slab, own_shape[1])] * 2
     vmem = pltpu.MemorySpace.VMEM if hasattr(pltpu, "MemorySpace") else pltpu.VMEM
+    kernel = functools.partial(
+        solve_kernel, has_base=base is not None, last=last, own_rows=own_shape[0], own_cols=own_shape[1], slab=slab
+    )
     return pl.pallas_call(
-        solve_kernel,
-        out_shape=jax.ShapeDtypeStruct(out_shape, resid_planes.dtype),
+        kernel,
+        out_shape=[jax.ShapeDtypeStruct(s, dtype) for s in shapes],
         in_specs=[pl.BlockSpec(memory_space=pltpu.SMEM)] + [pl.BlockSpec(memory_space=vmem)] * (4 + len(extra)),
-        out_specs=pl.BlockSpec(memory_space=vmem),
+        out_specs=[pl.BlockSpec(memory_space=vmem)] * len(shapes),
         interpret=interpret,
     )(rect, resid_planes, data_ext, row_mats, col_mats, *extra)
 
@@ -366,22 +386,32 @@
     row_mats, col_mats = line_matrices(row_blocks, col_blocks)
     width = block + 1
     edges = (row_rank == 0, row_rank == row_count - 1, col_rank == 0, col_rank == col_count - 1)
+    slab = -(-width // 8) * 8
     solution = None
     base = None
     for iteration in range(ITERS):
+        last = iteration == ITERS - 1
         if iteration == 0:
             resid_planes = stacked_ext
         else:
-            before, after = exchange_axis(solution, "gx", 2, width)
+            peers = lax.axis_size("gx")
+            up = [(i, i + 1) for i in range(peers - 1)]
+            down = [(j, i) for i, j in up]
+            before = lax.ppermute(bottom, "gx", up)[:, :, slab - width :]
+            after = lax.ppermute(top, "gx", down)[:, :, :width]
             tall = jnp.concatenate([before, solution, after], axis=2)
             left, right = exchange_axis(tall, "gy", 3, width)
             padded = jnp.concatenate([left, tall, right], axis=3)
             padded = grid_ghost(padded, width, edges, signs)
             resid_ext = sources_ext - apply_operator(padded, wave_ext, signs)
             resid_planes = resid_ext.reshape((4,) + resid_ext.shape[2:])
-        correction = solve_local_kernel(resid_planes, stacked_ext, row_mats, col_mats, live_rect, base=base)
-        base = correction
-        solution = correction[:, :, block : block + own_rows, block : block + own_cols]
+        outs = solve_local_kernel(
+            resid_planes, stacked_ext, row_mats, col_mats, live_rect, (own_rows, own_cols), slab, base=base, last=last
+        )
+        if last:
+            solution = outs[0]
+        else:
+            base, solution, top, bottom = outs
     return solution
 
 

time: 103 us -> 101 us (0.981)
  the two profiles are of different devices: /device:TPU:6 before, /device:TPU:97 now
where the time goes in v5:
time: 101 us; the launch traced here: 100 us
  waiting for transfers between devices  28.3 us (28%)
  Pallas kernels  24.9 us (25%)
  starting transfers between devices  20.7 us (20%)
  local copies, waits for them, and re-layouts  12.1 us (12%)
  other arithmetic  11.1 us (11%)
  between operations  3.06 us (3%)
    pallas_call x2, Pallas kernels, solve_local_kernel(): pl.pallas_call(kernel, out_shape=[jax.ShapeDtypeStruct(s, dtype) for s in...  24.9 us
    ppermute x6, waiting for transfers between devices, exchange_axis(): return (lax.ppermute(last, axis, up), lax.ppermute(first, axis, down))  23.1 us
    ppermute x6, starting transfers between devices, exchange_axis(): return (lax.ppermute(last, axis, up), lax.ppermute(first, axis, down))  17 us
    ppermute x1, waiting for transfers between devices, shards(): after = lax.ppermute(top, 'gx', down)[:, :, :width]  4.23 us
    sub x1, other arithmetic, shards(): resid_ext = sources_ext - apply_operator(padded, wave_ext, signs)  2.7 us
    ppermute x1, starting transfers between devices, shards(): before = lax.ppermute(bottom, 'gx', up)[:, :, slab - width:]  2.38 us
  transfers between devices with their start and end apart: 8, of which 7 were waited for; matrix products, arithmetic and copies ran while one was open for 5% of the time, Pallas kernels for 0%

profile of v5, /device:TPU:97, one launch (start us, length us, event | category | flops | bytes accessed | tf_op | source)
XLA Modules:
  0.0 100.0 jit_solution(13645911515197340553)
XLA Ops:
  0.0 0.9 fusion.18
  1.0 0.1 reshape_squeeze.12
  1.0 0.9 fusion.8
  2.0 3.1 %collective-permute-start = (f32[6,64,128]{2,1,0:T(8,128)S(1)}, f32[6,64,128]{2,1,0:T(8,128)S(1)}, u32[]{:S(2)}, u32[]{:S(2)}) collective-permute-start(f32[6,64,128]{2,1,0:T(8,128)S(1)} %pad_maximum_fusion.7), channel_id=1, source_target_pairs={{0,16},{16,32},{32,48},{48,64},{64,80},{80,96},{96,112},{1,17},{17... | collective-permute-start | bytes 589832 | tf_op jit(solution)/shard_map/ppermute | solution.py:195
  5.1 0.1 reshape_squeeze.13
  5.2 0.9 fusion.7
  6.1 1.3 %collective-permute-start.1 = (f32[6,64,128]{2,1,0:T(8,128)S(1)}, f32[6,64,128]{2,1,0:T(8,128)S(1)}, u32[]{:S(2)}, u32[]{:S(2)}) collective-permute-start(f32[6,64,128]{2,1,0:T(8,128)S(1)} %fusion.7), channel_id=1, source_target_pairs={{16,0},{32,16},{48,32},{64,48},{80,64},{96,80},{112,96},{17,1},{33... | collective-permute-start | bytes 589832 | tf_op jit(solution)/shard_map/ppermute | solution.py:195
  7.5 0.7 fusion.19
  10.8 4.2 %collective-permute-done.1 = f32[6,64,128]{2,1,0:T(8,128)S(1)} collective-permute-done((f32[6,64,128]{2,1,0:T(8,128)S(1)}, f32[6,64,128]{2,1,0:T(8,128)S(1)}, u32[]{:S(2)}, u32[]{:S(2)}) %collective-permute-start.1) | collective-permute-done | bytes 196640 | tf_op jit(solution)/shard_map/ppermute | solution.py:195
  15.1 0.2 fusion.15
  15.3 0.3 copy-done.6
  15.7 0.1 select_maximum_fusion.1
  15.7 0.2 copy.11
  16.0 0.0 slice-start.1
  16.0 0.0 copy-start.4
  16.0 4.7 %collective-permute-start.2 = (f32[6,256,64]{1,2,0:T(8,128)S(1)}, f32[6,256,64]{1,2,0:T(8,128)S(1)}, u32[]{:S(2)}, u32[]{:S(2)}) collective-permute-start(f32[6,256,64]{1,2,0:T(8,128)S(1)} %copy.11), channel_id=1, source_target_pairs={{0,1},{1,2},{2,3},{3,4},{4,5},{5,6},{6,7},{7,8},{8,9},{9,10},{10,1... | collective-permute-start | bytes 1179656 | tf_op jit(solution)/shard_map/ppermute | solution.py:195
  20.7 0.1 select_maximum_fusion
  20.8 0.2 copy.13
  21.1 1.9 %collective-permute-start.3 = (f32[6,256,64]{1,2,0:T(8,128)S(1)}, f32[6,256,64]{1,2,0:T(8,128)}, u32[]{:S(2)}, u32[]{:S(2)}) collective-permute-start(f32[6,256,64]{1,2,0:T(8,128)S(1)} %copy.13), channel_id=1, source_target_pairs={{1,0},{2,1},{3,2},{4,3},{5,4},{6,5},{7,6},{8,7},{9,8},{10,9},{11,1... | collective-permute-start | bytes 1179656 | tf_op jit(solution)/shard_map/ppermute | solution.py:195
  23.0 0.7 pad_add_fusion.rect_ref
  23.7 0.1 reshape.96
  23.7 0.1 reshape.97
  23.8 0.3 multiply_bitcast_fusion
  24.1 1.0 %reshape.100.wcol_ref = f32[2,256,128]{2,1,0:T(8,128)} reshape(f32[2,2,2,64,2,64]{5,4,3,2,1,0:T(2,128)S(1)} %multiply_bitcast_fusion) | data formatting | bytes 524288 | tf_op jit(solution)/shard_map/reshape | solution.py:314
  25.1 0.3 collective-permute-done.2
  25.5 0.2 copy.27
  25.7 8.2 %collective-permute-done.3 = f32[6,256,64]{1,2,0:T(8,128)} collective-permute-done((f32[6,256,64]{1,2,0:T(8,128)S(1)}, f32[6,256,64]{1,2,0:T(8,128)}, u32[]{:S(2)}, u32[]{:S(2)}) %collective-permute-start.3) | collective-permute-done | bytes 393248 | tf_op jit(solution)/shard_map/ppermute | solution.py:195
  33.9 1.0 slice.185
  34.9 0.2 copy.28
  35.1 0.1 copy.23
  35.2 0.8 slice.188
  36.0 0.1 copy.24
  36.1 0.2 copy.17
  36.3 0.2 multiply_bitcast_fusion.1
  36.5 1.1 %reshape.95.wrow_ref = f32[2,128,256]{2,1,0:T(8,128)} reshape(f32[2,2,64,2,2,64]{5,4,3,2,1,0:T(2,128)S(1)} %multiply_bitcast_fusion.1) | data formatting | bytes 524288 | tf_op jit(solution)/shard_map/reshape | solution.py:312
  37.7 1.7 %pad_maximum_fusion.1.resid_ref.data_ref = f32[5,256,256]{2,1,0:T(8,128)} fusion(f32[5,256,64]{2,1,0:T(8,128)S(1)} %copy.28, f32[5,64,128]{2,1,0:T(8,128)S(1)} %slice.181, f32[1,128,128]{2,1,0:T(8,128)S(1)} %bitcast.48, f32[4,128,128]{2,1,0:T(8,128)S(1)} %bitcast.44, f32[5,64,128]{2,1,0:T(8,128)S(1)} %slice.180, f32[5,256,64]{2,1,0:T(8,128)S(1)} %copy.27), kind=kLoop, calls=%fused_computation.4 | loop fusion | flops 1638400 | bytes 2621440 | tf_op jit(solution)/shard_map/concatenate | solution.py:375
  39.3 12.5 %shard_map.64 = (f32[2,2,256,256]{3,2,1,0:T(8,128)}, f32[2,2,128,128]{3,2,1,0:T(8,128)}, f32[2,2,72,128]{3,2,1,0:T(8,128)}, f32[2,2,72,128]{3,2,1,0:T(8,128)}) custom-call(s32[4]{0:T(128)} %pad_add_fusion.rect_ref, f32[5,256,256]{2,1,0:T(8,128)} %pad_maximum_fusion.1.resid_ref.data_ref, f32[5,256,256]{2,1,0:T(8,128)} %pad_maximum_fusion.1.resid_ref.data_ref, ...), custom_call_target="tpu_custom_call" | custom-call | tf_op jit(solution)/shard_map/pallas_call | solution.py:331
  51.8 2.4 %collective-permute-start.4 = (f32[2,2,72,128]{3,2,1,0:T(8,128)}, f32[2,2,72,128]{3,2,1,0:T(8,128)S(1)}, u32[]{:S(2)}, u32[]{:S(2)}) collective-permute-start(f32[2,2,72,128]{3,2,1,0:T(8,128)} %get-tuple-element.9), channel_id=1, source_target_pairs={{0,16},{16,32},{32,48},{48,64},{64,80},{80,96},{96,112},{1,17},{17... | collective-permute-start | bytes 442376 | tf_op jit(solution)/shard_map/ppermute | solution.py:400
  54.2 1.3 %collective-permute-start.5 = (f32[2,2,72,128]{3,2,1,0:T(8,128)}, f32[2,2,72,128]{3,2,1,0:T(8,128)S(1)}, u32[]{:S(2)}, u32[]{:S(2)}) collective-permute-start(f32[2,2,72,128]{3,2,1,0:T(8,128)} %get-tuple-element.11), channel_id=1, source_target_pairs={{16,0},{32,16},{48,32},{64,48},{80,64},{96,80},{112,96},{17,1},{33... | collective-permute-start | bytes 442376 | tf_op jit(solution)/shard_map/ppermute | solution.py:401
  55.5 0.1 or_or_fusion
  55.7 1.0 collective-permute-done.4
  56.6 4.2 %collective-permute-done.5 = f32[2,2,72,128]{3,2,1,0:T(8,128)S(1)} collective-permute-done((f32[2,2,72,128]{3,2,1,0:T(8,128)}, f32[2,2,72,128]{3,2,1,0:T(8,128)S(1)}, u32[]{:S(2)}, u32[]{:S(2)}) %collective-permute-start.5) | collective-permute-done | bytes 147488 | tf_op jit(solution)/shard_map/ppermute | solution.py:401
  60.9 1.0 pad_maximum_fusion.3
  61.8 0.2 fusion.16
  62.1 0.3 copy.19
  62.4 3.9 %collective-permute-start.6 = (f32[2,2,258,65]{2,1,3,0:T(2,128)S(1)}, f32[2,2,258,65]{2,1,3,0:T(2,128)S(1)}, u32[]{:S(2)}, u32[]{:S(2)}) collective-permute-start(f32[2,2,258,65]{2,1,3,0:T(2,128)S(1)} %copy.19), channel_id=1, source_target_pairs={{0,1},{1,2},{2,3},{3,4},{4,5},{5,6},{6,7},{7,8},{8,9},{9,10},{10,1... | collective-permute-start | bytes 804968 | tf_op jit(solution)/shard_map/ppermute | solution.py:195
  66.2 0.3 copy.20
  66.5 2.1 %collective-permute-start.7 = (f32[2,2,258,65]{2,1,3,0:T(2,128)S(1)}, f32[2,2,258,65]{2,1,3,0:T(2,128)}, u32[]{:S(2)}, u32[]{:S(2)}) collective-permute-start(f32[2,2,258,65]{2,1,3,0:T(2,128)S(1)} %copy.20), channel_id=1, source_target_pairs={{1,0},{2,1},{3,2},{4,3},{5,4},{6,5},{7,6},{8,7},{9,8},{10,9},{11,1... | collective-permute-start | bytes 804968 | tf_op jit(solution)/shard_map/ppermute | solution.py:195
  68.7 0.0 copy-start.3
  68.7 2.3 %collective-permute-done.6 = f32[2,2,258,65]{2,1,3,0:T(2,128)S(1)} collective-permute-done((f32[2,2,258,65]{2,1,3,0:T(2,128)S(1)}, f32[2,2,258,65]{2,1,3,0:T(2,128)S(1)}, u32[]{:S(2)}, u32[]{:S(2)}) %collective-permute-start.6) | collective-permute-done | bytes 268352 | tf_op jit(solution)/shard_map/ppermute | solution.py:195
  71.0 0.3 copy.21
  71.3 8.1 %collective-permute-done.7 = f32[2,2,258,65]{2,1,3,0:T(2,128)} collective-permute-done((f32[2,2,258,65]{2,1,3,0:T(2,128)S(1)}, f32[2,2,258,65]{2,1,3,0:T(2,128)}, u32[]{:S(2)}, u32[]{:S(2)}) %collective-permute-start.7) | collective-permute-done | bytes 268352 | tf_op jit(solution)/shard_map/ppermute | solution.py:195
  79.4 1.2 %copy.22 = f32[2,2,258,65]{3,2,1,0:T(8,128)S(1)} copy(f32[2,2,258,65]{2,1,3,0:T(2,128)} %collective-permute-done.7) | data formatting | bytes 536640 | tf_op jit(solution)/shard_map/ppermute | solution.py:195
  80.7 0.6 pad_maximum_fusion
  81.4 0.2 select_select_fusion.1
  81.6 0.8 slice_reduce_fusion.1
  82.4 0.4 select_select_fusion
  82.9 0.2 copy-done.7
  83.1 0.2 multiply_add_fusion
  83.3 0.5 maximum_select_fusion
  83.8 0.3 multiply_subtract_fusion.1
  84.1 0.9 slice-done
  85.0 2.7 %fusion.4 = f32[2,2,256,256]{3,2,1,0:T(8,128)} fusion(f32[2,2,256,256]{3,2,1,0:T(8,128)S(1)} %bitcast.39, f32[2,2,258,258]{3,2,1,0:T(8,128)S(1)} %maximum_select_fusion, f32[2,1,256,256]{3,2,1,0:T(8,128)S(1)} %get-tuple-element.16, f32[2,1,256,256]{3,2,1,0:T(8,128)S(1)} %get-tuple-element.15, f32[256,256]{1,0:T(8,128)S(1)} %slice_bitcast_fusion), kind=kLoop, calls=%fused_computation.10 | loop fusion | flops 4194304 | bytes 12845056 | tf_op jit(solution)/shard_map/sub | solution.py:406
  87.7 12.4 %shard_map.65 = f32[2,2,128,128]{3,2,1,0:T(8,128)} custom-call(s32[4]{0:T(128)} %pad_add_fusion.rect_ref, f32[4,256,256]{2,1,0:T(8,128)} %bitcast.40, f32[5,256,256]{2,1,0:T(8,128)} %pad_maximum_fusion.1.resid_ref.data_ref, f32[2,128,256]{2,1,0:T(8,128)} %reshape.95.wrow_ref, f32[2,256,128]{2,1,0:T(8,128)} %reshape.100.wcol_ref, ...), custom_call_target="tpu_custom_call" | custom-call | tf_op jit(solution)/shard_map/pallas_call | solution.py:331
  (36 shorter events, 0.3 us)
Async XLA Ops:
  0.0 15.0 %copy-start.1 = (f32[2,2,128,128]{3,2,1,0:T(8,128)S(1)}, f32[2,2,128,128]{3,2,1,0:T(8,128)}, u32[]{:S(2)}) copy-start(f32[2,2,128,128]{3,2,1,0:T(8,128)} %param.6) | copy-start | bytes 786436
  0.0 15.0 %copy-start.2 = (f32[128,128]{1,0:T(8,128)S(1)}, f32[128,128]{1,0:T(8,128)}, u32[]{:S(2)}) copy-start(f32[128,128]{1,0:T(8,128)} %param.7) | copy-start | bytes 196612
  0.0 7.5 %copy-start.8 = (s32[1,1,4]{2,1,0:T(1,128)S(1)}, s32[1,1,4]{2,1,0:T(1,128)}, u32[]{:S(2)}) copy-start(s32[1,1,4]{2,1,0:T(1,128)} %param.10) | copy-start | bytes 52
  0.0 10.8 %copy-start.5 = (f32[2,2,64,64]{3,2,1,0:T(8,128)S(1)}, f32[2,2,64,64]{3,2,1,0:T(8,128)}, u32[]{:S(2)}) copy-start(f32[2,2,64,64]{3,2,1,0:T(8,128)} %param.8) | copy-start | bytes 196612
  2.0 8.8 %collective-permute-start = (f32[6,64,128]{2,1,0:T(8,128)S(1)}, f32[6,64,128]{2,1,0:T(8,128)S(1)}, u32[]{:S(2)}, u32[]{:S(2)}) collective-permute-start(f32[6,64,128]{2,1,0:T(8,128)S(1)} %pad_maximum_fusion.7), channel_id=1, source_target_pairs={{0,16},{16,32},{32,48},{48,64},{64,80},{80,96},{96,112},{1,17},{17... | collective-permute-start | bytes 589832 | tf_op jit(solution)/shard_map/ppermute | solution.py:195
  6.1 8.9 %collective-permute-start.1 = (f32[6,64,128]{2,1,0:T(8,128)S(1)}, f32[6,64,128]{2,1,0:T(8,128)S(1)}, u32[]{:S(2)}, u32[]{:S(2)}) collective-permute-start(f32[6,64,128]{2,1,0:T(8,128)S(1)} %fusion.7), channel_id=1, source_target_pairs={{16,0},{32,16},{48,32},{64,48},{80,64},{96,80},{112,96},{17,1},{33... | collective-permute-start | bytes 589832 | tf_op jit(solution)/shard_map/ppermute | solution.py:195
  15.0 0.7 copy-start.6
  16.0 7.7 %slice-start.1 = ((f32[6,64,128]{2,1,0:T(8,128)}), f32[1,64,128]{2,1,0:T(8,128)S(1)}, s32[]{:S(2)}) async-start(f32[6,64,128]{2,1,0:T(8,128)} %copy-done.6), calls=%async_computation.1 | async-start | bytes 65536 | tf_op jit(solution)/shard_map/slice | solution.py:381
  16.0 7.8 %copy-start.4 = (f32[2,2,64,64]{3,2,1,0:T(8,128)S(1)}, f32[2,2,64,64]{3,2,1,0:T(8,128)}, u32[]{:S(2)}) copy-start(f32[2,2,64,64]{3,2,1,0:T(8,128)} %param.9) | copy-start | bytes 196612
  16.0 9.4 %collective-permute-start.2 = (f32[6,256,64]{1,2,0:T(8,128)S(1)}, f32[6,256,64]{1,2,0:T(8,128)S(1)}, u32[]{:S(2)}, u32[]{:S(2)}) collective-permute-start(f32[6,256,64]{1,2,0:T(8,128)S(1)} %copy.11), channel_id=1, source_target_pairs={{0,1},{1,2},{2,3},{3,4},{4,5},{5,6},{6,7},{7,8},{8,9},{9,10},{10,1... | collective-permute-start | bytes 1179656 | tf_op jit(solution)/shard_map/ppermute | solution.py:195
  21.1 12.8 %collective-permute-start.3 = (f32[6,256,64]{1,2,0:T(8,128)S(1)}, f32[6,256,64]{1,2,0:T(8,128)}, u32[]{:S(2)}, u32[]{:S(2)}) collective-permute-start(f32[6,256,64]{1,2,0:T(8,128)S(1)} %copy.13), channel_id=1, source_target_pairs={{1,0},{2,1},{3,2},{4,3},{5,4},{6,5},{7,6},{8,7},{9,8},{10,9},{11,1... | collective-permute-start | bytes 1179656 | tf_op jit(solution)/shard_map/ppermute | solution.py:195
  51.8 4.8 %collective-permute-start.4 = (f32[2,2,72,128]{3,2,1,0:T(8,128)}, f32[2,2,72,128]{3,2,1,0:T(8,128)S(1)}, u32[]{:S(2)}, u32[]{:S(2)}) collective-permute-start(f32[2,2,72,128]{3,2,1,0:T(8,128)} %get-tuple-element.9), channel_id=1, source_target_pairs={{0,16},{16,32},{32,48},{48,64},{64,80},{80,96},{96,112},{1,17},{17... | collective-permute-start | bytes 442376 | tf_op jit(solution)/shard_map/ppermute | solution.py:400
  54.2 6.6 %collective-permute-start.5 = (f32[2,2,72,128]{3,2,1,0:T(8,128)}, f32[2,2,72,128]{3,2,1,0:T(8,128)S(1)}, u32[]{:S(2)}, u32[]{:S(2)}) collective-permute-start(f32[2,2,72,128]{3,2,1,0:T(8,128)} %get-tuple-element.11), channel_id=1, source_target_pairs={{16,0},{32,16},{48,32},{64,48},{80,64},{96,80},{112,96},{17,1},{33... | collective-permute-start | bytes 442376 | tf_op jit(solution)/shard_map/ppermute | solution.py:401
  62.4 6.3 %copy-start = (f32[5,256,256]{2,1,0:T(8,128)S(1)}, f32[5,256,256]{2,1,0:T(8,128)}, u32[]{:S(2)}) copy-start(f32[5,256,256]{2,1,0:T(8,128)} %pad_maximum_fusion.1.resid_ref.data_ref) | copy-start | bytes 3932164
  62.4 8.6 %collective-permute-start.6 = (f32[2,2,258,65]{2,1,3,0:T(2,128)S(1)}, f32[2,2,258,65]{2,1,3,0:T(2,128)S(1)}, u32[]{:S(2)}, u32[]{:S(2)}) collective-permute-start(f32[2,2,258,65]{2,1,3,0:T(2,128)S(1)} %copy.19), channel_id=1, source_target_pairs={{0,1},{1,2},{2,3},{3,4},{4,5},{5,6},{6,7},{7,8},{8,9},{9,10},{10,1... | collective-permute-start | bytes 804968 | tf_op jit(solution)/shard_map/ppermute | solution.py:195
  66.5 12.9 %collective-permute-start.7 = (f32[2,2,258,65]{2,1,3,0:T(2,128)S(1)}, f32[2,2,258,65]{2,1,3,0:T(2,128)}, u32[]{:S(2)}, u32[]{:S(2)}) collective-permute-start(f32[2,2,258,65]{2,1,3,0:T(2,128)S(1)} %copy.20), channel_id=1, source_target_pairs={{1,0},{2,1},{3,2},{4,3},{5,4},{6,5},{7,6},{8,7},{9,8},{10,9},{11,1... | collective-permute-start | bytes 804968 | tf_op jit(solution)/shard_map/ppermute | solution.py:195
  68.7 12.0 %copy-start.3 = (f32[2,2,128,128]{3,2,1,0:T(8,128)S(1)}, f32[2,2,128,128]{3,2,1,0:T(8,128)}, u32[]{:S(2)}) copy-start(f32[2,2,128,128]{3,2,1,0:T(8,128)} %get-tuple-element.10) | copy-start | bytes 786436
  82.4 0.7 copy-start.7
  83.8 1.2 %slice-start = ((f32[5,256,256]{2,1,0:T(8,128)}), f32[4,256,256]{2,1,0:T(8,128)S(1)}, s32[]{:S(2)}) async-start(f32[5,256,256]{2,1,0:T(8,128)} %pad_maximum_fusion.1.resid_ref.data_ref), calls=%async_computation | async-start | bytes 2097152 | tf_op jit(solution)/shard_map/slice | solution.py:376

commit v6 on v5

--- a/solution.py
+++ b/solution.py
@@ -206,7 +206,39 @@
     return jnp.concatenate(rows, axis=-2)
 
 
-def solve_kernel(rect_ref, resid_ref, data_ref, wrow_ref, wcol_ref, *refs, has_base, last, own_rows, own_cols, slab):
+def grid_residual(fields_ref, data_ref, res_ref):
+    height, breadth = (res_ref.shape[1], res_ref.shape[2])
+
+    def ahead(x, step, axis):
+        return pltpu.roll(x, x.shape[axis] - step, axis)
+
+    for problem in range(res_ref.shape[0] // 2):
+        sign = 1.0 - 2.0 * problem
+        totals, centres = ([], [])
+        for part in range(2):
+            padded = fields_ref[2 * problem + part]
+            outer = padded + ahead(padded, 2, 0)
+            middle = ahead(padded, 1, 0)
+            edge = ahead(outer, 1, 1) + middle + ahead(middle, 2, 1)
+            corner = outer + ahead(outer, 2, 1)
+            totals.append((4.0 * edge + corner)[:height, :breadth])
+            centres.append(ahead(middle, 1, 1)[:height, :breadth])
+        real_part, imag_part = centres
+        wave = data_ref[4]
+        lap_r = (totals[0] - 20.0 * real_part) / 6.0
+        lap_i = (totals[1] - 20.0 * imag_part) / 6.0
+        mass_r = real_part - sign * DAMPING * imag_part
+        mass_i = imag_part + sign * DAMPING * real_part
+        res_ref[2 * problem] = data_ref[2 * problem] - (-lap_r - wave * mass_r)
+        res_ref[2 * problem + 1] = data_ref[2 * problem + 1] - (-lap_i - wave * mass_i)
+
+
+def solve_kernel(rect_ref, resid_ref, data_ref, wrow_ref, wcol_ref, *refs, has_base, last, own_rows, own_cols, slab,
+                 from_fields):
+    if from_fields:
+        grid_residual(resid_ref, data_ref, refs[-1])
+        resid_ref = refs[-1]
+        refs = refs[:-1]
     base_ref = refs[0] if has_base else None
     outs = refs[1:] if has_base else refs
     full_ref = None if last else outs[0]
@@ -316,23 +348,27 @@
 
 
 def solve_local_kernel(resid_planes, data_ext, row_mats, col_mats, live_rect, own_shape, slab, base=None, last=False,
-                       interpret=False):
+                       from_fields=False, interpret=False):
     extra = [] if base is None else [base]
     rect = jnp.stack([to_index(v) for v in live_rect])
     dtype = resid_planes.dtype
-    shapes = [] if last else [(2, 2) + resid_planes.shape[1:]]
+    ext_shape = data_ext.shape[1:]
+    shapes = [] if last else [(2, 2) + ext_shape]
     shapes.append((2, 2) + own_shape)
     if not last:
         shapes += [(2, 2, slab, own_shape[1])] * 2
     vmem = pltpu.MemorySpace.VMEM if hasattr(pltpu, "MemorySpace") else pltpu.VMEM
     kernel = functools.partial(
-        solve_kernel, has_base=base is not None, last=last, own_rows=own_shape[0], own_cols=own_shape[1], slab=slab
-    )
+        solve_kernel, has_base=base is not None, last=last, own_rows=own_shape[0], own_cols=own_shape[1], slab=slab,
+        from_fields=from_fields,
+    )
+    scratch = [pltpu.VMEM((4,) + ext_shape, jnp.float32)] if from_fields else []
     return pl.pallas_call(
         kernel,
         out_shape=[jax.ShapeDtypeStruct(s, dtype) for s in shapes],
         in_specs=[pl.BlockSpec(memory_space=pltpu.SMEM)] + [pl.BlockSpec(memory_space=vmem)] * (4 + len(extra)),
         out_specs=[pl.BlockSpec(memory_space=vmem)] * len(shapes),
+        scratch_shapes=scratch,
         interpret=interpret,
     )(rect, resid_planes, data_ext, row_mats, col_mats, *extra)
 
@@ -403,10 +439,13 @@
             left, right = exchange_axis(tall, "gy", 3, width)
             padded = jnp.concatenate([left, tall, right], axis=3)
             padded = grid_ghost(padded, width, edges, signs)
-            resid_ext = sources_ext - apply_operator(padded, wave_ext, signs)
-            resid_planes = resid_ext.reshape((4,) + resid_ext.shape[2:])
+            tile_rows = -(-padded.shape[2] // 8) * 8 - padded.shape[2]
+            tile_cols = -(-padded.shape[3] // 128) * 128 - padded.shape[3]
+            padded = jnp.pad(padded, ((0, 0), (0, 0), (0, tile_rows), (0, tile_cols)))
+            resid_planes = padded.reshape((4,) + padded.shape[2:])
         outs = solve_local_kernel(
-            resid_planes, stacked_ext, row_mats, col_mats, live_rect, (own_rows, own_cols), slab, base=base, last=last
+            resid_planes, stacked_ext, row_mats, col_mats, live_rect, (own_rows, own_cols), slab, base=base, last=last,
+            from_fields=iteration > 0,
         )
         if last:
             solution = outs[0]

time: 101 us -> 99 us (0.980)
  the two profiles are of different devices: /device:TPU:97 before, /device:TPU:6 now
where the time goes in v6:
time: 99 us; the launch traced here: 97.2 us
  starting transfers between devices  30.5 us (31%)
  Pallas kernels  27 us (27%)
  waiting for transfers between devices  17.3 us (17%)
  local copies, waits for them, and re-layouts  11.5 us (12%)
  other arithmetic  7.89 us (8%)
  between operations  2.97 us (3%)
    pallas_call x2, Pallas kernels, solve_local_kernel(): pl.pallas_call(kernel, out_shape=[jax.ShapeDtypeStruct(s, dtype) for s in...  27 us
    ppermute x6, starting transfers between devices, exchange_axis(): return (lax.ppermute(last, axis, up), lax.ppermute(first, axis, down))  24.6 us
    ppermute x6, waiting for transfers between devices, exchange_axis(): return (lax.ppermute(last, axis, up), lax.ppermute(first, axis, down))  11.5 us
    ppermute x1, waiting for transfers between devices, shards(): after = lax.ppermute(top, 'gx', down)[:, :, :width]  3.89 us
    ppermute x1, starting transfers between devices, shards(): before = lax.ppermute(bottom, 'gx', up)[:, :, slab - width:]  3.57 us
    ppermute x1, starting transfers between devices, shards(): after = lax.ppermute(top, 'gx', down)[:, :, :width]  2.26 us
  transfers between devices with their start and end apart: 8, of which 7 were waited for; matrix products, arithmetic and copies ran while one was open for 5% of the time, Pallas kernels for 0%

profile of v6, /device:TPU:6, one launch (start us, length us, event | category | flops | bytes accessed | tf_op | source)
XLA Modules:
  0.0 97.2 jit_solution(5457928547371675252)
XLA Ops:
  0.0 0.9 fusion.11
  1.0 0.1 reshape_squeeze.12
  1.0 0.9 fusion.1
  2.0 3.8 %collective-permute-start = (f32[6,64,128]{2,1,0:T(8,128)S(1)}, f32[6,64,128]{2,1,0:T(8,128)S(1)}, u32[]{:S(2)}, u32[]{:S(2)}) collective-permute-start(f32[6,64,128]{2,1,0:T(8,128)S(1)} %pad_maximum_fusion.7), channel_id=1, source_target_pairs={{0,16},{16,32},{32,48},{48,64},{64,80},{80,96},{96,112},{1,17},{17... | collective-permute-start | bytes 589832 | tf_op jit(solution)/shard_map/ppermute | solution.py:195
  5.7 0.1 reshape_squeeze.13
  5.8 0.9 fusion
  6.8 2.1 %collective-permute-start.1 = (f32[6,64,128]{2,1,0:T(8,128)S(1)}, f32[6,64,128]{2,1,0:T(8,128)S(1)}, u32[]{:S(2)}, u32[]{:S(2)}) collective-permute-start(f32[6,64,128]{2,1,0:T(8,128)S(1)} %fusion), channel_id=1, source_target_pairs={{16,0},{32,16},{48,32},{64,48},{80,64},{96,80},{112,96},{17,1},{33... | collective-permute-start | bytes 589832 | tf_op jit(solution)/shard_map/ppermute | solution.py:195
  8.9 0.7 fusion.12
  12.1 0.0 collective-permute-done
  12.2 3.7 %collective-permute-done.1 = f32[6,64,128]{2,1,0:T(8,128)S(1)} collective-permute-done((f32[6,64,128]{2,1,0:T(8,128)S(1)}, f32[6,64,128]{2,1,0:T(8,128)S(1)}, u32[]{:S(2)}, u32[]{:S(2)}) %collective-permute-start.1) | collective-permute-done | bytes 196640 | tf_op jit(solution)/shard_map/ppermute | solution.py:195
  16.0 0.2 fusion.8
  16.2 0.3 copy-done.5
  16.6 0.1 select_maximum_fusion.1
  16.6 0.2 copy.11
  16.9 0.0 slice-start
  16.9 0.0 copy-start.3
  16.9 2.1 %collective-permute-start.2 = (f32[6,256,64]{1,2,0:T(8,128)S(1)}, f32[6,256,64]{1,2,0:T(8,128)S(1)}, u32[]{:S(2)}, u32[]{:S(2)}) collective-permute-start(f32[6,256,64]{1,2,0:T(8,128)S(1)} %copy.11), channel_id=1, source_target_pairs={{0,1},{1,2},{2,3},{3,4},{4,5},{5,6},{6,7},{7,8},{8,9},{9,10},{10,1... | collective-permute-start | bytes 1179656 | tf_op jit(solution)/shard_map/ppermute | solution.py:195
  19.0 0.1 select_maximum_fusion
  19.0 0.2 copy.13
  19.3 7.3 %collective-permute-start.3 = (f32[6,256,64]{1,2,0:T(8,128)S(1)}, f32[6,256,64]{1,2,0:T(8,128)}, u32[]{:S(2)}, u32[]{:S(2)}) collective-permute-start(f32[6,256,64]{1,2,0:T(8,128)S(1)} %copy.13), channel_id=1, source_target_pairs={{1,0},{2,1},{3,2},{4,3},{5,4},{6,5},{7,6},{8,7},{9,8},{10,9},{11,1... | collective-permute-start | bytes 1179656 | tf_op jit(solution)/shard_map/ppermute | solution.py:195
  26.6 0.6 pad_add_fusion.rect_ref
  27.1 0.1 reshape.91
  27.2 0.1 reshape.92
  27.3 0.3 multiply_bitcast_fusion
  27.6 1.0 %reshape.95.wcol_ref = f32[2,256,128]{2,1,0:T(8,128)} reshape(f32[2,2,2,64,2,64]{5,4,3,2,1,0:T(2,128)S(1)} %multiply_bitcast_fusion) | data formatting | bytes 524288 | tf_op jit(solution)/shard_map/reshape | solution.py:346
  28.6 1.2 %collective-permute-done.2 = f32[6,256,64]{1,2,0:T(8,128)S(1)} collective-permute-done((f32[6,256,64]{1,2,0:T(8,128)S(1)}, f32[6,256,64]{1,2,0:T(8,128)S(1)}, u32[]{:S(2)}, u32[]{:S(2)}) %collective-permute-start.2) | collective-permute-done | bytes 393248 | tf_op jit(solution)/shard_map/ppermute | solution.py:195
  29.8 0.2 copy.27
  30.0 1.8 %collective-permute-done.3 = f32[6,256,64]{1,2,0:T(8,128)} collective-permute-done((f32[6,256,64]{1,2,0:T(8,128)S(1)}, f32[6,256,64]{1,2,0:T(8,128)}, u32[]{:S(2)}, u32[]{:S(2)}) %collective-permute-start.3) | collective-permute-done | bytes 393248 | tf_op jit(solution)/shard_map/ppermute | solution.py:195
  31.8 1.0 %slice.131 = f32[5,256,64]{1,2,0:T(8,128)S(1)} slice(f32[6,256,64]{1,2,0:T(8,128)} %collective-permute-done.3), slice={[0:5], [0:256], [0:64]} | slice | bytes 655360 | tf_op jit(solution)/shard_map/slice | solution.py:411
  32.8 0.2 copy.28
  33.1 0.1 copy.23
  33.2 0.8 slice.133
  33.9 0.1 copy.24
  34.1 0.2 copy.17
  34.2 0.2 multiply_bitcast_fusion.1
  34.5 1.2 %reshape.90.wrow_ref = f32[2,128,256]{2,1,0:T(8,128)} reshape(f32[2,2,64,2,2,64]{5,4,3,2,1,0:T(2,128)S(1)} %multiply_bitcast_fusion.1) | data formatting | bytes 524288 | tf_op jit(solution)/shard_map/reshape | solution.py:344
  35.6 1.6 %pad_maximum_fusion.1.resid_ref.data_ref = f32[5,256,256]{2,1,0:T(8,128)} fusion(f32[5,256,64]{2,1,0:T(8,128)S(1)} %copy.28, f32[5,64,128]{2,1,0:T(8,128)S(1)} %slice.127, f32[1,128,128]{2,1,0:T(8,128)S(1)} %bitcast.44, f32[4,128,128]{2,1,0:T(8,128)S(1)} %bitcast.40, f32[5,64,128]{2,1,0:T(8,128)S(1)} %slice.126, f32[5,256,64]{2,1,0:T(8,128)S(1)} %copy.27), kind=kLoop, calls=%fused_computation.4 | loop fusion | flops 1638400 | bytes 2621440 | tf_op jit(solution)/shard_map/concatenate | solution.py:411
  37.3 12.5 %shard_map.64 = (f32[2,2,256,256]{3,2,1,0:T(8,128)}, f32[2,2,128,128]{3,2,1,0:T(8,128)}, f32[2,2,72,128]{3,2,1,0:T(8,128)}, f32[2,2,72,128]{3,2,1,0:T(8,128)}) custom-call(s32[4]{0:T(128)} %pad_add_fusion.rect_ref, f32[5,256,256]{2,1,0:T(8,128)} %pad_maximum_fusion.1.resid_ref.data_ref, f32[5,256,256]{2,1,0:T(8,128)} %pad_maximum_fusion.1.resid_ref.data_ref, ...), custom_call_target="tpu_custom_call" | custom-call | tf_op jit(solution)/shard_map/pallas_call | solution.py:366
  49.8 3.6 %collective-permute-start.4 = (f32[2,2,72,128]{3,2,1,0:T(8,128)}, f32[2,2,72,128]{3,2,1,0:T(8,128)S(1)}, u32[]{:S(2)}, u32[]{:S(2)}) collective-permute-start(f32[2,2,72,128]{3,2,1,0:T(8,128)} %get-tuple-element.9), channel_id=1, source_target_pairs={{0,16},{16,32},{32,48},{48,64},{64,80},{80,96},{96,112},{1,17},{17... | collective-permute-start | bytes 442376 | tf_op jit(solution)/shard_map/ppermute | solution.py:436
  53.3 2.3 %collective-permute-start.5 = (f32[2,2,72,128]{3,2,1,0:T(8,128)}, f32[2,2,72,128]{3,2,1,0:T(8,128)S(1)}, u32[]{:S(2)}, u32[]{:S(2)}) collective-permute-start(f32[2,2,72,128]{3,2,1,0:T(8,128)} %get-tuple-element.11), channel_id=1, source_target_pairs={{16,0},{32,16},{48,32},{64,48},{80,64},{96,80},{112,96},{17,1},{33... | collective-permute-start | bytes 442376 | tf_op jit(solution)/shard_map/ppermute | solution.py:437
  55.7 1.9 %collective-permute-done.4 = f32[2,2,72,128]{3,2,1,0:T(8,128)S(1)} collective-permute-done((f32[2,2,72,128]{3,2,1,0:T(8,128)}, f32[2,2,72,128]{3,2,1,0:T(8,128)S(1)}, u32[]{:S(2)}, u32[]{:S(2)}) %collective-permute-start.4) | collective-permute-done | bytes 147488 | tf_op jit(solution)/shard_map/ppermute | solution.py:436
  57.6 3.9 %collective-permute-done.5 = f32[2,2,72,128]{3,2,1,0:T(8,128)S(1)} collective-permute-done((f32[2,2,72,128]{3,2,1,0:T(8,128)}, f32[2,2,72,128]{3,2,1,0:T(8,128)S(1)}, u32[]{:S(2)}, u32[]{:S(2)}) %collective-permute-start.5) | collective-permute-done | bytes 147488 | tf_op jit(solution)/shard_map/ppermute | solution.py:437
  61.5 1.0 %pad_maximum_fusion.3 = f32[2,2,258,128]{3,2,1,0:T(8,128)S(1)} fusion(f32[2,2,65,128]{3,2,1,0:T(8,128)S(1)} %bitcast.47, f32[2,2,128,128]{3,2,1,0:T(8,128)} %get-tuple-element.10, f32[2,2,65,128]{3,2,1,0:T(8,128)S(1)} %slice.136), kind=kLoop, calls=%fused_computation.13 | loop fusion | flops 264192 | bytes 1056768 | tf_op jit(solution)/shard_map/concatenate | solution.py:438
  62.5 0.2 fusion.9
  62.7 0.3 copy.19
  63.0 0.0 copy-start.2
  63.0 2.1 %collective-permute-start.6 = (f32[2,2,258,65]{2,1,3,0:T(2,128)S(1)}, f32[2,2,258,65]{2,1,3,0:T(2,128)S(1)}, u32[]{:S(2)}, u32[]{:S(2)}) collective-permute-start(f32[2,2,258,65]{2,1,3,0:T(2,128)S(1)} %copy.19), channel_id=1, source_target_pairs={{0,1},{1,2},{2,3},{3,4},{4,5},{5,6},{6,7},{7,8},{8,9},{9,10},{10,1... | collective-permute-start | bytes 804968 | tf_op jit(solution)/shard_map/ppermute | solution.py:195
  65.1 0.3 copy.20
  65.4 7.4 %collective-permute-start.7 = (f32[2,2,258,65]{2,1,3,0:T(2,128)S(1)}, f32[2,2,258,65]{2,1,3,0:T(2,128)S(1)}, u32[]{:S(2)}, u32[]{:S(2)}) collective-permute-start(f32[2,2,258,65]{2,1,3,0:T(2,128)S(1)} %copy.20), channel_id=1, source_target_pairs={{1,0},{2,1},{3,2},{4,3},{5,4},{6,5},{7,6},{8,7},{9,8},{10,9},{11,1... | collective-permute-start | bytes 804968 | tf_op jit(solution)/shard_map/ppermute | solution.py:195
  72.8 0.1 or_or_fusion
  73.0 3.0 %collective-permute-done.6 = f32[2,2,258,65]{2,1,3,0:T(2,128)S(1)} collective-permute-done((f32[2,2,258,65]{2,1,3,0:T(2,128)S(1)}, f32[2,2,258,65]{2,1,3,0:T(2,128)S(1)}, u32[]{:S(2)}, u32[]{:S(2)}) %collective-permute-start.6) | collective-permute-done | bytes 268352 | tf_op jit(solution)/shard_map/ppermute | solution.py:195
  75.9 0.3 copy.21
  76.2 1.8 %collective-permute-done.7 = f32[2,2,258,65]{2,1,3,0:T(2,128)S(1)} collective-permute-done((f32[2,2,258,65]{2,1,3,0:T(2,128)S(1)}, f32[2,2,258,65]{2,1,3,0:T(2,128)S(1)}, u32[]{:S(2)}, u32[]{:S(2)}) %collective-permute-start.7) | collective-permute-done | bytes 268352 | tf_op jit(solution)/shard_map/ppermute | solution.py:195
  78.0 0.3 copy.22
  78.3 0.6 pad_maximum_fusion
  78.9 0.2 select_select_fusion.1
  79.2 0.8 slice_reduce_fusion.1
  80.0 0.0 copy-start.6
  80.0 0.4 select_select_fusion
  80.4 0.2 copy-done.6
  80.7 0.2 multiply_add_fusion
  80.9 0.5 maximum_select_fusion
  81.3 1.3 %pad.13 = f32[2,2,264,384]{3,2,1,0:T(8,128)} pad(f32[2,2,258,258]{3,2,1,0:T(8,128)S(1)} %maximum_select_fusion, f32[]{:T(128)} %constant.31.clone.1), padding=0_0x0_0x0_6x0_126 | pad | bytes 2687044 | tf_op jit(solution)/shard_map/jit(_pad)/pad | solution.py:444
  82.6 14.5 %shard_map.65 = f32[2,2,128,128]{3,2,1,0:T(8,128)} custom-call(s32[4]{0:T(128)} %pad_add_fusion.rect_ref, f32[4,264,384]{2,1,0:T(8,128)} %bitcast.36, f32[5,256,256]{2,1,0:T(8,128)} %pad_maximum_fusion.1.resid_ref.data_ref, f32[2,128,256]{2,1,0:T(8,128)} %reshape.90.wrow_ref, f32[2,256,128]{2,1,0:T(8,128)} %reshape.95.wcol_ref, ...), custom_call_target="tpu_custom_call" | custom-call | tf_op jit(solution)/shard_map/pallas_call | solution.py:366
  (30 shorter events, 0.3 us)
Async XLA Ops:
  0.0 15.9 %copy-start = (f32[2,2,128,128]{3,2,1,0:T(8,128)S(1)}, f32[2,2,128,128]{3,2,1,0:T(8,128)}, u32[]{:S(2)}) copy-start(f32[2,2,128,128]{3,2,1,0:T(8,128)} %param.6) | copy-start | bytes 786436
  0.0 15.9 %copy-start.1 = (f32[128,128]{1,0:T(8,128)S(1)}, f32[128,128]{1,0:T(8,128)}, u32[]{:S(2)}) copy-start(f32[128,128]{1,0:T(8,128)} %param.7) | copy-start | bytes 196612
  0.0 8.9 %copy-start.7 = (s32[1,1,4]{2,1,0:T(1,128)S(1)}, s32[1,1,4]{2,1,0:T(1,128)}, u32[]{:S(2)}) copy-start(s32[1,1,4]{2,1,0:T(1,128)} %param.10) | copy-start | bytes 52
  0.0 12.1 %copy-start.4 = (f32[2,2,64,64]{3,2,1,0:T(8,128)S(1)}, f32[2,2,64,64]{3,2,1,0:T(8,128)}, u32[]{:S(2)}) copy-start(f32[2,2,64,64]{3,2,1,0:T(8,128)} %param.8) | copy-start | bytes 196612
  2.0 10.2 %collective-permute-start = (f32[6,64,128]{2,1,0:T(8,128)S(1)}, f32[6,64,128]{2,1,0:T(8,128)S(1)}, u32[]{:S(2)}, u32[]{:S(2)}) collective-permute-start(f32[6,64,128]{2,1,0:T(8,128)S(1)} %pad_maximum_fusion.7), channel_id=1, source_target_pairs={{0,16},{16,32},{32,48},{48,64},{64,80},{80,96},{96,112},{1,17},{17... | collective-permute-start | bytes 589832 | tf_op jit(solution)/shard_map/ppermute | solution.py:195
  6.8 9.2 %collective-permute-start.1 = (f32[6,64,128]{2,1,0:T(8,128)S(1)}, f32[6,64,128]{2,1,0:T(8,128)S(1)}, u32[]{:S(2)}, u32[]{:S(2)}) collective-permute-start(f32[6,64,128]{2,1,0:T(8,128)S(1)} %fusion), channel_id=1, source_target_pairs={{16,0},{32,16},{48,32},{64,48},{80,64},{96,80},{112,96},{17,1},{33... | collective-permute-start | bytes 589832 | tf_op jit(solution)/shard_map/ppermute | solution.py:195
  15.9 0.7 copy-start.5
  16.9 10.3 %slice-start = ((f32[6,64,128]{2,1,0:T(8,128)}), f32[1,64,128]{2,1,0:T(8,128)S(1)}, s32[]{:S(2)}) async-start(f32[6,64,128]{2,1,0:T(8,128)} %copy-done.5), calls=%async_computation | async-start | bytes 65536 | tf_op jit(solution)/shard_map/slice | solution.py:417
  16.9 10.4 %copy-start.3 = (f32[2,2,64,64]{3,2,1,0:T(8,128)S(1)}, f32[2,2,64,64]{3,2,1,0:T(8,128)}, u32[]{:S(2)}) copy-start(f32[2,2,64,64]{3,2,1,0:T(8,128)} %param.9) | copy-start | bytes 196612
  16.9 12.8 %collective-permute-start.2 = (f32[6,256,64]{1,2,0:T(8,128)S(1)}, f32[6,256,64]{1,2,0:T(8,128)S(1)}, u32[]{:S(2)}, u32[]{:S(2)}) collective-permute-start(f32[6,256,64]{1,2,0:T(8,128)S(1)} %copy.11), channel_id=1, source_target_pairs={{0,1},{1,2},{2,3},{3,4},{4,5},{5,6},{6,7},{7,8},{8,9},{9,10},{10,1... | collective-permute-start | bytes 1179656 | tf_op jit(solution)/shard_map/ppermute | solution.py:195
  19.3 12.5 %collective-permute-start.3 = (f32[6,256,64]{1,2,0:T(8,128)S(1)}, f32[6,256,64]{1,2,0:T(8,128)}, u32[]{:S(2)}, u32[]{:S(2)}) collective-permute-start(f32[6,256,64]{1,2,0:T(8,128)S(1)} %copy.13), channel_id=1, source_target_pairs={{1,0},{2,1},{3,2},{4,3},{5,4},{6,5},{7,6},{8,7},{9,8},{10,9},{11,1... | collective-permute-start | bytes 1179656 | tf_op jit(solution)/shard_map/ppermute | solution.py:195
  49.8 7.8 %collective-permute-start.4 = (f32[2,2,72,128]{3,2,1,0:T(8,128)}, f32[2,2,72,128]{3,2,1,0:T(8,128)S(1)}, u32[]{:S(2)}, u32[]{:S(2)}) collective-permute-start(f32[2,2,72,128]{3,2,1,0:T(8,128)} %get-tuple-element.9), channel_id=1, source_target_pairs={{0,16},{16,32},{32,48},{48,64},{64,80},{80,96},{96,112},{1,17},{17... | collective-permute-start | bytes 442376 | tf_op jit(solution)/shard_map/ppermute | solution.py:436
  53.3 8.1 %collective-permute-start.5 = (f32[2,2,72,128]{3,2,1,0:T(8,128)}, f32[2,2,72,128]{3,2,1,0:T(8,128)S(1)}, u32[]{:S(2)}, u32[]{:S(2)}) collective-permute-start(f32[2,2,72,128]{3,2,1,0:T(8,128)} %get-tuple-element.11), channel_id=1, source_target_pairs={{16,0},{32,16},{48,32},{64,48},{80,64},{96,80},{112,96},{17,1},{33... | collective-permute-start | bytes 442376 | tf_op jit(solution)/shard_map/ppermute | solution.py:437
  63.0 15.2 %copy-start.2 = (f32[2,2,128,128]{3,2,1,0:T(8,128)S(1)}, f32[2,2,128,128]{3,2,1,0:T(8,128)}, u32[]{:S(2)}) copy-start(f32[2,2,128,128]{3,2,1,0:T(8,128)} %get-tuple-element.10) | copy-start | bytes 786436
  63.0 12.9 %collective-permute-start.6 = (f32[2,2,258,65]{2,1,3,0:T(2,128)S(1)}, f32[2,2,258,65]{2,1,3,0:T(2,128)S(1)}, u32[]{:S(2)}, u32[]{:S(2)}) collective-permute-start(f32[2,2,258,65]{2,1,3,0:T(2,128)S(1)} %copy.19), channel_id=1, source_target_pairs={{0,1},{1,2},{2,3},{3,4},{4,5},{5,6},{6,7},{7,8},{8,9},{9,10},{10,1... | collective-permute-start | bytes 804968 | tf_op jit(solution)/shard_map/ppermute | solution.py:195
  65.4 12.6 %collective-permute-start.7 = (f32[2,2,258,65]{2,1,3,0:T(2,128)S(1)}, f32[2,2,258,65]{2,1,3,0:T(2,128)S(1)}, u32[]{:S(2)}, u32[]{:S(2)}) collective-permute-start(f32[2,2,258,65]{2,1,3,0:T(2,128)S(1)} %copy.20), channel_id=1, source_target_pairs={{1,0},{2,1},{3,2},{4,3},{5,4},{6,5},{7,6},{8,7},{9,8},{10,9},{11,1... | collective-permute-start | bytes 804968 | tf_op jit(solution)/shard_map/ppermute | solution.py:195
  80.0 0.7 copy-start.6

commit v7 on v6

--- a/solution.py
+++ b/solution.py
@@ -290,12 +290,17 @@
     def dot(a, b):
         return jnp.dot(a, b, precision=lax.Precision.HIGH, preferred_element_type=jnp.float32)
 
+    def dot_t(a, b):
+        return lax.dot_general(
+            a, b, (((1,), (1,)), ((), ())), precision=lax.Precision.HIGH, preferred_element_type=jnp.float32
+        )
+
     def rows_apply(real_part, imag_part, sign):
         outs_r, outs_i = ([], [])
         for h in range(breadth // half):
             cols = slice(h * half, (h + 1) * half)
-            prod_r = dot(real_part[:, cols], wrow_ref[h])
-            prod_i = dot(imag_part[:, cols], wrow_ref[h])
+            prod_r = dot_t(real_part[:, cols], wrow_ref[h])
+            prod_i = dot_t(imag_part[:, cols], wrow_ref[h])
             outs_r.append(prod_r[:, :half] - sign * prod_i[:, half:])
             outs_i.append(prod_i[:, :half] + sign * prod_r[:, half:])
         return (jnp.concatenate(outs_r, axis=1), jnp.concatenate(outs_i, axis=1))
@@ -338,13 +343,18 @@
 
 def line_matrices(row_blocks, col_blocks):
     block = row_blocks.shape[-1]
-    eye = jnp.eye(2, dtype=row_blocks.dtype)
-    halves = row_blocks.shape[0] // 2
-    rows_t = jnp.transpose(row_blocks, (0, 3, 1, 2)).reshape(halves, 2, block, 2, block)
-    row_mats = jnp.einsum("hakmo,ab->hakmbo", rows_t, eye).reshape(halves, 2 * block, 4 * block)
-    cols = col_blocks.reshape(halves, 2, 2, block, block)
-    col_mats = jnp.einsum("hamok,ab->hmaobk", cols, eye).reshape(halves, 4 * block, 2 * block)
-    return row_mats, col_mats
+
+    def pairs(blocks):
+        mats = []
+        for h in range(blocks.shape[0] // 2):
+            parts = []
+            for m in range(2):
+                for a in range(2):
+                    parts.append(jnp.pad(blocks[2 * h + a, m], ((0, 0), (a * block, (1 - a) * block))))
+            mats.append(jnp.concatenate(parts, axis=0))
+        return jnp.stack(mats)
+
+    return pairs(row_blocks), pairs(col_blocks)
 
 
 def solve_local_kernel(resid_planes, data_ext, row_mats, col_mats, live_rect, own_shape, slab, base=None, last=False,

time: 99 us -> 99.3 us (level)
  waiting for transfers between devices: 17.3 us -> 22.8 us
  local copies, waits for them, and re-layouts: 11.5 us -> 7.53 us
  starting transfers between devices: 30.5 us -> 28.2 us
  other arithmetic: 7.89 us -> 9.25 us
    ppermute x6, waiting for transfers between devices: 11.5 us -> 17.3 us  [exchange_axis(): return (lax.ppermute(last, axis, up), lax.ppermute(first, axis, down))]
    reshape x5 -> x0, local copies, waits for them, and re-layouts: 2.52 us -> none  [the longest x1 1.16 us: line_matrices(): jnp.einsum('hakmo,ab->hakmbo', rows_t, eye)]
    ppermute x6, starting transfers between devices: 24.6 us -> 22.4 us  [exchange_axis(): return (lax.ppermute(last, axis, up), lax.ppermute(first, axis, down))]
    another operation x1 -> x6, other arithmetic: 0.01 us -> 1.82 us  [pairs(): return jnp.stack(mats)]
where the time goes in v7:
time: 99.3 us; the launch traced here: 97.6 us
  starting transfers between devices  28.2 us (28%)
  Pallas kernels  26.9 us (27%)
  waiting for transfers between devices  22.8 us (23%)
  other arithmetic  9.25 us (9%)
  local copies, waits for them, and re-layouts  7.53 us (8%)
  between operations  3.01 us (3%)
    pallas_call x2, Pallas kernels, solve_local_kernel(): pl.pallas_call(kernel, out_shape=[jax.ShapeDtypeStruct(s, dtype) for s in...  26.9 us
    ppermute x6, starting transfers between devices, exchange_axis(): return (lax.ppermute(last, axis, up), lax.ppermute(first, axis, down))  22.4 us
    ppermute x6, waiting for transfers between devices, exchange_axis(): return (lax.ppermute(last, axis, up), lax.ppermute(first, axis, down))  17.3 us
    ppermute x1, waiting for transfers between devices, shards(): after = lax.ppermute(top, 'gx', down)[:, :, :width]  4.08 us
    ppermute x1, starting transfers between devices, shards(): before = lax.ppermute(bottom, 'gx', up)[:, :, slab - width:]  3.17 us
    ppermute x1, starting transfers between devices, shards(): after = lax.ppermute(top, 'gx', down)[:, :, :width]  2.66 us
  transfers between devices with their start and end apart: 8, of which 7 were waited for; matrix products, arithmetic and copies ran while one was open for 5% of the time, Pallas kernels for 0%

profile of v7, /device:TPU:6, one launch (start us, length us, event | category | flops | bytes accessed | tf_op | source)
XLA Modules:
  0.0 97.6 jit_solution(13513261929447322187)
XLA Ops:
  0.0 0.0 copy-start.4
  0.0 0.9 fusion.17
  1.0 0.1 reshape_squeeze.12
  1.0 0.9 fusion.1
  2.0 3.8 %collective-permute-start = (f32[6,64,128]{2,1,0:T(8,128)S(1)}, f32[6,64,128]{2,1,0:T(8,128)S(1)}, u32[]{:S(2)}, u32[]{:S(2)}) collective-permute-start(f32[6,64,128]{2,1,0:T(8,128)S(1)} %pad_maximum_fusion.7), channel_id=1, source_target_pairs={{0,16},{16,32},{32,48},{48,64},{64,80},{80,96},{96,112},{1,17},{17... | collective-permute-start | bytes 589832 | tf_op jit(solution)/shard_map/ppermute | solution.py:195
  5.7 0.1 reshape_squeeze.13
  5.8 0.9 fusion
  6.8 2.1 %collective-permute-start.1 = (f32[6,64,128]{2,1,0:T(8,128)S(1)}, f32[6,64,128]{2,1,0:T(8,128)S(1)}, u32[]{:S(2)}, u32[]{:S(2)}) collective-permute-start(f32[6,64,128]{2,1,0:T(8,128)S(1)} %fusion), channel_id=1, source_target_pairs={{16,0},{32,16},{48,32},{64,48},{80,64},{96,80},{112,96},{17,1},{33... | collective-permute-start | bytes 589832 | tf_op jit(solution)/shard_map/ppermute | solution.py:195
  8.9 0.7 fusion.18
  12.1 0.7 pad_add_fusion.rect_ref
  12.8 0.0 collective-permute-done
  12.9 3.1 %collective-permute-done.1 = f32[6,64,128]{2,1,0:T(8,128)S(1)} collective-permute-done((f32[6,64,128]{2,1,0:T(8,128)S(1)}, f32[6,64,128]{2,1,0:T(8,128)S(1)}, u32[]{:S(2)}, u32[]{:S(2)}) %collective-permute-start.1) | collective-permute-done | bytes 196640 | tf_op jit(solution)/shard_map/ppermute | solution.py:195
  16.0 0.2 fusion.14
  16.2 0.3 copy-done.5
  16.6 0.1 select_maximum_fusion
  16.6 0.2 copy.9
  16.9 0.0 slice-start
  16.9 0.0 copy-start.3
  16.9 5.1 %collective-permute-start.3 = (f32[6,256,64]{1,2,0:T(8,128)S(1)}, f32[6,256,64]{1,2,0:T(8,128)S(1)}, u32[]{:S(2)}, u32[]{:S(2)}) collective-permute-start(f32[6,256,64]{1,2,0:T(8,128)S(1)} %copy.9), channel_id=1, source_target_pairs={{1,0},{2,1},{3,2},{4,3},{5,4},{6,5},{7,6},{8,7},{9,8},{10,9},{11,1... | collective-permute-start | bytes 1179656 | tf_op jit(solution)/shard_map/ppermute | solution.py:195
  22.1 0.1 select_maximum_fusion.1
  22.1 0.2 copy.7
  22.4 1.9 %collective-permute-start.2 = (f32[6,256,64]{1,2,0:T(8,128)S(1)}, f32[6,256,64]{1,2,0:T(8,128)S(1)}, u32[]{:S(2)}, u32[]{:S(2)}) collective-permute-start(f32[6,256,64]{1,2,0:T(8,128)S(1)} %copy.7), channel_id=1, source_target_pairs={{0,1},{1,2},{2,3},{3,4},{4,5},{5,6},{6,7},{7,8},{8,9},{9,10},{10,1... | collective-permute-start | bytes 1179656 | tf_op jit(solution)/shard_map/ppermute | solution.py:195
  24.3 0.1 reshape.73
  24.4 0.1 reshape.72
  24.5 0.1 fusion.2
  24.6 0.1 fusion.3
  24.7 0.7 pad_maximum_fusion.5.wcol_ref
  25.4 1.9 %collective-permute-done.3 = f32[6,256,64]{1,2,0:T(8,128)S(1)} collective-permute-done((f32[6,256,64]{1,2,0:T(8,128)S(1)}, f32[6,256,64]{1,2,0:T(8,128)S(1)}, u32[]{:S(2)}, u32[]{:S(2)}) %collective-permute-start.3) | collective-permute-done | bytes 393248 | tf_op jit(solution)/shard_map/ppermute | solution.py:195
  27.3 0.1 copy.12
  27.5 7.6 %collective-permute-done.2 = f32[6,256,64]{1,2,0:T(8,128)S(1)} collective-permute-done((f32[6,256,64]{1,2,0:T(8,128)S(1)}, f32[6,256,64]{1,2,0:T(8,128)S(1)}, u32[]{:S(2)}, u32[]{:S(2)}) %collective-permute-start.2) | collective-permute-done | bytes 393248 | tf_op jit(solution)/shard_map/ppermute | solution.py:195
  35.1 0.1 copy.11
  35.2 0.2 copy.19
  35.5 0.2 copy.20
  35.7 0.1 fusion.4
  35.8 0.1 fusion.5
  35.9 0.7 pad_maximum_fusion.4.wrow_ref
  36.6 1.6 %pad_maximum_fusion.1.resid_ref.data_ref = f32[5,256,256]{2,1,0:T(8,128)} fusion(f32[5,256,64]{2,1,0:T(8,128)S(1)} %copy.20, f32[5,64,128]{2,1,0:T(8,128)S(1)} %slice.191, f32[1,128,128]{2,1,0:T(8,128)S(1)} %bitcast.74, f32[4,128,128]{2,1,0:T(8,128)S(1)} %bitcast.70, f32[5,64,128]{2,1,0:T(8,128)S(1)} %slice.190, f32[5,256,64]{2,1,0:T(8,128)S(1)} %copy.19), kind=kLoop, calls=%fused_computation.4 | loop fusion | flops 1638400 | bytes 2621440 | tf_op jit(solution)/shard_map/concatenate | solution.py:421
  38.3 12.4 %shard_map.64 = (f32[2,2,256,256]{3,2,1,0:T(8,128)}, f32[2,2,128,128]{3,2,1,0:T(8,128)}, f32[2,2,72,128]{3,2,1,0:T(8,128)}, f32[2,2,72,128]{3,2,1,0:T(8,128)}) custom-call(s32[4]{0:T(128)} %pad_add_fusion.rect_ref, f32[5,256,256]{2,1,0:T(8,128)} %pad_maximum_fusion.1.resid_ref.data_ref, f32[5,256,256]{2,1,0:T(8,128)} %pad_maximum_fusion.1.resid_ref.data_ref, ...), custom_call_target="tpu_custom_call" | custom-call | tf_op jit(solution)/shard_map/pallas_call | solution.py:376
  50.7 3.2 %collective-permute-start.4 = (f32[2,2,72,128]{3,2,1,0:T(8,128)}, f32[2,2,72,128]{3,2,1,0:T(8,128)S(1)}, u32[]{:S(2)}, u32[]{:S(2)}) collective-permute-start(f32[2,2,72,128]{3,2,1,0:T(8,128)} %get-tuple-element.9), channel_id=1, source_target_pairs={{0,16},{16,32},{32,48},{48,64},{64,80},{80,96},{96,112},{1,17},{17... | collective-permute-start | bytes 442376 | tf_op jit(solution)/shard_map/ppermute | solution.py:446
  53.9 2.7 %collective-permute-start.5 = (f32[2,2,72,128]{3,2,1,0:T(8,128)}, f32[2,2,72,128]{3,2,1,0:T(8,128)S(1)}, u32[]{:S(2)}, u32[]{:S(2)}) collective-permute-start(f32[2,2,72,128]{3,2,1,0:T(8,128)} %get-tuple-element.11), channel_id=1, source_target_pairs={{16,0},{32,16},{48,32},{64,48},{80,64},{96,80},{112,96},{17,1},{33... | collective-permute-start | bytes 442376 | tf_op jit(solution)/shard_map/ppermute | solution.py:447
  56.6 1.4 %collective-permute-done.4 = f32[2,2,72,128]{3,2,1,0:T(8,128)S(1)} collective-permute-done((f32[2,2,72,128]{3,2,1,0:T(8,128)}, f32[2,2,72,128]{3,2,1,0:T(8,128)S(1)}, u32[]{:S(2)}, u32[]{:S(2)}) %collective-permute-start.4) | collective-permute-done | bytes 147488 | tf_op jit(solution)/shard_map/ppermute | solution.py:446
  57.9 4.1 %collective-permute-done.5 = f32[2,2,72,128]{3,2,1,0:T(8,128)S(1)} collective-permute-done((f32[2,2,72,128]{3,2,1,0:T(8,128)}, f32[2,2,72,128]{3,2,1,0:T(8,128)S(1)}, u32[]{:S(2)}, u32[]{:S(2)}) %collective-permute-start.5) | collective-permute-done | bytes 147488 | tf_op jit(solution)/shard_map/ppermute | solution.py:447
  62.0 1.0 %pad_maximum_fusion.3 = f32[2,2,258,128]{3,2,1,0:T(8,128)S(1)} fusion(f32[2,2,65,128]{3,2,1,0:T(8,128)S(1)} %bitcast.75, f32[2,2,128,128]{3,2,1,0:T(8,128)} %get-tuple-element.10, f32[2,2,65,128]{3,2,1,0:T(8,128)S(1)} %slice.208), kind=kLoop, calls=%fused_computation.13 | loop fusion | flops 264192 | bytes 1056768 | tf_op jit(solution)/shard_map/concatenate | solution.py:448
  63.0 0.2 fusion.15
  63.2 0.3 copy.13
  63.5 0.0 copy-start.2
  63.5 2.1 %collective-permute-start.6 = (f32[2,2,258,65]{2,1,3,0:T(2,128)S(1)}, f32[2,2,258,65]{2,1,3,0:T(2,128)S(1)}, u32[]{:S(2)}, u32[]{:S(2)}) collective-permute-start(f32[2,2,258,65]{2,1,3,0:T(2,128)S(1)} %copy.13), channel_id=1, source_target_pairs={{0,1},{1,2},{2,3},{3,4},{4,5},{5,6},{6,7},{7,8},{8,9},{9,10},{10,1... | collective-permute-start | bytes 804968 | tf_op jit(solution)/shard_map/ppermute | solution.py:195
  65.6 0.3 copy.14
  65.9 7.4 %collective-permute-start.7 = (f32[2,2,258,65]{2,1,3,0:T(2,128)S(1)}, f32[2,2,258,65]{2,1,3,0:T(2,128)S(1)}, u32[]{:S(2)}, u32[]{:S(2)}) collective-permute-start(f32[2,2,258,65]{2,1,3,0:T(2,128)S(1)} %copy.14), channel_id=1, source_target_pairs={{1,0},{2,1},{3,2},{4,3},{5,4},{6,5},{7,6},{8,7},{9,8},{10,9},{11,1... | collective-permute-start | bytes 804968 | tf_op jit(solution)/shard_map/ppermute | solution.py:195
  73.3 0.1 or_or_fusion
  73.5 3.0 %collective-permute-done.6 = f32[2,2,258,65]{2,1,3,0:T(2,128)S(1)} collective-permute-done((f32[2,2,258,65]{2,1,3,0:T(2,128)S(1)}, f32[2,2,258,65]{2,1,3,0:T(2,128)S(1)}, u32[]{:S(2)}, u32[]{:S(2)}) %collective-permute-start.6) | collective-permute-done | bytes 268352 | tf_op jit(solution)/shard_map/ppermute | solution.py:195
  76.4 0.3 copy.15
  76.7 1.8 %collective-permute-done.7 = f32[2,2,258,65]{2,1,3,0:T(2,128)S(1)} collective-permute-done((f32[2,2,258,65]{2,1,3,0:T(2,128)S(1)}, f32[2,2,258,65]{2,1,3,0:T(2,128)S(1)}, u32[]{:S(2)}, u32[]{:S(2)}) %collective-permute-start.7) | collective-permute-done | bytes 268352 | tf_op jit(solution)/shard_map/ppermute | solution.py:195
  78.5 0.3 copy.16
  78.8 0.6 pad_maximum_fusion
  79.5 0.2 select_select_fusion.1
  79.7 0.8 slice_reduce_fusion.1
  80.5 0.0 copy-start.6
  80.5 0.4 select_select_fusion
  81.0 0.2 copy-done.6
  81.2 0.2 multiply_add_fusion
  81.4 0.5 maximum_select_fusion
  81.8 1.3 %pad.79 = f32[2,2,264,384]{3,2,1,0:T(8,128)} pad(f32[2,2,258,258]{3,2,1,0:T(8,128)S(1)} %maximum_select_fusion, f32[]{:T(128)} %constant.31.clone.1), padding=0_0x0_0x0_6x0_126 | pad | bytes 2687044 | tf_op jit(solution)/shard_map/jit(_pad)/pad | solution.py:454
  83.2 14.5 %shard_map.65 = f32[2,2,128,128]{3,2,1,0:T(8,128)} custom-call(s32[4]{0:T(128)} %pad_add_fusion.rect_ref, f32[4,264,384]{2,1,0:T(8,128)} %bitcast.66, f32[5,256,256]{2,1,0:T(8,128)} %pad_maximum_fusion.1.resid_ref.data_ref, f32[2,256,128]{2,1,0:T(8,128)} %pad_maximum_fusion.4.wrow_ref, f32[2,256,128]{2,1,0:T(8,128)} %pad_maximum_fusion.5.wcol_ref, ...), custom_call_target="tpu_custom_call" | custom-call | tf_op jit(solution)/shard_map/pallas_call | solution.py:376
  (33 shorter events, 0.3 us)
Async XLA Ops:
  0.0 15.9 %copy-start = (f32[2,2,128,128]{3,2,1,0:T(8,128)S(1)}, f32[2,2,128,128]{3,2,1,0:T(8,128)}, u32[]{:S(2)}) copy-start(f32[2,2,128,128]{3,2,1,0:T(8,128)} %param.6) | copy-start | bytes 786436
  0.0 15.9 %copy-start.1 = (f32[128,128]{1,0:T(8,128)S(1)}, f32[128,128]{1,0:T(8,128)}, u32[]{:S(2)}) copy-start(f32[128,128]{1,0:T(8,128)} %param.7) | copy-start | bytes 196612
  0.0 8.9 %copy-start.7 = (s32[1,1,4]{2,1,0:T(1,128)S(1)}, s32[1,1,4]{2,1,0:T(1,128)}, u32[]{:S(2)}) copy-start(s32[1,1,4]{2,1,0:T(1,128)} %param.10) | copy-start | bytes 52
  0.0 12.8 %copy-start.4 = (f32[2,2,64,64]{3,2,1,0:T(8,128)S(1)}, f32[2,2,64,64]{3,2,1,0:T(8,128)}, u32[]{:S(2)}) copy-start(f32[2,2,64,64]{3,2,1,0:T(8,128)} %param.8) | copy-start | bytes 196612
  2.0 10.8 %collective-permute-start = (f32[6,64,128]{2,1,0:T(8,128)S(1)}, f32[6,64,128]{2,1,0:T(8,128)S(1)}, u32[]{:S(2)}, u32[]{:S(2)}) collective-permute-start(f32[6,64,128]{2,1,0:T(8,128)S(1)} %pad_maximum_fusion.7), channel_id=1, source_target_pairs={{0,16},{16,32},{32,48},{48,64},{64,80},{80,96},{96,112},{1,17},{17... | collective-permute-start | bytes 589832 | tf_op jit(solution)/shard_map/ppermute | solution.py:195
  6.8 9.2 %collective-permute-start.1 = (f32[6,64,128]{2,1,0:T(8,128)S(1)}, f32[6,64,128]{2,1,0:T(8,128)S(1)}, u32[]{:S(2)}, u32[]{:S(2)}) collective-permute-start(f32[6,64,128]{2,1,0:T(8,128)S(1)} %fusion), channel_id=1, source_target_pairs={{16,0},{32,16},{48,32},{64,48},{80,64},{96,80},{112,96},{17,1},{33... | collective-permute-start | bytes 589832 | tf_op jit(solution)/shard_map/ppermute | solution.py:195
  15.9 0.7 copy-start.5
  16.9 7.4 %slice-start = ((f32[6,64,128]{2,1,0:T(8,128)}), f32[1,64,128]{2,1,0:T(8,128)S(1)}, s32[]{:S(2)}) async-start(f32[6,64,128]{2,1,0:T(8,128)} %copy-done.5), calls=%async_computation | async-start | bytes 65536 | tf_op jit(solution)/shard_map/slice | solution.py:427
  16.9 7.5 %copy-start.3 = (f32[2,2,64,64]{3,2,1,0:T(8,128)S(1)}, f32[2,2,64,64]{3,2,1,0:T(8,128)}, u32[]{:S(2)}) copy-start(f32[2,2,64,64]{3,2,1,0:T(8,128)} %param.9) | copy-start | bytes 196612
  16.9 10.4 %collective-permute-start.3 = (f32[6,256,64]{1,2,0:T(8,128)S(1)}, f32[6,256,64]{1,2,0:T(8,128)S(1)}, u32[]{:S(2)}, u32[]{:S(2)}) collective-permute-start(f32[6,256,64]{1,2,0:T(8,128)S(1)} %copy.9), channel_id=1, source_target_pairs={{1,0},{2,1},{3,2},{4,3},{5,4},{6,5},{7,6},{8,7},{9,8},{10,9},{11,1... | collective-permute-start | bytes 1179656 | tf_op jit(solution)/shard_map/ppermute | solution.py:195
  22.4 12.7 %collective-permute-start.2 = (f32[6,256,64]{1,2,0:T(8,128)S(1)}, f32[6,256,64]{1,2,0:T(8,128)S(1)}, u32[]{:S(2)}, u32[]{:S(2)}) collective-permute-start(f32[6,256,64]{1,2,0:T(8,128)S(1)} %copy.7), channel_id=1, source_target_pairs={{0,1},{1,2},{2,3},{3,4},{4,5},{5,6},{6,7},{7,8},{8,9},{9,10},{10,1... | collective-permute-start | bytes 1179656 | tf_op jit(solution)/shard_map/ppermute | solution.py:195
  50.7 7.2 %collective-permute-start.4 = (f32[2,2,72,128]{3,2,1,0:T(8,128)}, f32[2,2,72,128]{3,2,1,0:T(8,128)S(1)}, u32[]{:S(2)}, u32[]{:S(2)}) collective-permute-start(f32[2,2,72,128]{3,2,1,0:T(8,128)} %get-tuple-element.9), channel_id=1, source_target_pairs={{0,16},{16,32},{32,48},{48,64},{64,80},{80,96},{96,112},{1,17},{17... | collective-permute-start | bytes 442376 | tf_op jit(solution)/shard_map/ppermute | solution.py:446
  53.9 8.1 %collective-permute-start.5 = (f32[2,2,72,128]{3,2,1,0:T(8,128)}, f32[2,2,72,128]{3,2,1,0:T(8,128)S(1)}, u32[]{:S(2)}, u32[]{:S(2)}) collective-permute-start(f32[2,2,72,128]{3,2,1,0:T(8,128)} %get-tuple-element.11), channel_id=1, source_target_pairs={{16,0},{32,16},{48,32},{64,48},{80,64},{96,80},{112,96},{17,1},{33... | collective-permute-start | bytes 442376 | tf_op jit(solution)/shard_map/ppermute | solution.py:447
  63.5 15.2 %copy-start.2 = (f32[2,2,128,128]{3,2,1,0:T(8,128)S(1)}, f32[2,2,128,128]{3,2,1,0:T(8,128)}, u32[]{:S(2)}) copy-start(f32[2,2,128,128]{3,2,1,0:T(8,128)} %get-tuple-element.10) | copy-start | bytes 786436
  63.5 12.9 %collective-permute-start.6 = (f32[2,2,258,65]{2,1,3,0:T(2,128)S(1)}, f32[2,2,258,65]{2,1,3,0:T(2,128)S(1)}, u32[]{:S(2)}, u32[]{:S(2)}) collective-permute-start(f32[2,2,258,65]{2,1,3,0:T(2,128)S(1)} %copy.13), channel_id=1, source_target_pairs={{0,1},{1,2},{2,3},{3,4},{4,5},{5,6},{6,7},{7,8},{8,9},{9,10},{10,1... | collective-permute-start | bytes 804968 | tf_op jit(solution)/shard_map/ppermute | solution.py:195
  65.9 12.6 %collective-permute-start.7 = (f32[2,2,258,65]{2,1,3,0:T(2,128)S(1)}, f32[2,2,258,65]{2,1,3,0:T(2,128)S(1)}, u32[]{:S(2)}, u32[]{:S(2)}) collective-permute-start(f32[2,2,258,65]{2,1,3,0:T(2,128)S(1)} %copy.14), channel_id=1, source_target_pairs={{1,0},{2,1},{3,2},{4,3},{5,4},{6,5},{7,6},{8,7},{9,8},{10,9},{11,1... | collective-permute-start | bytes 804968 | tf_op jit(solution)/shard_map/ppermute | solution.py:195
  80.5 0.7 copy-start.6

commit v8 on v7

--- a/solution.py
+++ b/solution.py
@@ -61,22 +61,27 @@
     return jnp.where(inside, values, ghost_cycle)
 
 
-def grid_ghost(values, width, edges, signs):
+def grid_ghost(values, width, extent, edges, signs):
     at_top, at_bottom, at_left, at_right = edges
-    height, breadth = (values.shape[2], values.shape[3])
-    row_ids = lax.broadcasted_iota(jnp.int32, (height, 1), 0)
-    col_ids = lax.broadcasted_iota(jnp.int32, (1, breadth), 1)
+    height, breadth = extent
+    row_ids = lax.broadcasted_iota(jnp.int32, (values.shape[2], 1), 0)
+    col_ids = lax.broadcasted_iota(jnp.int32, (1, values.shape[3]), 1)
     above = at_top & (row_ids < width)
     below = at_bottom & (row_ids >= height - width)
-    values = jnp.where(
-        above, values[:, :, width : width + 1], jnp.where(below, values[:, :, height - width - 1 : height - width], values)
-    )
     before = at_left & (col_ids < width)
     after = at_right & (col_ids >= breadth - width)
-    values = jnp.where(
-        before, values[:, :, :, width : width + 1],
-        jnp.where(after, values[:, :, :, breadth - width - 1 : breadth - width], values),
-    )
+    first_row, last_row = (width, height - width - 1)
+    first_col, last_col = (width, breadth - width - 1)
+
+    def rows_filled(part):
+        return jnp.where(
+            above, part[:, :, first_row : first_row + 1], jnp.where(below, part[:, :, last_row : last_row + 1], part)
+        )
+
+    filled = rows_filled(values)
+    left_col = rows_filled(values[:, :, :, first_col : first_col + 1])
+    right_col = rows_filled(values[:, :, :, last_col : last_col + 1])
+    values = jnp.where(before, left_col, jnp.where(after, right_col, filled))
     outside = above | below | before | after
     real_part = values[:, 0]
     imag_part = values[:, 1]
@@ -445,13 +450,15 @@
             down = [(j, i) for i, j in up]
             before = lax.ppermute(bottom, "gx", up)[:, :, slab - width :]
             after = lax.ppermute(top, "gx", down)[:, :, :width]
-            tall = jnp.concatenate([before, solution, after], axis=2)
+            extent = (own_rows + 2 * width, own_cols + 2 * width)
+            tile_rows = -(-extent[0] // 8) * 8 - extent[0]
+            tile_cols = -(-extent[1] // 128) * 128 - extent[1]
+            fill_rows = jnp.zeros(solution.shape[:2] + (tile_rows, own_cols), solution.dtype)
+            tall = jnp.concatenate([before, solution, after, fill_rows], axis=2)
             left, right = exchange_axis(tall, "gy", 3, width)
-            padded = jnp.concatenate([left, tall, right], axis=3)
-            padded = grid_ghost(padded, width, edges, signs)
-            tile_rows = -(-padded.shape[2] // 8) * 8 - padded.shape[2]
-            tile_cols = -(-padded.shape[3] // 128) * 128 - padded.shape[3]
-            padded = jnp.pad(padded, ((0, 0), (0, 0), (0, tile_rows), (0, tile_cols)))
+            fill_cols = jnp.zeros(tall.shape[:3] + (tile_cols,), solution.dtype)
+            padded = jnp.concatenate([left, tall, right, fill_cols], axis=3)
+            padded = grid_ghost(padded, width, extent, edges, signs)
             resid_planes = padded.reshape((4,) + padded.shape[2:])
         outs = solve_local_kernel(
             resid_planes, stacked_ext, row_mats, col_mats, live_rect, (own_rows, own_cols), slab, base=base, last=last,

time: 99.3 us -> 99.6 us (level); the launches traced: 97.6 us -> 99.1 us
  other arithmetic: 9.25 us -> 12.5 us
  waiting for transfers between devices: 22.8 us -> 20.5 us
  starting transfers between devices: 28.2 us -> 29.4 us
    ppermute x6, waiting for transfers between devices: 17.3 us -> 14.9 us  [exchange_axis(): return (lax.ppermute(last, axis, up), lax.ppermute(first, axis, down))]
    select_n x1, other arithmetic: 0.46 us -> 2.4 us  [grid_ghost(): return jnp.where(outside, ghost_cycle, values)]
    pad x1 -> x0, local copies, waits for them, and re-layouts: 1.32 us -> none  [shards(): padded = jnp.pad(padded, ((0, 0), (0, 0), (0, tile_rows), (0, tile_cols)))]
    ppermute x6, starting transfers between devices: 22.4 us -> 23.6 us  [exchange_axis(): return (lax.ppermute(last, axis, up), lax.ppermute(first, axis, down))]
    select_n x2, other arithmetic: 0.66 us -> 1.81 us  [the longest x1 1.05 us: grid_ghost(): values = jnp.where(before, left_col, jnp.where(after, right_col, filled))]
  transfers between devices with their start and end apart: 8 -> 8, of which waited for: 7 -> 6; matrix products, arithmetic and copies ran while one was open for 5% -> 7% of each run, Pallas kernels for 0% -> 0%
where the time goes in v8:
time: 99.6 us; the launch traced here: 99.1 us
  starting transfers between devices  29.4 us (30%)
  Pallas kernels  26.9 us (27%)
  waiting for transfers between devices  20.5 us (21%)
  other arithmetic  12.5 us (13%)
  local copies, waits for them, and re-layouts  6.91 us (7%)
  between operations  2.95 us (3%)
    pallas_call x2, Pallas kernels, solve_local_kernel(): pl.pallas_call(kernel, out_shape=[jax.ShapeDtypeStruct(s, dtype) for s in...  26.9 us
    ppermute x6, starting transfers between devices, exchange_axis(): return (lax.ppermute(last, axis, up), lax.ppermute(first, axis, down))  23.6 us
    ppermute x6, waiting for transfers between devices, exchange_axis(): return (lax.ppermute(last, axis, up), lax.ppermute(first, axis, down))  14.9 us
    ppermute x1, waiting for transfers between devices, shards(): after = lax.ppermute(top, 'gx', down)[:, :, :width]  4.15 us
    ppermute x1, starting transfers between devices, shards(): before = lax.ppermute(bottom, 'gx', up)[:, :, slab - width:]  3.56 us
    select_n x1, other arithmetic, grid_ghost(): return jnp.where(outside, ghost_cycle, values)  2.4 us
    ppermute x1, starting transfers between devices, shards(): after = lax.ppermute(top, 'gx', down)[:, :, :width]  2.27 us
  transfers between devices with their start and end apart: 8, of which 6 were waited for; matrix products, arithmetic and copies ran while one was open for 7% of the time, Pallas kernels for 0%

profile of v8, /device:TPU:6, one launch (start us, length us, event | category | flops | bytes accessed | tf_op | source)
XLA Modules:
  0.0 99.1 jit_solution(7327289577137920067)
XLA Ops:
  0.0 0.9 fusion.24
  0.9 0.1 reshape_squeeze.12
  1.0 1.0 fusion.9
  2.0 3.8 %collective-permute-start = (f32[6,64,128]{2,1,0:T(8,128)S(1)}, f32[6,64,128]{2,1,0:T(8,128)S(1)}, u32[]{:S(2)}, u32[]{:S(2)}) collective-permute-start(f32[6,64,128]{2,1,0:T(8,128)S(1)} %pad_maximum_fusion.7), channel_id=1, source_target_pairs={{0,16},{16,32},{32,48},{48,64},{64,80},{80,96},{96,112},{1,17},{17... | collective-permute-start | bytes 589832 | tf_op jit(solution)/shard_map/ppermute | solution.py:200
  5.8 0.1 reshape_squeeze.13
  5.9 0.9 fusion.8
  6.8 2.1 %collective-permute-start.1 = (f32[6,64,128]{2,1,0:T(8,128)S(1)}, f32[6,64,128]{2,1,0:T(8,128)S(1)}, u32[]{:S(2)}, u32[]{:S(2)}) collective-permute-start(f32[6,64,128]{2,1,0:T(8,128)S(1)} %fusion.8), channel_id=1, source_target_pairs={{16,0},{32,16},{48,32},{64,48},{80,64},{96,80},{112,96},{17,1},{33... | collective-permute-start | bytes 589832 | tf_op jit(solution)/shard_map/ppermute | solution.py:200
  9.0 0.7 fusion.25
  12.2 0.6 pad_add_fusion.rect_ref
  12.8 0.0 collective-permute-done
  12.9 0.1 reshape.91
  12.9 3.0 %collective-permute-done.1 = f32[6,64,128]{2,1,0:T(8,128)S(1)} collective-permute-done((f32[6,64,128]{2,1,0:T(8,128)S(1)}, f32[6,64,128]{2,1,0:T(8,128)S(1)}, u32[]{:S(2)}, u32[]{:S(2)}) %collective-permute-start.1) | collective-permute-done | bytes 196640 | tf_op jit(solution)/shard_map/ppermute | solution.py:200
  16.0 0.1 reshape.92
  16.1 0.0 copy-done
  16.1 0.0 copy-done.2
  16.2 0.2 fusion.21
  16.4 0.1 select_maximum_fusion.1
  16.5 0.2 copy.7
  16.7 1.9 %collective-permute-start.2 = (f32[6,256,64]{1,2,0:T(8,128)S(1)}, f32[6,256,64]{1,2,0:T(8,128)}, u32[]{:S(2)}, u32[]{:S(2)}) collective-permute-start(f32[6,256,64]{1,2,0:T(8,128)S(1)} %copy.7), channel_id=1, source_target_pairs={{0,1},{1,2},{2,3},{3,4},{4,5},{5,6},{6,7},{7,8},{8,9},{9,10},{10,1... | collective-permute-start | bytes 1179656 | tf_op jit(solution)/shard_map/ppermute | solution.py:200
  18.7 0.1 select_maximum_fusion
  18.7 0.2 copy.9
  19.0 7.3 %collective-permute-start.3 = (f32[6,256,64]{1,2,0:T(8,128)S(1)}, f32[6,256,64]{1,2,0:T(8,128)S(1)}, u32[]{:S(2)}, u32[]{:S(2)}) collective-permute-start(f32[6,256,64]{1,2,0:T(8,128)S(1)} %copy.9), channel_id=1, source_target_pairs={{1,0},{2,1},{3,2},{4,3},{5,4},{6,5},{7,6},{8,7},{9,8},{10,9},{11,1... | collective-permute-start | bytes 1179656 | tf_op jit(solution)/shard_map/ppermute | solution.py:200
  26.2 0.1 fusion.10
  26.3 0.1 fusion.11
  26.4 0.7 pad_maximum_fusion.5.wcol_ref
  27.1 2.4 %collective-permute-done.2 = f32[6,256,64]{1,2,0:T(8,128)} collective-permute-done((f32[6,256,64]{1,2,0:T(8,128)S(1)}, f32[6,256,64]{1,2,0:T(8,128)}, u32[]{:S(2)}, u32[]{:S(2)}) %collective-permute-start.2) | collective-permute-done | bytes 393248 | tf_op jit(solution)/shard_map/ppermute | solution.py:200
  29.6 0.8 slice.220
  30.3 0.1 copy.11
  30.4 1.0 %slice.217 = f32[5,256,64]{1,2,0:T(8,128)S(1)} slice(f32[6,256,64]{1,2,0:T(8,128)} %collective-permute-done.2), slice={[0:5], [0:256], [0:64]} | slice | bytes 655360 | tf_op jit(solution)/shard_map/slice | solution.py:426
  31.4 0.2 copy.23
  31.7 0.0 collective-permute-done.3
  31.7 0.1 copy.12
  31.8 0.2 copy.24
  32.1 0.1 fusion.12
  32.2 0.1 fusion.13
  32.2 0.7 pad_maximum_fusion.4.wrow_ref
  33.0 1.6 %pad_maximum_fusion.1.resid_ref.data_ref = f32[5,256,256]{2,1,0:T(8,128)} fusion(f32[5,256,64]{2,1,0:T(8,128)S(1)} %copy.24, f32[5,64,128]{2,1,0:T(8,128)S(1)} %slice.215, f32[1,128,128]{2,1,0:T(8,128)S(1)} %bitcast.83, f32[4,128,128]{2,1,0:T(8,128)S(1)} %bitcast.76, f32[5,64,128]{2,1,0:T(8,128)S(1)} %slice.214, f32[5,256,64]{2,1,0:T(8,128)S(1)} %copy.23), kind=kLoop, calls=%fused_computation.8 | loop fusion | flops 1638400 | bytes 2621440 | tf_op jit(solution)/shard_map/concatenate | solution.py:426
  34.6 12.4 %shard_map.64 = (f32[2,2,256,256]{3,2,1,0:T(8,128)}, f32[2,2,128,128]{3,2,1,0:T(8,128)}, f32[2,2,72,128]{3,2,1,0:T(8,128)}, f32[2,2,72,128]{3,2,1,0:T(8,128)}) custom-call(s32[4]{0:T(128)} %pad_add_fusion.rect_ref, f32[5,256,256]{2,1,0:T(8,128)} %pad_maximum_fusion.1.resid_ref.data_ref, f32[5,256,256]{2,1,0:T(8,128)} %pad_maximum_fusion.1.resid_ref.data_ref, ...), custom_call_target="tpu_custom_call" | custom-call | tf_op jit(solution)/shard_map/pallas_call | solution.py:381
  47.0 3.6 %collective-permute-start.4 = (f32[2,2,72,128]{3,2,1,0:T(8,128)}, f32[2,2,72,128]{3,2,1,0:T(8,128)S(1)}, u32[]{:S(2)}, u32[]{:S(2)}) collective-permute-start(f32[2,2,72,128]{3,2,1,0:T(8,128)} %get-tuple-element.10), channel_id=1, source_target_pairs={{0,16},{16,32},{32,48},{48,64},{64,80},{80,96},{96,112},{1,17},{17... | collective-permute-start | bytes 442376 | tf_op jit(solution)/shard_map/ppermute | solution.py:451
  50.6 2.3 %collective-permute-start.5 = (f32[2,2,72,128]{3,2,1,0:T(8,128)}, f32[2,2,72,128]{3,2,1,0:T(8,128)S(1)}, u32[]{:S(2)}, u32[]{:S(2)}) collective-permute-start(f32[2,2,72,128]{3,2,1,0:T(8,128)} %get-tuple-element.11), channel_id=1, source_target_pairs={{16,0},{32,16},{48,32},{64,48},{80,64},{96,80},{112,96},{17,1},{33... | collective-permute-start | bytes 442376 | tf_op jit(solution)/shard_map/ppermute | solution.py:452
  52.8 0.1 or_or_fusion
  53.0 0.1 pad.87.clone
  53.1 1.5 %collective-permute-done.4 = f32[2,2,72,128]{3,2,1,0:T(8,128)S(1)} collective-permute-done((f32[2,2,72,128]{3,2,1,0:T(8,128)}, f32[2,2,72,128]{3,2,1,0:T(8,128)S(1)}, u32[]{:S(2)}, u32[]{:S(2)}) %collective-permute-start.4) | collective-permute-done | bytes 147488 | tf_op jit(solution)/shard_map/ppermute | solution.py:451
  54.6 4.2 %collective-permute-done.5 = f32[2,2,72,128]{3,2,1,0:T(8,128)S(1)} collective-permute-done((f32[2,2,72,128]{3,2,1,0:T(8,128)}, f32[2,2,72,128]{3,2,1,0:T(8,128)S(1)}, u32[]{:S(2)}, u32[]{:S(2)}) %collective-permute-start.5) | collective-permute-done | bytes 147488 | tf_op jit(solution)/shard_map/ppermute | solution.py:452
  58.7 1.0 %pad_maximum_fusion.3 = f32[2,2,264,128]{3,2,1,0:T(8,128)S(1)} fusion(f32[2,2,6,128]{3,2,1,0:T(8,128)S(1)} %broadcast_in_dim.148, f32[2,2,65,128]{3,2,1,0:T(8,128)S(1)} %bitcast.77, f32[2,2,128,128]{3,2,1,0:T(8,128)} %get-tuple-element.9, f32[2,2,65,128]{3,2,1,0:T(8,128)S(1)} %slice.232), kind=kLoop, calls=%fused_computation.21 | loop fusion | flops 405504 | bytes 1081344 | tf_op jit(solution)/shard_map/concatenate | solution.py:457
  59.7 0.0 copy-start.1
  59.7 0.2 fusion.22
  59.9 0.3 copy.13
  60.2 0.3 copy.14
  60.5 6.4 %collective-permute-start.7 = (f32[2,2,264,65]{2,1,3,0:T(2,128)S(1)}, f32[2,2,264,65]{2,1,3,0:T(2,128)S(1)}, u32[]{:S(2)}, u32[]{:S(2)}) collective-permute-start(f32[2,2,264,65]{2,1,3,0:T(2,128)S(1)} %copy.14), channel_id=1, source_target_pairs={{1,0},{2,1},{3,2},{4,3},{5,4},{6,5},{7,6},{8,7},{9,8},{10,9},{11,1... | collective-permute-start | bytes 823688 | tf_op jit(solution)/shard_map/ppermute | solution.py:200
  67.0 2.1 %collective-permute-start.6 = (f32[2,2,264,65]{2,1,3,0:T(2,128)S(1)}, f32[2,2,264,65]{2,1,3,0:T(2,128)S(1)}, u32[]{:S(2)}, u32[]{:S(2)}) collective-permute-start(f32[2,2,264,65]{2,1,3,0:T(2,128)S(1)} %copy.13), channel_id=1, source_target_pairs={{0,1},{1,2},{2,3},{3,4},{4,5},{5,6},{6,7},{7,8},{8,9},{9,10},{10,1... | collective-permute-start | bytes 823688 | tf_op jit(solution)/shard_map/ppermute | solution.py:200
  69.1 0.2 slice_reduce_fusion.3
  69.3 0.8 fusion.7
  70.1 2.2 %collective-permute-done.7 = f32[2,2,264,65]{2,1,3,0:T(2,128)S(1)} collective-permute-done((f32[2,2,264,65]{2,1,3,0:T(2,128)S(1)}, f32[2,2,264,65]{2,1,3,0:T(2,128)S(1)}, u32[]{:S(2)}, u32[]{:S(2)}) %collective-permute-start.7) | collective-permute-done | bytes 274592 | tf_op jit(solution)/shard_map/ppermute | solution.py:200
  72.3 0.3 copy.16
  72.6 7.2 %collective-permute-done.6 = f32[2,2,264,65]{2,1,3,0:T(2,128)S(1)} collective-permute-done((f32[2,2,264,65]{2,1,3,0:T(2,128)S(1)}, f32[2,2,264,65]{2,1,3,0:T(2,128)S(1)}, u32[]{:S(2)}, u32[]{:S(2)}) %collective-permute-start.6) | collective-permute-done | bytes 274592 | tf_op jit(solution)/shard_map/ppermute | solution.py:200
  79.8 0.3 copy.15
  80.0 0.7 maximum_maximum_fusion
  80.8 0.0 copy-start.5
  80.8 1.0 %select_select_fusion = f32[2,2,264,384]{3,2,1,0:T(8,128)S(1)} fusion(f32[2,2,384]{2,1,0:T(2,128)S(1)} %bitcast.88, f32[2,2,384]{2,1,0:T(2,128)S(1)} %bitcast.89, f32[2,2,264]{2,1,0:T(2,128)S(1)} %get-tuple-element.16, f32[2,2,264]{2,1,0:T(2,128)S(1)} %get-tuple-element.15, pred[264]{0:T(512)(128)(4,1)S(1)} %get-tuple-element.62, ...), kind=kLoop, calls=%fused_computation.7 | loop fusion | flops 4055040 | bytes 2735376 | tf_op jit(solution)/shard_map/jit(_where)/select_n | solution.py:84
  81.9 0.2 multiply_add_fusion
  82.1 0.1 pad_maximum_fusion
  82.2 2.4 %fusion.3.resid_ref = f32[4,264,384]{2,1,0:T(8,128)} fusion(f32[4,264,65]{2,1,0:T(8,128)S(1)} %bitcast.71, f32[4,264,128]{2,1,0:T(8,128)S(1)} %bitcast.70, f32[4,264,65]{2,1,0:T(8,128)S(1)} %bitcast.72, f32[2,2,264,384]{3,2,1,0:T(8,128)S(1)} %pad_maximum_fusion, f32[384]{0:T(512)S(1)} %pad.87.clone, f32[4,384]{1,0:T(4,128)S(1)} %broadcast_in_dim.175, ...), kind=kLoop, calls=%fused_computation.6 | loop fusion | flops 3244032 | bytes 4458768 | tf_op jit(solution)/shard_map/jit(_where)/select_n | solution.py:92
  84.6 14.5 %shard_map.65 = f32[2,2,128,128]{3,2,1,0:T(8,128)} custom-call(s32[4]{0:T(128)} %pad_add_fusion.rect_ref, f32[4,264,384]{2,1,0:T(8,128)} %fusion.3.resid_ref, f32[5,256,256]{2,1,0:T(8,128)} %pad_maximum_fusion.1.resid_ref.data_ref, f32[2,256,128]{2,1,0:T(8,128)} %pad_maximum_fusion.4.wrow_ref, f32[2,256,128]{2,1,0:T(8,128)} %pad_maximum_fusion.5.wcol_ref, ...), custom_call_target="tpu_custom_call" | custom-call | tf_op jit(solution)/shard_map/pallas_call | solution.py:381
  (37 shorter events, 0.4 us)
Async XLA Ops:
  0.0 16.0 %copy-start.3 = (f32[2,2,64,64]{3,2,1,0:T(8,128)S(1)}, f32[2,2,64,64]{3,2,1,0:T(8,128)}, u32[]{:S(2)}) copy-start(f32[2,2,64,64]{3,2,1,0:T(8,128)} %param.9) | copy-start | bytes 196612
  0.0 8.9 %copy-start.6 = (s32[1,1,4]{2,1,0:T(1,128)S(1)}, s32[1,1,4]{2,1,0:T(1,128)}, u32[]{:S(2)}) copy-start(s32[1,1,4]{2,1,0:T(1,128)} %param.10) | copy-start | bytes 52
  0.0 12.8 %copy-start.4 = (f32[2,2,64,64]{3,2,1,0:T(8,128)S(1)}, f32[2,2,64,64]{3,2,1,0:T(8,128)}, u32[]{:S(2)}) copy-start(f32[2,2,64,64]{3,2,1,0:T(8,128)} %param.8) | copy-start | bytes 196612
  1.0 15.1 %copy-start = (f32[2,2,128,128]{3,2,1,0:T(8,128)S(1)}, f32[2,2,128,128]{3,2,1,0:T(8,128)}, u32[]{:S(2)}) copy-start(f32[2,2,128,128]{3,2,1,0:T(8,128)} %param.6) | copy-start | bytes 786436
  1.0 15.1 %copy-start.2 = (f32[128,128]{1,0:T(8,128)S(1)}, f32[128,128]{1,0:T(8,128)}, u32[]{:S(2)}) copy-start(f32[128,128]{1,0:T(8,128)} %param.7) | copy-start | bytes 196612
  2.0 10.8 %collective-permute-start = (f32[6,64,128]{2,1,0:T(8,128)S(1)}, f32[6,64,128]{2,1,0:T(8,128)S(1)}, u32[]{:S(2)}, u32[]{:S(2)}) collective-permute-start(f32[6,64,128]{2,1,0:T(8,128)S(1)} %pad_maximum_fusion.7), channel_id=1, source_target_pairs={{0,16},{16,32},{32,48},{48,64},{64,80},{80,96},{96,112},{1,17},{17... | collective-permute-start | bytes 589832 | tf_op jit(solution)/shard_map/ppermute | solution.py:200
  6.8 9.2 %collective-permute-start.1 = (f32[6,64,128]{2,1,0:T(8,128)S(1)}, f32[6,64,128]{2,1,0:T(8,128)S(1)}, u32[]{:S(2)}, u32[]{:S(2)}) collective-permute-start(f32[6,64,128]{2,1,0:T(8,128)S(1)} %fusion.8), channel_id=1, source_target_pairs={{16,0},{32,16},{48,32},{64,48},{80,64},{96,80},{112,96},{17,1},{33... | collective-permute-start | bytes 589832 | tf_op jit(solution)/shard_map/ppermute | solution.py:200
  16.7 12.8 %collective-permute-start.2 = (f32[6,256,64]{1,2,0:T(8,128)S(1)}, f32[6,256,64]{1,2,0:T(8,128)}, u32[]{:S(2)}, u32[]{:S(2)}) collective-permute-start(f32[6,256,64]{1,2,0:T(8,128)S(1)} %copy.7), channel_id=1, source_target_pairs={{0,1},{1,2},{2,3},{3,4},{4,5},{5,6},{6,7},{7,8},{8,9},{9,10},{10,1... | collective-permute-start | bytes 1179656 | tf_op jit(solution)/shard_map/ppermute | solution.py:200
  19.0 12.7 %collective-permute-start.3 = (f32[6,256,64]{1,2,0:T(8,128)S(1)}, f32[6,256,64]{1,2,0:T(8,128)S(1)}, u32[]{:S(2)}, u32[]{:S(2)}) collective-permute-start(f32[6,256,64]{1,2,0:T(8,128)S(1)} %copy.9), channel_id=1, source_target_pairs={{1,0},{2,1},{3,2},{4,3},{5,4},{6,5},{7,6},{8,7},{9,8},{10,9},{11,1... | collective-permute-start | bytes 1179656 | tf_op jit(solution)/shard_map/ppermute | solution.py:200
  47.0 7.5 %collective-permute-start.4 = (f32[2,2,72,128]{3,2,1,0:T(8,128)}, f32[2,2,72,128]{3,2,1,0:T(8,128)S(1)}, u32[]{:S(2)}, u32[]{:S(2)}) collective-permute-start(f32[2,2,72,128]{3,2,1,0:T(8,128)} %get-tuple-element.10), channel_id=1, source_target_pairs={{0,16},{16,32},{32,48},{48,64},{64,80},{80,96},{96,112},{1,17},{17... | collective-permute-start | bytes 442376 | tf_op jit(solution)/shard_map/ppermute | solution.py:451
  50.6 8.1 %collective-permute-start.5 = (f32[2,2,72,128]{3,2,1,0:T(8,128)}, f32[2,2,72,128]{3,2,1,0:T(8,128)S(1)}, u32[]{:S(2)}, u32[]{:S(2)}) collective-permute-start(f32[2,2,72,128]{3,2,1,0:T(8,128)} %get-tuple-element.11), channel_id=1, source_target_pairs={{16,0},{32,16},{48,32},{64,48},{80,64},{96,80},{112,96},{17,1},{33... | collective-permute-start | bytes 442376 | tf_op jit(solution)/shard_map/ppermute | solution.py:452
  59.7 9.4 %copy-start.1 = (f32[2,2,128,128]{3,2,1,0:T(8,128)S(1)}, f32[2,2,128,128]{3,2,1,0:T(8,128)}, u32[]{:S(2)}) copy-start(f32[2,2,128,128]{3,2,1,0:T(8,128)} %get-tuple-element.9) | copy-start | bytes 786436
  60.5 11.8 %collective-permute-start.7 = (f32[2,2,264,65]{2,1,3,0:T(2,128)S(1)}, f32[2,2,264,65]{2,1,3,0:T(2,128)S(1)}, u32[]{:S(2)}, u32[]{:S(2)}) collective-permute-start(f32[2,2,264,65]{2,1,3,0:T(2,128)S(1)} %copy.14), channel_id=1, source_target_pairs={{1,0},{2,1},{3,2},{4,3},{5,4},{6,5},{7,6},{8,7},{9,8},{10,9},{11,1... | collective-permute-start | bytes 823688 | tf_op jit(solution)/shard_map/ppermute | solution.py:200
  67.0 12.8 %collective-permute-start.6 = (f32[2,2,264,65]{2,1,3,0:T(2,128)S(1)}, f32[2,2,264,65]{2,1,3,0:T(2,128)S(1)}, u32[]{:S(2)}, u32[]{:S(2)}) collective-permute-start(f32[2,2,264,65]{2,1,3,0:T(2,128)S(1)} %copy.13), channel_id=1, source_target_pairs={{0,1},{1,2},{2,3},{3,4},{4,5},{5,6},{6,7},{7,8},{8,9},{9,10},{10,1... | collective-permute-start | bytes 823688 | tf_op jit(solution)/shard_map/ppermute | solution.py:200
  80.8 1.1 %copy-start.5 = (f32[2]{0:T(128)S(1)}, f32[2]{0:T(128)}, u32[]{:S(2)}) copy-start(f32[2]{0:T(128)} %constant.75) | copy-start | bytes 28

commit v9 on v8

--- a/solution.py
+++ b/solution.py
@@ -409,23 +409,40 @@
         block - left_w,
         block + own_cols + right_w,
     )
-    stacked = jnp.concatenate([sources.reshape(4, own_rows, own_cols), wavenumber[None]], axis=0)
-    lead = stacked.shape[0]
+    planes = [sources.reshape(4, own_rows, own_cols), wavenumber[None]]
+    lead = 5
     col_pair = col_inverse.shape[0]
     row_pair = row_inverse.shape[0]
     inv_rows = col_inverse.shape[1] * block * block // own_cols
-    before, after = exchange_axis(
-        stacked, "gx", 1, block,
-        col_inverse[col_pair - 1].reshape(1, inv_rows, own_cols), col_inverse[0].reshape(1, inv_rows, own_cols),
-    )
-    tall = jnp.concatenate([before[:lead, :block], stacked, after[:lead, :block]], axis=1)
+    peers_x, peers_y = (lax.axis_size("gx"), lax.axis_size("gy"))
+    up_x = [(i, i + 1) for i in range(peers_x - 1)]
+    up_y = [(i, i + 1) for i in range(peers_y - 1)]
+    last_rows = jnp.concatenate(
+        [p[:, own_rows - block :] for p in planes] + [col_inverse[col_pair - 1].reshape(1, inv_rows, own_cols)], axis=0
+    )
+    first_rows = jnp.concatenate(
+        [p[:, :block] for p in planes] + [col_inverse[0].reshape(1, inv_rows, own_cols)], axis=0
+    )
+    before = lax.ppermute(last_rows, "gx", up_x)
+    after = lax.ppermute(first_rows, "gx", [(j, i) for i, j in up_x])
+    column_parts = [before[:lead]] + [jnp.concatenate(planes, axis=0)] + [after[:lead]]
+    ext_rows = own_rows + 2 * block
+
     def inv_slab(mats):
         flat = mats.reshape(1, -1, block)
-        return jnp.pad(flat, ((0, 0), (0, tall.shape[1] - flat.shape[1]), (0, 0)))
-    left, right = exchange_axis(tall, "gy", 2, block, inv_slab(row_inverse[row_pair - 1]), inv_slab(row_inverse[0]))
+        return jnp.pad(flat, ((0, 0), (0, ext_rows - flat.shape[1]), (0, 0)))
+
+    last_cols = jnp.concatenate(
+        [jnp.concatenate([p[:, :, own_cols - block :] for p in column_parts], axis=1), inv_slab(row_inverse[row_pair - 1])],
+        axis=0,
+    )
+    first_cols = jnp.concatenate(
+        [jnp.concatenate([p[:, :, :block] for p in column_parts], axis=1), inv_slab(row_inverse[0])], axis=0
+    )
+    left = lax.ppermute(last_cols, "gy", up_y)
+    right = lax.ppermute(first_cols, "gy", [(j, i) for i, j in up_y])
+    tall = jnp.concatenate(column_parts, axis=1)
     stacked_ext = jnp.concatenate([left[:lead], tall, right[:lead]], axis=2)
-    sources_ext = stacked_ext[:4].reshape(2, 2, own_rows + 2 * block, own_cols + 2 * block)
-    wave_ext = stacked_ext[4]
     inv_shape = (1,) + row_inverse.shape[1:]
     inv_size = row_inverse.shape[1] * block * block // block
     col_blocks = jnp.concatenate(

time: 99.6 us -> 101 us (1.014)
  local copies, waits for them, and re-layouts: 6.91 us -> 10.4 us
  waiting for transfers between devices: 20.5 us -> 17.8 us
  starting transfers between devices: 29.4 us -> 31.7 us
  other arithmetic: 12.5 us -> 10.8 us
    ppermute x0 -> x4, starting transfers between devices: none -> 15.9 us  [the longest x1 7.26 us: shards(): right = lax.ppermute(first_cols, 'gy', [(j, i) for i, j in up_y])]
    ppermute x6 -> x2, starting transfers between devices: 23.6 us -> 8.59 us  [exchange_axis(): return (lax.ppermute(last, axis, up), lax.ppermute(first, axis, down))]
    ppermute x6 -> x2, waiting for transfers between devices: 14.9 us -> 9.41 us  [exchange_axis(): return (lax.ppermute(last, axis, up), lax.ppermute(first, axis, down))]
    ppermute x0 -> x4, waiting for transfers between devices: none -> 2.43 us  [the longest x1 2.4 us: shards(): left = lax.ppermute(last_cols, 'gy', up_y)]
    slice x2 -> x8, local copies, waits for them, and re-layouts: 0.03 us -> 2.04 us  [the longest x2 1.83 us: shards(): p[:, own_rows - block:]]
    concatenate x6 -> x5, other arithmetic: 2.1 us -> 0.28 us  [the longest x1 0.14 us: shards(): jnp.concatenate(planes, axis=0)]
    ppermute x1, starting transfers between devices: 3.56 us -> 5.27 us  [shards(): before = lax.ppermute(bottom, 'gx', up)[:, :, slab - width:]]
  transfers between devices with their start and end apart: 8 -> 8, of which waited for: 6 -> 5; matrix products, arithmetic and copies ran while one was open for 7% -> 6% of each run, Pallas kernels for 0% -> 0%
where the time goes in v9:
time: 101 us
  starting transfers between devices  31.7 us (31%)
  Pallas kernels  26.9 us (27%)
  waiting for transfers between devices  17.8 us (18%)
  other arithmetic  10.8 us (11%)
  local copies, waits for them, and re-layouts  10.4 us (10%)
  between operations  2.99 us (3%)
    pallas_call x2, Pallas kernels, solve_local_kernel(): pl.pallas_call(kernel, out_shape=[jax.ShapeDtypeStruct(s, dtype) for s in...  26.9 us
    ppermute x2, waiting for transfers between devices, exchange_axis(): return (lax.ppermute(last, axis, up), lax.ppermute(first, axis, down))  9.41 us
    ppermute x2, starting transfers between devices, exchange_axis(): return (lax.ppermute(last, axis, up), lax.ppermute(first, axis, down))  8.59 us
    ppermute x1, starting transfers between devices, shards(): right = lax.ppermute(first_cols, 'gy', [(j, i) for i, j in up_y])  7.26 us
    ppermute x1, starting transfers between devices, shards(): before = lax.ppermute(bottom, 'gx', up)[:, :, slab - width:]  5.27 us
    ppermute x1, waiting for transfers between devices, shards(): after = lax.ppermute(top, 'gx', down)[:, :, :width]  4.17 us
    ppermute x1, starting transfers between devices, shards(): before = lax.ppermute(last_rows, 'gx', up_x)  4 us
    ppermute x1, starting transfers between devices, shards(): after = lax.ppermute(first_rows, 'gx', [(j, i) for i, j in up_x])  2.74 us
  transfers between devices with their start and end apart: 8, of which 5 were waited for; matrix products, arithmetic and copies ran while one was open for 6% of the time, Pallas kernels for 0%

profile of v9, /device:TPU:6, one launch (start us, length us, event | category | flops | bytes accessed | tf_op | source)
XLA Modules:
  0.0 100.7 jit_solution(4382106588979026235)
XLA Ops:
  0.0 0.8 fusion.27
  0.9 0.9 fusion.26
  1.8 0.1 reshape_squeeze.13
  1.8 1.0 fusion.22
  2.8 2.7 %collective-permute-start.1 = (f32[6,64,128]{2,1,0:T(8,128)S(1)}, f32[6,64,128]{2,1,0:T(8,128)S(1)}, u32[]{:S(2)}, u32[]{:S(2)}) collective-permute-start(f32[6,64,128]{2,1,0:T(8,128)S(1)} %pad_maximum_fusion.7), channel_id=1, source_target_pairs={{16,0},{32,16},{48,32},{64,48},{80,64},{96,80},{112,96},{17,1},{33... | collective-permute-start | bytes 589832 | tf_op jit(solution)/shard_map/ppermute | solution.py:427
  5.6 0.1 reshape_squeeze.12
  5.7 4.0 %collective-permute-start = (f32[6,64,128]{2,1,0:T(8,128)S(1)}, f32[6,64,128]{2,1,0:T(8,128)S(1)}, u32[]{:S(2)}, u32[]{:S(2)}) collective-permute-start(f32[6,64,128]{2,1,0:T(8,128)S(1)} %pad_maximum_fusion.6), channel_id=1, source_target_pairs={{0,16},{16,32},{32,48},{48,64},{64,80},{80,96},{96,112},{1,17},{17... | collective-permute-start | bytes 589832 | tf_op jit(solution)/shard_map/ppermute | solution.py:426
  9.7 0.1 slice_maximum_fusion
  9.9 0.7 fusion.28
  13.1 0.6 pad_add_fusion.rect_ref
  13.8 0.0 copy-start.2
  13.8 0.1 reshape.92
  13.9 0.0 collective-permute-done
  13.9 0.1 reshape.91
  14.0 0.1 fusion.24
  14.1 0.1 fusion.23
  14.3 0.1 select_maximum_fusion.1
  14.3 0.2 copy.7
  14.6 1.9 %collective-permute-start.2 = (f32[6,256,64]{1,2,0:T(8,128)S(1)}, f32[6,256,64]{1,2,0:T(8,128)}, u32[]{:S(2)}, u32[]{:S(2)}) collective-permute-start(f32[6,256,64]{1,2,0:T(8,128)S(1)} %copy.7), channel_id=1, source_target_pairs={{0,1},{1,2},{2,3},{3,4},{4,5},{5,6},{6,7},{7,8},{8,9},{9,10},{10,1... | collective-permute-start | bytes 1179656 | tf_op jit(solution)/shard_map/ppermute | solution.py:442
  16.5 0.1 select_maximum_fusion
  16.6 0.2 copy.9
  16.8 7.3 %collective-permute-start.3 = (f32[6,256,64]{1,2,0:T(8,128)S(1)}, f32[6,256,64]{1,2,0:T(8,128)}, u32[]{:S(2)}, u32[]{:S(2)}) collective-permute-start(f32[6,256,64]{1,2,0:T(8,128)S(1)} %copy.9), channel_id=1, source_target_pairs={{1,0},{2,1},{3,2},{4,3},{5,4},{6,5},{7,6},{8,7},{9,8},{10,9},{11,1... | collective-permute-start | bytes 1179656 | tf_op jit(solution)/shard_map/ppermute | solution.py:443
  24.1 0.1 fusion.10
  24.2 0.1 fusion.11
  24.3 0.7 pad_maximum_fusion.5.wcol_ref
  25.0 2.4 %collective-permute-done.2 = f32[6,256,64]{1,2,0:T(8,128)} collective-permute-done((f32[6,256,64]{1,2,0:T(8,128)S(1)}, f32[6,256,64]{1,2,0:T(8,128)}, u32[]{:S(2)}, u32[]{:S(2)}) %collective-permute-start.2) | collective-permute-done | bytes 393248 | tf_op jit(solution)/shard_map/ppermute | solution.py:442
  27.4 0.8 slice.254
  28.1 0.1 copy.11
  28.2 1.0 slice.248
  29.2 0.2 copy.23
  29.5 0.8 slice.257
  30.3 0.1 copy.12
  30.5 1.0 slice.253
  31.5 0.2 copy.24
  31.7 0.1 fusion.12
  31.8 0.1 fusion.13
  31.9 0.7 pad_maximum_fusion.4.wrow_ref
  32.6 1.7 %pad_maximum_fusion.1.resid_ref.data_ref = f32[5,256,256]{2,1,0:T(8,128)} fusion(f32[5,256,64]{2,1,0:T(8,128)S(1)} %copy.24, f32[5,64,128]{2,1,0:T(8,128)S(1)} %slice-done, f32[1,128,128]{2,1,0:T(8,128)S(1)} %bitcast.83, f32[4,128,128]{2,1,0:T(8,128)S(1)} %bitcast.76, f32[5,64,128]{2,1,0:T(8,128)S(1)} %slice-done.1, f32[5,256,64]{2,1,0:T(8,128)S(1)} %copy.23), kind=kLoop, calls=%fused_computation.8 | loop fusion | flops 1638400 | bytes 2621440 | tf_op jit(solution)/shard_map/concatenate | solution.py:445
  34.3 12.5 %shard_map.64 = (f32[2,2,256,256]{3,2,1,0:T(8,128)}, f32[2,2,128,128]{3,2,1,0:T(8,128)}, f32[2,2,72,128]{3,2,1,0:T(8,128)}, f32[2,2,72,128]{3,2,1,0:T(8,128)}) custom-call(s32[4]{0:T(128)} %pad_add_fusion.rect_ref, f32[5,256,256]{2,1,0:T(8,128)} %pad_maximum_fusion.1.resid_ref.data_ref, f32[5,256,256]{2,1,0:T(8,128)} %pad_maximum_fusion.1.resid_ref.data_ref, ...), custom_call_target="tpu_custom_call" | custom-call | tf_op jit(solution)/shard_map/pallas_call | solution.py:381
  46.7 5.3 %collective-permute-start.4 = (f32[2,2,72,128]{3,2,1,0:T(8,128)}, f32[2,2,72,128]{3,2,1,0:T(8,128)S(1)}, u32[]{:S(2)}, u32[]{:S(2)}) collective-permute-start(f32[2,2,72,128]{3,2,1,0:T(8,128)} %get-tuple-element.10), channel_id=1, source_target_pairs={{0,16},{16,32},{32,48},{48,64},{64,80},{80,96},{96,112},{1,17},{17... | collective-permute-start | bytes 442376 | tf_op jit(solution)/shard_map/ppermute | solution.py:468
  52.0 1.9 %collective-permute-start.5 = (f32[2,2,72,128]{3,2,1,0:T(8,128)}, f32[2,2,72,128]{3,2,1,0:T(8,128)S(1)}, u32[]{:S(2)}, u32[]{:S(2)}) collective-permute-start(f32[2,2,72,128]{3,2,1,0:T(8,128)} %get-tuple-element.11), channel_id=1, source_target_pairs={{16,0},{32,16},{48,32},{64,48},{80,64},{96,80},{112,96},{17,1},{33... | collective-permute-start | bytes 442376 | tf_op jit(solution)/shard_map/ppermute | solution.py:469
  53.9 0.1 or_or_fusion
  54.1 0.1 pad.87.clone
  54.2 1.8 %collective-permute-done.4 = f32[2,2,72,128]{3,2,1,0:T(8,128)S(1)} collective-permute-done((f32[2,2,72,128]{3,2,1,0:T(8,128)}, f32[2,2,72,128]{3,2,1,0:T(8,128)S(1)}, u32[]{:S(2)}, u32[]{:S(2)}) %collective-permute-start.4) | collective-permute-done | bytes 147488 | tf_op jit(solution)/shard_map/ppermute | solution.py:468
  56.0 4.2 %collective-permute-done.5 = f32[2,2,72,128]{3,2,1,0:T(8,128)S(1)} collective-permute-done((f32[2,2,72,128]{3,2,1,0:T(8,128)}, f32[2,2,72,128]{3,2,1,0:T(8,128)S(1)}, u32[]{:S(2)}, u32[]{:S(2)}) %collective-permute-start.5) | collective-permute-done | bytes 147488 | tf_op jit(solution)/shard_map/ppermute | solution.py:469
  60.2 1.0 pad_maximum_fusion.3
  61.2 0.2 fusion.21
  61.4 0.3 copy.13
  61.7 0.3 copy.14
  62.0 6.5 %collective-permute-start.7 = (f32[2,2,264,65]{2,1,3,0:T(2,128)S(1)}, f32[2,2,264,65]{2,1,3,0:T(2,128)S(1)}, u32[]{:S(2)}, u32[]{:S(2)}) collective-permute-start(f32[2,2,264,65]{2,1,3,0:T(2,128)S(1)} %copy.14), channel_id=1, source_target_pairs={{1,0},{2,1},{3,2},{4,3},{5,4},{6,5},{7,6},{8,7},{9,8},{10,9},{11,1... | collective-permute-start | bytes 823688 | tf_op jit(solution)/shard_map/ppermute | solution.py:200
  68.5 2.1 %collective-permute-start.6 = (f32[2,2,264,65]{2,1,3,0:T(2,128)S(1)}, f32[2,2,264,65]{2,1,3,0:T(2,128)S(1)}, u32[]{:S(2)}, u32[]{:S(2)}) collective-permute-start(f32[2,2,264,65]{2,1,3,0:T(2,128)S(1)} %copy.13), channel_id=1, source_target_pairs={{0,1},{1,2},{2,3},{3,4},{4,5},{5,6},{6,7},{7,8},{8,9},{9,10},{10,1... | collective-permute-start | bytes 823688 | tf_op jit(solution)/shard_map/ppermute | solution.py:200
  70.6 0.2 slice_reduce_fusion.3
  70.8 0.8 fusion.9
  71.6 2.2 %collective-permute-done.7 = f32[2,2,264,65]{2,1,3,0:T(2,128)S(1)} collective-permute-done((f32[2,2,264,65]{2,1,3,0:T(2,128)S(1)}, f32[2,2,264,65]{2,1,3,0:T(2,128)S(1)}, u32[]{:S(2)}, u32[]{:S(2)}) %collective-permute-start.7) | collective-permute-done | bytes 274592 | tf_op jit(solution)/shard_map/ppermute | solution.py:200
  73.8 0.3 copy.16
  74.1 7.2 %collective-permute-done.6 = f32[2,2,264,65]{2,1,3,0:T(2,128)S(1)} collective-permute-done((f32[2,2,264,65]{2,1,3,0:T(2,128)S(1)}, f32[2,2,264,65]{2,1,3,0:T(2,128)S(1)}, u32[]{:S(2)}, u32[]{:S(2)}) %collective-permute-start.6) | collective-permute-done | bytes 274592 | tf_op jit(solution)/shard_map/ppermute | solution.py:200
  81.3 0.3 copy.15
  81.5 0.7 maximum_maximum_fusion
  82.3 0.0 copy-start.7
  82.3 1.0 %select_select_fusion = f32[2,2,264,384]{3,2,1,0:T(8,128)S(1)} fusion(f32[2,2,384]{2,1,0:T(2,128)S(1)} %bitcast.88, f32[2,2,384]{2,1,0:T(2,128)S(1)} %bitcast.89, f32[2,2,264]{2,1,0:T(2,128)S(1)} %get-tuple-element.16, f32[2,2,264]{2,1,0:T(2,128)S(1)} %get-tuple-element.15, pred[264]{0:T(512)(128)(4,1)S(1)} %get-tuple-element.68, ...), kind=kLoop, calls=%fused_computation.7 | loop fusion | flops 4055040 | bytes 2735376 | tf_op jit(solution)/shard_map/jit(_where)/select_n | solution.py:84
  83.4 0.2 multiply_add_fusion
  83.6 0.1 pad_maximum_fusion
  83.7 2.5 %fusion.3.resid_ref = f32[4,264,384]{2,1,0:T(8,128)} fusion(f32[4,264,65]{2,1,0:T(8,128)S(1)} %bitcast.71, f32[4,264,128]{2,1,0:T(8,128)S(1)} %bitcast.70, f32[4,264,65]{2,1,0:T(8,128)S(1)} %bitcast.72, f32[2,2,264,384]{3,2,1,0:T(8,128)S(1)} %pad_maximum_fusion, f32[384]{0:T(512)S(1)} %pad.87.clone, f32[4,384]{1,0:T(4,128)S(1)} %broadcast_in_dim.175, ...), kind=kLoop, calls=%fused_computation.6 | loop fusion | flops 3244032 | bytes 4458768 | tf_op jit(solution)/shard_map/jit(_where)/select_n | solution.py:92
  86.2 14.5 %shard_map.65 = f32[2,2,128,128]{3,2,1,0:T(8,128)} custom-call(s32[4]{0:T(128)} %pad_add_fusion.rect_ref, f32[4,264,384]{2,1,0:T(8,128)} %fusion.3.resid_ref, f32[5,256,256]{2,1,0:T(8,128)} %pad_maximum_fusion.1.resid_ref.data_ref, f32[2,256,128]{2,1,0:T(8,128)} %pad_maximum_fusion.4.wrow_ref, f32[2,256,128]{2,1,0:T(8,128)} %pad_maximum_fusion.5.wcol_ref, ...), custom_call_target="tpu_custom_call" | custom-call | tf_op jit(solution)/shard_map/pallas_call | solution.py:381
  (45 shorter events, 0.3 us)
Async XLA Ops:
  0.0 9.7 %copy-start.4 = (f32[128,128]{1,0:T(8,128)S(1)}, f32[128,128]{1,0:T(8,128)}, u32[]{:S(2)}) copy-start(f32[128,128]{1,0:T(8,128)} %param.7) | copy-start | bytes 196612
  0.0 13.9 %copy-start.5 = (f32[2,2,64,64]{3,2,1,0:T(8,128)S(1)}, f32[2,2,64,64]{3,2,1,0:T(8,128)}, u32[]{:S(2)}) copy-start(f32[2,2,64,64]{3,2,1,0:T(8,128)} %param.9) | copy-start | bytes 196612
  0.0 9.7 %copy-start = (f32[2,2,128,128]{3,2,1,0:T(8,128)S(1)}, f32[2,2,128,128]{3,2,1,0:T(8,128)}, u32[]{:S(2)}) copy-start(f32[2,2,128,128]{3,2,1,0:T(8,128)} %param.6) | copy-start | bytes 786436
  0.0 9.9 %copy-start.8 = (s32[1,1,4]{2,1,0:T(1,128)S(1)}, s32[1,1,4]{2,1,0:T(1,128)}, u32[]{:S(2)}) copy-start(s32[1,1,4]{2,1,0:T(1,128)} %param.10) | copy-start | bytes 52
  0.0 13.7 %copy-start.6 = (f32[2,2,64,64]{3,2,1,0:T(8,128)S(1)}, f32[2,2,64,64]{3,2,1,0:T(8,128)}, u32[]{:S(2)}) copy-start(f32[2,2,64,64]{3,2,1,0:T(8,128)} %param.8) | copy-start | bytes 196612
  2.8 10.9 %collective-permute-start.1 = (f32[6,64,128]{2,1,0:T(8,128)S(1)}, f32[6,64,128]{2,1,0:T(8,128)S(1)}, u32[]{:S(2)}, u32[]{:S(2)}) collective-permute-start(f32[6,64,128]{2,1,0:T(8,128)S(1)} %pad_maximum_fusion.7), channel_id=1, source_target_pairs={{16,0},{32,16},{48,32},{64,48},{80,64},{96,80},{112,96},{17,1},{33... | collective-permute-start | bytes 589832 | tf_op jit(solution)/shard_map/ppermute | solution.py:427
  5.7 8.3 %collective-permute-start = (f32[6,64,128]{2,1,0:T(8,128)S(1)}, f32[6,64,128]{2,1,0:T(8,128)S(1)}, u32[]{:S(2)}, u32[]{:S(2)}) collective-permute-start(f32[6,64,128]{2,1,0:T(8,128)S(1)} %pad_maximum_fusion.6), channel_id=1, source_target_pairs={{0,16},{16,32},{32,48},{48,64},{64,80},{80,96},{96,112},{1,17},{17... | collective-permute-start | bytes 589832 | tf_op jit(solution)/shard_map/ppermute | solution.py:426
  13.8 10.5 %copy-start.2 = (f32[6,64,128]{2,1,0:T(8,128)}, f32[6,64,128]{2,1,0:T(8,128)S(1)}, u32[]{:S(2)}) copy-start(f32[6,64,128]{2,1,0:T(8,128)S(1)} %collective-permute-done.1) | copy-start | bytes 589828
  13.9 10.3 %copy-start.3 = (f32[6,64,128]{2,1,0:T(8,128)}, f32[6,64,128]{2,1,0:T(8,128)S(1)}, u32[]{:S(2)}) copy-start(f32[6,64,128]{2,1,0:T(8,128)S(1)} %collective-permute-done) | copy-start | bytes 589828
  14.6 12.8 %collective-permute-start.2 = (f32[6,256,64]{1,2,0:T(8,128)S(1)}, f32[6,256,64]{1,2,0:T(8,128)}, u32[]{:S(2)}, u32[]{:S(2)}) collective-permute-start(f32[6,256,64]{1,2,0:T(8,128)S(1)} %copy.7), channel_id=1, source_target_pairs={{0,1},{1,2},{2,3},{3,4},{4,5},{5,6},{6,7},{7,8},{8,9},{9,10},{10,1... | collective-permute-start | bytes 1179656 | tf_op jit(solution)/shard_map/ppermute | solution.py:442
  16.8 12.7 %collective-permute-start.3 = (f32[6,256,64]{1,2,0:T(8,128)S(1)}, f32[6,256,64]{1,2,0:T(8,128)}, u32[]{:S(2)}, u32[]{:S(2)}) collective-permute-start(f32[6,256,64]{1,2,0:T(8,128)S(1)} %copy.9), channel_id=1, source_target_pairs={{1,0},{2,1},{3,2},{4,3},{5,4},{6,5},{7,6},{8,7},{9,8},{10,9},{11,1... | collective-permute-start | bytes 1179656 | tf_op jit(solution)/shard_map/ppermute | solution.py:443
  29.5 3.1 %slice-start = ((f32[6,64,128]{2,1,0:T(8,128)}), f32[5,64,128]{2,1,0:T(8,128)S(1)}, s32[]{:S(2)}) async-start(f32[6,64,128]{2,1,0:T(8,128)} %copy-done.2), calls=%async_computation | async-start | bytes 327680 | tf_op jit(solution)/shard_map/slice | solution.py:428
  29.5 3.1 %slice-start.1 = ((f32[6,64,128]{2,1,0:T(8,128)}), f32[5,64,128]{2,1,0:T(8,128)S(1)}, s32[]{:S(2)}) async-start(f32[6,64,128]{2,1,0:T(8,128)} %copy-done.3), calls=%async_computation.1 | async-start | bytes 327680 | tf_op jit(solution)/shard_map/slice | solution.py:428
  46.7 9.2 %collective-permute-start.4 = (f32[2,2,72,128]{3,2,1,0:T(8,128)}, f32[2,2,72,128]{3,2,1,0:T(8,128)S(1)}, u32[]{:S(2)}, u32[]{:S(2)}) collective-permute-start(f32[2,2,72,128]{3,2,1,0:T(8,128)} %get-tuple-element.10), channel_id=1, source_target_pairs={{0,16},{16,32},{32,48},{48,64},{64,80},{80,96},{96,112},{1,17},{17... | collective-permute-start | bytes 442376 | tf_op jit(solution)/shard_map/ppermute | solution.py:468
  52.0 8.1 %collective-permute-start.5 = (f32[2,2,72,128]{3,2,1,0:T(8,128)}, f32[2,2,72,128]{3,2,1,0:T(8,128)S(1)}, u32[]{:S(2)}, u32[]{:S(2)}) collective-permute-start(f32[2,2,72,128]{3,2,1,0:T(8,128)} %get-tuple-element.11), channel_id=1, source_target_pairs={{16,0},{32,16},{48,32},{64,48},{80,64},{96,80},{112,96},{17,1},{33... | collective-permute-start | bytes 442376 | tf_op jit(solution)/shard_map/ppermute | solution.py:469
  61.2 9.4 %copy-start.1 = (f32[2,2,128,128]{3,2,1,0:T(8,128)S(1)}, f32[2,2,128,128]{3,2,1,0:T(8,128)}, u32[]{:S(2)}) copy-start(f32[2,2,128,128]{3,2,1,0:T(8,128)} %get-tuple-element.9) | copy-start | bytes 786436
  62.0 11.8 %collective-permute-start.7 = (f32[2,2,264,65]{2,1,3,0:T(2,128)S(1)}, f32[2,2,264,65]{2,1,3,0:T(2,128)S(1)}, u32[]{:S(2)}, u32[]{:S(2)}) collective-permute-start(f32[2,2,264,65]{2,1,3,0:T(2,128)S(1)} %copy.14), channel_id=1, source_target_pairs={{1,0},{2,1},{3,2},{4,3},{5,4},{6,5},{7,6},{8,7},{9,8},{10,9},{11,1... | collective-permute-start | bytes 823688 | tf_op jit(solution)/shard_map/ppermute | solution.py:200
  68.5 12.8 %collective-permute-start.6 = (f32[2,2,264,65]{2,1,3,0:T(2,128)S(1)}, f32[2,2,264,65]{2,1,3,0:T(2,128)S(1)}, u32[]{:S(2)}, u32[]{:S(2)}) collective-permute-start(f32[2,2,264,65]{2,1,3,0:T(2,128)S(1)} %copy.13), channel_id=1, source_target_pairs={{0,1},{1,2},{2,3},{3,4},{4,5},{5,6},{6,7},{7,8},{8,9},{9,10},{10,1... | collective-permute-start | bytes 823688 | tf_op jit(solution)/shard_map/ppermute | solution.py:200
  82.3 1.1 %copy-start.7 = (f32[2]{0:T(128)S(1)}, f32[2]{0:T(128)}, u32[]{:S(2)}) copy-start(f32[2]{0:T(128)} %constant.75) | copy-start | bytes 28

commit v10 on v7

--- a/solution.py
+++ b/solution.py
@@ -408,26 +408,27 @@
     lead = stacked.shape[0]
     col_pair = col_inverse.shape[0]
     row_pair = row_inverse.shape[0]
-    inv_rows = col_inverse.shape[1] * block * block // own_cols
-    before, after = exchange_axis(
-        stacked, "gx", 1, block,
-        col_inverse[col_pair - 1].reshape(1, inv_rows, own_cols), col_inverse[0].reshape(1, inv_rows, own_cols),
-    )
-    tall = jnp.concatenate([before[:lead, :block], stacked, after[:lead, :block]], axis=1)
+    inv_cols = row_inverse.shape[1] * block * block // own_rows
+    left, right = exchange_axis(
+        stacked, "gy", 2, block,
+        row_inverse[row_pair - 1].reshape(1, own_rows, inv_cols), row_inverse[0].reshape(1, own_rows, inv_cols),
+    )
+    wide = jnp.concatenate([left[:lead, :, :block], stacked, right[:lead, :, :block]], axis=2)
+
     def inv_slab(mats):
-        flat = mats.reshape(1, -1, block)
-        return jnp.pad(flat, ((0, 0), (0, tall.shape[1] - flat.shape[1]), (0, 0)))
-    left, right = exchange_axis(tall, "gy", 2, block, inv_slab(row_inverse[row_pair - 1]), inv_slab(row_inverse[0]))
-    stacked_ext = jnp.concatenate([left[:lead], tall, right[:lead]], axis=2)
-    sources_ext = stacked_ext[:4].reshape(2, 2, own_rows + 2 * block, own_cols + 2 * block)
-    wave_ext = stacked_ext[4]
+        flat = mats.reshape(1, block, -1)
+        return jnp.pad(flat, ((0, 0), (0, 0), (0, wide.shape[2] - flat.shape[2])))
+
+    before, after = exchange_axis(wide, "gx", 1, block, inv_slab(col_inverse[col_pair - 1]), inv_slab(col_inverse[0]))
+    stacked_ext = jnp.concatenate([before[:lead], wide, after[:lead]], axis=1)
     inv_shape = (1,) + row_inverse.shape[1:]
-    inv_size = row_inverse.shape[1] * block * block // block
+    inv_size = col_inverse.shape[1] * block * block // block
+    row_blocks = jnp.concatenate(
+        [left[lead:].reshape(inv_shape), row_inverse, right[lead:].reshape(inv_shape)], axis=0
+    )
     col_blocks = jnp.concatenate(
-        [before[lead:].reshape(inv_shape), col_inverse, after[lead:].reshape(inv_shape)], axis=0
-    )
-    row_blocks = jnp.concatenate(
-        [left[lead:, :inv_size].reshape(inv_shape), row_inverse, right[lead:, :inv_size].reshape(inv_shape)], axis=0
+        [before[lead:, :, :inv_size].reshape(inv_shape), col_inverse, after[lead:, :, :inv_size].reshape(inv_shape)],
+        axis=0,
     )
     row_mats, col_mats = line_matrices(row_blocks, col_blocks)
     width = block + 1

time: 99.3 us -> 101 us (1.017); the launches traced: 97.6 us -> 101 us
  waiting for transfers between devices: 22.8 us -> 28 us
  local copies, waits for them, and re-layouts: 7.53 us -> 5.87 us
    ppermute x6, waiting for transfers between devices: 17.3 us -> 21.9 us  [exchange_axis(): return (lax.ppermute(last, axis, up), lax.ppermute(first, axis, down))]
    ppermute x1, starting transfers between devices: 3.17 us -> 5.28 us  [shards(): before = lax.ppermute(bottom, 'gx', up)[:, :, slab - width:]]
  transfers between devices with their start and end apart: 8 -> 8, of which waited for: 7 -> 7; matrix products, arithmetic and copies ran while one was open for 5% -> 3% of each run, Pallas kernels for 0% -> 0%
where the time goes in v10:
time: 101 us
  starting transfers between devices  28.7 us (28%)
  waiting for transfers between devices  28 us (28%)
  Pallas kernels  26.9 us (27%)
  other arithmetic  8.45 us (8%)
  local copies, waits for them, and re-layouts  5.87 us (6%)
  between operations  2.97 us (3%)
    pallas_call x2, Pallas kernels, solve_local_kernel(): pl.pallas_call(kernel, out_shape=[jax.ShapeDtypeStruct(s, dtype) for s in...  26.9 us
    ppermute x6, waiting for transfers between devices, exchange_axis(): return (lax.ppermute(last, axis, up), lax.ppermute(first, axis, down))  21.9 us
    ppermute x6, starting transfers between devices, exchange_axis(): return (lax.ppermute(last, axis, up), lax.ppermute(first, axis, down))  21.5 us
    ppermute x1, starting transfers between devices, shards(): before = lax.ppermute(bottom, 'gx', up)[:, :, slab - width:]  5.28 us
    ppermute x1, waiting for transfers between devices, shards(): after = lax.ppermute(top, 'gx', down)[:, :, :width]  4.98 us
  transfers between devices with their start and end apart: 8, of which 7 were waited for; matrix products, arithmetic and copies ran while one was open for 3% of the time, Pallas kernels for 0%

profile of v10, /device:TPU:6, one launch (start us, length us, event | category | flops | bytes accessed | tf_op | source)
XLA Modules:
  0.0 100.9 jit_solution(6758072934181546488)
XLA Ops:
  0.0 0.0 copy-start
  0.0 0.0 copy-start.1
  0.0 0.0 copy-start.4
  0.0 0.0 copy-start.6
  0.0 0.9 fusion.16
  1.0 1.1 %slice_maximum_fusion = f32[5,128,64]{2,1,0:T(8,128)S(1)} fusion(f32[1,128,128]{2,1,0:T(8,128)} %bitcast.71, f32[4,128,128]{2,1,0:T(8,128)} %bitcast.67), kind=kLoop, calls=%fused_computation.18 | loop fusion | flops 40960 | bytes 491520 | tf_op jit(solution)/shard_map/concatenate | solution.py:407
  2.1 1.9 %collective-permute-start = (f32[6,128,64]{2,1,0:T(8,128)S(1)}, f32[6,128,64]{2,1,0:T(8,128)S(1)}, u32[]{:S(2)}, u32[]{:S(2)}) collective-permute-start(f32[6,128,64]{2,1,0:T(8,128)S(1)} %pad_maximum_fusion.5), channel_id=1, source_target_pairs={{0,1},{1,2},{2,3},{3,4},{4,5},{5,6},{6,7},{7,8},{8,9},{9,10},{10,1... | collective-permute-start | bytes 589832 | tf_op jit(solution)/shard_map/ppermute | solution.py:195
  4.1 0.0 copy-done
  4.1 0.0 copy-done.1
  4.1 7.3 %collective-permute-start.1 = (f32[6,128,64]{2,1,0:T(8,128)S(1)}, f32[6,128,64]{2,1,0:T(8,128)S(1)}, u32[]{:S(2)}, u32[]{:S(2)}) collective-permute-start(f32[6,128,64]{2,1,0:T(8,128)S(1)} %fusion), channel_id=1, source_target_pairs={{1,0},{2,1},{3,2},{4,3},{5,4},{6,5},{7,6},{8,7},{9,8},{10,9},{11,1... | collective-permute-start | bytes 589832 | tf_op jit(solution)/shard_map/ppermute | solution.py:195
  11.4 0.0 copy-done.4
  11.4 0.1 reshape_squeeze.15
  11.5 0.1 reshape_squeeze.14
  11.6 0.0 copy-done.6
  11.6 0.7 fusion.17
  14.8 0.6 pad_add_fusion.rect_ref
  15.4 0.0 collective-permute-done
  15.4 1.2 %collective-permute-done.1 = f32[6,128,64]{2,1,0:T(8,128)S(1)} collective-permute-done((f32[6,128,64]{2,1,0:T(8,128)S(1)}, f32[6,128,64]{2,1,0:T(8,128)S(1)}, u32[]{:S(2)}, u32[]{:S(2)}) %collective-permute-start.1) | collective-permute-done | bytes 196640 | tf_op jit(solution)/shard_map/ppermute | solution.py:195
  16.7 0.3 pad_maximum_fusion.2
  17.0 0.0 copy-start.3
  17.1 2.7 %collective-permute-start.3 = (f32[6,64,256]{2,1,0:T(8,128)S(1)}, f32[6,64,256]{2,1,0:T(8,128)S(1)}, u32[]{:S(2)}, u32[]{:S(2)}) collective-permute-start(f32[6,64,256]{2,1,0:T(8,128)S(1)} %select_maximum_fusion), channel_id=1, source_target_pairs={{16,0},{32,16},{48,32},{64,48},{80,64},{96,80},{112,96},{17,1},{33... | collective-permute-start | bytes 1179656 | tf_op jit(solution)/shard_map/ppermute | solution.py:195
  19.9 4.0 %collective-permute-start.2 = (f32[6,64,256]{2,1,0:T(8,128)S(1)}, f32[6,64,256]{2,1,0:T(8,128)S(1)}, u32[]{:S(2)}, u32[]{:S(2)}) collective-permute-start(f32[6,64,256]{2,1,0:T(8,128)S(1)} %select_maximum_fusion.1), channel_id=1, source_target_pairs={{0,16},{16,32},{32,48},{48,64},{64,80},{80,96},{96,112},{1,17},{17... | collective-permute-start | bytes 1179656 | tf_op jit(solution)/shard_map/ppermute | solution.py:195
  23.9 0.0 copy-done.3
  24.0 0.1 fusion.3
  24.1 0.1 fusion.4
  24.2 0.7 pad_maximum_fusion.6.wrow_ref
  24.9 7.1 %collective-permute-done.3 = f32[6,64,256]{2,1,0:T(8,128)S(1)} collective-permute-done((f32[6,64,256]{2,1,0:T(8,128)S(1)}, f32[6,64,256]{2,1,0:T(8,128)S(1)}, u32[]{:S(2)}, u32[]{:S(2)}) %collective-permute-start.3) | collective-permute-done | bytes 393248 | tf_op jit(solution)/shard_map/ppermute | solution.py:195
  32.0 0.1 reshape.73
  32.1 3.3 %collective-permute-done.2 = f32[6,64,256]{2,1,0:T(8,128)S(1)} collective-permute-done((f32[6,64,256]{2,1,0:T(8,128)S(1)}, f32[6,64,256]{2,1,0:T(8,128)S(1)}, u32[]{:S(2)}, u32[]{:S(2)}) %collective-permute-start.2) | collective-permute-done | bytes 393248 | tf_op jit(solution)/shard_map/ppermute | solution.py:195
  35.4 0.1 reshape.72
  35.5 0.1 fusion.1
  35.6 0.1 fusion.2
  35.6 0.7 pad_maximum_fusion.7.wcol_ref
  36.4 1.4 %pad_maximum_fusion.1.resid_ref.data_ref = f32[5,256,256]{2,1,0:T(8,128)} fusion(f32[5,64,256]{2,1,0:T(8,128)S(1)} %slice.195, f32[5,128,64]{2,1,0:T(8,128)S(1)} %slice.191, f32[1,128,128]{2,1,0:T(8,128)S(1)} %bitcast.74, f32[4,128,128]{2,1,0:T(8,128)S(1)} %bitcast.70, f32[5,128,64]{2,1,0:T(8,128)S(1)} %slice.190, f32[5,64,256]{2,1,0:T(8,128)S(1)} %slice.193), kind=kLoop, calls=%fused_computation.4 | loop fusion | flops 1638400 | bytes 2621440 | tf_op jit(solution)/shard_map/concatenate | solution.py:423
  37.8 12.4 %shard_map.64 = (f32[2,2,256,256]{3,2,1,0:T(8,128)}, f32[2,2,128,128]{3,2,1,0:T(8,128)}, f32[2,2,72,128]{3,2,1,0:T(8,128)}, f32[2,2,72,128]{3,2,1,0:T(8,128)}) custom-call(s32[4]{0:T(128)} %pad_add_fusion.rect_ref, f32[5,256,256]{2,1,0:T(8,128)} %pad_maximum_fusion.1.resid_ref.data_ref, f32[5,256,256]{2,1,0:T(8,128)} %pad_maximum_fusion.1.resid_ref.data_ref, ...), custom_call_target="tpu_custom_call" | custom-call | tf_op jit(solution)/shard_map/pallas_call | solution.py:376
  50.2 5.3 %collective-permute-start.4 = (f32[2,2,72,128]{3,2,1,0:T(8,128)}, f32[2,2,72,128]{3,2,1,0:T(8,128)S(1)}, u32[]{:S(2)}, u32[]{:S(2)}) collective-permute-start(f32[2,2,72,128]{3,2,1,0:T(8,128)} %get-tuple-element.9), channel_id=1, source_target_pairs={{0,16},{16,32},{32,48},{48,64},{64,80},{80,96},{96,112},{1,17},{17... | collective-permute-start | bytes 442376 | tf_op jit(solution)/shard_map/ppermute | solution.py:447
  55.5 1.9 %collective-permute-start.5 = (f32[2,2,72,128]{3,2,1,0:T(8,128)}, f32[2,2,72,128]{3,2,1,0:T(8,128)S(1)}, u32[]{:S(2)}, u32[]{:S(2)}) collective-permute-start(f32[2,2,72,128]{3,2,1,0:T(8,128)} %get-tuple-element.11), channel_id=1, source_target_pairs={{16,0},{32,16},{48,32},{64,48},{80,64},{96,80},{112,96},{17,1},{33... | collective-permute-start | bytes 442376 | tf_op jit(solution)/shard_map/ppermute | solution.py:448
  57.5 1.2 %collective-permute-done.4 = f32[2,2,72,128]{3,2,1,0:T(8,128)S(1)} collective-permute-done((f32[2,2,72,128]{3,2,1,0:T(8,128)}, f32[2,2,72,128]{3,2,1,0:T(8,128)S(1)}, u32[]{:S(2)}, u32[]{:S(2)}) %collective-permute-start.4) | collective-permute-done | bytes 147488 | tf_op jit(solution)/shard_map/ppermute | solution.py:447
  58.7 5.0 %collective-permute-done.5 = f32[2,2,72,128]{3,2,1,0:T(8,128)S(1)} collective-permute-done((f32[2,2,72,128]{3,2,1,0:T(8,128)}, f32[2,2,72,128]{3,2,1,0:T(8,128)S(1)}, u32[]{:S(2)}, u32[]{:S(2)}) %collective-permute-start.5) | collective-permute-done | bytes 147488 | tf_op jit(solution)/shard_map/ppermute | solution.py:448
  63.7 1.0 pad_maximum_fusion.3
  64.7 0.2 fusion.14
  64.9 0.3 copy.8
  65.2 0.0 copy-start.2
  65.2 3.5 %collective-permute-start.7 = (f32[2,2,258,65]{2,1,3,0:T(2,128)S(1)}, f32[2,2,258,65]{2,1,3,0:T(2,128)S(1)}, u32[]{:S(2)}, u32[]{:S(2)}) collective-permute-start(f32[2,2,258,65]{2,1,3,0:T(2,128)S(1)} %copy.8), channel_id=1, source_target_pairs={{1,0},{2,1},{3,2},{4,3},{5,4},{6,5},{7,6},{8,7},{9,8},{10,9},{11,1... | collective-permute-start | bytes 804968 | tf_op jit(solution)/shard_map/ppermute | solution.py:195
  68.7 0.3 copy.7
  69.0 2.1 %collective-permute-start.6 = (f32[2,2,258,65]{2,1,3,0:T(2,128)S(1)}, f32[2,2,258,65]{2,1,3,0:T(2,128)S(1)}, u32[]{:S(2)}, u32[]{:S(2)}) collective-permute-start(f32[2,2,258,65]{2,1,3,0:T(2,128)S(1)} %copy.7), channel_id=1, source_target_pairs={{0,1},{1,2},{2,3},{3,4},{4,5},{5,6},{6,7},{7,8},{8,9},{9,10},{10,1... | collective-permute-start | bytes 804968 | tf_op jit(solution)/shard_map/ppermute | solution.py:195
  71.1 0.1 or_or_fusion
  71.3 2.8 %collective-permute-done.7 = f32[2,2,258,65]{2,1,3,0:T(2,128)S(1)} collective-permute-done((f32[2,2,258,65]{2,1,3,0:T(2,128)S(1)}, f32[2,2,258,65]{2,1,3,0:T(2,128)S(1)}, u32[]{:S(2)}, u32[]{:S(2)}) %collective-permute-start.7) | collective-permute-done | bytes 268352 | tf_op jit(solution)/shard_map/ppermute | solution.py:195
  74.1 0.3 copy.10
  74.3 7.5 %collective-permute-done.6 = f32[2,2,258,65]{2,1,3,0:T(2,128)S(1)} collective-permute-done((f32[2,2,258,65]{2,1,3,0:T(2,128)S(1)}, f32[2,2,258,65]{2,1,3,0:T(2,128)S(1)}, u32[]{:S(2)}, u32[]{:S(2)}) %collective-permute-start.6) | collective-permute-done | bytes 268352 | tf_op jit(solution)/shard_map/ppermute | solution.py:195
  81.8 0.3 copy.9
  82.1 0.0 copy-done.2
  82.1 0.6 pad_maximum_fusion
  82.8 0.2 select_select_fusion.1
  83.0 0.8 slice_reduce_fusion.1
  83.8 0.0 copy-start.5
  83.8 0.4 select_select_fusion
  84.3 0.2 copy-done.5
  84.5 0.2 multiply_add_fusion
  84.7 0.5 maximum_select_fusion
  85.2 1.3 %pad.79 = f32[2,2,264,384]{3,2,1,0:T(8,128)} pad(f32[2,2,258,258]{3,2,1,0:T(8,128)S(1)} %maximum_select_fusion, f32[]{:T(128)} %constant.31.clone.1), padding=0_0x0_0x0_6x0_126 | pad | bytes 2687044 | tf_op jit(solution)/shard_map/jit(_pad)/pad | solution.py:455
  86.5 14.5 %shard_map.65 = f32[2,2,128,128]{3,2,1,0:T(8,128)} custom-call(s32[4]{0:T(128)} %pad_add_fusion.rect_ref, f32[4,264,384]{2,1,0:T(8,128)} %bitcast.66, f32[5,256,256]{2,1,0:T(8,128)} %pad_maximum_fusion.1.resid_ref.data_ref, f32[2,256,128]{2,1,0:T(8,128)} %pad_maximum_fusion.6.wrow_ref, f32[2,256,128]{2,1,0:T(8,128)} %pad_maximum_fusion.7.wcol_ref, ...), custom_call_target="tpu_custom_call" | custom-call | tf_op jit(solution)/shard_map/pallas_call | solution.py:376
  (26 shorter events, 0.4 us)
Async XLA Ops:
  0.0 4.1 %copy-start = (f32[2,2,128,128]{3,2,1,0:T(8,128)S(1)}, f32[2,2,128,128]{3,2,1,0:T(8,128)}, u32[]{:S(2)}) copy-start(f32[2,2,128,128]{3,2,1,0:T(8,128)} %param.6) | copy-start | bytes 786436
  0.0 4.1 %copy-start.1 = (f32[128,128]{1,0:T(8,128)S(1)}, f32[128,128]{1,0:T(8,128)}, u32[]{:S(2)}) copy-start(f32[128,128]{1,0:T(8,128)} %param.7) | copy-start | bytes 196612
  0.0 11.4 %copy-start.4 = (f32[2,2,64,64]{3,2,1,0:T(8,128)S(1)}, f32[2,2,64,64]{3,2,1,0:T(8,128)}, u32[]{:S(2)}) copy-start(f32[2,2,64,64]{3,2,1,0:T(8,128)} %param.9) | copy-start | bytes 196612
  0.0 11.6 %copy-start.6 = (s32[1,1,4]{2,1,0:T(1,128)S(1)}, s32[1,1,4]{2,1,0:T(1,128)}, u32[]{:S(2)}) copy-start(s32[1,1,4]{2,1,0:T(1,128)} %param.10) | copy-start | bytes 52
  2.1 13.3 %collective-permute-start = (f32[6,128,64]{2,1,0:T(8,128)S(1)}, f32[6,128,64]{2,1,0:T(8,128)S(1)}, u32[]{:S(2)}, u32[]{:S(2)}) collective-permute-start(f32[6,128,64]{2,1,0:T(8,128)S(1)} %pad_maximum_fusion.5), channel_id=1, source_target_pairs={{0,1},{1,2},{2,3},{3,4},{4,5},{5,6},{6,7},{7,8},{8,9},{9,10},{10,1... | collective-permute-start | bytes 589832 | tf_op jit(solution)/shard_map/ppermute | solution.py:195
  4.1 12.5 %collective-permute-start.1 = (f32[6,128,64]{2,1,0:T(8,128)S(1)}, f32[6,128,64]{2,1,0:T(8,128)S(1)}, u32[]{:S(2)}, u32[]{:S(2)}) collective-permute-start(f32[6,128,64]{2,1,0:T(8,128)S(1)} %fusion), channel_id=1, source_target_pairs={{1,0},{2,1},{3,2},{4,3},{5,4},{6,5},{7,6},{8,7},{9,8},{10,9},{11,1... | collective-permute-start | bytes 589832 | tf_op jit(solution)/shard_map/ppermute | solution.py:195
  17.0 6.9 %copy-start.3 = (f32[2,2,64,64]{3,2,1,0:T(8,128)S(1)}, f32[2,2,64,64]{3,2,1,0:T(8,128)}, u32[]{:S(2)}) copy-start(f32[2,2,64,64]{3,2,1,0:T(8,128)} %param.8) | copy-start | bytes 196612
  17.1 14.8 %collective-permute-start.3 = (f32[6,64,256]{2,1,0:T(8,128)S(1)}, f32[6,64,256]{2,1,0:T(8,128)S(1)}, u32[]{:S(2)}, u32[]{:S(2)}) collective-permute-start(f32[6,64,256]{2,1,0:T(8,128)S(1)} %select_maximum_fusion), channel_id=1, source_target_pairs={{16,0},{32,16},{48,32},{64,48},{80,64},{96,80},{112,96},{17,1},{33... | collective-permute-start | bytes 1179656 | tf_op jit(solution)/shard_map/ppermute | solution.py:195
  19.9 15.5 %collective-permute-start.2 = (f32[6,64,256]{2,1,0:T(8,128)S(1)}, f32[6,64,256]{2,1,0:T(8,128)S(1)}, u32[]{:S(2)}, u32[]{:S(2)}) collective-permute-start(f32[6,64,256]{2,1,0:T(8,128)S(1)} %select_maximum_fusion.1), channel_id=1, source_target_pairs={{0,16},{16,32},{32,48},{48,64},{64,80},{80,96},{96,112},{1,17},{17... | collective-permute-start | bytes 1179656 | tf_op jit(solution)/shard_map/ppermute | solution.py:195
  50.2 8.4 %collective-permute-start.4 = (f32[2,2,72,128]{3,2,1,0:T(8,128)}, f32[2,2,72,128]{3,2,1,0:T(8,128)S(1)}, u32[]{:S(2)}, u32[]{:S(2)}) collective-permute-start(f32[2,2,72,128]{3,2,1,0:T(8,128)} %get-tuple-element.9), channel_id=1, source_target_pairs={{0,16},{16,32},{32,48},{48,64},{64,80},{80,96},{96,112},{1,17},{17... | collective-permute-start | bytes 442376 | tf_op jit(solution)/shard_map/ppermute | solution.py:447
  55.5 8.1 %collective-permute-start.5 = (f32[2,2,72,128]{3,2,1,0:T(8,128)}, f32[2,2,72,128]{3,2,1,0:T(8,128)S(1)}, u32[]{:S(2)}, u32[]{:S(2)}) collective-permute-start(f32[2,2,72,128]{3,2,1,0:T(8,128)} %get-tuple-element.11), channel_id=1, source_target_pairs={{16,0},{32,16},{48,32},{64,48},{80,64},{96,80},{112,96},{17,1},{33... | collective-permute-start | bytes 442376 | tf_op jit(solution)/shard_map/ppermute | solution.py:448
  65.2 16.9 %copy-start.2 = (f32[2,2,128,128]{3,2,1,0:T(8,128)S(1)}, f32[2,2,128,128]{3,2,1,0:T(8,128)}, u32[]{:S(2)}) copy-start(f32[2,2,128,128]{3,2,1,0:T(8,128)} %get-tuple-element.10) | copy-start | bytes 786436
  65.2 8.9 %collective-permute-start.7 = (f32[2,2,258,65]{2,1,3,0:T(2,128)S(1)}, f32[2,2,258,65]{2,1,3,0:T(2,128)S(1)}, u32[]{:S(2)}, u32[]{:S(2)}) collective-permute-start(f32[2,2,258,65]{2,1,3,0:T(2,128)S(1)} %copy.8), channel_id=1, source_target_pairs={{1,0},{2,1},{3,2},{4,3},{5,4},{6,5},{7,6},{8,7},{9,8},{10,9},{11,1... | collective-permute-start | bytes 804968 | tf_op jit(solution)/shard_map/ppermute | solution.py:195
  69.0 12.8 %collective-permute-start.6 = (f32[2,2,258,65]{2,1,3,0:T(2,128)S(1)}, f32[2,2,258,65]{2,1,3,0:T(2,128)S(1)}, u32[]{:S(2)}, u32[]{:S(2)}) collective-permute-start(f32[2,2,258,65]{2,1,3,0:T(2,128)S(1)} %copy.7), channel_id=1, source_target_pairs={{0,1},{1,2},{2,3},{3,4},{4,5},{5,6},{6,7},{7,8},{8,9},{9,10},{10,1... | collective-permute-start | bytes 804968 | tf_op jit(solution)/shard_map/ppermute | solution.py:195
  83.8 0.7 copy-start.5

commit v11 on v6

--- a/solution.py
+++ b/solution.py
@@ -241,9 +241,8 @@
         refs = refs[:-1]
     base_ref = refs[0] if has_base else None
     outs = refs[1:] if has_base else refs
-    full_ref = None if last else outs[0]
-    own_ref = outs[-1] if last else outs[1]
-    top_ref, bottom_ref = (None, None) if last else outs[2:4]
+    own_ref = outs[0]
+    top_ref, bottom_ref = (None, None) if last else outs[1:3]
     height, breadth = (resid_ref.shape[1], resid_ref.shape[2])
     half = height // 2
     upper, lower, left, right = (rect_ref[0], rect_ref[1], rect_ref[2], rect_ref[3])
@@ -320,13 +319,11 @@
             apply = cols_apply if step % 2 == 0 else rows_apply
             up_r, up_i = apply(loc_r, loc_i, sign)
             cor_r, cor_i = (cor_r + mask(up_r), cor_i + mask(up_i))
-        if base_ref is not None:
-            cor_r, cor_i = (cor_r + base_ref[problem, 0], cor_i + base_ref[problem, 1])
         first_row = (height - own_rows) // 2
         for part, value in ((0, cor_r), (1, cor_i)):
-            if full_ref is not None:
-                full_ref[problem, part] = value
             own = pltpu.roll(value, breadth - (breadth - own_cols) // 2, 1)[first_row : first_row + own_rows, :own_cols]
+            if base_ref is not None:
+                own = own + base_ref[problem, part]
             own_ref[problem, part] = own
             if top_ref is not None:
                 top_ref[problem, part] = own[:slab]
@@ -353,8 +350,7 @@
     rect = jnp.stack([to_index(v) for v in live_rect])
     dtype = resid_planes.dtype
     ext_shape = data_ext.shape[1:]
-    shapes = [] if last else [(2, 2) + ext_shape]
-    shapes.append((2, 2) + own_shape)
+    shapes = [(2, 2) + own_shape]
     if not last:
         shapes += [(2, 2, slab, own_shape[1])] * 2
     vmem = pltpu.MemorySpace.VMEM if hasattr(pltpu, "MemorySpace") else pltpu.VMEM
@@ -447,10 +443,10 @@
             resid_planes, stacked_ext, row_mats, col_mats, live_rect, (own_rows, own_cols), slab, base=base, last=last,
             from_fields=iteration > 0,
         )
-        if last:
-            solution = outs[0]
-        else:
-            base, solution, top, bottom = outs
+        solution = outs[0]
+        if not last:
+            solution, top, bottom = outs
+        base = solution
     return solution
 
 

time: 99 us -> 98.5 us (level)
  no operation moved by 1% of the time
where the time goes in v11:
time: 98.5 us; the launch traced here: 96.6 us
  starting transfers between devices  30.5 us (31%)
  Pallas kernels  26.4 us (27%)
  waiting for transfers between devices  17.2 us (17%)
  local copies, waits for them, and re-layouts  11.6 us (12%)
  other arithmetic  7.97 us (8%)
  between operations  2.96 us (3%)
    pallas_call x2, Pallas kernels, solve_local_kernel(): pl.pallas_call(kernel, out_shape=[jax.ShapeDtypeStruct(s, dtype) for s in...  26.4 us
    ppermute x6, starting transfers between devices, exchange_axis(): return (lax.ppermute(last, axis, up), lax.ppermute(first, axis, down))  24.6 us
    ppermute x6, waiting for transfers between devices, exchange_axis(): return (lax.ppermute(last, axis, up), lax.ppermute(first, axis, down))  11.4 us
    ppermute x1, waiting for transfers between devices, shards(): after = lax.ppermute(top, 'gx', down)[:, :, :width]  3.89 us
    ppermute x1, starting transfers between devices, shards(): before = lax.ppermute(bottom, 'gx', up)[:, :, slab - width:]  3.58 us
    ppermute x1, starting transfers between devices, shards(): after = lax.ppermute(top, 'gx', down)[:, :, :width]  2.25 us
  transfers between devices with their start and end apart: 8, of which 7 were waited for; matrix products, arithmetic and copies ran while one was open for 5% of the time, Pallas kernels for 0%

profile of v11, /device:TPU:6, one launch (start us, length us, event | category | flops | bytes accessed | tf_op | source)
XLA Modules:
  0.0 96.6 jit_solution(3859432210390964881)
XLA Ops:
  0.0 0.9 fusion.11
  1.0 0.1 reshape_squeeze.12
  1.0 0.9 fusion.1
  2.0 3.8 %collective-permute-start = (f32[6,64,128]{2,1,0:T(8,128)S(1)}, f32[6,64,128]{2,1,0:T(8,128)S(1)}, u32[]{:S(2)}, u32[]{:S(2)}) collective-permute-start(f32[6,64,128]{2,1,0:T(8,128)S(1)} %pad_maximum_fusion.7), channel_id=1, source_target_pairs={{0,16},{16,32},{32,48},{48,64},{64,80},{80,96},{96,112},{1,17},{17... | collective-permute-start | bytes 589832 | tf_op jit(solution)/shard_map/ppermute | solution.py:195
  5.7 0.1 reshape_squeeze.13
  5.8 0.9 fusion
  6.8 2.1 %collective-permute-start.1 = (f32[6,64,128]{2,1,0:T(8,128)S(1)}, f32[6,64,128]{2,1,0:T(8,128)S(1)}, u32[]{:S(2)}, u32[]{:S(2)}) collective-permute-start(f32[6,64,128]{2,1,0:T(8,128)S(1)} %fusion), channel_id=1, source_target_pairs={{16,0},{32,16},{48,32},{64,48},{80,64},{96,80},{112,96},{17,1},{33... | collective-permute-start | bytes 589832 | tf_op jit(solution)/shard_map/ppermute | solution.py:195
  8.9 0.7 fusion.12
  12.1 0.0 collective-permute-done
  12.2 3.7 %collective-permute-done.1 = f32[6,64,128]{2,1,0:T(8,128)S(1)} collective-permute-done((f32[6,64,128]{2,1,0:T(8,128)S(1)}, f32[6,64,128]{2,1,0:T(8,128)S(1)}, u32[]{:S(2)}, u32[]{:S(2)}) %collective-permute-start.1) | collective-permute-done | bytes 196640 | tf_op jit(solution)/shard_map/ppermute | solution.py:195
  16.0 0.2 fusion.8
  16.2 0.3 copy-done.5
  16.6 0.1 select_maximum_fusion.1
  16.6 0.2 copy.11
  16.9 0.0 slice-start
  16.9 0.0 copy-start.3
  16.9 2.1 %collective-permute-start.2 = (f32[6,256,64]{1,2,0:T(8,128)S(1)}, f32[6,256,64]{1,2,0:T(8,128)S(1)}, u32[]{:S(2)}, u32[]{:S(2)}) collective-permute-start(f32[6,256,64]{1,2,0:T(8,128)S(1)} %copy.11), channel_id=1, source_target_pairs={{0,1},{1,2},{2,3},{3,4},{4,5},{5,6},{6,7},{7,8},{8,9},{9,10},{10,1... | collective-permute-start | bytes 1179656 | tf_op jit(solution)/shard_map/ppermute | solution.py:195
  19.0 0.1 select_maximum_fusion
  19.0 0.2 copy.13
  19.3 7.3 %collective-permute-start.3 = (f32[6,256,64]{1,2,0:T(8,128)S(1)}, f32[6,256,64]{1,2,0:T(8,128)}, u32[]{:S(2)}, u32[]{:S(2)}) collective-permute-start(f32[6,256,64]{1,2,0:T(8,128)S(1)} %copy.13), channel_id=1, source_target_pairs={{1,0},{2,1},{3,2},{4,3},{5,4},{6,5},{7,6},{8,7},{9,8},{10,9},{11,1... | collective-permute-start | bytes 1179656 | tf_op jit(solution)/shard_map/ppermute | solution.py:195
  26.6 0.6 pad_add_fusion.rect_ref
  27.2 0.1 reshape.91
  27.3 0.1 reshape.92
  27.4 0.0 copy-done.3
  27.4 0.3 multiply_bitcast_fusion
  27.7 1.0 %reshape.95.wcol_ref = f32[2,256,128]{2,1,0:T(8,128)} reshape(f32[2,2,2,64,2,64]{5,4,3,2,1,0:T(2,128)S(1)} %multiply_bitcast_fusion) | data formatting | bytes 524288 | tf_op jit(solution)/shard_map/reshape | solution.py:343
  28.7 1.1 %collective-permute-done.2 = f32[6,256,64]{1,2,0:T(8,128)S(1)} collective-permute-done((f32[6,256,64]{1,2,0:T(8,128)S(1)}, f32[6,256,64]{1,2,0:T(8,128)S(1)}, u32[]{:S(2)}, u32[]{:S(2)}) %collective-permute-start.2) | collective-permute-done | bytes 393248 | tf_op jit(solution)/shard_map/ppermute | solution.py:195
  29.8 0.2 copy.27
  30.0 1.8 %collective-permute-done.3 = f32[6,256,64]{1,2,0:T(8,128)} collective-permute-done((f32[6,256,64]{1,2,0:T(8,128)S(1)}, f32[6,256,64]{1,2,0:T(8,128)}, u32[]{:S(2)}, u32[]{:S(2)}) %collective-permute-start.3) | collective-permute-done | bytes 393248 | tf_op jit(solution)/shard_map/ppermute | solution.py:195
  31.8 1.0 %slice.131 = f32[5,256,64]{1,2,0:T(8,128)S(1)} slice(f32[6,256,64]{1,2,0:T(8,128)} %collective-permute-done.3), slice={[0:5], [0:256], [0:64]} | slice | bytes 655360 | tf_op jit(solution)/shard_map/slice | solution.py:407
  32.8 0.2 copy.28
  33.1 0.1 copy.23
  33.2 0.8 slice.133
  33.9 0.1 copy.24
  34.1 0.2 copy.17
  34.2 0.2 multiply_bitcast_fusion.1
  34.5 1.2 %reshape.90.wrow_ref = f32[2,128,256]{2,1,0:T(8,128)} reshape(f32[2,2,64,2,2,64]{5,4,3,2,1,0:T(2,128)S(1)} %multiply_bitcast_fusion.1) | data formatting | bytes 524288 | tf_op jit(solution)/shard_map/reshape | solution.py:341
  35.7 1.6 %pad_maximum_fusion.1.resid_ref.data_ref = f32[5,256,256]{2,1,0:T(8,128)} fusion(f32[5,256,64]{2,1,0:T(8,128)S(1)} %copy.28, f32[5,64,128]{2,1,0:T(8,128)S(1)} %slice.127, f32[1,128,128]{2,1,0:T(8,128)S(1)} %bitcast.44, f32[4,128,128]{2,1,0:T(8,128)S(1)} %bitcast.40, f32[5,64,128]{2,1,0:T(8,128)S(1)} %slice.126, f32[5,256,64]{2,1,0:T(8,128)S(1)} %copy.27), kind=kLoop, calls=%fused_computation.4 | loop fusion | flops 1638400 | bytes 2621440 | tf_op jit(solution)/shard_map/concatenate | solution.py:407
  37.3 12.2 %shard_map.64 = (f32[2,2,128,128]{3,2,1,0:T(8,128)}, f32[2,2,72,128]{3,2,1,0:T(8,128)}, f32[2,2,72,128]{3,2,1,0:T(8,128)}) custom-call(s32[4]{0:T(128)} %pad_add_fusion.rect_ref, f32[5,256,256]{2,1,0:T(8,128)} %pad_maximum_fusion.1.resid_ref.data_ref, f32[5,256,256]{2,1,0:T(8,128)} %pad_maximum_fusion.1.resid_ref.data_ref, f32[2,128,256]{2,1,0:T(8,128)} %reshape.90.wrow_ref, ...), custom_call_target="tpu_custom_call" | custom-call | tf_op jit(solution)/shard_map/pallas_call | solution.py:362
  49.5 3.6 %collective-permute-start.4 = (f32[2,2,72,128]{3,2,1,0:T(8,128)}, f32[2,2,72,128]{3,2,1,0:T(8,128)S(1)}, u32[]{:S(2)}, u32[]{:S(2)}) collective-permute-start(f32[2,2,72,128]{3,2,1,0:T(8,128)} %get-tuple-element.8), channel_id=1, source_target_pairs={{0,16},{16,32},{32,48},{48,64},{64,80},{80,96},{96,112},{1,17},{17... | collective-permute-start | bytes 442376 | tf_op jit(solution)/shard_map/ppermute | solution.py:432
  53.1 2.3 %collective-permute-start.5 = (f32[2,2,72,128]{3,2,1,0:T(8,128)}, f32[2,2,72,128]{3,2,1,0:T(8,128)S(1)}, u32[]{:S(2)}, u32[]{:S(2)}) collective-permute-start(f32[2,2,72,128]{3,2,1,0:T(8,128)} %get-tuple-element.10), channel_id=1, source_target_pairs={{16,0},{32,16},{48,32},{64,48},{80,64},{96,80},{112,96},{17,1},{33... | collective-permute-start | bytes 442376 | tf_op jit(solution)/shard_map/ppermute | solution.py:433
  55.4 1.9 %collective-permute-done.4 = f32[2,2,72,128]{3,2,1,0:T(8,128)S(1)} collective-permute-done((f32[2,2,72,128]{3,2,1,0:T(8,128)}, f32[2,2,72,128]{3,2,1,0:T(8,128)S(1)}, u32[]{:S(2)}, u32[]{:S(2)}) %collective-permute-start.4) | collective-permute-done | bytes 147488 | tf_op jit(solution)/shard_map/ppermute | solution.py:432
  57.4 3.9 %collective-permute-done.5 = f32[2,2,72,128]{3,2,1,0:T(8,128)S(1)} collective-permute-done((f32[2,2,72,128]{3,2,1,0:T(8,128)}, f32[2,2,72,128]{3,2,1,0:T(8,128)S(1)}, u32[]{:S(2)}, u32[]{:S(2)}) %collective-permute-start.5) | collective-permute-done | bytes 147488 | tf_op jit(solution)/shard_map/ppermute | solution.py:433
  61.2 1.0 %pad_maximum_fusion.3 = f32[2,2,258,128]{3,2,1,0:T(8,128)S(1)} fusion(f32[2,2,65,128]{3,2,1,0:T(8,128)S(1)} %bitcast.47, f32[2,2,128,128]{3,2,1,0:T(8,128)} %get-tuple-element.9.refs_0_, f32[2,2,65,128]{3,2,1,0:T(8,128)S(1)} %slice.136), kind=kLoop, calls=%fused_computation.13 | loop fusion | flops 264192 | bytes 1056768 | tf_op jit(solution)/shard_map/concatenate | solution.py:434
  62.2 0.2 fusion.9
  62.4 0.3 copy.19
  62.8 2.1 %collective-permute-start.6 = (f32[2,2,258,65]{2,1,3,0:T(2,128)S(1)}, f32[2,2,258,65]{2,1,3,0:T(2,128)S(1)}, u32[]{:S(2)}, u32[]{:S(2)}) collective-permute-start(f32[2,2,258,65]{2,1,3,0:T(2,128)S(1)} %copy.19), channel_id=1, source_target_pairs={{0,1},{1,2},{2,3},{3,4},{4,5},{5,6},{6,7},{7,8},{8,9},{9,10},{10,1... | collective-permute-start | bytes 804968 | tf_op jit(solution)/shard_map/ppermute | solution.py:195
  64.8 0.3 copy.20
  65.1 7.4 %collective-permute-start.7 = (f32[2,2,258,65]{2,1,3,0:T(2,128)S(1)}, f32[2,2,258,65]{2,1,3,0:T(2,128)S(1)}, u32[]{:S(2)}, u32[]{:S(2)}) collective-permute-start(f32[2,2,258,65]{2,1,3,0:T(2,128)S(1)} %copy.20), channel_id=1, source_target_pairs={{1,0},{2,1},{3,2},{4,3},{5,4},{6,5},{7,6},{8,7},{9,8},{10,9},{11,1... | collective-permute-start | bytes 804968 | tf_op jit(solution)/shard_map/ppermute | solution.py:195
  72.6 0.1 or_or_fusion
  72.7 3.0 %collective-permute-done.6 = f32[2,2,258,65]{2,1,3,0:T(2,128)S(1)} collective-permute-done((f32[2,2,258,65]{2,1,3,0:T(2,128)S(1)}, f32[2,2,258,65]{2,1,3,0:T(2,128)S(1)}, u32[]{:S(2)}, u32[]{:S(2)}) %collective-permute-start.6) | collective-permute-done | bytes 268352 | tf_op jit(solution)/shard_map/ppermute | solution.py:195
  75.7 0.3 copy.21
  75.9 1.8 %collective-permute-done.7 = f32[2,2,258,65]{2,1,3,0:T(2,128)S(1)} collective-permute-done((f32[2,2,258,65]{2,1,3,0:T(2,128)S(1)}, f32[2,2,258,65]{2,1,3,0:T(2,128)S(1)}, u32[]{:S(2)}, u32[]{:S(2)}) %collective-permute-start.7) | collective-permute-done | bytes 268352 | tf_op jit(solution)/shard_map/ppermute | solution.py:195
  77.7 0.3 copy.22
  78.0 0.6 pad_maximum_fusion
  78.7 0.2 select_select_fusion.1
  78.9 0.8 slice_reduce_fusion.1
  79.7 0.0 copy-start.6
  79.8 0.4 select_select_fusion
  80.2 0.2 copy-done.6
  80.4 0.2 multiply_add_fusion
  80.6 0.5 maximum_select_fusion
  81.1 1.3 %pad.13 = f32[2,2,264,384]{3,2,1,0:T(8,128)} pad(f32[2,2,258,258]{3,2,1,0:T(8,128)S(1)} %maximum_select_fusion, f32[]{:T(128)} %constant.31.clone.1), padding=0_0x0_0x0_6x0_126 | pad | bytes 2687044 | tf_op jit(solution)/shard_map/jit(_pad)/pad | solution.py:440
  82.4 14.2 %shard_map.65 = f32[2,2,128,128]{3,2,1,0:T(8,128)} custom-call(s32[4]{0:T(128)} %pad_add_fusion.rect_ref, f32[4,264,384]{2,1,0:T(8,128)} %bitcast.36, f32[5,256,256]{2,1,0:T(8,128)} %pad_maximum_fusion.1.resid_ref.data_ref, f32[2,128,256]{2,1,0:T(8,128)} %reshape.90.wrow_ref, f32[2,256,128]{2,1,0:T(8,128)} %reshape.95.wcol_ref, ...), custom_call_target="tpu_custom_call" | custom-call | tf_op jit(solution)/shard_map/pallas_call | solution.py:362
  (30 shorter events, 0.3 us)
Async XLA Ops:
  0.0 15.9 %copy-start = (f32[2,2,128,128]{3,2,1,0:T(8,128)S(1)}, f32[2,2,128,128]{3,2,1,0:T(8,128)}, u32[]{:S(2)}) copy-start(f32[2,2,128,128]{3,2,1,0:T(8,128)} %param.6) | copy-start | bytes 786436
  0.0 15.9 %copy-start.2 = (f32[128,128]{1,0:T(8,128)S(1)}, f32[128,128]{1,0:T(8,128)}, u32[]{:S(2)}) copy-start(f32[128,128]{1,0:T(8,128)} %param.7) | copy-start | bytes 196612
  0.0 8.9 %copy-start.7 = (s32[1,1,4]{2,1,0:T(1,128)S(1)}, s32[1,1,4]{2,1,0:T(1,128)}, u32[]{:S(2)}) copy-start(s32[1,1,4]{2,1,0:T(1,128)} %param.10) | copy-start | bytes 52
  0.0 12.1 %copy-start.4 = (f32[2,2,64,64]{3,2,1,0:T(8,128)S(1)}, f32[2,2,64,64]{3,2,1,0:T(8,128)}, u32[]{:S(2)}) copy-start(f32[2,2,64,64]{3,2,1,0:T(8,128)} %param.8) | copy-start | bytes 196612
  2.0 10.2 %collective-permute-start = (f32[6,64,128]{2,1,0:T(8,128)S(1)}, f32[6,64,128]{2,1,0:T(8,128)S(1)}, u32[]{:S(2)}, u32[]{:S(2)}) collective-permute-start(f32[6,64,128]{2,1,0:T(8,128)S(1)} %pad_maximum_fusion.7), channel_id=1, source_target_pairs={{0,16},{16,32},{32,48},{48,64},{64,80},{80,96},{96,112},{1,17},{17... | collective-permute-start | bytes 589832 | tf_op jit(solution)/shard_map/ppermute | solution.py:195
  6.8 9.2 %collective-permute-start.1 = (f32[6,64,128]{2,1,0:T(8,128)S(1)}, f32[6,64,128]{2,1,0:T(8,128)S(1)}, u32[]{:S(2)}, u32[]{:S(2)}) collective-permute-start(f32[6,64,128]{2,1,0:T(8,128)S(1)} %fusion), channel_id=1, source_target_pairs={{16,0},{32,16},{48,32},{64,48},{80,64},{96,80},{112,96},{17,1},{33... | collective-permute-start | bytes 589832 | tf_op jit(solution)/shard_map/ppermute | solution.py:195
  15.9 0.7 copy-start.5
  16.9 10.4 %slice-start = ((f32[6,64,128]{2,1,0:T(8,128)}), f32[1,64,128]{2,1,0:T(8,128)S(1)}, s32[]{:S(2)}) async-start(f32[6,64,128]{2,1,0:T(8,128)} %copy-done.5), calls=%async_computation | async-start | bytes 65536 | tf_op jit(solution)/shard_map/slice | solution.py:413
  16.9 10.5 %copy-start.3 = (f32[2,2,64,64]{3,2,1,0:T(8,128)S(1)}, f32[2,2,64,64]{3,2,1,0:T(8,128)}, u32[]{:S(2)}) copy-start(f32[2,2,64,64]{3,2,1,0:T(8,128)} %param.9) | copy-start | bytes 196612
  16.9 12.8 %collective-permute-start.2 = (f32[6,256,64]{1,2,0:T(8,128)S(1)}, f32[6,256,64]{1,2,0:T(8,128)S(1)}, u32[]{:S(2)}, u32[]{:S(2)}) collective-permute-start(f32[6,256,64]{1,2,0:T(8,128)S(1)} %copy.11), channel_id=1, source_target_pairs={{0,1},{1,2},{2,3},{3,4},{4,5},{5,6},{6,7},{7,8},{8,9},{9,10},{10,1... | collective-permute-start | bytes 1179656 | tf_op jit(solution)/shard_map/ppermute | solution.py:195
  19.3 12.5 %collective-permute-start.3 = (f32[6,256,64]{1,2,0:T(8,128)S(1)}, f32[6,256,64]{1,2,0:T(8,128)}, u32[]{:S(2)}, u32[]{:S(2)}) collective-permute-start(f32[6,256,64]{1,2,0:T(8,128)S(1)} %copy.13), channel_id=1, source_target_pairs={{1,0},{2,1},{3,2},{4,3},{5,4},{6,5},{7,6},{8,7},{9,8},{10,9},{11,1... | collective-permute-start | bytes 1179656 | tf_op jit(solution)/shard_map/ppermute | solution.py:195
  49.5 7.8 %collective-permute-start.4 = (f32[2,2,72,128]{3,2,1,0:T(8,128)}, f32[2,2,72,128]{3,2,1,0:T(8,128)S(1)}, u32[]{:S(2)}, u32[]{:S(2)}) collective-permute-start(f32[2,2,72,128]{3,2,1,0:T(8,128)} %get-tuple-element.8), channel_id=1, source_target_pairs={{0,16},{16,32},{32,48},{48,64},{64,80},{80,96},{96,112},{1,17},{17... | collective-permute-start | bytes 442376 | tf_op jit(solution)/shard_map/ppermute | solution.py:432
  53.1 8.1 %collective-permute-start.5 = (f32[2,2,72,128]{3,2,1,0:T(8,128)}, f32[2,2,72,128]{3,2,1,0:T(8,128)S(1)}, u32[]{:S(2)}, u32[]{:S(2)}) collective-permute-start(f32[2,2,72,128]{3,2,1,0:T(8,128)} %get-tuple-element.10), channel_id=1, source_target_pairs={{16,0},{32,16},{48,32},{64,48},{80,64},{96,80},{112,96},{17,1},{33... | collective-permute-start | bytes 442376 | tf_op jit(solution)/shard_map/ppermute | solution.py:433
  62.8 15.2 %copy-start.1 = (f32[2,2,128,128]{3,2,1,0:T(8,128)S(1)}, f32[2,2,128,128]{3,2,1,0:T(8,128)}, u32[]{:S(2)}) copy-start(f32[2,2,128,128]{3,2,1,0:T(8,128)} %get-tuple-element.9.refs_0_) | copy-start | bytes 786436
  62.8 12.9 %collective-permute-start.6 = (f32[2,2,258,65]{2,1,3,0:T(2,128)S(1)}, f32[2,2,258,65]{2,1,3,0:T(2,128)S(1)}, u32[]{:S(2)}, u32[]{:S(2)}) collective-permute-start(f32[2,2,258,65]{2,1,3,0:T(2,128)S(1)} %copy.19), channel_id=1, source_target_pairs={{0,1},{1,2},{2,3},{3,4},{4,5},{5,6},{6,7},{7,8},{8,9},{9,10},{10,1... | collective-permute-start | bytes 804968 | tf_op jit(solution)/shard_map/ppermute | solution.py:195
  65.1 12.6 %collective-permute-start.7 = (f32[2,2,258,65]{2,1,3,0:T(2,128)S(1)}, f32[2,2,258,65]{2,1,3,0:T(2,128)S(1)}, u32[]{:S(2)}, u32[]{:S(2)}) collective-permute-start(f32[2,2,258,65]{2,1,3,0:T(2,128)S(1)} %copy.20), channel_id=1, source_target_pairs={{1,0},{2,1},{3,2},{4,3},{5,4},{6,5},{7,6},{8,7},{9,8},{10,9},{11,1... | collective-permute-start | bytes 804968 | tf_op jit(solution)/shard_map/ppermute | solution.py:195
  79.7 0.7 copy-start.6

commit v12 on v11

--- a/solution.py
+++ b/solution.py
@@ -348,7 +348,7 @@
                        from_fields=False, interpret=False):
     extra = [] if base is None else [base]
     rect = jnp.stack([to_index(v) for v in live_rect])
-    dtype = resid_planes.dtype
+    dtype = data_ext.dtype
     ext_shape = data_ext.shape[1:]
     shapes = [(2, 2) + own_shape]
     if not last:
@@ -359,14 +359,22 @@
         from_fields=from_fields,
     )
     scratch = [pltpu.VMEM((4,) + ext_shape, jnp.float32)] if from_fields else []
+    operands = [data_ext, row_mats, col_mats] + extra
+    if resid_planes is None:
+        inner = kernel
+
+        def kernel(rect_ref, data_ref, *refs):
+            return inner(rect_ref, data_ref, data_ref, *refs)
+    else:
+        operands = [resid_planes] + operands
     return pl.pallas_call(
         kernel,
         out_shape=[jax.ShapeDtypeStruct(s, dtype) for s in shapes],
-        in_specs=[pl.BlockSpec(memory_space=pltpu.SMEM)] + [pl.BlockSpec(memory_space=vmem)] * (4 + len(extra)),
+        in_specs=[pl.BlockSpec(memory_space=pltpu.SMEM)] + [pl.BlockSpec(memory_space=vmem)] * len(operands),
         out_specs=[pl.BlockSpec(memory_space=vmem)] * len(shapes),
         scratch_shapes=scratch,
         interpret=interpret,
-    )(rect, resid_planes, data_ext, row_mats, col_mats, *extra)
+    )(rect, *operands)
 
 
 def shards(sources, wavenumber, row_inverse, col_inverse, reach_steps):
@@ -424,7 +432,7 @@
     for iteration in range(ITERS):
         last = iteration == ITERS - 1
         if iteration == 0:
-            resid_planes = stacked_ext
+            resid_planes = None
         else:
             peers = lax.axis_size("gx")
             up = [(i, i + 1) for i in range(peers - 1)]

time: 98.5 us -> 98.1 us (level)
  no operation moved by 1% of the time
where the time goes in v12:
time: 98.1 us; the launch traced here: 96.2 us
  starting transfers between devices  30.5 us (31%)
  Pallas kernels  26 us (27%)
  waiting for transfers between devices  17.2 us (18%)
  local copies, waits for them, and re-layouts  11.6 us (12%)
  other arithmetic  7.97 us (8%)
  between operations  2.96 us (3%)
    pallas_call x2, Pallas kernels, solve_local_kernel(): pl.pallas_call(kernel, out_shape=[jax.ShapeDtypeStruct(s, dtype) for s in...  26 us
    ppermute x6, starting transfers between devices, exchange_axis(): return (lax.ppermute(last, axis, up), lax.ppermute(first, axis, down))  24.6 us
    ppermute x6, waiting for transfers between devices, exchange_axis(): return (lax.ppermute(last, axis, up), lax.ppermute(first, axis, down))  11.4 us
    ppermute x1, waiting for transfers between devices, shards(): after = lax.ppermute(top, 'gx', down)[:, :, :width]  3.88 us
    ppermute x1, starting transfers between devices, shards(): before = lax.ppermute(bottom, 'gx', up)[:, :, slab - width:]  3.57 us
    ppermute x1, starting transfers between devices, shards(): after = lax.ppermute(top, 'gx', down)[:, :, :width]  2.26 us
  transfers between devices with their start and end apart: 8, of which 7 were waited for; matrix products, arithmetic and copies ran while one was open for 5% of the time, Pallas kernels for 0%

profile of v12, /device:TPU:6, one launch (start us, length us, event | category | flops | bytes accessed | tf_op | source)
XLA Modules:
  0.0 96.2 jit_solution(13301485907895574733)
XLA Ops:
  0.0 0.9 fusion.11
  1.0 0.1 reshape_squeeze.12
  1.0 0.9 fusion.1
  2.0 3.8 %collective-permute-start = (f32[6,64,128]{2,1,0:T(8,128)S(1)}, f32[6,64,128]{2,1,0:T(8,128)S(1)}, u32[]{:S(2)}, u32[]{:S(2)}) collective-permute-start(f32[6,64,128]{2,1,0:T(8,128)S(1)} %pad_maximum_fusion.7), channel_id=1, source_target_pairs={{0,16},{16,32},{32,48},{48,64},{64,80},{80,96},{96,112},{1,17},{17... | collective-permute-start | bytes 589832 | tf_op jit(solution)/shard_map/ppermute | solution.py:195
  5.7 0.1 reshape_squeeze.13
  5.8 0.9 fusion
  6.8 2.1 %collective-permute-start.1 = (f32[6,64,128]{2,1,0:T(8,128)S(1)}, f32[6,64,128]{2,1,0:T(8,128)S(1)}, u32[]{:S(2)}, u32[]{:S(2)}) collective-permute-start(f32[6,64,128]{2,1,0:T(8,128)S(1)} %fusion), channel_id=1, source_target_pairs={{16,0},{32,16},{48,32},{64,48},{80,64},{96,80},{112,96},{17,1},{33... | collective-permute-start | bytes 589832 | tf_op jit(solution)/shard_map/ppermute | solution.py:195
  8.9 0.7 fusion.12
  12.1 0.0 collective-permute-done
  12.2 3.7 %collective-permute-done.1 = f32[6,64,128]{2,1,0:T(8,128)S(1)} collective-permute-done((f32[6,64,128]{2,1,0:T(8,128)S(1)}, f32[6,64,128]{2,1,0:T(8,128)S(1)}, u32[]{:S(2)}, u32[]{:S(2)}) %collective-permute-start.1) | collective-permute-done | bytes 196640 | tf_op jit(solution)/shard_map/ppermute | solution.py:195
  16.0 0.2 fusion.8
  16.2 0.3 copy-done.5
  16.6 0.1 select_maximum_fusion.1
  16.6 0.2 copy.11
  16.9 0.0 slice-start
  16.9 0.0 copy-start.3
  16.9 2.1 %collective-permute-start.2 = (f32[6,256,64]{1,2,0:T(8,128)S(1)}, f32[6,256,64]{1,2,0:T(8,128)S(1)}, u32[]{:S(2)}, u32[]{:S(2)}) collective-permute-start(f32[6,256,64]{1,2,0:T(8,128)S(1)} %copy.11), channel_id=1, source_target_pairs={{0,1},{1,2},{2,3},{3,4},{4,5},{5,6},{6,7},{7,8},{8,9},{9,10},{10,1... | collective-permute-start | bytes 1179656 | tf_op jit(solution)/shard_map/ppermute | solution.py:195
  19.0 0.1 select_maximum_fusion
  19.0 0.2 copy.13
  19.3 7.3 %collective-permute-start.3 = (f32[6,256,64]{1,2,0:T(8,128)S(1)}, f32[6,256,64]{1,2,0:T(8,128)}, u32[]{:S(2)}, u32[]{:S(2)}) collective-permute-start(f32[6,256,64]{1,2,0:T(8,128)S(1)} %copy.13), channel_id=1, source_target_pairs={{1,0},{2,1},{3,2},{4,3},{5,4},{6,5},{7,6},{8,7},{9,8},{10,9},{11,1... | collective-permute-start | bytes 1179656 | tf_op jit(solution)/shard_map/ppermute | solution.py:195
  26.6 0.6 pad_add_fusion.rect_ref
  27.2 0.1 reshape.91
  27.3 0.1 reshape.92
  27.4 0.0 copy-done.3
  27.4 0.3 multiply_bitcast_fusion
  27.7 1.0 %reshape.95.refs_1_.wcol_ref = f32[2,256,128]{2,1,0:T(8,128)} reshape(f32[2,2,2,64,2,64]{5,4,3,2,1,0:T(2,128)S(1)} %multiply_bitcast_fusion) | data formatting | bytes 524288 | tf_op jit(solution)/shard_map/reshape | solution.py:343
  28.7 1.1 %collective-permute-done.2 = f32[6,256,64]{1,2,0:T(8,128)S(1)} collective-permute-done((f32[6,256,64]{1,2,0:T(8,128)S(1)}, f32[6,256,64]{1,2,0:T(8,128)S(1)}, u32[]{:S(2)}, u32[]{:S(2)}) %collective-permute-start.2) | collective-permute-done | bytes 393248 | tf_op jit(solution)/shard_map/ppermute | solution.py:195
  29.8 0.2 copy.27
  30.0 1.8 %collective-permute-done.3 = f32[6,256,64]{1,2,0:T(8,128)} collective-permute-done((f32[6,256,64]{1,2,0:T(8,128)S(1)}, f32[6,256,64]{1,2,0:T(8,128)}, u32[]{:S(2)}, u32[]{:S(2)}) %collective-permute-start.3) | collective-permute-done | bytes 393248 | tf_op jit(solution)/shard_map/ppermute | solution.py:195
  31.8 1.0 %slice.131 = f32[5,256,64]{1,2,0:T(8,128)S(1)} slice(f32[6,256,64]{1,2,0:T(8,128)} %collective-permute-done.3), slice={[0:5], [0:256], [0:64]} | slice | bytes 655360 | tf_op jit(solution)/shard_map/slice | solution.py:415
  32.8 0.2 copy.28
  33.1 0.1 copy.23
  33.2 0.8 slice.133
  33.9 0.1 copy.24
  34.1 0.2 copy.17
  34.2 0.2 multiply_bitcast_fusion.1
  34.5 1.2 %reshape.90.refs_0_.wrow_ref = f32[2,128,256]{2,1,0:T(8,128)} reshape(f32[2,2,64,2,2,64]{5,4,3,2,1,0:T(2,128)S(1)} %multiply_bitcast_fusion.1) | data formatting | bytes 524288 | tf_op jit(solution)/shard_map/reshape | solution.py:341
  35.7 1.6 %pad_maximum_fusion.1.data_ref = f32[5,256,256]{2,1,0:T(8,128)} fusion(f32[5,256,64]{2,1,0:T(8,128)S(1)} %copy.28, f32[5,64,128]{2,1,0:T(8,128)S(1)} %slice.127, f32[1,128,128]{2,1,0:T(8,128)S(1)} %bitcast.44, f32[4,128,128]{2,1,0:T(8,128)S(1)} %bitcast.40, f32[5,64,128]{2,1,0:T(8,128)S(1)} %slice.126, f32[5,256,64]{2,1,0:T(8,128)S(1)} %copy.27), kind=kLoop, calls=%fused_computation.4 | loop fusion | flops 1638400 | bytes 2621440 | tf_op jit(solution)/shard_map/concatenate | solution.py:415
  37.3 11.8 %shard_map.64 = (f32[2,2,128,128]{3,2,1,0:T(8,128)}, f32[2,2,72,128]{3,2,1,0:T(8,128)}, f32[2,2,72,128]{3,2,1,0:T(8,128)}) custom-call(s32[4]{0:T(128)} %pad_add_fusion.rect_ref, f32[5,256,256]{2,1,0:T(8,128)} %pad_maximum_fusion.1.data_ref, f32[2,128,256]{2,1,0:T(8,128)} %reshape.90.refs_0_.wrow_ref, f32[2,256,128]{2,1,0:T(8,128)} %reshape.95.refs_1_.wcol_ref), custom_call_target="tpu_custom_call" | custom-call | tf_op jit(solution)/shard_map/pallas_call | solution.py:370
  49.1 3.6 %collective-permute-start.4 = (f32[2,2,72,128]{3,2,1,0:T(8,128)}, f32[2,2,72,128]{3,2,1,0:T(8,128)S(1)}, u32[]{:S(2)}, u32[]{:S(2)}) collective-permute-start(f32[2,2,72,128]{3,2,1,0:T(8,128)} %get-tuple-element.8), channel_id=1, source_target_pairs={{0,16},{16,32},{32,48},{48,64},{64,80},{80,96},{96,112},{1,17},{17... | collective-permute-start | bytes 442376 | tf_op jit(solution)/shard_map/ppermute | solution.py:440
  52.7 2.3 %collective-permute-start.5 = (f32[2,2,72,128]{3,2,1,0:T(8,128)}, f32[2,2,72,128]{3,2,1,0:T(8,128)S(1)}, u32[]{:S(2)}, u32[]{:S(2)}) collective-permute-start(f32[2,2,72,128]{3,2,1,0:T(8,128)} %get-tuple-element.10), channel_id=1, source_target_pairs={{16,0},{32,16},{48,32},{64,48},{80,64},{96,80},{112,96},{17,1},{33... | collective-permute-start | bytes 442376 | tf_op jit(solution)/shard_map/ppermute | solution.py:441
  55.0 1.9 %collective-permute-done.4 = f32[2,2,72,128]{3,2,1,0:T(8,128)S(1)} collective-permute-done((f32[2,2,72,128]{3,2,1,0:T(8,128)}, f32[2,2,72,128]{3,2,1,0:T(8,128)S(1)}, u32[]{:S(2)}, u32[]{:S(2)}) %collective-permute-start.4) | collective-permute-done | bytes 147488 | tf_op jit(solution)/shard_map/ppermute | solution.py:440
  56.9 3.9 %collective-permute-done.5 = f32[2,2,72,128]{3,2,1,0:T(8,128)S(1)} collective-permute-done((f32[2,2,72,128]{3,2,1,0:T(8,128)}, f32[2,2,72,128]{3,2,1,0:T(8,128)S(1)}, u32[]{:S(2)}, u32[]{:S(2)}) %collective-permute-start.5) | collective-permute-done | bytes 147488 | tf_op jit(solution)/shard_map/ppermute | solution.py:441
  60.8 1.0 %pad_maximum_fusion.3 = f32[2,2,258,128]{3,2,1,0:T(8,128)S(1)} fusion(f32[2,2,65,128]{3,2,1,0:T(8,128)S(1)} %bitcast.47, f32[2,2,128,128]{3,2,1,0:T(8,128)} %get-tuple-element.9.refs_0_, f32[2,2,65,128]{3,2,1,0:T(8,128)S(1)} %slice.136), kind=kLoop, calls=%fused_computation.13 | loop fusion | flops 264192 | bytes 1056768 | tf_op jit(solution)/shard_map/concatenate | solution.py:442
  61.8 0.2 fusion.9
  62.0 0.3 copy.19
  62.3 2.1 %collective-permute-start.6 = (f32[2,2,258,65]{2,1,3,0:T(2,128)S(1)}, f32[2,2,258,65]{2,1,3,0:T(2,128)S(1)}, u32[]{:S(2)}, u32[]{:S(2)}) collective-permute-start(f32[2,2,258,65]{2,1,3,0:T(2,128)S(1)} %copy.19), channel_id=1, source_target_pairs={{0,1},{1,2},{2,3},{3,4},{4,5},{5,6},{6,7},{7,8},{8,9},{9,10},{10,1... | collective-permute-start | bytes 804968 | tf_op jit(solution)/shard_map/ppermute | solution.py:195
  64.4 0.3 copy.20
  64.7 7.4 %collective-permute-start.7 = (f32[2,2,258,65]{2,1,3,0:T(2,128)S(1)}, f32[2,2,258,65]{2,1,3,0:T(2,128)S(1)}, u32[]{:S(2)}, u32[]{:S(2)}) collective-permute-start(f32[2,2,258,65]{2,1,3,0:T(2,128)S(1)} %copy.20), channel_id=1, source_target_pairs={{1,0},{2,1},{3,2},{4,3},{5,4},{6,5},{7,6},{8,7},{9,8},{10,9},{11,1... | collective-permute-start | bytes 804968 | tf_op jit(solution)/shard_map/ppermute | solution.py:195
  72.1 0.1 or_or_fusion
  72.3 3.0 %collective-permute-done.6 = f32[2,2,258,65]{2,1,3,0:T(2,128)S(1)} collective-permute-done((f32[2,2,258,65]{2,1,3,0:T(2,128)S(1)}, f32[2,2,258,65]{2,1,3,0:T(2,128)S(1)}, u32[]{:S(2)}, u32[]{:S(2)}) %collective-permute-start.6) | collective-permute-done | bytes 268352 | tf_op jit(solution)/shard_map/ppermute | solution.py:195
  75.2 0.3 copy.21
  75.5 1.8 %collective-permute-done.7 = f32[2,2,258,65]{2,1,3,0:T(2,128)S(1)} collective-permute-done((f32[2,2,258,65]{2,1,3,0:T(2,128)S(1)}, f32[2,2,258,65]{2,1,3,0:T(2,128)S(1)}, u32[]{:S(2)}, u32[]{:S(2)}) %collective-permute-start.7) | collective-permute-done | bytes 268352 | tf_op jit(solution)/shard_map/ppermute | solution.py:195
  77.3 0.3 copy.22
  77.6 0.6 pad_maximum_fusion
  78.2 0.2 select_select_fusion.1
  78.5 0.8 slice_reduce_fusion.1
  79.3 0.0 copy-start.6
  79.3 0.4 select_select_fusion
  79.7 0.2 copy-done.6
  80.0 0.2 multiply_add_fusion
  80.2 0.5 maximum_select_fusion
  80.6 1.3 %pad.13 = f32[2,2,264,384]{3,2,1,0:T(8,128)} pad(f32[2,2,258,258]{3,2,1,0:T(8,128)S(1)} %maximum_select_fusion, f32[]{:T(128)} %constant.31.clone.1), padding=0_0x0_0x0_6x0_126 | pad | bytes 2687044 | tf_op jit(solution)/shard_map/jit(_pad)/pad | solution.py:448
  81.9 14.2 %shard_map.65 = f32[2,2,128,128]{3,2,1,0:T(8,128)} custom-call(s32[4]{0:T(128)} %pad_add_fusion.rect_ref, f32[4,264,384]{2,1,0:T(8,128)} %bitcast.36, f32[5,256,256]{2,1,0:T(8,128)} %pad_maximum_fusion.1.data_ref, f32[2,128,256]{2,1,0:T(8,128)} %reshape.90.refs_0_.wrow_ref, f32[2,256,128]{2,1,0:T(8,128)} %reshape.95.refs_1_.wcol_ref, ...), custom_call_target="tpu_custom_call" | custom-call | tf_op jit(solution)/shard_map/pallas_call | solution.py:370
  (30 shorter events, 0.3 us)
Async XLA Ops:
  0.0 15.9 %copy-start = (f32[2,2,128,128]{3,2,1,0:T(8,128)S(1)}, f32[2,2,128,128]{3,2,1,0:T(8,128)}, u32[]{:S(2)}) copy-start(f32[2,2,128,128]{3,2,1,0:T(8,128)} %param.6) | copy-start | bytes 786436
  0.0 15.9 %copy-start.2 = (f32[128,128]{1,0:T(8,128)S(1)}, f32[128,128]{1,0:T(8,128)}, u32[]{:S(2)}) copy-start(f32[128,128]{1,0:T(8,128)} %param.7) | copy-start | bytes 196612
  0.0 8.9 %copy-start.7 = (s32[1,1,4]{2,1,0:T(1,128)S(1)}, s32[1,1,4]{2,1,0:T(1,128)}, u32[]{:S(2)}) copy-start(s32[1,1,4]{2,1,0:T(1,128)} %param.10) | copy-start | bytes 52
  0.0 12.1 %copy-start.4 = (f32[2,2,64,64]{3,2,1,0:T(8,128)S(1)}, f32[2,2,64,64]{3,2,1,0:T(8,128)}, u32[]{:S(2)}) copy-start(f32[2,2,64,64]{3,2,1,0:T(8,128)} %param.8) | copy-start | bytes 196612
  2.0 10.2 %collective-permute-start = (f32[6,64,128]{2,1,0:T(8,128)S(1)}, f32[6,64,128]{2,1,0:T(8,128)S(1)}, u32[]{:S(2)}, u32[]{:S(2)}) collective-permute-start(f32[6,64,128]{2,1,0:T(8,128)S(1)} %pad_maximum_fusion.7), channel_id=1, source_target_pairs={{0,16},{16,32},{32,48},{48,64},{64,80},{80,96},{96,112},{1,17},{17... | collective-permute-start | bytes 589832 | tf_op jit(solution)/shard_map/ppermute | solution.py:195
  6.8 9.2 %collective-permute-start.1 = (f32[6,64,128]{2,1,0:T(8,128)S(1)}, f32[6,64,128]{2,1,0:T(8,128)S(1)}, u32[]{:S(2)}, u32[]{:S(2)}) collective-permute-start(f32[6,64,128]{2,1,0:T(8,128)S(1)} %fusion), channel_id=1, source_target_pairs={{16,0},{32,16},{48,32},{64,48},{80,64},{96,80},{112,96},{17,1},{33... | collective-permute-start | bytes 589832 | tf_op jit(solution)/shard_map/ppermute | solution.py:195
  15.9 0.7 copy-start.5
  16.9 10.4 %slice-start = ((f32[6,64,128]{2,1,0:T(8,128)}), f32[1,64,128]{2,1,0:T(8,128)S(1)}, s32[]{:S(2)}) async-start(f32[6,64,128]{2,1,0:T(8,128)} %copy-done.5), calls=%async_computation | async-start | bytes 65536 | tf_op jit(solution)/shard_map/slice | solution.py:421
  16.9 10.5 %copy-start.3 = (f32[2,2,64,64]{3,2,1,0:T(8,128)S(1)}, f32[2,2,64,64]{3,2,1,0:T(8,128)}, u32[]{:S(2)}) copy-start(f32[2,2,64,64]{3,2,1,0:T(8,128)} %param.9) | copy-start | bytes 196612
  16.9 12.8 %collective-permute-start.2 = (f32[6,256,64]{1,2,0:T(8,128)S(1)}, f32[6,256,64]{1,2,0:T(8,128)S(1)}, u32[]{:S(2)}, u32[]{:S(2)}) collective-permute-start(f32[6,256,64]{1,2,0:T(8,128)S(1)} %copy.11), channel_id=1, source_target_pairs={{0,1},{1,2},{2,3},{3,4},{4,5},{5,6},{6,7},{7,8},{8,9},{9,10},{10,1... | collective-permute-start | bytes 1179656 | tf_op jit(solution)/shard_map/ppermute | solution.py:195
  19.3 12.5 %collective-permute-start.3 = (f32[6,256,64]{1,2,0:T(8,128)S(1)}, f32[6,256,64]{1,2,0:T(8,128)}, u32[]{:S(2)}, u32[]{:S(2)}) collective-permute-start(f32[6,256,64]{1,2,0:T(8,128)S(1)} %copy.13), channel_id=1, source_target_pairs={{1,0},{2,1},{3,2},{4,3},{5,4},{6,5},{7,6},{8,7},{9,8},{10,9},{11,1... | collective-permute-start | bytes 1179656 | tf_op jit(solution)/shard_map/ppermute | solution.py:195
  49.1 7.8 %collective-permute-start.4 = (f32[2,2,72,128]{3,2,1,0:T(8,128)}, f32[2,2,72,128]{3,2,1,0:T(8,128)S(1)}, u32[]{:S(2)}, u32[]{:S(2)}) collective-permute-start(f32[2,2,72,128]{3,2,1,0:T(8,128)} %get-tuple-element.8), channel_id=1, source_target_pairs={{0,16},{16,32},{32,48},{48,64},{64,80},{80,96},{96,112},{1,17},{17... | collective-permute-start | bytes 442376 | tf_op jit(solution)/shard_map/ppermute | solution.py:440
  52.7 8.1 %collective-permute-start.5 = (f32[2,2,72,128]{3,2,1,0:T(8,128)}, f32[2,2,72,128]{3,2,1,0:T(8,128)S(1)}, u32[]{:S(2)}, u32[]{:S(2)}) collective-permute-start(f32[2,2,72,128]{3,2,1,0:T(8,128)} %get-tuple-element.10), channel_id=1, source_target_pairs={{16,0},{32,16},{48,32},{64,48},{80,64},{96,80},{112,96},{17,1},{33... | collective-permute-start | bytes 442376 | tf_op jit(solution)/shard_map/ppermute | solution.py:441
  62.3 15.2 %copy-start.1 = (f32[2,2,128,128]{3,2,1,0:T(8,128)S(1)}, f32[2,2,128,128]{3,2,1,0:T(8,128)}, u32[]{:S(2)}) copy-start(f32[2,2,128,128]{3,2,1,0:T(8,128)} %get-tuple-element.9.refs_0_) | copy-start | bytes 786436
  62.3 12.9 %collective-permute-start.6 = (f32[2,2,258,65]{2,1,3,0:T(2,128)S(1)}, f32[2,2,258,65]{2,1,3,0:T(2,128)S(1)}, u32[]{:S(2)}, u32[]{:S(2)}) collective-permute-start(f32[2,2,258,65]{2,1,3,0:T(2,128)S(1)} %copy.19), channel_id=1, source_target_pairs={{0,1},{1,2},{2,3},{3,4},{4,5},{5,6},{6,7},{7,8},{8,9},{9,10},{10,1... | collective-permute-start | bytes 804968 | tf_op jit(solution)/shard_map/ppermute | solution.py:195
  64.7 12.6 %collective-permute-start.7 = (f32[2,2,258,65]{2,1,3,0:T(2,128)S(1)}, f32[2,2,258,65]{2,1,3,0:T(2,128)S(1)}, u32[]{:S(2)}, u32[]{:S(2)}) collective-permute-start(f32[2,2,258,65]{2,1,3,0:T(2,128)S(1)} %copy.20), channel_id=1, source_target_pairs={{1,0},{2,1},{3,2},{4,3},{5,4},{6,5},{7,6},{8,7},{9,8},{10,9},{11,1... | collective-permute-start | bytes 804968 | tf_op jit(solution)/shard_map/ppermute | solution.py:195
  79.3 0.7 copy-start.6

commit v13 on v12

--- a/solution.py
+++ b/solution.py
@@ -442,7 +442,8 @@
             tall = jnp.concatenate([before, solution, after], axis=2)
             left, right = exchange_axis(tall, "gy", 3, width)
             padded = jnp.concatenate([left, tall, right], axis=3)
-            padded = grid_ghost(padded, width, edges, signs)
+            on_edge = edges[0] | edges[1] | edges[2] | edges[3]
+            padded = lax.cond(on_edge, lambda v: grid_ghost(v, width, edges, signs), lambda v: v, padded)
             tile_rows = -(-padded.shape[2] // 8) * 8 - padded.shape[2]
             tile_cols = -(-padded.shape[3] // 128) * 128 - padded.shape[3]
             padded = jnp.pad(padded, ((0, 0), (0, 0), (0, tile_rows), (0, tile_cols)))

time: 98.1 us -> 98.7 us (level)
  the two profiles are of different devices: /device:TPU:6 before, /device:TPU:97 now
where the time goes in v13:
time: 98.7 us; the launch traced here: 98.1 us
  waiting for transfers between devices  28.6 us (29%)
  Pallas kernels  26 us (26%)
  starting transfers between devices  20.5 us (21%)
  local copies, waits for them, and re-layouts  11.5 us (12%)
  other arithmetic  8.16 us (8%)
  between operations  2.96 us (3%)
    pallas_call x2, Pallas kernels, solve_local_kernel(): pl.pallas_call(kernel, out_shape=[jax.ShapeDtypeStruct(s, dtype) for s in...  26 us
    ppermute x6, waiting for transfers between devices, exchange_axis(): return (lax.ppermute(last, axis, up), lax.ppermute(first, axis, down))  23.3 us
    ppermute x6, starting transfers between devices, exchange_axis(): return (lax.ppermute(last, axis, up), lax.ppermute(first, axis, down))  16.8 us
    ppermute x1, waiting for transfers between devices, shards(): after = lax.ppermute(top, 'gx', down)[:, :, :width]  4.23 us
    ppermute x1, starting transfers between devices, shards(): before = lax.ppermute(bottom, 'gx', up)[:, :, slab - width:]  2.38 us
  transfers between devices with their start and end apart: 8, of which 7 were waited for; matrix products, arithmetic and copies ran while one was open for 5% of the time, Pallas kernels for 0%

profile of v13, /device:TPU:97, one launch (start us, length us, event | category | flops | bytes accessed | tf_op | source)
XLA Modules:
  0.0 98.1 jit_solution(5949443996312237817)
XLA Ops:
  0.0 0.9 fusion.11
  1.0 0.1 reshape_squeeze.12
  1.0 0.9 fusion.6
  2.0 3.1 %collective-permute-start = (f32[6,64,128]{2,1,0:T(8,128)S(1)}, f32[6,64,128]{2,1,0:T(8,128)S(1)}, u32[]{:S(2)}, u32[]{:S(2)}) collective-permute-start(f32[6,64,128]{2,1,0:T(8,128)S(1)} %pad_maximum_fusion.7), channel_id=1, source_target_pairs={{0,16},{16,32},{32,48},{48,64},{64,80},{80,96},{96,112},{1,17},{17... | collective-permute-start | bytes 589832 | tf_op jit(solution)/shard_map/ppermute | solution.py:195
  5.1 0.1 reshape_squeeze.13
  5.2 0.9 fusion.5
  6.1 1.3 %collective-permute-start.1 = (f32[6,64,128]{2,1,0:T(8,128)S(1)}, f32[6,64,128]{2,1,0:T(8,128)S(1)}, u32[]{:S(2)}, u32[]{:S(2)}) collective-permute-start(f32[6,64,128]{2,1,0:T(8,128)S(1)} %fusion.5), channel_id=1, source_target_pairs={{16,0},{32,16},{48,32},{64,48},{80,64},{96,80},{112,96},{17,1},{33... | collective-permute-start | bytes 589832 | tf_op jit(solution)/shard_map/ppermute | solution.py:195
  7.5 0.7 fusion.12
  10.8 0.0 collective-permute-done
  10.8 4.2 %collective-permute-done.1 = f32[6,64,128]{2,1,0:T(8,128)S(1)} collective-permute-done((f32[6,64,128]{2,1,0:T(8,128)S(1)}, f32[6,64,128]{2,1,0:T(8,128)S(1)}, u32[]{:S(2)}, u32[]{:S(2)}) %collective-permute-start.1) | collective-permute-done | bytes 196640 | tf_op jit(solution)/shard_map/ppermute | solution.py:195
  15.1 0.2 fusion.8
  15.3 0.3 copy-done.5
  15.7 0.1 select_maximum_fusion.1
  15.7 0.2 copy.18
  16.0 0.0 slice-start
  16.0 0.0 copy-start.3
  16.0 4.7 %collective-permute-start.2 = (f32[6,256,64]{1,2,0:T(8,128)S(1)}, f32[6,256,64]{1,2,0:T(8,128)S(1)}, u32[]{:S(2)}, u32[]{:S(2)}) collective-permute-start(f32[6,256,64]{1,2,0:T(8,128)S(1)} %copy.18), channel_id=1, source_target_pairs={{0,1},{1,2},{2,3},{3,4},{4,5},{5,6},{6,7},{7,8},{8,9},{9,10},{10,1... | collective-permute-start | bytes 1179656 | tf_op jit(solution)/shard_map/ppermute | solution.py:195
  20.7 0.1 select_maximum_fusion
  20.8 0.2 copy.20
  21.1 1.9 %collective-permute-start.3 = (f32[6,256,64]{1,2,0:T(8,128)S(1)}, f32[6,256,64]{1,2,0:T(8,128)}, u32[]{:S(2)}, u32[]{:S(2)}) collective-permute-start(f32[6,256,64]{1,2,0:T(8,128)S(1)} %copy.20), channel_id=1, source_target_pairs={{1,0},{2,1},{3,2},{4,3},{5,4},{6,5},{7,6},{8,7},{9,8},{10,9},{11,1... | collective-permute-start | bytes 1179656 | tf_op jit(solution)/shard_map/ppermute | solution.py:195
  23.0 0.6 pad_add_fusion.rect_ref
  23.6 0.1 reshape.92
  23.7 0.1 reshape.93
  23.8 0.3 multiply_bitcast_fusion
  24.1 1.0 %reshape.96.refs_1_.wcol_ref = f32[2,256,128]{2,1,0:T(8,128)} reshape(f32[2,2,2,64,2,64]{5,4,3,2,1,0:T(2,128)S(1)} %multiply_bitcast_fusion) | data formatting | bytes 524288 | tf_op jit(solution)/shard_map/reshape | solution.py:343
  25.1 0.4 collective-permute-done.2
  25.5 0.2 copy.34
  25.7 8.2 %collective-permute-done.3 = f32[6,256,64]{1,2,0:T(8,128)} collective-permute-done((f32[6,256,64]{1,2,0:T(8,128)S(1)}, f32[6,256,64]{1,2,0:T(8,128)}, u32[]{:S(2)}, u32[]{:S(2)}) %collective-permute-start.3) | collective-permute-done | bytes 393248 | tf_op jit(solution)/shard_map/ppermute | solution.py:195
  33.9 1.0 %slice.135 = f32[5,256,64]{1,2,0:T(8,128)S(1)} slice(f32[6,256,64]{1,2,0:T(8,128)} %collective-permute-done.3), slice={[0:5], [0:256], [0:64]} | slice | bytes 655360 | tf_op jit(solution)/shard_map/slice | solution.py:415
  34.9 0.2 copy.35
  35.1 0.1 copy.30
  35.2 0.8 slice.137
  36.0 0.1 copy.31
  36.1 0.2 copy.24
  36.3 0.2 multiply_bitcast_fusion.1
  36.5 1.2 %reshape.91.refs_0_.wrow_ref = f32[2,128,256]{2,1,0:T(8,128)} reshape(f32[2,2,64,2,2,64]{5,4,3,2,1,0:T(2,128)S(1)} %multiply_bitcast_fusion.1) | data formatting | bytes 524288 | tf_op jit(solution)/shard_map/reshape | solution.py:341
  37.7 1.6 %pad_maximum_fusion.1.data_ref = f32[5,256,256]{2,1,0:T(8,128)} fusion(f32[5,256,64]{2,1,0:T(8,128)S(1)} %copy.35, f32[5,64,128]{2,1,0:T(8,128)S(1)} %slice.131, f32[1,128,128]{2,1,0:T(8,128)S(1)} %bitcast.44, f32[4,128,128]{2,1,0:T(8,128)S(1)} %bitcast.40, f32[5,64,128]{2,1,0:T(8,128)S(1)} %slice.130, f32[5,256,64]{2,1,0:T(8,128)S(1)} %copy.34), kind=kLoop, calls=%fused_computation.18 | loop fusion | flops 1638400 | bytes 2621440 | tf_op jit(solution)/shard_map/concatenate | solution.py:415
  39.3 11.8 %shard_map.66 = (f32[2,2,128,128]{3,2,1,0:T(8,128)}, f32[2,2,72,128]{3,2,1,0:T(8,128)}, f32[2,2,72,128]{3,2,1,0:T(8,128)}) custom-call(s32[4]{0:T(128)} %pad_add_fusion.rect_ref, f32[5,256,256]{2,1,0:T(8,128)} %pad_maximum_fusion.1.data_ref, f32[2,128,256]{2,1,0:T(8,128)} %reshape.91.refs_0_.wrow_ref, f32[2,256,128]{2,1,0:T(8,128)} %reshape.96.refs_1_.wcol_ref), custom_call_target="tpu_custom_call" | custom-call | tf_op jit(solution)/shard_map/pallas_call | solution.py:370
  51.1 2.4 %collective-permute-start.4 = (f32[2,2,72,128]{3,2,1,0:T(8,128)}, f32[2,2,72,128]{3,2,1,0:T(8,128)S(1)}, u32[]{:S(2)}, u32[]{:S(2)}) collective-permute-start(f32[2,2,72,128]{3,2,1,0:T(8,128)} %get-tuple-element.37), channel_id=1, source_target_pairs={{0,16},{16,32},{32,48},{48,64},{64,80},{80,96},{96,112},{1,17},{17... | collective-permute-start | bytes 442376 | tf_op jit(solution)/shard_map/ppermute | solution.py:440
  53.5 1.3 %collective-permute-start.5 = (f32[2,2,72,128]{3,2,1,0:T(8,128)}, f32[2,2,72,128]{3,2,1,0:T(8,128)S(1)}, u32[]{:S(2)}, u32[]{:S(2)}) collective-permute-start(f32[2,2,72,128]{3,2,1,0:T(8,128)} %get-tuple-element.39), channel_id=1, source_target_pairs={{16,0},{32,16},{48,32},{64,48},{80,64},{96,80},{112,96},{17,1},{33... | collective-permute-start | bytes 442376 | tf_op jit(solution)/shard_map/ppermute | solution.py:441
  54.8 1.1 %collective-permute-done.4 = f32[2,2,72,128]{3,2,1,0:T(8,128)S(1)} collective-permute-done((f32[2,2,72,128]{3,2,1,0:T(8,128)}, f32[2,2,72,128]{3,2,1,0:T(8,128)S(1)}, u32[]{:S(2)}, u32[]{:S(2)}) %collective-permute-start.4) | collective-permute-done | bytes 147488 | tf_op jit(solution)/shard_map/ppermute | solution.py:440
  55.9 4.2 %collective-permute-done.5 = f32[2,2,72,128]{3,2,1,0:T(8,128)S(1)} collective-permute-done((f32[2,2,72,128]{3,2,1,0:T(8,128)}, f32[2,2,72,128]{3,2,1,0:T(8,128)S(1)}, u32[]{:S(2)}, u32[]{:S(2)}) %collective-permute-start.5) | collective-permute-done | bytes 147488 | tf_op jit(solution)/shard_map/ppermute | solution.py:441
  60.1 1.0 %pad_maximum_fusion.3 = f32[2,2,258,128]{3,2,1,0:T(8,128)S(1)} fusion(f32[2,2,65,128]{3,2,1,0:T(8,128)S(1)} %bitcast.47, f32[2,2,128,128]{3,2,1,0:T(8,128)} %get-tuple-element.38.refs_0_, f32[2,2,65,128]{3,2,1,0:T(8,128)S(1)} %slice.140), kind=kLoop, calls=%fused_computation.23 | loop fusion | flops 264192 | bytes 1056768 | tf_op jit(solution)/shard_map/concatenate | solution.py:442
  61.1 0.2 fusion.9
  61.3 0.3 copy.26
  61.6 3.9 %collective-permute-start.6 = (f32[2,2,258,65]{2,1,3,0:T(2,128)S(1)}, f32[2,2,258,65]{2,1,3,0:T(2,128)S(1)}, u32[]{:S(2)}, u32[]{:S(2)}) collective-permute-start(f32[2,2,258,65]{2,1,3,0:T(2,128)S(1)} %copy.26), channel_id=1, source_target_pairs={{0,1},{1,2},{2,3},{3,4},{4,5},{5,6},{6,7},{7,8},{8,9},{9,10},{10,1... | collective-permute-start | bytes 804968 | tf_op jit(solution)/shard_map/ppermute | solution.py:195
  65.5 0.3 copy.27
  65.8 1.9 %collective-permute-start.7 = (f32[2,2,258,65]{2,1,3,0:T(2,128)S(1)}, f32[2,2,258,65]{2,1,3,0:T(2,128)S(1)}, u32[]{:S(2)}, u32[]{:S(2)}) collective-permute-start(f32[2,2,258,65]{2,1,3,0:T(2,128)S(1)} %copy.27), channel_id=1, source_target_pairs={{1,0},{2,1},{3,2},{4,3},{5,4},{6,5},{7,6},{8,7},{9,8},{10,9},{11,1... | collective-permute-start | bytes 804968 | tf_op jit(solution)/shard_map/ppermute | solution.py:195
  67.8 2.5 %collective-permute-done.6 = f32[2,2,258,65]{2,1,3,0:T(2,128)S(1)} collective-permute-done((f32[2,2,258,65]{2,1,3,0:T(2,128)S(1)}, f32[2,2,258,65]{2,1,3,0:T(2,128)S(1)}, u32[]{:S(2)}, u32[]{:S(2)}) %collective-permute-start.6) | collective-permute-done | bytes 268352 | tf_op jit(solution)/shard_map/ppermute | solution.py:195
  70.3 0.3 copy.28
  70.6 8.0 %collective-permute-done.7 = f32[2,2,258,65]{2,1,3,0:T(2,128)S(1)} collective-permute-done((f32[2,2,258,65]{2,1,3,0:T(2,128)S(1)}, f32[2,2,258,65]{2,1,3,0:T(2,128)S(1)}, u32[]{:S(2)}, u32[]{:S(2)}) %collective-permute-start.7) | collective-permute-done | bytes 268352 | tf_op jit(solution)/shard_map/ppermute | solution.py:195
  78.6 0.3 copy.29
  78.9 0.6 pad_maximum_fusion
  79.5 3.0 %conditional.1 = (f32[2,2,258,258]{3,2,1,0:T(8,128)S(1)}) conditional(s32[]{:T(128)} %convert_element_type.9, f32[2,2,258,258]{3,2,1,0:T(8,128)S(1)} %pad_maximum_fusion, (pred[]{:T(512)}, pred[]{:T(512)}, pred[]{:T(512)}, pred[]{:T(512)}, f32[2,2,258,258]{3,2,1,0:T(8,128)S(1)}) %tuple.26), branch_computations={%region_0.1_spmd, %region_1.2_spmd.clone} | conditional | flops 3863550 | bytes 9813886 | solution.py:446
  79.8 0.2 select_select_fusion.1
  80.0 0.8 slice_reduce_fusion.1
  80.8 0.0 copy-start.6
  80.9 0.4 select_select_fusion
  81.3 0.2 copy-done.6
  81.5 0.2 multiply_add_fusion
  81.7 0.1 or_or_fusion
  81.9 0.7 maximum_select_fusion
  82.5 1.3 %pad.23 = f32[2,2,264,384]{3,2,1,0:T(8,128)} pad(f32[2,2,258,258]{3,2,1,0:T(8,128)S(1)} %get-tuple-element.58, f32[]{:T(128)} %constant.32.clone.1), padding=0_0x0_0x0_6x0_126 | pad | bytes 2687044 | tf_op jit(solution)/shard_map/jit(_pad)/pad | solution.py:449
  83.8 14.2 %shard_map.67 = f32[2,2,128,128]{3,2,1,0:T(8,128)} custom-call(s32[4]{0:T(128)} %pad_add_fusion.rect_ref, f32[4,264,384]{2,1,0:T(8,128)} %bitcast.36, f32[5,256,256]{2,1,0:T(8,128)} %pad_maximum_fusion.1.data_ref, f32[2,128,256]{2,1,0:T(8,128)} %reshape.91.refs_0_.wrow_ref, f32[2,256,128]{2,1,0:T(8,128)} %reshape.96.refs_1_.wcol_ref, ...), custom_call_target="tpu_custom_call" | custom-call | tf_op jit(solution)/shard_map/pallas_call | solution.py:370
  (31 shorter events, 0.3 us)
Async XLA Ops:
  0.0 15.0 %copy-start = (f32[2,2,128,128]{3,2,1,0:T(8,128)S(1)}, f32[2,2,128,128]{3,2,1,0:T(8,128)}, u32[]{:S(2)}) copy-start(f32[2,2,128,128]{3,2,1,0:T(8,128)} %param.8) | copy-start | bytes 786436
  0.0 15.0 %copy-start.2 = (f32[128,128]{1,0:T(8,128)S(1)}, f32[128,128]{1,0:T(8,128)}, u32[]{:S(2)}) copy-start(f32[128,128]{1,0:T(8,128)} %param.9) | copy-start | bytes 196612
  0.0 7.4 %copy-start.7 = (s32[1,1,4]{2,1,0:T(1,128)S(1)}, s32[1,1,4]{2,1,0:T(1,128)}, u32[]{:S(2)}) copy-start(s32[1,1,4]{2,1,0:T(1,128)} %param.12) | copy-start | bytes 52
  0.0 10.7 %copy-start.4 = (f32[2,2,64,64]{3,2,1,0:T(8,128)S(1)}, f32[2,2,64,64]{3,2,1,0:T(8,128)}, u32[]{:S(2)}) copy-start(f32[2,2,64,64]{3,2,1,0:T(8,128)} %param.10) | copy-start | bytes 196612
  2.0 8.8 %collective-permute-start = (f32[6,64,128]{2,1,0:T(8,128)S(1)}, f32[6,64,128]{2,1,0:T(8,128)S(1)}, u32[]{:S(2)}, u32[]{:S(2)}) collective-permute-start(f32[6,64,128]{2,1,0:T(8,128)S(1)} %pad_maximum_fusion.7), channel_id=1, source_target_pairs={{0,16},{16,32},{32,48},{48,64},{64,80},{80,96},{96,112},{1,17},{17... | collective-permute-start | bytes 589832 | tf_op jit(solution)/shard_map/ppermute | solution.py:195
  6.1 8.9 %collective-permute-start.1 = (f32[6,64,128]{2,1,0:T(8,128)S(1)}, f32[6,64,128]{2,1,0:T(8,128)S(1)}, u32[]{:S(2)}, u32[]{:S(2)}) collective-permute-start(f32[6,64,128]{2,1,0:T(8,128)S(1)} %fusion.5), channel_id=1, source_target_pairs={{16,0},{32,16},{48,32},{64,48},{80,64},{96,80},{112,96},{17,1},{33... | collective-permute-start | bytes 589832 | tf_op jit(solution)/shard_map/ppermute | solution.py:195
  15.0 0.7 copy-start.5
  16.0 7.7 %slice-start = ((f32[6,64,128]{2,1,0:T(8,128)}), f32[1,64,128]{2,1,0:T(8,128)S(1)}, s32[]{:S(2)}) async-start(f32[6,64,128]{2,1,0:T(8,128)} %copy-done.5), calls=%async_computation | async-start | bytes 65536 | tf_op jit(solution)/shard_map/slice | solution.py:421
  16.0 7.8 %copy-start.3 = (f32[2,2,64,64]{3,2,1,0:T(8,128)S(1)}, f32[2,2,64,64]{3,2,1,0:T(8,128)}, u32[]{:S(2)}) copy-start(f32[2,2,64,64]{3,2,1,0:T(8,128)} %param.11) | copy-start | bytes 196612
  16.0 9.4 %collective-permute-start.2 = (f32[6,256,64]{1,2,0:T(8,128)S(1)}, f32[6,256,64]{1,2,0:T(8,128)S(1)}, u32[]{:S(2)}, u32[]{:S(2)}) collective-permute-start(f32[6,256,64]{1,2,0:T(8,128)S(1)} %copy.18), channel_id=1, source_target_pairs={{0,1},{1,2},{2,3},{3,4},{4,5},{5,6},{6,7},{7,8},{8,9},{9,10},{10,1... | collective-permute-start | bytes 1179656 | tf_op jit(solution)/shard_map/ppermute | solution.py:195
  21.1 12.8 %collective-permute-start.3 = (f32[6,256,64]{1,2,0:T(8,128)S(1)}, f32[6,256,64]{1,2,0:T(8,128)}, u32[]{:S(2)}, u32[]{:S(2)}) collective-permute-start(f32[6,256,64]{1,2,0:T(8,128)S(1)} %copy.20), channel_id=1, source_target_pairs={{1,0},{2,1},{3,2},{4,3},{5,4},{6,5},{7,6},{8,7},{9,8},{10,9},{11,1... | collective-permute-start | bytes 1179656 | tf_op jit(solution)/shard_map/ppermute | solution.py:195
  51.1 4.8 %collective-permute-start.4 = (f32[2,2,72,128]{3,2,1,0:T(8,128)}, f32[2,2,72,128]{3,2,1,0:T(8,128)S(1)}, u32[]{:S(2)}, u32[]{:S(2)}) collective-permute-start(f32[2,2,72,128]{3,2,1,0:T(8,128)} %get-tuple-element.37), channel_id=1, source_target_pairs={{0,16},{16,32},{32,48},{48,64},{64,80},{80,96},{96,112},{1,17},{17... | collective-permute-start | bytes 442376 | tf_op jit(solution)/shard_map/ppermute | solution.py:440
  53.5 6.6 %collective-permute-start.5 = (f32[2,2,72,128]{3,2,1,0:T(8,128)}, f32[2,2,72,128]{3,2,1,0:T(8,128)S(1)}, u32[]{:S(2)}, u32[]{:S(2)}) collective-permute-start(f32[2,2,72,128]{3,2,1,0:T(8,128)} %get-tuple-element.39), channel_id=1, source_target_pairs={{16,0},{32,16},{48,32},{64,48},{80,64},{96,80},{112,96},{17,1},{33... | collective-permute-start | bytes 442376 | tf_op jit(solution)/shard_map/ppermute | solution.py:441
  61.6 17.2 %copy-start.1 = (f32[2,2,128,128]{3,2,1,0:T(8,128)S(1)}, f32[2,2,128,128]{3,2,1,0:T(8,128)}, u32[]{:S(2)}) copy-start(f32[2,2,128,128]{3,2,1,0:T(8,128)} %get-tuple-element.38.refs_0_) | copy-start | bytes 786436
  61.6 8.6 %collective-permute-start.6 = (f32[2,2,258,65]{2,1,3,0:T(2,128)S(1)}, f32[2,2,258,65]{2,1,3,0:T(2,128)S(1)}, u32[]{:S(2)}, u32[]{:S(2)}) collective-permute-start(f32[2,2,258,65]{2,1,3,0:T(2,128)S(1)} %copy.26), channel_id=1, source_target_pairs={{0,1},{1,2},{2,3},{3,4},{4,5},{5,6},{6,7},{7,8},{8,9},{9,10},{10,1... | collective-permute-start | bytes 804968 | tf_op jit(solution)/shard_map/ppermute | solution.py:195
  65.8 12.8 %collective-permute-start.7 = (f32[2,2,258,65]{2,1,3,0:T(2,128)S(1)}, f32[2,2,258,65]{2,1,3,0:T(2,128)S(1)}, u32[]{:S(2)}, u32[]{:S(2)}) collective-permute-start(f32[2,2,258,65]{2,1,3,0:T(2,128)S(1)} %copy.27), channel_id=1, source_target_pairs={{1,0},{2,1},{3,2},{4,3},{5,4},{6,5},{7,6},{8,7},{9,8},{10,9},{11,1... | collective-permute-start | bytes 804968 | tf_op jit(solution)/shard_map/ppermute | solution.py:195
  80.8 0.7 copy-start.6

commit v14 on v12

--- a/solution.py
+++ b/solution.py
@@ -286,15 +286,27 @@
         mass_i = imag_part + sign * DAMPING * real_part
         return (-lap_r - wave * mass_r, -lap_i - wave * mass_i)
 
-    def dot(a, b):
-        return jnp.dot(a, b, precision=lax.Precision.HIGH, preferred_element_type=jnp.float32)
+    def split(x):
+        high = x.astype(jnp.bfloat16)
+        return high, (x - high.astype(jnp.float32)).astype(jnp.bfloat16)
+
+    def bdot(a, b):
+        return jnp.dot(a, b, preferred_element_type=jnp.float32)
+
+    def dot_w(x, w_ref, h):
+        x_hi, x_lo = split(x)
+        return bdot(x_hi, w_ref[0, h]) + (bdot(x_hi, w_ref[1, h]) + bdot(x_lo, w_ref[0, h]))
+
+    def w_dot(w_ref, h, x):
+        x_hi, x_lo = split(x)
+        return bdot(w_ref[0, h], x_hi) + (bdot(w_ref[1, h], x_hi) + bdot(w_ref[0, h], x_lo))
 
     def rows_apply(real_part, imag_part, sign):
         outs_r, outs_i = ([], [])
         for h in range(breadth // half):
             cols = slice(h * half, (h + 1) * half)
-            prod_r = dot(real_part[:, cols], wrow_ref[h])
-            prod_i = dot(imag_part[:, cols], wrow_ref[h])
+            prod_r = dot_w(real_part[:, cols], wrow_ref, h)
+            prod_i = dot_w(imag_part[:, cols], wrow_ref, h)
             outs_r.append(prod_r[:, :half] - sign * prod_i[:, half:])
             outs_i.append(prod_i[:, :half] + sign * prod_r[:, half:])
         return (jnp.concatenate(outs_r, axis=1), jnp.concatenate(outs_i, axis=1))
@@ -303,8 +315,8 @@
         outs_r, outs_i = ([], [])
         for h in range(height // half):
             rows = slice(h * half, (h + 1) * half)
-            prod_r = dot(wcol_ref[h], real_part[rows, :])
-            prod_i = dot(wcol_ref[h], imag_part[rows, :])
+            prod_r = w_dot(wcol_ref, h, real_part[rows, :])
+            prod_i = w_dot(wcol_ref, h, imag_part[rows, :])
             outs_r.append(prod_r[:half] - sign * prod_i[half:])
             outs_i.append(prod_i[:half] + sign * prod_r[half:])
         return (jnp.concatenate(outs_r, axis=0), jnp.concatenate(outs_i, axis=0))
@@ -424,6 +436,12 @@
         [left[lead:, :inv_size].reshape(inv_shape), row_inverse, right[lead:, :inv_size].reshape(inv_shape)], axis=0
     )
     row_mats, col_mats = line_matrices(row_blocks, col_blocks)
+
+    def split_parts(mats):
+        high = lax.reduce_precision(mats, exponent_bits=8, mantissa_bits=7)
+        return jnp.stack([high.astype(jnp.bfloat16), (mats - high).astype(jnp.bfloat16)])
+
+    row_mats, col_mats = (split_parts(row_mats), split_parts(col_mats))
     width = block + 1
     edges = (row_rank == 0, row_rank == row_count - 1, col_rank == 0, col_rank == col_count - 1)
     slab = -(-width // 8) * 8

time: 98.1 us -> 98.7 us (level)
  other arithmetic: 7.97 us -> 9.48 us
  local copies, waits for them, and re-layouts: 11.6 us -> 10.1 us
    another operation x1 -> x3, other arithmetic: 0.01 us -> 1.47 us  [the longest x2 1.46 us: split_parts(): jnp.stack([high.astype(jnp.bfloat16), (mats - high).astype(jnp.bfloat16)])]
where the time goes in v14:
time: 98.7 us; the launch traced here: 96.9 us
  starting transfers between devices  30.5 us (31%)
  Pallas kernels  26.5 us (27%)
  waiting for transfers between devices  17.2 us (17%)
  local copies, waits for them, and re-layouts  10.1 us (10%)
  other arithmetic  9.48 us (10%)
  between operations  3.09 us (3%)
    pallas_call x2, Pallas kernels, solve_local_kernel(): pl.pallas_call(kernel, out_shape=[jax.ShapeDtypeStruct(s, dtype) for s in...  26.5 us
    ppermute x6, starting transfers between devices, exchange_axis(): return (lax.ppermute(last, axis, up), lax.ppermute(first, axis, down))  24.6 us
    ppermute x6, waiting for transfers between devices, exchange_axis(): return (lax.ppermute(last, axis, up), lax.ppermute(first, axis, down))  11.4 us
    ppermute x1, waiting for transfers between devices, shards(): after = lax.ppermute(top, 'gx', down)[:, :, :width]  3.89 us
    ppermute x1, starting transfers between devices, shards(): before = lax.ppermute(bottom, 'gx', up)[:, :, slab - width:]  3.57 us
    ppermute x1, starting transfers between devices, shards(): after = lax.ppermute(top, 'gx', down)[:, :, :width]  2.26 us
  transfers between devices with their start and end apart: 8, of which 7 were waited for; matrix products, arithmetic and copies ran while one was open for 5% of the time, Pallas kernels for 0%

profile of v14, /device:TPU:6, one launch (start us, length us, event | category | flops | bytes accessed | tf_op | source)
XLA Modules:
  0.0 96.9 jit_solution(2309569677937053)
XLA Ops:
  0.0 0.9 fusion.13
  1.0 0.1 reshape_squeeze.12
  1.0 0.9 fusion.3
  2.0 3.8 %collective-permute-start = (f32[6,64,128]{2,1,0:T(8,128)S(1)}, f32[6,64,128]{2,1,0:T(8,128)S(1)}, u32[]{:S(2)}, u32[]{:S(2)}) collective-permute-start(f32[6,64,128]{2,1,0:T(8,128)S(1)} %pad_maximum_fusion.9), channel_id=1, source_target_pairs={{0,16},{16,32},{32,48},{48,64},{64,80},{80,96},{96,112},{1,17},{17... | collective-permute-start | bytes 589832 | tf_op jit(solution)/shard_map/ppermute | solution.py:195
  5.7 0.1 reshape_squeeze.13
  5.8 0.9 fusion.2
  6.8 2.1 %collective-permute-start.1 = (f32[6,64,128]{2,1,0:T(8,128)S(1)}, f32[6,64,128]{2,1,0:T(8,128)S(1)}, u32[]{:S(2)}, u32[]{:S(2)}) collective-permute-start(f32[6,64,128]{2,1,0:T(8,128)S(1)} %fusion.2), channel_id=1, source_target_pairs={{16,0},{32,16},{48,32},{64,48},{80,64},{96,80},{112,96},{17,1},{33... | collective-permute-start | bytes 589832 | tf_op jit(solution)/shard_map/ppermute | solution.py:195
  8.9 0.7 fusion.14
  12.2 0.6 pad_add_fusion.rect_ref
  12.9 3.0 %collective-permute-done.1 = f32[6,64,128]{2,1,0:T(8,128)S(1)} collective-permute-done((f32[6,64,128]{2,1,0:T(8,128)S(1)}, f32[6,64,128]{2,1,0:T(8,128)S(1)}, u32[]{:S(2)}, u32[]{:S(2)}) %collective-permute-start.1) | collective-permute-done | bytes 196640 | tf_op jit(solution)/shard_map/ppermute | solution.py:195
  16.0 0.2 fusion.10
  16.2 0.3 copy-done.5
  16.6 0.1 select_maximum_fusion.1
  16.6 0.2 copy.11
  16.9 0.0 slice-start
  16.9 0.0 copy-start.3
  16.9 2.1 %collective-permute-start.2 = (f32[6,256,64]{1,2,0:T(8,128)S(1)}, f32[6,256,64]{1,2,0:T(8,128)S(1)}, u32[]{:S(2)}, u32[]{:S(2)}) collective-permute-start(f32[6,256,64]{1,2,0:T(8,128)S(1)} %copy.11), channel_id=1, source_target_pairs={{0,1},{1,2},{2,3},{3,4},{4,5},{5,6},{6,7},{7,8},{8,9},{9,10},{10,1... | collective-permute-start | bytes 1179656 | tf_op jit(solution)/shard_map/ppermute | solution.py:195
  19.0 0.1 select_maximum_fusion
  19.0 0.2 copy.13
  19.3 7.3 %collective-permute-start.3 = (f32[6,256,64]{1,2,0:T(8,128)S(1)}, f32[6,256,64]{1,2,0:T(8,128)}, u32[]{:S(2)}, u32[]{:S(2)}) collective-permute-start(f32[6,256,64]{1,2,0:T(8,128)S(1)} %copy.13), channel_id=1, source_target_pairs={{1,0},{2,1},{3,2},{4,3},{5,4},{6,5},{7,6},{8,7},{9,8},{10,9},{11,1... | collective-permute-start | bytes 1179656 | tf_op jit(solution)/shard_map/ppermute | solution.py:195
  26.6 0.1 reshape.149
  26.7 0.1 reshape.150
  26.8 0.3 multiply_bitcast_fusion
  27.0 0.3 reshape.153
  27.4 0.7 pad_maximum_fusion.7.refs_1_.wcol_ref
  28.1 1.7 %collective-permute-done.2 = f32[6,256,64]{1,2,0:T(8,128)S(1)} collective-permute-done((f32[6,256,64]{1,2,0:T(8,128)S(1)}, f32[6,256,64]{1,2,0:T(8,128)S(1)}, u32[]{:S(2)}, u32[]{:S(2)}) %collective-permute-start.2) | collective-permute-done | bytes 393248 | tf_op jit(solution)/shard_map/ppermute | solution.py:195
  29.8 0.1 copy.23
  29.9 2.0 %collective-permute-done.3 = f32[6,256,64]{1,2,0:T(8,128)} collective-permute-done((f32[6,256,64]{1,2,0:T(8,128)S(1)}, f32[6,256,64]{1,2,0:T(8,128)}, u32[]{:S(2)}, u32[]{:S(2)}) %collective-permute-start.3) | collective-permute-done | bytes 393248 | tf_op jit(solution)/shard_map/ppermute | solution.py:195
  31.8 0.8 slice.133
  32.6 0.1 copy.24
  32.7 0.2 copy.17
  32.9 0.2 multiply_bitcast_fusion.1
  33.1 0.5 reshape.148
  33.7 0.2 copy.27
  33.9 1.0 %slice.131 = f32[5,256,64]{1,2,0:T(8,128)S(1)} slice(f32[6,256,64]{1,2,0:T(8,128)} %collective-permute-done.3), slice={[0:5], [0:256], [0:64]} | slice | bytes 655360 | tf_op jit(solution)/shard_map/slice | solution.py:427
  34.9 0.2 copy.28
  35.1 0.7 pad_maximum_fusion.5.refs_0_.wrow_ref
  35.9 1.6 %pad_maximum_fusion.1.data_ref = f32[5,256,256]{2,1,0:T(8,128)} fusion(f32[5,256,64]{2,1,0:T(8,128)S(1)} %copy.28, f32[5,64,128]{2,1,0:T(8,128)S(1)} %slice.127, f32[1,128,128]{2,1,0:T(8,128)S(1)} %bitcast.44, f32[4,128,128]{2,1,0:T(8,128)S(1)} %bitcast.40, f32[5,64,128]{2,1,0:T(8,128)S(1)} %slice.126, f32[5,256,64]{2,1,0:T(8,128)S(1)} %copy.27), kind=kLoop, calls=%fused_computation.4 | loop fusion | flops 1638400 | bytes 2621440 | tf_op jit(solution)/shard_map/concatenate | solution.py:427
  37.5 12.0 %shard_map.64 = (f32[2,2,128,128]{3,2,1,0:T(8,128)}, f32[2,2,72,128]{3,2,1,0:T(8,128)}, f32[2,2,72,128]{3,2,1,0:T(8,128)}) custom-call(s32[4]{0:T(128)} %pad_add_fusion.rect_ref, f32[5,256,256]{2,1,0:T(8,128)} %pad_maximum_fusion.1.data_ref, bf16[2,2,128,256]{3,2,1,0:T(8,128)(2,1)} %pad_maximum_fusion.5.refs_0_.wrow_ref, ...), custom_call_target="tpu_custom_call" | custom-call | tf_op jit(solution)/shard_map/pallas_call | solution.py:382
  49.5 3.6 %collective-permute-start.4 = (f32[2,2,72,128]{3,2,1,0:T(8,128)}, f32[2,2,72,128]{3,2,1,0:T(8,128)S(1)}, u32[]{:S(2)}, u32[]{:S(2)}) collective-permute-start(f32[2,2,72,128]{3,2,1,0:T(8,128)} %get-tuple-element.8), channel_id=1, source_target_pairs={{0,16},{16,32},{32,48},{48,64},{64,80},{80,96},{96,112},{1,17},{17... | collective-permute-start | bytes 442376 | tf_op jit(solution)/shard_map/ppermute | solution.py:458
  53.1 2.3 %collective-permute-start.5 = (f32[2,2,72,128]{3,2,1,0:T(8,128)}, f32[2,2,72,128]{3,2,1,0:T(8,128)S(1)}, u32[]{:S(2)}, u32[]{:S(2)}) collective-permute-start(f32[2,2,72,128]{3,2,1,0:T(8,128)} %get-tuple-element.10), channel_id=1, source_target_pairs={{16,0},{32,16},{48,32},{64,48},{80,64},{96,80},{112,96},{17,1},{33... | collective-permute-start | bytes 442376 | tf_op jit(solution)/shard_map/ppermute | solution.py:459
  55.4 1.9 %collective-permute-done.4 = f32[2,2,72,128]{3,2,1,0:T(8,128)S(1)} collective-permute-done((f32[2,2,72,128]{3,2,1,0:T(8,128)}, f32[2,2,72,128]{3,2,1,0:T(8,128)S(1)}, u32[]{:S(2)}, u32[]{:S(2)}) %collective-permute-start.4) | collective-permute-done | bytes 147488 | tf_op jit(solution)/shard_map/ppermute | solution.py:458
  57.4 3.9 %collective-permute-done.5 = f32[2,2,72,128]{3,2,1,0:T(8,128)S(1)} collective-permute-done((f32[2,2,72,128]{3,2,1,0:T(8,128)}, f32[2,2,72,128]{3,2,1,0:T(8,128)S(1)}, u32[]{:S(2)}, u32[]{:S(2)}) %collective-permute-start.5) | collective-permute-done | bytes 147488 | tf_op jit(solution)/shard_map/ppermute | solution.py:459
  61.2 1.0 %pad_maximum_fusion.3 = f32[2,2,258,128]{3,2,1,0:T(8,128)S(1)} fusion(f32[2,2,65,128]{3,2,1,0:T(8,128)S(1)} %bitcast.47, f32[2,2,128,128]{3,2,1,0:T(8,128)} %get-tuple-element.9.refs_0_, f32[2,2,65,128]{3,2,1,0:T(8,128)S(1)} %slice.136), kind=kLoop, calls=%fused_computation.13 | loop fusion | flops 264192 | bytes 1056768 | tf_op jit(solution)/shard_map/concatenate | solution.py:460
  62.2 0.2 fusion.11
  62.4 0.3 copy.19
  62.8 2.1 %collective-permute-start.6 = (f32[2,2,258,65]{2,1,3,0:T(2,128)S(1)}, f32[2,2,258,65]{2,1,3,0:T(2,128)S(1)}, u32[]{:S(2)}, u32[]{:S(2)}) collective-permute-start(f32[2,2,258,65]{2,1,3,0:T(2,128)S(1)} %copy.19), channel_id=1, source_target_pairs={{0,1},{1,2},{2,3},{3,4},{4,5},{5,6},{6,7},{7,8},{8,9},{9,10},{10,1... | collective-permute-start | bytes 804968 | tf_op jit(solution)/shard_map/ppermute | solution.py:195
  64.8 0.3 copy.20
  65.1 7.4 %collective-permute-start.7 = (f32[2,2,258,65]{2,1,3,0:T(2,128)S(1)}, f32[2,2,258,65]{2,1,3,0:T(2,128)S(1)}, u32[]{:S(2)}, u32[]{:S(2)}) collective-permute-start(f32[2,2,258,65]{2,1,3,0:T(2,128)S(1)} %copy.20), channel_id=1, source_target_pairs={{1,0},{2,1},{3,2},{4,3},{5,4},{6,5},{7,6},{8,7},{9,8},{10,9},{11,1... | collective-permute-start | bytes 804968 | tf_op jit(solution)/shard_map/ppermute | solution.py:195
  72.6 0.1 or_or_fusion
  72.7 3.0 %collective-permute-done.6 = f32[2,2,258,65]{2,1,3,0:T(2,128)S(1)} collective-permute-done((f32[2,2,258,65]{2,1,3,0:T(2,128)S(1)}, f32[2,2,258,65]{2,1,3,0:T(2,128)S(1)}, u32[]{:S(2)}, u32[]{:S(2)}) %collective-permute-start.6) | collective-permute-done | bytes 268352 | tf_op jit(solution)/shard_map/ppermute | solution.py:195
  75.7 0.3 copy.21
  75.9 1.8 %collective-permute-done.7 = f32[2,2,258,65]{2,1,3,0:T(2,128)S(1)} collective-permute-done((f32[2,2,258,65]{2,1,3,0:T(2,128)S(1)}, f32[2,2,258,65]{2,1,3,0:T(2,128)S(1)}, u32[]{:S(2)}, u32[]{:S(2)}) %collective-permute-start.7) | collective-permute-done | bytes 268352 | tf_op jit(solution)/shard_map/ppermute | solution.py:195
  77.7 0.3 copy.22
  78.0 0.6 pad_maximum_fusion
  78.7 0.2 select_select_fusion.1
  78.9 0.8 slice_reduce_fusion.1
  79.7 0.0 copy-start.6
  79.7 0.4 select_select_fusion
  80.2 0.2 copy-done.6
  80.4 0.2 multiply_add_fusion
  80.6 0.5 maximum_select_fusion
  81.1 1.3 %pad.13 = f32[2,2,264,384]{3,2,1,0:T(8,128)} pad(f32[2,2,258,258]{3,2,1,0:T(8,128)S(1)} %maximum_select_fusion, f32[]{:T(128)} %constant.31.clone.1), padding=0_0x0_0x0_6x0_126 | pad | bytes 2687044 | tf_op jit(solution)/shard_map/jit(_pad)/pad | solution.py:466
  82.4 14.5 %shard_map.65 = f32[2,2,128,128]{3,2,1,0:T(8,128)} custom-call(s32[4]{0:T(128)} %pad_add_fusion.rect_ref, f32[4,264,384]{2,1,0:T(8,128)} %bitcast.36, f32[5,256,256]{2,1,0:T(8,128)} %pad_maximum_fusion.1.data_ref, bf16[2,2,128,256]{3,2,1,0:T(8,128)(2,1)} %pad_maximum_fusion.5.refs_0_.wrow_ref, bf16[2,2,256,128]{3,2,1,0:T(8,128)(2,1)} %pad_maximum_fusion.7.refs_1_.wcol_ref, ...), custom_call_target="tpu_custom_call" | custom-call | tf_op jit(solution)/shard_map/pallas_call | solution.py:382
  (34 shorter events, 0.3 us)
Async XLA Ops:
  0.0 15.9 %copy-start = (f32[2,2,128,128]{3,2,1,0:T(8,128)S(1)}, f32[2,2,128,128]{3,2,1,0:T(8,128)}, u32[]{:S(2)}) copy-start(f32[2,2,128,128]{3,2,1,0:T(8,128)} %param.6) | copy-start | bytes 786436
  0.0 15.9 %copy-start.2 = (f32[128,128]{1,0:T(8,128)S(1)}, f32[128,128]{1,0:T(8,128)}, u32[]{:S(2)}) copy-start(f32[128,128]{1,0:T(8,128)} %param.7) | copy-start | bytes 196612
  0.0 8.9 %copy-start.7 = (s32[1,1,4]{2,1,0:T(1,128)S(1)}, s32[1,1,4]{2,1,0:T(1,128)}, u32[]{:S(2)}) copy-start(s32[1,1,4]{2,1,0:T(1,128)} %param.10) | copy-start | bytes 52
  0.0 12.8 %copy-start.4 = (f32[2,2,64,64]{3,2,1,0:T(8,128)S(1)}, f32[2,2,64,64]{3,2,1,0:T(8,128)}, u32[]{:S(2)}) copy-start(f32[2,2,64,64]{3,2,1,0:T(8,128)} %param.8) | copy-start | bytes 196612
  2.0 10.9 %collective-permute-start = (f32[6,64,128]{2,1,0:T(8,128)S(1)}, f32[6,64,128]{2,1,0:T(8,128)S(1)}, u32[]{:S(2)}, u32[]{:S(2)}) collective-permute-start(f32[6,64,128]{2,1,0:T(8,128)S(1)} %pad_maximum_fusion.9), channel_id=1, source_target_pairs={{0,16},{16,32},{32,48},{48,64},{64,80},{80,96},{96,112},{1,17},{17... | collective-permute-start | bytes 589832 | tf_op jit(solution)/shard_map/ppermute | solution.py:195
  6.8 9.2 %collective-permute-start.1 = (f32[6,64,128]{2,1,0:T(8,128)S(1)}, f32[6,64,128]{2,1,0:T(8,128)S(1)}, u32[]{:S(2)}, u32[]{:S(2)}) collective-permute-start(f32[6,64,128]{2,1,0:T(8,128)S(1)} %fusion.2), channel_id=1, source_target_pairs={{16,0},{32,16},{48,32},{64,48},{80,64},{96,80},{112,96},{17,1},{33... | collective-permute-start | bytes 589832 | tf_op jit(solution)/shard_map/ppermute | solution.py:195
  15.9 0.7 copy-start.5
  16.9 9.8 %slice-start = ((f32[6,64,128]{2,1,0:T(8,128)}), f32[1,64,128]{2,1,0:T(8,128)S(1)}, s32[]{:S(2)}) async-start(f32[6,64,128]{2,1,0:T(8,128)} %copy-done.5), calls=%async_computation | async-start | bytes 65536 | tf_op jit(solution)/shard_map/slice | solution.py:433
  16.9 9.8 %copy-start.3 = (f32[2,2,64,64]{3,2,1,0:T(8,128)S(1)}, f32[2,2,64,64]{3,2,1,0:T(8,128)}, u32[]{:S(2)}) copy-start(f32[2,2,64,64]{3,2,1,0:T(8,128)} %param.9) | copy-start | bytes 196612
  16.9 12.8 %collective-permute-start.2 = (f32[6,256,64]{1,2,0:T(8,128)S(1)}, f32[6,256,64]{1,2,0:T(8,128)S(1)}, u32[]{:S(2)}, u32[]{:S(2)}) collective-permute-start(f32[6,256,64]{1,2,0:T(8,128)S(1)} %copy.11), channel_id=1, source_target_pairs={{0,1},{1,2},{2,3},{3,4},{4,5},{5,6},{6,7},{7,8},{8,9},{9,10},{10,1... | collective-permute-start | bytes 1179656 | tf_op jit(solution)/shard_map/ppermute | solution.py:195
  19.3 12.5 %collective-permute-start.3 = (f32[6,256,64]{1,2,0:T(8,128)S(1)}, f32[6,256,64]{1,2,0:T(8,128)}, u32[]{:S(2)}, u32[]{:S(2)}) collective-permute-start(f32[6,256,64]{1,2,0:T(8,128)S(1)} %copy.13), channel_id=1, source_target_pairs={{1,0},{2,1},{3,2},{4,3},{5,4},{6,5},{7,6},{8,7},{9,8},{10,9},{11,1... | collective-permute-start | bytes 1179656 | tf_op jit(solution)/shard_map/ppermute | solution.py:195
  49.5 7.8 %collective-permute-start.4 = (f32[2,2,72,128]{3,2,1,0:T(8,128)}, f32[2,2,72,128]{3,2,1,0:T(8,128)S(1)}, u32[]{:S(2)}, u32[]{:S(2)}) collective-permute-start(f32[2,2,72,128]{3,2,1,0:T(8,128)} %get-tuple-element.8), channel_id=1, source_target_pairs={{0,16},{16,32},{32,48},{48,64},{64,80},{80,96},{96,112},{1,17},{17... | collective-permute-start | bytes 442376 | tf_op jit(solution)/shard_map/ppermute | solution.py:458
  53.1 8.1 %collective-permute-start.5 = (f32[2,2,72,128]{3,2,1,0:T(8,128)}, f32[2,2,72,128]{3,2,1,0:T(8,128)S(1)}, u32[]{:S(2)}, u32[]{:S(2)}) collective-permute-start(f32[2,2,72,128]{3,2,1,0:T(8,128)} %get-tuple-element.10), channel_id=1, source_target_pairs={{16,0},{32,16},{48,32},{64,48},{80,64},{96,80},{112,96},{17,1},{33... | collective-permute-start | bytes 442376 | tf_op jit(solution)/shard_map/ppermute | solution.py:459
  62.7 15.2 %copy-start.1 = (f32[2,2,128,128]{3,2,1,0:T(8,128)S(1)}, f32[2,2,128,128]{3,2,1,0:T(8,128)}, u32[]{:S(2)}) copy-start(f32[2,2,128,128]{3,2,1,0:T(8,128)} %get-tuple-element.9.refs_0_) | copy-start | bytes 786436
  62.8 12.9 %collective-permute-start.6 = (f32[2,2,258,65]{2,1,3,0:T(2,128)S(1)}, f32[2,2,258,65]{2,1,3,0:T(2,128)S(1)}, u32[]{:S(2)}, u32[]{:S(2)}) collective-permute-start(f32[2,2,258,65]{2,1,3,0:T(2,128)S(1)} %copy.19), channel_id=1, source_target_pairs={{0,1},{1,2},{2,3},{3,4},{4,5},{5,6},{6,7},{7,8},{8,9},{9,10},{10,1... | collective-permute-start | bytes 804968 | tf_op jit(solution)/shard_map/ppermute | solution.py:195
  65.1 12.6 %collective-permute-start.7 = (f32[2,2,258,65]{2,1,3,0:T(2,128)S(1)}, f32[2,2,258,65]{2,1,3,0:T(2,128)S(1)}, u32[]{:S(2)}, u32[]{:S(2)}) collective-permute-start(f32[2,2,258,65]{2,1,3,0:T(2,128)S(1)} %copy.20), channel_id=1, source_target_pairs={{1,0},{2,1},{3,2},{4,3},{5,4},{6,5},{7,6},{8,7},{9,8},{10,9},{11,1... | collective-permute-start | bytes 804968 | tf_op jit(solution)/shard_map/ppermute | solution.py:195
  79.7 0.7 copy-start.6

commit v15 on v12

--- a/solution.py
+++ b/solution.py
@@ -434,14 +434,7 @@
         if iteration == 0:
             resid_planes = None
         else:
-            peers = lax.axis_size("gx")
-            up = [(i, i + 1) for i in range(peers - 1)]
-            down = [(j, i) for i, j in up]
-            before = lax.ppermute(bottom, "gx", up)[:, :, slab - width :]
-            after = lax.ppermute(top, "gx", down)[:, :, :width]
-            tall = jnp.concatenate([before, solution, after], axis=2)
-            left, right = exchange_axis(tall, "gy", 3, width)
-            padded = jnp.concatenate([left, tall, right], axis=3)
+            padded = assemble(exchange(solution, width, width), solution, 2)
             padded = grid_ghost(padded, width, edges, signs)
             tile_rows = -(-padded.shape[2] // 8) * 8 - padded.shape[2]
             tile_cols = -(-padded.shape[3] // 128) * 128 - padded.shape[3]

time: 98.1 us -> 106 us (1.081)
  the two profiles are of different devices: /device:TPU:6 before, /device:TPU:12 now
where the time goes in v15:
time: 106 us; the launch traced here: 105 us
  starting transfers between devices  44.8 us (42%)
  Pallas kernels  26 us (25%)
  local copies, waits for them, and re-layouts  14.2 us (13%)
  waiting for transfers between devices  10.2 us (10%)
  other arithmetic  6.72 us (6%)
  between operations  3.14 us (3%)
    ppermute x8, starting transfers between devices, exchange(): pieces[dr, dc] = lax.ppermute(slab, ('gx', 'gy'), perm)  28.7 us
    pallas_call x2, Pallas kernels, solve_local_kernel(): pl.pallas_call(kernel, out_shape=[jax.ShapeDtypeStruct(s, dtype) for s in...  26 us
    ppermute x4, starting transfers between devices, exchange_axis(): return (lax.ppermute(last, axis, up), lax.ppermute(first, axis, down))  16.1 us
    ppermute x8, waiting for transfers between devices, exchange(): pieces[dr, dc] = lax.ppermute(slab, ('gx', 'gy'), perm)  5.79 us
    ppermute x4, waiting for transfers between devices, exchange_axis(): return (lax.ppermute(last, axis, up), lax.ppermute(first, axis, down))  4.36 us
    slice x2, local copies, waits for them, and re-layouts, exchange(): slab = lax.slice_in_dim(slab, breadth - col_width, breadth, axis=x.ndim - 1)  2.51 us
  transfers between devices with their start and end apart: 12, of which 5 were waited for; matrix products, arithmetic and copies ran while one was open for 5% of the time, Pallas kernels for 0%

profile of v15, /device:TPU:12, one launch (start us, length us, event | category | flops | bytes accessed | tf_op | source)
XLA Modules:
  0.0 105.0 jit_solution(10516808478088133660)
XLA Ops:
  0.0 0.9 fusion.13
  1.0 0.1 reshape_squeeze.12
  1.0 0.9 fusion.2
  2.0 3.1 %collective-permute-start = (f32[6,64,128]{2,1,0:T(8,128)S(1)}, f32[6,64,128]{2,1,0:T(8,128)S(1)}, u32[]{:S(2)}, u32[]{:S(2)}) collective-permute-start(f32[6,64,128]{2,1,0:T(8,128)S(1)} %pad_maximum_fusion.5), channel_id=1, source_target_pairs={{0,16},{16,32},{32,48},{48,64},{64,80},{80,96},{96,112},{1,17},{17... | collective-permute-start | bytes 589832 | tf_op jit(solution)/shard_map/ppermute | solution.py:195
  5.1 0.1 reshape_squeeze.13
  5.2 0.9 fusion.1
  6.1 3.6 %collective-permute-start.1 = (f32[6,64,128]{2,1,0:T(8,128)S(1)}, f32[6,64,128]{2,1,0:T(8,128)S(1)}, u32[]{:S(2)}, u32[]{:S(2)}) collective-permute-start(f32[6,64,128]{2,1,0:T(8,128)S(1)} %fusion.1), channel_id=1, source_target_pairs={{16,0},{32,16},{48,32},{64,48},{80,64},{96,80},{112,96},{17,1},{33... | collective-permute-start | bytes 589832 | tf_op jit(solution)/shard_map/ppermute | solution.py:195
  9.8 0.7 fusion.14
  13.2 0.1 or_or_fusion
  13.3 0.0 collective-permute-done
  13.4 2.4 %collective-permute-done.1 = f32[6,64,128]{2,1,0:T(8,128)S(1)} collective-permute-done((f32[6,64,128]{2,1,0:T(8,128)S(1)}, f32[6,64,128]{2,1,0:T(8,128)S(1)}, u32[]{:S(2)}, u32[]{:S(2)}) %collective-permute-start.1) | collective-permute-done | bytes 196640 | tf_op jit(solution)/shard_map/ppermute | solution.py:195
  15.8 0.2 fusion.8
  16.1 0.1 select_maximum_fusion.1
  16.1 0.2 copy.11
  16.4 0.0 copy-start.3
  16.4 2.1 %collective-permute-start.2 = (f32[6,256,64]{1,2,0:T(8,128)S(1)}, f32[6,256,64]{1,2,0:T(8,128)}, u32[]{:S(2)}, u32[]{:S(2)}) collective-permute-start(f32[6,256,64]{1,2,0:T(8,128)S(1)} %copy.11), channel_id=1, source_target_pairs={{0,1},{1,2},{2,3},{3,4},{4,5},{5,6},{6,7},{7,8},{8,9},{9,10},{10,1... | collective-permute-start | bytes 1179656 | tf_op jit(solution)/shard_map/ppermute | solution.py:195
  18.5 0.1 select_maximum_fusion
  18.5 0.2 copy.13
  18.8 7.3 %collective-permute-start.3 = (f32[6,256,64]{1,2,0:T(8,128)S(1)}, f32[6,256,64]{1,2,0:T(8,128)}, u32[]{:S(2)}, u32[]{:S(2)}) collective-permute-start(f32[6,256,64]{1,2,0:T(8,128)S(1)} %copy.13), channel_id=1, source_target_pairs={{1,0},{2,1},{3,2},{4,3},{5,4},{6,5},{7,6},{8,7},{9,8},{10,9},{11,1... | collective-permute-start | bytes 1179656 | tf_op jit(solution)/shard_map/ppermute | solution.py:195
  26.0 0.6 pad_add_fusion.rect_ref
  26.6 0.1 reshape.91
  26.7 0.1 reshape.92
  26.8 0.3 multiply_bitcast_fusion
  27.1 1.0 reshape.95.refs_1_.wcol_ref
  28.1 1.2 %collective-permute-done.2 = f32[6,256,64]{1,2,0:T(8,128)} collective-permute-done((f32[6,256,64]{1,2,0:T(8,128)S(1)}, f32[6,256,64]{1,2,0:T(8,128)}, u32[]{:S(2)}, u32[]{:S(2)}) %collective-permute-start.2) | collective-permute-done | bytes 393248 | tf_op jit(solution)/shard_map/ppermute | solution.py:195
  29.3 1.0 slice.153
  30.3 0.2 copy.23
  30.6 0.7 collective-permute-done.3
  31.3 1.0 slice.155
  32.3 0.2 copy.24
  32.5 0.8 slice.156
  33.3 0.1 copy.19
  33.4 0.8 slice.157
  34.2 0.1 copy.20
  34.3 0.2 copy.17
  34.5 0.2 multiply_bitcast_fusion.1
  34.7 1.2 %reshape.90.refs_0_.wrow_ref = f32[2,128,256]{2,1,0:T(8,128)} reshape(f32[2,2,64,2,2,64]{5,4,3,2,1,0:T(2,128)S(1)} %multiply_bitcast_fusion.1) | data formatting | bytes 524288 | tf_op jit(solution)/shard_map/reshape | solution.py:341
  35.9 1.6 %pad_maximum_fusion.data_ref = f32[5,256,256]{2,1,0:T(8,128)} fusion(f32[5,256,64]{2,1,0:T(8,128)S(1)} %copy.24, f32[5,64,128]{2,1,0:T(8,128)S(1)} %slice.151, f32[1,128,128]{2,1,0:T(8,128)S(1)} %bitcast.43, f32[4,128,128]{2,1,0:T(8,128)S(1)} %bitcast.39, f32[5,64,128]{2,1,0:T(8,128)S(1)} %slice.150, f32[5,256,64]{2,1,0:T(8,128)S(1)} %copy.23), kind=kLoop, calls=%fused_computation.4 | loop fusion | flops 1638400 | bytes 2621440 | tf_op jit(solution)/shard_map/concatenate | solution.py:415
  37.5 11.8 %shard_map.64 = (f32[2,2,128,128]{3,2,1,0:T(8,128)}, f32[2,2,72,128]{3,2,1,0:T(8,128)}, f32[2,2,72,128]{3,2,1,0:T(8,128)}) custom-call(s32[4]{0:T(128)} %pad_add_fusion.rect_ref, f32[5,256,256]{2,1,0:T(8,128)} %pad_maximum_fusion.data_ref, f32[2,128,256]{2,1,0:T(8,128)} %reshape.90.refs_0_.wrow_ref, f32[2,256,128]{2,1,0:T(8,128)} %reshape.95.refs_1_.wcol_ref), custom_call_target="tpu_custom_call" | custom-call | tf_op jit(solution)/shard_map/pallas_call | solution.py:370
  49.3 1.2 %fusion.11 = (f32[2,2,128,65]{3,2,1,0:T(8,128)S(1)}, f32[2,2,128,65]{3,2,1,0:T(8,128)S(1)}) fusion(f32[2,2,128,128]{3,2,1,0:T(8,128)} %get-tuple-element.6.refs_0_), kind=kLoop, calls=%fused_computation.42 | loop fusion | bytes 532480 | tf_op jit(solution)/shard_map/slice | solution.py:171
  50.5 1.3 %fusion.9 = (f32[2,2,65,65]{3,2,1,0:T(8,128)S(1)}, f32[2,2,65,65]{3,2,1,0:T(8,128)S(1)}, f32[2,2,65,65]{3,2,1,0:T(8,128)S(1)}, f32[2,2,65,65]{3,2,1,0:T(8,128)S(1)}) fusion(f32[2,2,128,128]{3,2,1,0:T(8,128)} %get-tuple-element.6.refs_0_), kind=kLoop, calls=%fused_computation.40 | loop fusion | bytes 540800 | tf_op jit(solution)/shard_map/slice | solution.py:171
  51.8 1.9 %collective-permute-start.4 = (f32[2,2,128,65]{3,2,1,0:T(8,128)S(1)}, f32[2,2,128,65]{3,2,1,0:T(8,128)S(1)}, u32[]{:S(2)}, u32[]{:S(2)}) collective-permute-start(f32[2,2,128,65]{3,2,1,0:T(8,128)S(1)} %get-tuple-element.21), channel_id=1, source_target_pairs={{0,1},{1,2},{2,3},{3,4},{4,5},{5,6},{6,7},{7,8},{8,9},{9,10},{10,1... | collective-permute-start | bytes 399368 | tf_op jit(solution)/shard_map/ppermute | solution.py:182
  53.8 7.5 %collective-permute-start.5 = (f32[2,2,128,65]{3,2,1,0:T(8,128)S(1)}, f32[2,2,128,65]{3,2,1,0:T(8,128)S(1)}, u32[]{:S(2)}, u32[]{:S(2)}) collective-permute-start(f32[2,2,128,65]{3,2,1,0:T(8,128)S(1)} %get-tuple-element.22), channel_id=1, source_target_pairs={{1,0},{2,1},{3,2},{4,3},{5,4},{6,5},{7,6},{8,7},{9,8},{10,9},{11,1... | collective-permute-start | bytes 399368 | tf_op jit(solution)/shard_map/ppermute | solution.py:182
  61.3 1.9 %collective-permute-start.11 = (f32[2,2,65,65]{3,2,1,0:T(8,128)S(1)}, f32[2,2,65,65]{3,2,1,0:T(8,128)S(1)}, u32[]{:S(2)}, u32[]{:S(2)}) collective-permute-start(f32[2,2,65,65]{3,2,1,0:T(8,128)S(1)} %get-tuple-element.16), channel_id=1, source_target_pairs={{17,0},{18,1},{19,2},{20,3},{21,4},{22,5},{23,6},{24,7},{25,8},{26... | collective-permute-start | bytes 202808 | tf_op jit(solution)/shard_map/ppermute | solution.py:182
  63.2 3.6 %collective-permute-start.6 = (f32[2,2,65,65]{3,2,1,0:T(8,128)S(1)}, f32[2,2,65,65]{3,2,1,0:T(8,128)S(1)}, u32[]{:S(2)}, u32[]{:S(2)}) collective-permute-start(f32[2,2,65,65]{3,2,1,0:T(8,128)S(1)} %get-tuple-element.15), channel_id=1, source_target_pairs={{0,17},{1,18},{2,19},{3,20},{4,21},{5,22},{6,23},{7,24},{8,25},{9,... | collective-permute-start | bytes 202808 | tf_op jit(solution)/shard_map/ppermute | solution.py:182
  66.9 4.7 %collective-permute-start.8 = (f32[2,2,65,65]{3,2,1,0:T(8,128)S(1)}, f32[2,2,65,65]{3,2,1,0:T(8,128)S(1)}, u32[]{:S(2)}, u32[]{:S(2)}) collective-permute-start(f32[2,2,65,65]{3,2,1,0:T(8,128)S(1)} %get-tuple-element.18), channel_id=1, source_target_pairs={{1,16},{2,17},{3,18},{4,19},{5,20},{6,21},{7,22},{8,23},{9,24},{10... | collective-permute-start | bytes 202808 | tf_op jit(solution)/shard_map/ppermute | solution.py:182
  71.7 0.0 collective-permute-done.4
  71.7 1.9 %collective-permute-start.9 = (f32[2,2,65,65]{3,2,1,0:T(8,128)S(1)}, f32[2,2,65,65]{3,2,1,0:T(8,128)S(1)}, u32[]{:S(2)}, u32[]{:S(2)}) collective-permute-start(f32[2,2,65,65]{3,2,1,0:T(8,128)S(1)} %get-tuple-element.17), channel_id=1, source_target_pairs={{16,1},{17,2},{18,3},{19,4},{20,5},{21,6},{22,7},{23,8},{24,9},{25... | collective-permute-start | bytes 202808 | tf_op jit(solution)/shard_map/ppermute | solution.py:182
  73.6 0.0 collective-permute-done.5
  73.6 5.0 %collective-permute-start.10 = (f32[2,2,65,128]{3,2,1,0:T(8,128)S(1)}, f32[2,2,65,128]{3,2,1,0:T(8,128)S(1)}, u32[]{:S(2)}, u32[]{:S(2)}) collective-permute-start(f32[2,2,65,128]{3,2,1,0:T(8,128)S(1)} %get-tuple-element.20), channel_id=1, source_target_pairs={{16,0},{17,1},{18,2},{19,3},{20,4},{21,5},{22,6},{23,7},{24,8},{25... | collective-permute-start | bytes 399368 | tf_op jit(solution)/shard_map/ppermute | solution.py:182
  78.6 0.1 pad_maximum_fusion.8
  78.7 0.0 collective-permute-done.11
  78.7 2.1 %collective-permute-start.7 = (f32[2,2,65,128]{3,2,1,0:T(8,128)S(1)}, f32[2,2,65,128]{3,2,1,0:T(8,128)S(1)}, u32[]{:S(2)}, u32[]{:S(2)}) collective-permute-start(f32[2,2,65,128]{3,2,1,0:T(8,128)S(1)} %get-tuple-element.19), channel_id=1, source_target_pairs={{0,16},{1,17},{2,18},{3,19},{4,20},{5,21},{6,22},{7,23},{8,24},{9,... | collective-permute-start | bytes 399368 | tf_op jit(solution)/shard_map/ppermute | solution.py:182
  80.8 0.0 collective-permute-done.6
  80.8 3.1 %collective-permute-done.10 = f32[2,2,65,128]{3,2,1,0:T(8,128)S(1)} collective-permute-done((f32[2,2,65,128]{3,2,1,0:T(8,128)S(1)}, f32[2,2,65,128]{3,2,1,0:T(8,128)S(1)}, u32[]{:S(2)}, u32[]{:S(2)}) %collective-permute-start.10) | collective-permute-done | bytes 133152 | tf_op jit(solution)/shard_map/ppermute | solution.py:182
  83.9 2.7 %collective-permute-done.7 = f32[2,2,65,128]{3,2,1,0:T(8,128)S(1)} collective-permute-done((f32[2,2,65,128]{3,2,1,0:T(8,128)S(1)}, f32[2,2,65,128]{3,2,1,0:T(8,128)S(1)}, u32[]{:S(2)}, u32[]{:S(2)}) %collective-permute-start.7) | collective-permute-done | bytes 133152 | tf_op jit(solution)/shard_map/ppermute | solution.py:182
  86.6 0.7 fusion
  87.4 0.8 slice_reduce_fusion.1
  88.2 0.3 select_select_fusion
  88.5 0.3 copy-done.5
  88.8 0.2 multiply_add_fusion
  89.0 0.4 maximum_select_fusion.1
  89.4 1.3 %pad.13 = f32[2,2,264,384]{3,2,1,0:T(8,128)} pad(f32[2,2,258,258]{3,2,1,0:T(8,128)S(1)} %maximum_select_fusion.1, f32[]{:T(128)} %constant.31.clone.1), padding=0_0x0_0x0_6x0_126 | pad | bytes 2687044 | tf_op jit(solution)/shard_map/jit(_pad)/pad | solution.py:441
  90.8 14.2 %shard_map.65 = f32[2,2,128,128]{3,2,1,0:T(8,128)} custom-call(s32[4]{0:T(128)} %pad_add_fusion.rect_ref, f32[4,264,384]{2,1,0:T(8,128)} %bitcast.35, f32[5,256,256]{2,1,0:T(8,128)} %pad_maximum_fusion.data_ref, f32[2,128,256]{2,1,0:T(8,128)} %reshape.90.refs_0_.wrow_ref, f32[2,256,128]{2,1,0:T(8,128)} %reshape.95.refs_1_.wcol_ref, ...), custom_call_target="tpu_custom_call" | custom-call | tf_op jit(solution)/shard_map/pallas_call | solution.py:370
  (30 shorter events, 0.2 us)
Async XLA Ops:
  0.0 15.8 %copy-start.1 = (f32[2,2,128,128]{3,2,1,0:T(8,128)S(1)}, f32[2,2,128,128]{3,2,1,0:T(8,128)}, u32[]{:S(2)}) copy-start(f32[2,2,128,128]{3,2,1,0:T(8,128)} %param.6) | copy-start | bytes 786436
  0.0 15.8 %copy-start.2 = (f32[128,128]{1,0:T(8,128)S(1)}, f32[128,128]{1,0:T(8,128)}, u32[]{:S(2)}) copy-start(f32[128,128]{1,0:T(8,128)} %param.7) | copy-start | bytes 196612
  0.0 9.8 %copy-start.4 = (f32[2,2,64,64]{3,2,1,0:T(8,128)S(1)}, f32[2,2,64,64]{3,2,1,0:T(8,128)}, u32[]{:S(2)}) copy-start(f32[2,2,64,64]{3,2,1,0:T(8,128)} %param.8) | copy-start | bytes 196612
  0.0 9.8 %copy-start.6 = (s32[1,1,4]{2,1,0:T(1,128)S(1)}, s32[1,1,4]{2,1,0:T(1,128)}, u32[]{:S(2)}) copy-start(s32[1,1,4]{2,1,0:T(1,128)} %param.10) | copy-start | bytes 52
  2.0 11.4 %collective-permute-start = (f32[6,64,128]{2,1,0:T(8,128)S(1)}, f32[6,64,128]{2,1,0:T(8,128)S(1)}, u32[]{:S(2)}, u32[]{:S(2)}) collective-permute-start(f32[6,64,128]{2,1,0:T(8,128)S(1)} %pad_maximum_fusion.5), channel_id=1, source_target_pairs={{0,16},{16,32},{32,48},{48,64},{64,80},{80,96},{96,112},{1,17},{17... | collective-permute-start | bytes 589832 | tf_op jit(solution)/shard_map/ppermute | solution.py:195
  6.1 9.6 %collective-permute-start.1 = (f32[6,64,128]{2,1,0:T(8,128)S(1)}, f32[6,64,128]{2,1,0:T(8,128)S(1)}, u32[]{:S(2)}, u32[]{:S(2)}) collective-permute-start(f32[6,64,128]{2,1,0:T(8,128)S(1)} %fusion.1), channel_id=1, source_target_pairs={{16,0},{32,16},{48,32},{64,48},{80,64},{96,80},{112,96},{17,1},{33... | collective-permute-start | bytes 589832 | tf_op jit(solution)/shard_map/ppermute | solution.py:195
  16.4 10.4 %copy-start.3 = (f32[2,2,64,64]{3,2,1,0:T(8,128)S(1)}, f32[2,2,64,64]{3,2,1,0:T(8,128)}, u32[]{:S(2)}) copy-start(f32[2,2,64,64]{3,2,1,0:T(8,128)} %param.9) | copy-start | bytes 196612
  16.4 12.9 %collective-permute-start.2 = (f32[6,256,64]{1,2,0:T(8,128)S(1)}, f32[6,256,64]{1,2,0:T(8,128)}, u32[]{:S(2)}, u32[]{:S(2)}) collective-permute-start(f32[6,256,64]{1,2,0:T(8,128)S(1)} %copy.11), channel_id=1, source_target_pairs={{0,1},{1,2},{2,3},{3,4},{4,5},{5,6},{6,7},{7,8},{8,9},{9,10},{10,1... | collective-permute-start | bytes 1179656 | tf_op jit(solution)/shard_map/ppermute | solution.py:195
  18.8 12.5 %collective-permute-start.3 = (f32[6,256,64]{1,2,0:T(8,128)S(1)}, f32[6,256,64]{1,2,0:T(8,128)}, u32[]{:S(2)}, u32[]{:S(2)}) collective-permute-start(f32[6,256,64]{1,2,0:T(8,128)S(1)} %copy.13), channel_id=1, source_target_pairs={{1,0},{2,1},{3,2},{4,3},{5,4},{6,5},{7,6},{8,7},{9,8},{10,9},{11,1... | collective-permute-start | bytes 1179656 | tf_op jit(solution)/shard_map/ppermute | solution.py:195
  49.3 22.3 %copy-start = (f32[2,2,128,128]{3,2,1,0:T(8,128)S(1)}, f32[2,2,128,128]{3,2,1,0:T(8,128)}, u32[]{:S(2)}) copy-start(f32[2,2,128,128]{3,2,1,0:T(8,128)} %get-tuple-element.6.refs_0_) | copy-start | bytes 786436
  51.8 19.8 %collective-permute-start.4 = (f32[2,2,128,65]{3,2,1,0:T(8,128)S(1)}, f32[2,2,128,65]{3,2,1,0:T(8,128)S(1)}, u32[]{:S(2)}, u32[]{:S(2)}) collective-permute-start(f32[2,2,128,65]{3,2,1,0:T(8,128)S(1)} %get-tuple-element.21), channel_id=1, source_target_pairs={{0,1},{1,2},{2,3},{3,4},{4,5},{5,6},{6,7},{7,8},{8,9},{9,10},{10,1... | collective-permute-start | bytes 399368 | tf_op jit(solution)/shard_map/ppermute | solution.py:182
  53.8 19.8 %collective-permute-start.5 = (f32[2,2,128,65]{3,2,1,0:T(8,128)S(1)}, f32[2,2,128,65]{3,2,1,0:T(8,128)S(1)}, u32[]{:S(2)}, u32[]{:S(2)}) collective-permute-start(f32[2,2,128,65]{3,2,1,0:T(8,128)S(1)} %get-tuple-element.22), channel_id=1, source_target_pairs={{1,0},{2,1},{3,2},{4,3},{5,4},{6,5},{7,6},{8,7},{9,8},{10,9},{11,1... | collective-permute-start | bytes 399368 | tf_op jit(solution)/shard_map/ppermute | solution.py:182
  61.3 17.4 %collective-permute-start.11 = (f32[2,2,65,65]{3,2,1,0:T(8,128)S(1)}, f32[2,2,65,65]{3,2,1,0:T(8,128)S(1)}, u32[]{:S(2)}, u32[]{:S(2)}) collective-permute-start(f32[2,2,65,65]{3,2,1,0:T(8,128)S(1)} %get-tuple-element.16), channel_id=1, source_target_pairs={{17,0},{18,1},{19,2},{20,3},{21,4},{22,5},{23,6},{24,7},{25,8},{26... | collective-permute-start | bytes 202808 | tf_op jit(solution)/shard_map/ppermute | solution.py:182
  63.2 17.6 %collective-permute-start.6 = (f32[2,2,65,65]{3,2,1,0:T(8,128)S(1)}, f32[2,2,65,65]{3,2,1,0:T(8,128)S(1)}, u32[]{:S(2)}, u32[]{:S(2)}) collective-permute-start(f32[2,2,65,65]{3,2,1,0:T(8,128)S(1)} %get-tuple-element.15), channel_id=1, source_target_pairs={{0,17},{1,18},{2,19},{3,20},{4,21},{5,22},{6,23},{7,24},{8,25},{9,... | collective-permute-start | bytes 202808 | tf_op jit(solution)/shard_map/ppermute | solution.py:182
  66.9 14.0 %collective-permute-start.8 = (f32[2,2,65,65]{3,2,1,0:T(8,128)S(1)}, f32[2,2,65,65]{3,2,1,0:T(8,128)S(1)}, u32[]{:S(2)}, u32[]{:S(2)}) collective-permute-start(f32[2,2,65,65]{3,2,1,0:T(8,128)S(1)} %get-tuple-element.18), channel_id=1, source_target_pairs={{1,16},{2,17},{3,18},{4,19},{5,20},{6,21},{7,22},{8,23},{9,24},{10... | collective-permute-start | bytes 202808 | tf_op jit(solution)/shard_map/ppermute | solution.py:182
  71.7 9.2 %collective-permute-start.9 = (f32[2,2,65,65]{3,2,1,0:T(8,128)S(1)}, f32[2,2,65,65]{3,2,1,0:T(8,128)S(1)}, u32[]{:S(2)}, u32[]{:S(2)}) collective-permute-start(f32[2,2,65,65]{3,2,1,0:T(8,128)S(1)} %get-tuple-element.17), channel_id=1, source_target_pairs={{16,1},{17,2},{18,3},{19,4},{20,5},{21,6},{22,7},{23,8},{24,9},{25... | collective-permute-start | bytes 202808 | tf_op jit(solution)/shard_map/ppermute | solution.py:182
  73.6 10.3 %collective-permute-start.10 = (f32[2,2,65,128]{3,2,1,0:T(8,128)S(1)}, f32[2,2,65,128]{3,2,1,0:T(8,128)S(1)}, u32[]{:S(2)}, u32[]{:S(2)}) collective-permute-start(f32[2,2,65,128]{3,2,1,0:T(8,128)S(1)} %get-tuple-element.20), channel_id=1, source_target_pairs={{16,0},{17,1},{18,2},{19,3},{20,4},{21,5},{22,6},{23,7},{24,8},{25... | collective-permute-start | bytes 399368 | tf_op jit(solution)/shard_map/ppermute | solution.py:182
  78.7 7.9 %collective-permute-start.7 = (f32[2,2,65,128]{3,2,1,0:T(8,128)S(1)}, f32[2,2,65,128]{3,2,1,0:T(8,128)S(1)}, u32[]{:S(2)}, u32[]{:S(2)}) collective-permute-start(f32[2,2,65,128]{3,2,1,0:T(8,128)S(1)} %get-tuple-element.19), channel_id=1, source_target_pairs={{0,16},{1,17},{2,18},{3,19},{4,20},{5,21},{6,22},{7,23},{8,24},{9,... | collective-permute-start | bytes 399368 | tf_op jit(solution)/shard_map/ppermute | solution.py:182
  88.2 0.7 copy-start.5

commit v16 on v12

--- a/solution.py
+++ b/solution.py
@@ -289,12 +289,17 @@
     def dot(a, b):
         return jnp.dot(a, b, precision=lax.Precision.HIGH, preferred_element_type=jnp.float32)
 
+    def dot_t(a, b):
+        return lax.dot_general(
+            a, b, (((1,), (1,)), ((), ())), precision=lax.Precision.HIGH, preferred_element_type=jnp.float32
+        )
+
     def rows_apply(real_part, imag_part, sign):
         outs_r, outs_i = ([], [])
         for h in range(breadth // half):
             cols = slice(h * half, (h + 1) * half)
-            prod_r = dot(real_part[:, cols], wrow_ref[h])
-            prod_i = dot(imag_part[:, cols], wrow_ref[h])
+            prod_r = dot_t(real_part[:, cols], wrow_ref[h])
+            prod_i = dot_t(imag_part[:, cols], wrow_ref[h])
             outs_r.append(prod_r[:, :half] - sign * prod_i[:, half:])
             outs_i.append(prod_i[:, :half] + sign * prod_r[:, half:])
         return (jnp.concatenate(outs_r, axis=1), jnp.concatenate(outs_i, axis=1))
@@ -335,13 +340,18 @@
 
 def line_matrices(row_blocks, col_blocks):
     block = row_blocks.shape[-1]
-    eye = jnp.eye(2, dtype=row_blocks.dtype)
-    halves = row_blocks.shape[0] // 2
-    rows_t = jnp.transpose(row_blocks, (0, 3, 1, 2)).reshape(halves, 2, block, 2, block)
-    row_mats = jnp.einsum("hakmo,ab->hakmbo", rows_t, eye).reshape(halves, 2 * block, 4 * block)
-    cols = col_blocks.reshape(halves, 2, 2, block, block)
-    col_mats = jnp.einsum("hamok,ab->hmaobk", cols, eye).reshape(halves, 4 * block, 2 * block)
-    return row_mats, col_mats
+
+    def pairs(blocks):
+        mats = []
+        for h in range(blocks.shape[0] // 2):
+            parts = []
+            for m in range(2):
+                for a in range(2):
+                    parts.append(jnp.pad(blocks[2 * h + a, m], ((0, 0), (a * block, (1 - a) * block))))
+            mats.append(jnp.concatenate(parts, axis=0))
+        return jnp.stack(mats)
+
+    return pairs(row_blocks), pairs(col_blocks)
 
 
 def solve_local_kernel(resid_planes, data_ext, row_mats, col_mats, live_rect, own_shape, slab, base=None, last=False,

time: 98.1 us -> 98.3 us (level)
  waiting for transfers between devices: 17.2 us -> 22.8 us
  local copies, waits for them, and re-layouts: 11.6 us -> 7.53 us
  starting transfers between devices: 30.5 us -> 28.2 us
  other arithmetic: 7.97 us -> 9.16 us
    ppermute x6, waiting for transfers between devices: 11.4 us -> 17.4 us  [exchange_axis(): return (lax.ppermute(last, axis, up), lax.ppermute(first, axis, down))]
    reshape x5 -> x0, local copies, waits for them, and re-layouts: 2.54 us -> none  [the longest x1 1.18 us: line_matrices(): jnp.einsum('hakmo,ab->hakmbo', rows_t, eye)]
    ppermute x6, starting transfers between devices: 24.6 us -> 22.4 us  [exchange_axis(): return (lax.ppermute(last, axis, up), lax.ppermute(first, axis, down))]
    another operation x1 -> x6, other arithmetic: 0.01 us -> 1.79 us  [pairs(): return jnp.stack(mats)]
where the time goes in v16:
time: 98.3 us; the launch traced here: 96.7 us
  starting transfers between devices  28.2 us (29%)
  Pallas kernels  25.9 us (26%)
  waiting for transfers between devices  22.8 us (23%)
  other arithmetic  9.16 us (9%)
  local copies, waits for them, and re-layouts  7.53 us (8%)
  between operations  3.01 us (3%)
    pallas_call x2, Pallas kernels, solve_local_kernel(): pl.pallas_call(kernel, out_shape=[jax.ShapeDtypeStruct(s, dtype) for s in...  25.9 us
    ppermute x6, starting transfers between devices, exchange_axis(): return (lax.ppermute(last, axis, up), lax.ppermute(first, axis, down))  22.4 us
    ppermute x6, waiting for transfers between devices, exchange_axis(): return (lax.ppermute(last, axis, up), lax.ppermute(first, axis, down))  17.4 us
    ppermute x1, waiting for transfers between devices, shards(): after = lax.ppermute(top, 'gx', down)[:, :, :width]  4.07 us
    ppermute x1, starting transfers between devices, shards(): before = lax.ppermute(bottom, 'gx', up)[:, :, slab - width:]  3.17 us
    ppermute x1, starting transfers between devices, shards(): after = lax.ppermute(top, 'gx', down)[:, :, :width]  2.66 us
  transfers between devices with their start and end apart: 8, of which 7 were waited for; matrix products, arithmetic and copies ran while one was open for 5% of the time, Pallas kernels for 0%

profile of v16, /device:TPU:6, one launch (start us, length us, event | category | flops | bytes accessed | tf_op | source)
XLA Modules:
  0.0 96.7 jit_solution(12452112776110233267)
XLA Ops:
  0.0 0.9 fusion.17
  1.0 0.1 reshape_squeeze.12
  1.0 0.9 fusion.1
  2.0 3.8 %collective-permute-start = (f32[6,64,128]{2,1,0:T(8,128)S(1)}, f32[6,64,128]{2,1,0:T(8,128)S(1)}, u32[]{:S(2)}, u32[]{:S(2)}) collective-permute-start(f32[6,64,128]{2,1,0:T(8,128)S(1)} %pad_maximum_fusion.7), channel_id=1, source_target_pairs={{0,16},{16,32},{32,48},{48,64},{64,80},{80,96},{96,112},{1,17},{17... | collective-permute-start | bytes 589832 | tf_op jit(solution)/shard_map/ppermute | solution.py:195
  5.7 0.1 reshape_squeeze.13
  5.8 0.9 fusion
  6.8 2.1 %collective-permute-start.1 = (f32[6,64,128]{2,1,0:T(8,128)S(1)}, f32[6,64,128]{2,1,0:T(8,128)S(1)}, u32[]{:S(2)}, u32[]{:S(2)}) collective-permute-start(f32[6,64,128]{2,1,0:T(8,128)S(1)} %fusion), channel_id=1, source_target_pairs={{16,0},{32,16},{48,32},{64,48},{80,64},{96,80},{112,96},{17,1},{33... | collective-permute-start | bytes 589832 | tf_op jit(solution)/shard_map/ppermute | solution.py:195
  8.9 0.7 fusion.18
  12.1 0.6 pad_add_fusion.rect_ref
  12.8 0.0 collective-permute-done
  12.8 3.1 %collective-permute-done.1 = f32[6,64,128]{2,1,0:T(8,128)S(1)} collective-permute-done((f32[6,64,128]{2,1,0:T(8,128)S(1)}, f32[6,64,128]{2,1,0:T(8,128)S(1)}, u32[]{:S(2)}, u32[]{:S(2)}) %collective-permute-start.1) | collective-permute-done | bytes 196640 | tf_op jit(solution)/shard_map/ppermute | solution.py:195
  15.9 0.0 copy-done
  15.9 0.0 copy-done.2
  16.0 0.2 fusion.14
  16.2 0.3 copy-done.5
  16.6 0.1 select_maximum_fusion
  16.6 0.2 copy.9
  16.9 0.0 slice-start
  16.9 0.0 copy-start.3
  16.9 5.1 %collective-permute-start.3 = (f32[6,256,64]{1,2,0:T(8,128)S(1)}, f32[6,256,64]{1,2,0:T(8,128)S(1)}, u32[]{:S(2)}, u32[]{:S(2)}) collective-permute-start(f32[6,256,64]{1,2,0:T(8,128)S(1)} %copy.9), channel_id=1, source_target_pairs={{1,0},{2,1},{3,2},{4,3},{5,4},{6,5},{7,6},{8,7},{9,8},{10,9},{11,1... | collective-permute-start | bytes 1179656 | tf_op jit(solution)/shard_map/ppermute | solution.py:195
  22.1 0.1 select_maximum_fusion.1
  22.1 0.2 copy.7
  22.4 1.9 %collective-permute-start.2 = (f32[6,256,64]{1,2,0:T(8,128)S(1)}, f32[6,256,64]{1,2,0:T(8,128)S(1)}, u32[]{:S(2)}, u32[]{:S(2)}) collective-permute-start(f32[6,256,64]{1,2,0:T(8,128)S(1)} %copy.7), channel_id=1, source_target_pairs={{0,1},{1,2},{2,3},{3,4},{4,5},{5,6},{6,7},{7,8},{8,9},{9,10},{10,1... | collective-permute-start | bytes 1179656 | tf_op jit(solution)/shard_map/ppermute | solution.py:195
  24.3 0.1 reshape.73
  24.4 0.1 reshape.72
  24.5 0.1 fusion.2
  24.6 0.1 fusion.3
  24.7 0.7 pad_maximum_fusion.5.refs_1_.wcol_ref
  25.4 1.9 %collective-permute-done.3 = f32[6,256,64]{1,2,0:T(8,128)S(1)} collective-permute-done((f32[6,256,64]{1,2,0:T(8,128)S(1)}, f32[6,256,64]{1,2,0:T(8,128)S(1)}, u32[]{:S(2)}, u32[]{:S(2)}) %collective-permute-start.3) | collective-permute-done | bytes 393248 | tf_op jit(solution)/shard_map/ppermute | solution.py:195
  27.3 0.1 copy.12
  27.5 7.6 %collective-permute-done.2 = f32[6,256,64]{1,2,0:T(8,128)S(1)} collective-permute-done((f32[6,256,64]{1,2,0:T(8,128)S(1)}, f32[6,256,64]{1,2,0:T(8,128)S(1)}, u32[]{:S(2)}, u32[]{:S(2)}) %collective-permute-start.2) | collective-permute-done | bytes 393248 | tf_op jit(solution)/shard_map/ppermute | solution.py:195
  35.1 0.1 copy.11
  35.2 0.2 copy.19
  35.5 0.2 copy.20
  35.7 0.1 fusion.4
  35.8 0.1 fusion.5
  35.9 0.7 pad_maximum_fusion.4.refs_0_.wrow_ref
  36.6 1.6 %pad_maximum_fusion.1.data_ref = f32[5,256,256]{2,1,0:T(8,128)} fusion(f32[5,256,64]{2,1,0:T(8,128)S(1)} %copy.20, f32[5,64,128]{2,1,0:T(8,128)S(1)} %slice.191, f32[1,128,128]{2,1,0:T(8,128)S(1)} %bitcast.74, f32[4,128,128]{2,1,0:T(8,128)S(1)} %bitcast.70, f32[5,64,128]{2,1,0:T(8,128)S(1)} %slice.190, f32[5,256,64]{2,1,0:T(8,128)S(1)} %copy.19), kind=kLoop, calls=%fused_computation.4 | loop fusion | flops 1638400 | bytes 2621440 | tf_op jit(solution)/shard_map/concatenate | solution.py:425
  38.3 11.7 %shard_map.64 = (f32[2,2,128,128]{3,2,1,0:T(8,128)}, f32[2,2,72,128]{3,2,1,0:T(8,128)}, f32[2,2,72,128]{3,2,1,0:T(8,128)}) custom-call(s32[4]{0:T(128)} %pad_add_fusion.rect_ref, f32[5,256,256]{2,1,0:T(8,128)} %pad_maximum_fusion.1.data_ref, f32[2,256,128]{2,1,0:T(8,128)} %pad_maximum_fusion.4.refs_0_.wrow_ref, f32[2,256,128]{2,1,0:T(8,128)} %pad_maximum_fusion.5.refs_1_.wcol_ref), custom_call_target="tpu_custom_call" | custom-call | tf_op jit(solution)/shard_map/pallas_call | solution.py:380
  50.0 3.2 %collective-permute-start.4 = (f32[2,2,72,128]{3,2,1,0:T(8,128)}, f32[2,2,72,128]{3,2,1,0:T(8,128)S(1)}, u32[]{:S(2)}, u32[]{:S(2)}) collective-permute-start(f32[2,2,72,128]{3,2,1,0:T(8,128)} %get-tuple-element.8), channel_id=1, source_target_pairs={{0,16},{16,32},{32,48},{48,64},{64,80},{80,96},{96,112},{1,17},{17... | collective-permute-start | bytes 442376 | tf_op jit(solution)/shard_map/ppermute | solution.py:450
  53.2 2.7 %collective-permute-start.5 = (f32[2,2,72,128]{3,2,1,0:T(8,128)}, f32[2,2,72,128]{3,2,1,0:T(8,128)S(1)}, u32[]{:S(2)}, u32[]{:S(2)}) collective-permute-start(f32[2,2,72,128]{3,2,1,0:T(8,128)} %get-tuple-element.10), channel_id=1, source_target_pairs={{16,0},{32,16},{48,32},{64,48},{80,64},{96,80},{112,96},{17,1},{33... | collective-permute-start | bytes 442376 | tf_op jit(solution)/shard_map/ppermute | solution.py:451
  55.9 1.4 %collective-permute-done.4 = f32[2,2,72,128]{3,2,1,0:T(8,128)S(1)} collective-permute-done((f32[2,2,72,128]{3,2,1,0:T(8,128)}, f32[2,2,72,128]{3,2,1,0:T(8,128)S(1)}, u32[]{:S(2)}, u32[]{:S(2)}) %collective-permute-start.4) | collective-permute-done | bytes 147488 | tf_op jit(solution)/shard_map/ppermute | solution.py:450
  57.2 4.1 %collective-permute-done.5 = f32[2,2,72,128]{3,2,1,0:T(8,128)S(1)} collective-permute-done((f32[2,2,72,128]{3,2,1,0:T(8,128)}, f32[2,2,72,128]{3,2,1,0:T(8,128)S(1)}, u32[]{:S(2)}, u32[]{:S(2)}) %collective-permute-start.5) | collective-permute-done | bytes 147488 | tf_op jit(solution)/shard_map/ppermute | solution.py:451
  61.3 1.0 %pad_maximum_fusion.3 = f32[2,2,258,128]{3,2,1,0:T(8,128)S(1)} fusion(f32[2,2,65,128]{3,2,1,0:T(8,128)S(1)} %bitcast.75, f32[2,2,128,128]{3,2,1,0:T(8,128)} %get-tuple-element.9.refs_0_, f32[2,2,65,128]{3,2,1,0:T(8,128)S(1)} %slice.208), kind=kLoop, calls=%fused_computation.13 | loop fusion | flops 264192 | bytes 1056768 | tf_op jit(solution)/shard_map/concatenate | solution.py:452
  62.3 0.2 fusion.15
  62.5 0.3 copy.13
  62.8 2.1 %collective-permute-start.6 = (f32[2,2,258,65]{2,1,3,0:T(2,128)S(1)}, f32[2,2,258,65]{2,1,3,0:T(2,128)S(1)}, u32[]{:S(2)}, u32[]{:S(2)}) collective-permute-start(f32[2,2,258,65]{2,1,3,0:T(2,128)S(1)} %copy.13), channel_id=1, source_target_pairs={{0,1},{1,2},{2,3},{3,4},{4,5},{5,6},{6,7},{7,8},{8,9},{9,10},{10,1... | collective-permute-start | bytes 804968 | tf_op jit(solution)/shard_map/ppermute | solution.py:195
  64.9 0.3 copy.14
  65.2 7.4 %collective-permute-start.7 = (f32[2,2,258,65]{2,1,3,0:T(2,128)S(1)}, f32[2,2,258,65]{2,1,3,0:T(2,128)S(1)}, u32[]{:S(2)}, u32[]{:S(2)}) collective-permute-start(f32[2,2,258,65]{2,1,3,0:T(2,128)S(1)} %copy.14), channel_id=1, source_target_pairs={{1,0},{2,1},{3,2},{4,3},{5,4},{6,5},{7,6},{8,7},{9,8},{10,9},{11,1... | collective-permute-start | bytes 804968 | tf_op jit(solution)/shard_map/ppermute | solution.py:195
  72.7 0.1 or_or_fusion
  72.8 3.0 %collective-permute-done.6 = f32[2,2,258,65]{2,1,3,0:T(2,128)S(1)} collective-permute-done((f32[2,2,258,65]{2,1,3,0:T(2,128)S(1)}, f32[2,2,258,65]{2,1,3,0:T(2,128)S(1)}, u32[]{:S(2)}, u32[]{:S(2)}) %collective-permute-start.6) | collective-permute-done | bytes 268352 | tf_op jit(solution)/shard_map/ppermute | solution.py:195
  75.7 0.3 copy.15
  76.0 1.8 %collective-permute-done.7 = f32[2,2,258,65]{2,1,3,0:T(2,128)S(1)} collective-permute-done((f32[2,2,258,65]{2,1,3,0:T(2,128)S(1)}, f32[2,2,258,65]{2,1,3,0:T(2,128)S(1)}, u32[]{:S(2)}, u32[]{:S(2)}) %collective-permute-start.7) | collective-permute-done | bytes 268352 | tf_op jit(solution)/shard_map/ppermute | solution.py:195
  77.8 0.3 copy.16
  78.1 0.6 pad_maximum_fusion
  78.8 0.2 select_select_fusion.1
  79.0 0.8 slice_reduce_fusion.1
  79.8 0.0 copy-start.6
  79.8 0.4 select_select_fusion
  80.3 0.2 copy-done.6
  80.5 0.2 multiply_add_fusion
  80.7 0.5 maximum_select_fusion
  81.2 1.3 %pad.79 = f32[2,2,264,384]{3,2,1,0:T(8,128)} pad(f32[2,2,258,258]{3,2,1,0:T(8,128)S(1)} %maximum_select_fusion, f32[]{:T(128)} %constant.31.clone.1), padding=0_0x0_0x0_6x0_126 | pad | bytes 2687044 | tf_op jit(solution)/shard_map/jit(_pad)/pad | solution.py:458
  82.5 14.2 %shard_map.65 = f32[2,2,128,128]{3,2,1,0:T(8,128)} custom-call(s32[4]{0:T(128)} %pad_add_fusion.rect_ref, f32[4,264,384]{2,1,0:T(8,128)} %bitcast.66, f32[5,256,256]{2,1,0:T(8,128)} %pad_maximum_fusion.1.data_ref, f32[2,256,128]{2,1,0:T(8,128)} %pad_maximum_fusion.4.refs_0_.wrow_ref, f32[2,256,128]{2,1,0:T(8,128)} %pad_maximum_fusion.5.refs_1_.wcol_ref, ...), custom_call_target="tpu_custom_call" | custom-call | tf_op jit(solution)/shard_map/pallas_call | solution.py:380
  (33 shorter events, 0.3 us)
Async XLA Ops:
  0.0 15.9 %copy-start = (f32[2,2,128,128]{3,2,1,0:T(8,128)S(1)}, f32[2,2,128,128]{3,2,1,0:T(8,128)}, u32[]{:S(2)}) copy-start(f32[2,2,128,128]{3,2,1,0:T(8,128)} %param.6) | copy-start | bytes 786436
  0.0 15.9 %copy-start.2 = (f32[128,128]{1,0:T(8,128)S(1)}, f32[128,128]{1,0:T(8,128)}, u32[]{:S(2)}) copy-start(f32[128,128]{1,0:T(8,128)} %param.7) | copy-start | bytes 196612
  0.0 8.9 %copy-start.7 = (s32[1,1,4]{2,1,0:T(1,128)S(1)}, s32[1,1,4]{2,1,0:T(1,128)}, u32[]{:S(2)}) copy-start(s32[1,1,4]{2,1,0:T(1,128)} %param.10) | copy-start | bytes 52
  0.0 12.7 %copy-start.4 = (f32[2,2,64,64]{3,2,1,0:T(8,128)S(1)}, f32[2,2,64,64]{3,2,1,0:T(8,128)}, u32[]{:S(2)}) copy-start(f32[2,2,64,64]{3,2,1,0:T(8,128)} %param.8) | copy-start | bytes 196612
  2.0 10.8 %collective-permute-start = (f32[6,64,128]{2,1,0:T(8,128)S(1)}, f32[6,64,128]{2,1,0:T(8,128)S(1)}, u32[]{:S(2)}, u32[]{:S(2)}) collective-permute-start(f32[6,64,128]{2,1,0:T(8,128)S(1)} %pad_maximum_fusion.7), channel_id=1, source_target_pairs={{0,16},{16,32},{32,48},{48,64},{64,80},{80,96},{96,112},{1,17},{17... | collective-permute-start | bytes 589832 | tf_op jit(solution)/shard_map/ppermute | solution.py:195
  6.8 9.2 %collective-permute-start.1 = (f32[6,64,128]{2,1,0:T(8,128)S(1)}, f32[6,64,128]{2,1,0:T(8,128)S(1)}, u32[]{:S(2)}, u32[]{:S(2)}) collective-permute-start(f32[6,64,128]{2,1,0:T(8,128)S(1)} %fusion), channel_id=1, source_target_pairs={{16,0},{32,16},{48,32},{64,48},{80,64},{96,80},{112,96},{17,1},{33... | collective-permute-start | bytes 589832 | tf_op jit(solution)/shard_map/ppermute | solution.py:195
  15.9 0.7 copy-start.5
  16.9 7.4 %slice-start = ((f32[6,64,128]{2,1,0:T(8,128)}), f32[1,64,128]{2,1,0:T(8,128)S(1)}, s32[]{:S(2)}) async-start(f32[6,64,128]{2,1,0:T(8,128)} %copy-done.5), calls=%async_computation | async-start | bytes 65536 | tf_op jit(solution)/shard_map/slice | solution.py:431
  16.9 7.5 %copy-start.3 = (f32[2,2,64,64]{3,2,1,0:T(8,128)S(1)}, f32[2,2,64,64]{3,2,1,0:T(8,128)}, u32[]{:S(2)}) copy-start(f32[2,2,64,64]{3,2,1,0:T(8,128)} %param.9) | copy-start | bytes 196612
  16.9 10.4 %collective-permute-start.3 = (f32[6,256,64]{1,2,0:T(8,128)S(1)}, f32[6,256,64]{1,2,0:T(8,128)S(1)}, u32[]{:S(2)}, u32[]{:S(2)}) collective-permute-start(f32[6,256,64]{1,2,0:T(8,128)S(1)} %copy.9), channel_id=1, source_target_pairs={{1,0},{2,1},{3,2},{4,3},{5,4},{6,5},{7,6},{8,7},{9,8},{10,9},{11,1... | collective-permute-start | bytes 1179656 | tf_op jit(solution)/shard_map/ppermute | solution.py:195
  22.4 12.7 %collective-permute-start.2 = (f32[6,256,64]{1,2,0:T(8,128)S(1)}, f32[6,256,64]{1,2,0:T(8,128)S(1)}, u32[]{:S(2)}, u32[]{:S(2)}) collective-permute-start(f32[6,256,64]{1,2,0:T(8,128)S(1)} %copy.7), channel_id=1, source_target_pairs={{0,1},{1,2},{2,3},{3,4},{4,5},{5,6},{6,7},{7,8},{8,9},{9,10},{10,1... | collective-permute-start | bytes 1179656 | tf_op jit(solution)/shard_map/ppermute | solution.py:195
  50.0 7.2 %collective-permute-start.4 = (f32[2,2,72,128]{3,2,1,0:T(8,128)}, f32[2,2,72,128]{3,2,1,0:T(8,128)S(1)}, u32[]{:S(2)}, u32[]{:S(2)}) collective-permute-start(f32[2,2,72,128]{3,2,1,0:T(8,128)} %get-tuple-element.8), channel_id=1, source_target_pairs={{0,16},{16,32},{32,48},{48,64},{64,80},{80,96},{96,112},{1,17},{17... | collective-permute-start | bytes 442376 | tf_op jit(solution)/shard_map/ppermute | solution.py:450
  53.2 8.1 %collective-permute-start.5 = (f32[2,2,72,128]{3,2,1,0:T(8,128)}, f32[2,2,72,128]{3,2,1,0:T(8,128)S(1)}, u32[]{:S(2)}, u32[]{:S(2)}) collective-permute-start(f32[2,2,72,128]{3,2,1,0:T(8,128)} %get-tuple-element.10), channel_id=1, source_target_pairs={{16,0},{32,16},{48,32},{64,48},{80,64},{96,80},{112,96},{17,1},{33... | collective-permute-start | bytes 442376 | tf_op jit(solution)/shard_map/ppermute | solution.py:451
  62.8 15.2 %copy-start.1 = (f32[2,2,128,128]{3,2,1,0:T(8,128)S(1)}, f32[2,2,128,128]{3,2,1,0:T(8,128)}, u32[]{:S(2)}) copy-start(f32[2,2,128,128]{3,2,1,0:T(8,128)} %get-tuple-element.9.refs_0_) | copy-start | bytes 786436
  62.8 12.9 %collective-permute-start.6 = (f32[2,2,258,65]{2,1,3,0:T(2,128)S(1)}, f32[2,2,258,65]{2,1,3,0:T(2,128)S(1)}, u32[]{:S(2)}, u32[]{:S(2)}) collective-permute-start(f32[2,2,258,65]{2,1,3,0:T(2,128)S(1)} %copy.13), channel_id=1, source_target_pairs={{0,1},{1,2},{2,3},{3,4},{4,5},{5,6},{6,7},{7,8},{8,9},{9,10},{10,1... | collective-permute-start | bytes 804968 | tf_op jit(solution)/shard_map/ppermute | solution.py:195
  65.2 12.6 %collective-permute-start.7 = (f32[2,2,258,65]{2,1,3,0:T(2,128)S(1)}, f32[2,2,258,65]{2,1,3,0:T(2,128)S(1)}, u32[]{:S(2)}, u32[]{:S(2)}) collective-permute-start(f32[2,2,258,65]{2,1,3,0:T(2,128)S(1)} %copy.14), channel_id=1, source_target_pairs={{1,0},{2,1},{3,2},{4,3},{5,4},{6,5},{7,6},{8,7},{9,8},{10,9},{11,1... | collective-permute-start | bytes 804968 | tf_op jit(solution)/shard_map/ppermute | solution.py:195
  79.8 0.7 copy-start.6
